TPU v7x, 32 devices: a whole 2x2x4 slice. The times are simulated.
32 devices in a mesh: row: 8 (over z, x), col: 4 (over y, core).
Axes of the slice: x: 2, y: 2, z: 4, core: 2. Of those that a mesh axis runs over, the one named last changes fastest.
Arguments:
- low_rhs: bfloat16 [32, 512, 128], P(('row', 'col')), may hold values from -6 to 6
- low_inv: bfloat16 [32, 512, 512], P(('row', 'col'))
- low_tiles: bfloat16 [32, 4, 512, 512], P(('row', 'col')), may hold values from -0.03125 to 0.03125
- tile_rows: int32 [32, 4], P(('row', 'col')), may hold values from -1 to 3, as said below
- tile_cols: int32 [32, 4], P(('row', 'col')), may hold values from 0 to 31, as said below
- top_rhs: bfloat16 [4, 512, 128], P(None, 'row'), may hold values from -6 to 6
- top_inv: bfloat16 [4, 512, 512], P(None, 'row')
- top_tiles: bfloat16 [6, 512, 512], P(None, 'row'), may hold values from -0.125 to 0.125
Outputs:
- low_solution: float32 [32, 512, 128], P(('row', 'col'))
- top_solution: float32 [4, 512, 128], P(None, 'row')
Inputs may be any that keep to these rules, and one draw needn't show every extreme that they name: `tile_rows`: in each block's list of 4 slots the used slots come first and name top-level blocks; the remaining slots hold -1. Some list has only its first slot used and some list is full. Slot s of block j names a block of j's aligned group of 4 blocks (j // 4 == tile_cols[j, s] // 4); an empty slot names j itself.
All inputs are finite; a program needn't handle non-finite values.
Results may differ from a plain program's by a relative error of at most 0.022.
Values may be sent and summed in bfloat16 or wider, within the bound.
No kernel may reach another device: no remote copies, remote signals or barrier semaphores. Data moves between devices by JAX's collectives and lax.ppermute only.
A program may use at most 64 MiB of HBM per device.

v0:
```python
import jax
import jax.numpy as jnp
from jax import lax
from jax.sharding import PartitionSpec as P


def local(low_rhs, low_inv, low_tiles, tile_rows, tile_cols, top_rhs, top_inv, top_tiles):
    peers = lax.axis_size("col")
    levels = top_rhs.shape[0]
    share = top_rhs.shape[1]
    position = lax.axis_index("row")
    slot_rows = tile_rows[0]
    slot_cols = tile_cols[0] % peers
    alive = slot_rows >= 0
    safe_rows = jnp.maximum(slot_rows, 0)
    own_tiles = low_tiles[0]
    low_forward = jnp.dot(low_inv[0], low_rhs[0], preferred_element_type=jnp.float32).astype(
        jnp.bfloat16
    )
    panels = lax.all_gather(low_forward[None], "col", axis=0, tiled=True)
    products = jnp.einsum(
        "sab,sbk->sak", own_tiles, panels[slot_cols], preferred_element_type=jnp.float32
    )
    pick_level = (slot_rows[:, None] == jnp.arange(levels, dtype=jnp.int32)[None, :]).astype(
        jnp.float32
    )
    coupling = jnp.einsum("st,sak->tak", pick_level, products, precision=lax.Precision.HIGHEST)
    whole_sum = lax.psum(coupling.astype(jnp.bfloat16), "col")
    coupled = lax.psum_scatter(whole_sum, "row", scatter_dimension=1, tiled=True).astype(
        jnp.float32
    )
    top_back = [None] * levels
    top_slices = [None] * levels
    top_forward = []
    for level in range(levels):
        residue = top_rhs[level].astype(jnp.float32) - coupled[level]
        if level > 0:
            first = level * (level - 1) // 2
            earlier = jnp.stack(top_forward)
            residue = residue - jnp.einsum(
                "uab,ubk->ak",
                top_tiles[first : first + level],
                earlier,
                preferred_element_type=jnp.float32,
            )
        whole_residue = lax.all_gather(residue.astype(jnp.bfloat16), "row", axis=0, tiled=True)
        solved_part = jnp.dot(
            top_inv[level], whole_residue, preferred_element_type=jnp.float32
        ).astype(jnp.bfloat16)
        top_forward.append(lax.all_gather(solved_part, "row", axis=0, tiled=True))
    for level in reversed(range(levels)):
        update = lax.dynamic_slice_in_dim(top_forward[level], position * share, share, 0).astype(
            jnp.float32
        )
        if level < levels - 1:
            later = list(range(level + 1, levels))
            tiles_below = jnp.stack([top_tiles[k * (k - 1) // 2 + level] for k in later])
            slices_below = jnp.stack(
                [lax.dynamic_slice_in_dim(top_back[k], position * share, share, 0) for k in later]
            )
            partial_term = jnp.einsum(
                "kab,kac->bc", tiles_below, slices_below, preferred_element_type=jnp.float32
            )
            update = update - lax.psum_scatter(
                partial_term.astype(jnp.bfloat16), "row", scatter_dimension=0, tiled=True
            ).astype(jnp.float32)
        local_part = jnp.einsum(
            "ab,ac->bc",
            top_inv[level],
            update.astype(jnp.bfloat16),
            preferred_element_type=jnp.float32,
        )
        solution = lax.psum(local_part.astype(jnp.bfloat16), "row").astype(jnp.float32)
        top_slices[level] = lax.dynamic_slice_in_dim(solution, position * share, share, 0)
        top_back[level] = solution.astype(jnp.bfloat16)
    back_stack = jnp.stack(top_back)
    products_back = jnp.einsum(
        "sab,sak->sbk", own_tiles, back_stack[safe_rows], preferred_element_type=jnp.float32
    )
    pick_peer = (
        (slot_cols[:, None] == jnp.arange(peers, dtype=jnp.int32)[None, :]) & alive[:, None]
    ).astype(jnp.float32)
    terms = jnp.einsum("sp,sbk->pbk", pick_peer, products_back, precision=lax.Precision.HIGHEST)
    returned = lax.psum_scatter(
        terms.astype(jnp.bfloat16), "col", scatter_dimension=0, tiled=True
    ).astype(jnp.float32)
    low_update = (low_forward.astype(jnp.float32) - returned[0]).astype(jnp.bfloat16)
    low_solution = jnp.einsum(
        "ab,ac->bc", low_inv[0], low_update, preferred_element_type=jnp.float32
    )
    return (low_solution[None], jnp.stack(top_slices))


def solution(mesh):
    in_specs = (
        P(("row", "col"), None, None),
        P(("row", "col"), None, None),
        P(("row", "col"), None, None, None),
        P(("row", "col"), None),
        P(("row", "col"), None),
        P(None, "row", None),
        P(None, "row", None),
        P(None, "row", None),
    )
    out_specs = (P(("row", "col"), None, None), P(None, "row", None))
    return jax.shard_map(local, mesh=mesh, in_specs=in_specs, out_specs=out_specs, check_vma=False)
```

profile of v0, /device:TPU:0, one launch (start us, length us, event | category | flops | bytes accessed | tf_op | source)
XLA Modules:
  0.0 905.1 jit_solution(3152110872918101658)
XLA Ops:
  7.2 1.5 convolution_convert_fusion.1
  8.7 8.7 all-gather
  17.4 0.7 fusion.99
  18.1 1.4 gather_fusion
  19.5 1.9 fusion.4
  21.4 1.3 copy.37
  22.7 3.2 convolution_convert_fusion
  26.0 0.6 dynamic-slice
  27.2 72.4 %all-reduce.18.cloned.1.call-done = bf16[4,512,128]{2,0,1:T(4,128)(2,1)} async-done(((bf16[4,512,128]{2,0,1:T(4,128)(2,1)}), bf16[4,512,128]{2,0,1:T(4,128)(2,1)}) %all-reduce.18.cloned.1.call-update) | async-done | bytes 524304
  99.6 0.9 constant_dynamic-slice_fusion.3
  100.5 0.6 copy.38
  101.2 32.1 %all-reduce.16.cloned.1.call-done = bf16[4,64,128]{2,1,0:T(8,128)(2,1)} async-done(((bf16[4,64,128]{2,1,0:T(8,128)(2,1)}), bf16[4,64,128]{2,1,0:T(8,128)(2,1)}) %all-reduce.16.cloned.1.call-update) | async-done | bytes 65552 | tf_op jit(solution)/shard_map/psum | solution.py:28
  133.2 0.8 convert_element_type.161
  134.1 30.7 %all-gather.1 = bf16[1,512,128]{2,1,0:T(8,128)(2,1)S(1)} all-gather(bf16[1,64,128]{2,1,0:T(8,128)(2,1)S(1)} %fusion.76), channel_id=3, replica_groups=mesh['row'=8,'col'=4] {'row'}, dimensions={1}, use_global_device_ids=true | all-gather | bytes 147456 | tf_op jit(solution)/shard_map/all_gather | solution.py:46
  164.8 0.2 fusion.23
  164.9 30.6 %all_gather.29 = bf16[512,128]{1,0:T(8,128)(2,1)S(1)} all-gather(bf16[64,128]{1,0:T(8,128)(2,1)S(1)} %fusion.23), channel_id=1, replica_groups=mesh['row'=8,'col'=4] {'row'}, dimensions={0}, use_global_device_ids=true | all-gather | bytes 147456 | tf_op jit(solution)/shard_map/all_gather | solution.py:50
  195.5 0.2 fusion.20
  195.6 30.5 %all_gather.30 = bf16[512,128]{1,0:T(8,128)(2,1)S(1)} all-gather(bf16[64,128]{1,0:T(8,128)(2,1)S(1)} %fusion.20), channel_id=1, replica_groups=mesh['row'=8,'col'=4] {'row'}, dimensions={0}, use_global_device_ids=true | all-gather | bytes 147456 | tf_op jit(solution)/shard_map/all_gather | solution.py:46
  226.2 0.2 fusion.24
  226.3 30.6 %all_gather.31 = bf16[512,128]{1,0:T(8,128)(2,1)S(1)} all-gather(bf16[64,128]{1,0:T(8,128)(2,1)S(1)} %fusion.24), channel_id=1, replica_groups=mesh['row'=8,'col'=4] {'row'}, dimensions={0}, use_global_device_ids=true | all-gather | bytes 147456 | tf_op jit(solution)/shard_map/all_gather | solution.py:50
  256.9 0.2 fusion.22
  257.1 30.6 %all_gather.32 = bf16[512,128]{1,0:T(8,128)(2,1)S(1)} all-gather(bf16[64,128]{1,0:T(8,128)(2,1)S(1)} %fusion.22), channel_id=1, replica_groups=mesh['row'=8,'col'=4] {'row'}, dimensions={0}, use_global_device_ids=true | all-gather | bytes 147456 | tf_op jit(solution)/shard_map/all_gather | solution.py:46
  287.7 0.2 fusion.25
  287.8 30.6 %all_gather.33 = bf16[512,128]{1,0:T(8,128)(2,1)S(1)} all-gather(bf16[64,128]{1,0:T(8,128)(2,1)S(1)} %fusion.25), channel_id=1, replica_groups=mesh['row'=8,'col'=4] {'row'}, dimensions={0}, use_global_device_ids=true | all-gather | bytes 147456 | tf_op jit(solution)/shard_map/all_gather | solution.py:50
  318.4 1.0 fusion.21
  319.4 30.5 %all_gather.34 = bf16[512,128]{1,0:T(8,128)(2,1)S(1)} all-gather(bf16[64,128]{1,0:T(8,128)(2,1)S(1)} %fusion.21), channel_id=1, replica_groups=mesh['row'=8,'col'=4] {'row'}, dimensions={0}, use_global_device_ids=true | all-gather | bytes 147456 | tf_op jit(solution)/shard_map/all_gather | solution.py:46
  349.9 0.2 fusion.26
  350.1 30.5 %all_gather.35 = bf16[512,128]{1,0:T(8,128)(2,1)S(1)} all-gather(bf16[64,128]{1,0:T(8,128)(2,1)S(1)} %fusion.26), channel_id=1, replica_groups=mesh['row'=8,'col'=4] {'row'}, dimensions={0}, use_global_device_ids=true | all-gather | bytes 147456 | tf_op jit(solution)/shard_map/all_gather | solution.py:50
  380.6 0.9 fusion.12
  381.5 70.7 %all-reduce.8.cloned.1.call-done = bf16[512,128]{0,1:T(8,128)(2,1)} async-done(((bf16[512,128]{0,1:T(8,128)(2,1)}), bf16[512,128]{0,1:T(8,128)(2,1)}) %all-reduce.8.cloned.1.call-update) | async-done | bytes 131088 | tf_op jit(solution)/shard_map/psum | solution.py:73
  452.2 0.9 constant_dynamic-slice_fusion.2
  453.1 0.9 fusion.13
  454.1 62.9 %reduce-scatter.5.cloned.1.call-done = bf16[64,128]{1,0:T(8,128)(2,1)} async-done(((bf16[512,128]{1,0:T(8,128)(2,1)}), bf16[64,128]{1,0:T(8,128)(2,1)}) %reduce-scatter.5.cloned.1.call-update) | async-done | bytes 16400 | tf_op jit(solution)/shard_map/reduce_scatter | solution.py:64
  516.9 1.6 fusion.14
  518.6 0.7 fusion.104
  519.3 0.1 copy.41
  519.3 70.9 %all-reduce.10.cloned.1.call-done = bf16[512,128]{0,1:T(8,128)(2,1)} async-done(((bf16[512,128]{0,1:T(8,128)(2,1)}), bf16[512,128]{0,1:T(8,128)(2,1)}) %all-reduce.10.cloned.1.call-update) | async-done | bytes 131088 | tf_op jit(solution)/shard_map/psum | solution.py:73
  590.3 0.9 constant_dynamic-slice_fusion.1
  591.2 0.1 copy.40
  591.3 1.8 fusion.10
  593.1 61.9 %reduce-scatter.7.cloned.1.call-done = bf16[64,128]{1,0:T(8,128)(2,1)} async-done(((bf16[512,128]{1,0:T(8,128)(2,1)}), bf16[64,128]{1,0:T(8,128)(2,1)}) %reduce-scatter.7.cloned.1.call-update) | async-done | bytes 16400 | tf_op jit(solution)/shard_map/reduce_scatter | solution.py:64
  655.0 1.6 fusion.15
  656.7 71.8 %all-reduce.12.cloned.1.call-done = bf16[512,128]{0,1:T(8,128)(2,1)} async-done(((bf16[512,128]{0,1:T(8,128)(2,1)}), bf16[512,128]{0,1:T(8,128)(2,1)}) %all-reduce.12.cloned.1.call-update) | async-done | bytes 131088 | tf_op jit(solution)/shard_map/psum | solution.py:73
  728.5 0.8 constant_dynamic-slice_fusion
  729.3 0.1 copy.42
  729.4 1.8 fusion.11
  731.3 62.1 %reduce-scatter.9.cloned.1.call-done = bf16[64,128]{1,0:T(8,128)(2,1)} async-done(((bf16[512,128]{1,0:T(8,128)(2,1)}), bf16[64,128]{1,0:T(8,128)(2,1)}) %reduce-scatter.9.cloned.1.call-update) | async-done | bytes 16400 | tf_op jit(solution)/shard_map/reduce_scatter | solution.py:64
  793.4 1.6 fusion.16
  795.1 71.8 %all-reduce.14.cloned.1.call-done = bf16[512,128]{0,1:T(8,128)(2,1)} async-done(((bf16[512,128]{0,1:T(8,128)(2,1)}), bf16[512,128]{0,1:T(8,128)(2,1)}) %all-reduce.14.cloned.1.call-update) | async-done | bytes 131088 | tf_op jit(solution)/shard_map/psum | solution.py:73
  866.9 1.0 pad_maximum_fusion
  868.0 1.4 gather_fusion.1
  869.3 1.5 fusion.7
  870.8 1.3 copy.43
  872.1 2.4 fusion.90
  874.5 0.9 copy.53
  875.4 0.1 copy.48
  875.5 0.1 copy.47
  875.6 0.1 copy.46
  875.7 0.9 dynamic-slice_convert_fusion
  876.5 0.1 copy.45
  876.6 0.7 pad_maximum_fusion.1
  877.3 19.0 %reduce-scatter.11.cloned.1.call-done = bf16[1,512,128]{2,1,0:T(8,128)(2,1)} async-done(((bf16[4,512,128]{2,1,0:T(8,128)(2,1)}), bf16[1,512,128]{2,1,0:T(8,128)(2,1)}) %reduce-scatter.11.cloned.1.call-update) | async-done | bytes 131088 | tf_op jit(solution)/shard_map/reduce_scatter | solution.py:84
  896.3 1.2 convolution_bitcast_fusion
  897.5 0.8 copy.49
  (62 shorter events, 0.7 us)
Async XLA Ops:
  7.2 12.3 %copy-start = (bf16[1,4,512,512]{3,2,1,0:T(8,128)(2,1)S(1)}, bf16[1,4,512,512]{3,2,1,0:T(8,128)(2,1)}, u32[]{:S(2)}) copy-start(bf16[1,4,512,512]{3,2,1,0:T(8,128)(2,1)} %param.10) | copy-start | bytes 6291460
  7.2 92.4 %all-reduce.18.cloned.1.call-start = ((), (), s32[]{:S(2)}) async-start(), calls=%async_computation.13 | async-start | bytes 1048576
  19.5 3.2 copy-start.14
  21.4 4.6 copy-start.16
  21.4 143.4 %copy-start.2 = (bf16[4,64,512]{2,1,0:T(8,128)(2,1)S(1)}, bf16[4,64,512]{2,1,0:T(8,128)(2,1)}, u32[]{:S(2)}) copy-start(bf16[4,64,512]{2,1,0:T(8,128)(2,1)} %param.14) | copy-start | bytes 786436
  22.7 111.4 %copy-start.13 = (bf16[4,64,128]{2,1,0:T(8,128)(2,1)S(1)}, bf16[4,64,128]{2,1,0:T(8,128)(2,1)}, u32[]{:S(2)}) copy-start(bf16[4,64,128]{2,1,0:T(8,128)(2,1)} %param.13) | copy-start | bytes 196612
  22.7 172.7 %copy-start.3 = (bf16[6,64,512]{2,1,0:T(8,128)(2,1)S(1)}, bf16[6,64,512]{2,1,0:T(8,128)(2,1)}, u32[]{:S(2)}) copy-start(bf16[6,64,512]{2,1,0:T(8,128)(2,1)} %param.15) | copy-start | bytes 1179652
  25.9 107.3 %all-reduce.16.cloned.1.call-start = ((), (), s32[]{:S(2)}) async-start(), calls=%async_computation.12 | async-start | bytes 131072 | tf_op jit(solution)/shard_map/psum | solution.py:28
  101.1 351.1 %all-reduce.8.cloned.1.call-start = ((), (), s32[]{:S(2)}) async-start(), calls=%async_computation.4 | async-start | bytes 262144 | tf_op jit(solution)/shard_map/psum | solution.py:73
  256.9 124.6 %copy-start.12 = (bf16[512,128]{1,0:T(8,128)(2,1)}, bf16[512,128]{1,0:T(8,128)(2,1)S(1)}, u32[]{:S(2)}) copy-start(bf16[512,128]{1,0:T(8,128)(2,1)S(1)} %all_gather.31) | copy-start | bytes 393220
  318.4 411.0 %slice-start = ((bf16[6,64,512]{2,1,0:T(8,128)(2,1)}), bf16[2,64,512]{2,1,0:T(8,128)(2,1)S(1)}, s32[]{:S(2)}) async-start(bf16[6,64,512]{2,1,0:T(8,128)(2,1)} %param.15), calls=%async_computation.14 | async-start | bytes 262144 | tf_op jit(solution)/shard_map/slice | solution.py:57
  319.4 411.9 %copy-start.15 = (s32[1,4]{1,0:T(1,128)S(1)}, s32[1,4]{1,0:T(1,128)}, u32[]{:S(2)}) copy-start(s32[1,4]{1,0:T(1,128)} %param.12) | copy-start | bytes 52
  381.5 135.4 %reduce-scatter.5.cloned.1.call-start = ((), (), s32[]{:S(2)}) async-start(), calls=%async_computation.5 | async-start | bytes 147456 | tf_op jit(solution)/shard_map/reduce_scatter | solution.py:64
  452.2 414.7 %copy-start.10 = (bf16[512,128]{0,1:T(8,128)(2,1)S(1)}, bf16[512,128]{0,1:T(8,128)(2,1)}, u32[]{:S(2)}) copy-start(bf16[512,128]{0,1:T(8,128)(2,1)} %all-reduce.8.cloned.1.call-done) | copy-start | bytes 393220
  453.1 414.8 %copy-start.4 = (bf16[64,128]{0,1:T(8,128)(2,1)}, bf16[64,128]{0,1:T(8,128)(2,1)S(1)}, u32[]{:S(2)}) copy-start(bf16[64,128]{0,1:T(8,128)(2,1)S(1)} %constant_dynamic-slice_fusion.2) | copy-start | bytes 49156
  454.0 136.2 %all-reduce.10.cloned.1.call-start = ((), (), s32[]{:S(2)}) async-start(), calls=%async_computation.6 | async-start | bytes 262144 | tf_op jit(solution)/shard_map/psum | solution.py:73
  518.5 136.5 %reduce-scatter.7.cloned.1.call-start = ((), (), s32[]{:S(2)}) async-start(), calls=%async_computation.7 | async-start | bytes 147456 | tf_op jit(solution)/shard_map/reduce_scatter | solution.py:64
  590.3 276.6 %copy-start.11 = (bf16[512,128]{0,1:T(8,128)(2,1)S(1)}, bf16[512,128]{0,1:T(8,128)(2,1)}, u32[]{:S(2)}) copy-start(bf16[512,128]{0,1:T(8,128)(2,1)} %all-reduce.10.cloned.1.call-done) | copy-start | bytes 393220
  591.2 276.8 %copy-start.6 = (bf16[64,128]{0,1:T(8,128)(2,1)}, bf16[64,128]{0,1:T(8,128)(2,1)S(1)}, u32[]{:S(2)}) copy-start(bf16[64,128]{0,1:T(8,128)(2,1)S(1)} %constant_dynamic-slice_fusion.1) | copy-start | bytes 49156
  593.0 135.4 %all-reduce.12.cloned.1.call-start = ((), (), s32[]{:S(2)}) async-start(), calls=%async_computation.8 | async-start | bytes 262144 | tf_op jit(solution)/shard_map/psum | solution.py:73
  656.6 136.8 %reduce-scatter.9.cloned.1.call-start = ((), (), s32[]{:S(2)}) async-start(), calls=%async_computation.9 | async-start | bytes 147456 | tf_op jit(solution)/shard_map/reduce_scatter | solution.py:64
  729.3 138.6 %copy-start.8 = (bf16[64,128]{0,1:T(8,128)(2,1)}, bf16[64,128]{0,1:T(8,128)(2,1)S(1)}, u32[]{:S(2)}) copy-start(bf16[64,128]{0,1:T(8,128)(2,1)S(1)} %constant_dynamic-slice_fusion) | copy-start | bytes 49156
  731.2 135.7 %all-reduce.14.cloned.1.call-start = ((), (), s32[]{:S(2)}) async-start(), calls=%async_computation.10 | async-start | bytes 262144 | tf_op jit(solution)/shard_map/psum | solution.py:73
  795.0 101.3 %reduce-scatter.11.cloned.1.call-start = ((), (), s32[]{:S(2)}) async-start(), calls=%async_computation.11 | async-start | bytes 655360 | tf_op jit(solution)/shard_map/reduce_scatter | solution.py:84
  872.1 3.3 copy-start.5
  872.1 3.3 copy-start.7
  872.1 3.4 copy-start.9
  872.1 24.2 %copy-start.1 = (bf16[1,512,512]{2,1,0:T(8,128)(2,1)S(1)}, bf16[1,512,512]{2,1,0:T(8,128)(2,1)}, u32[]{:S(2)}) copy-start(bf16[1,512,512]{2,1,0:T(8,128)(2,1)} %param.9) | copy-start | bytes 1572868
Sparse Core Ops, SparseCore 0:
  26.0 73.4 all-reduce.17
  102.5 30.7 all-reduce.15
  381.6 70.5 all-reduce.7
  455.9 60.9 reduce-scatter.4
  520.7 69.5 all-reduce.9
  594.0 60.9 reduce-scatter.6
  658.9 69.5 all-reduce.11
  732.4 60.9 reduce-scatter.8
  797.3 69.5 all-reduce.13
  875.5 20.7 reduce-scatter.10
where the time goes:
time: 906 us; the launch traced here: 905 us
  waiting for transfers between devices  596 us (66%)
  blocking collectives  253 us (28%)
  matrix products  23.5 us (3%)
  between operations  15.1 us (2%)
  local copies, waits for them, and re-layouts  13.2 us (1%)
    psum x4, waiting for transfers between devices, local(): lax.psum(local_part.astype(jnp.bfloat16), 'row').astype(jnp.float32)  285 us
    reduce_scatter x3, waiting for transfers between devices, local(): lax.psum_scatter(partial_term.astype(jnp.bfloat16), 'row', scatter_dimens...  187 us
    all_gather x4, blocking collectives, local(): lax.all_gather(residue.astype(jnp.bfloat16), 'row', axis=0, tiled=True)  122 us
    all_gather x4, blocking collectives, local(): top_forward.append(lax.all_gather(solved_part, 'row', axis=0, tiled=True))  122 us
    unnamed x11, waiting for transfers between devices  72.5 us
    psum x1, waiting for transfers between devices, local(): whole_sum = lax.psum(coupling.astype(jnp.bfloat16), 'col')  32.1 us
    reduce_scatter x1, waiting for transfers between devices, local(): lax.psum_scatter(terms.astype(jnp.bfloat16), 'col', scatter_dimension=0,...  19 us
  transfers between devices with their start and end apart: 10, of which 10 were waited for; matrix products, arithmetic and copies ran while one was open for 0% of the time, Pallas kernels for 0%

commit v1 on v0

v1 whole, which is shorter than its diff:
```python
import jax
import jax.numpy as jnp
from jax import lax
from jax.sharding import PartitionSpec as P


def shifted(x, axis, size, shift):
    return lax.ppermute(x, axis, [(i, (i + shift) % size) for i in range(size)])


def swapped(x, axis, size, bit):
    return lax.ppermute(x, axis, [(i, i ^ bit) for i in range(size)])


def butterfly_sum(x, axis, size):
    bit = 1
    while bit < size:
        x = x + swapped(x, axis, size, bit)
        bit *= 2
    return x


def local(low_rhs, low_inv, low_tiles, tile_rows, tile_cols, top_rhs, top_inv, top_tiles):
    peers = lax.axis_size("col")
    rows_n = lax.axis_size("row")
    levels = top_rhs.shape[0]
    share = top_rhs.shape[1]
    position = lax.axis_index("row")
    me = lax.axis_index("col")

    stacked = jnp.concatenate([top_inv, top_tiles], axis=0)
    whole = lax.all_gather(stacked, "row", axis=1, tiled=True)
    inv_all = whole[:levels]
    tiles_all = whole[levels:]

    slot_rows = tile_rows[0]
    slot_cols = tile_cols[0] % peers
    alive = slot_rows >= 0
    safe_rows = jnp.maximum(slot_rows, 0)
    own_tiles = low_tiles[0]
    low_forward = jnp.dot(low_inv[0], low_rhs[0], preferred_element_type=jnp.float32).astype(
        jnp.bfloat16
    )
    received = [low_forward] + [shifted(low_forward, "col", peers, s) for s in range(1, peers)]
    order = [(me - s) % peers for s in range(peers)]
    by_source = jnp.stack(received)
    source_of = jnp.stack(order)
    slot_pick = jnp.argmax(source_of[None, :] == slot_cols[:, None], axis=1)
    products = jnp.einsum(
        "sab,sbk->sak", own_tiles, by_source[slot_pick], preferred_element_type=jnp.float32
    )
    pick_level = (slot_rows[:, None] == jnp.arange(levels, dtype=jnp.int32)[None, :]).astype(
        jnp.float32
    )
    coupling = jnp.einsum("st,sak->tak", pick_level, products, precision=lax.Precision.HIGHEST)
    own_rhs = jnp.zeros((levels, share * rows_n, top_rhs.shape[2]), jnp.float32)
    own_rhs = lax.dynamic_update_slice_in_dim(own_rhs, top_rhs.astype(jnp.float32), position * share, 1)
    coupling = coupling - jnp.where(me == 0, own_rhs, 0.0)
    coupling = butterfly_sum(coupling, "col", peers)
    coupling = butterfly_sum(coupling, "row", rows_n)

    top_forward = []
    for level in range(levels):
        residue = -coupling[level]
        for u in range(level):
            residue = residue - jnp.dot(
                tiles_all[level * (level - 1) // 2 + u],
                top_forward[u],
                preferred_element_type=jnp.float32,
            )
        top_forward.append(
            jnp.dot(
                inv_all[level], residue.astype(jnp.bfloat16), preferred_element_type=jnp.float32
            ).astype(jnp.bfloat16)
        )
    top_back = [None] * levels
    top_slices = [None] * levels
    for level in reversed(range(levels)):
        update = top_forward[level].astype(jnp.float32)
        for k in range(level + 1, levels):
            update = update - lax.dot_general(
                tiles_all[k * (k - 1) // 2 + level],
                top_back[k],
                (((0,), (0,)), ((), ())),
                preferred_element_type=jnp.float32,
            )
        solved = lax.dot_general(
            inv_all[level],
            update.astype(jnp.bfloat16),
            (((0,), (0,)), ((), ())),
            preferred_element_type=jnp.float32,
        )
        top_slices[level] = lax.dynamic_slice_in_dim(solved, position * share, share, 0)
        top_back[level] = solved.astype(jnp.bfloat16)
    back_stack = jnp.stack(top_back)
    products_back = jnp.einsum(
        "sab,sak->sbk", own_tiles, back_stack[safe_rows], preferred_element_type=jnp.float32
    )
    pick_peer = (
        (slot_cols[:, None] == source_of[None, :]) & alive[:, None]
    ).astype(jnp.float32)
    terms = jnp.einsum(
        "sp,sbk->pbk", pick_peer, products_back, precision=lax.Precision.HIGHEST
    ).astype(jnp.bfloat16)
    returned = terms[0].astype(jnp.float32)
    for s in range(1, peers):
        returned = returned + shifted(terms[s], "col", peers, peers - s).astype(jnp.float32)
    low_update = (low_forward.astype(jnp.float32) - returned).astype(jnp.bfloat16)
    low_solution = lax.dot_general(
        low_inv[0], low_update, (((0,), (0,)), ((), ())), preferred_element_type=jnp.float32
    )
    return (low_solution[None], jnp.stack(top_slices))


def solution(mesh):
    in_specs = (
        P(("row", "col"), None, None),
        P(("row", "col"), None, None),
        P(("row", "col"), None, None, None),
        P(("row", "col"), None),
        P(("row", "col"), None),
        P(None, "row", None),
        P(None, "row", None),
        P(None, "row", None),
    )
    out_specs = (P(("row", "col"), None, None), P(None, "row", None))
    return jax.shard_map(local, mesh=mesh, in_specs=in_specs, out_specs=out_specs, check_vma=False)
```

time: 906 us -> 243 us (0.27)
  waiting for transfers between devices: 596 us -> 158 us
  blocking collectives: 253 us -> 0 us
  starting transfers between devices: 0.41 us -> 15.5 us
  matrix products: 23.5 us -> 34.4 us
    psum x5 -> x0, waiting for transfers between devices: 317 us -> none  [the longest x4 285 us: local(): lax.psum(local_part.astype(jnp.bfloat16), 'row').astype(jnp.float32)]
    all_gather x9 -> x0, blocking collectives: 253 us -> none  [the longest x4 122 us: local(): lax.all_gather(residue.astype(jnp.bfloat16), 'row', axis=0, tiled=True)]
    reduce_scatter x4 -> x0, waiting for transfers between devices: 206 us -> none  [the longest x3 187 us: local(): lax.psum_scatter(partial_term.astype(jnp.bfloat16), 'row', scatter_dimens...]
    ppermute x0 -> x11, waiting for transfers between devices: none -> 158 us  [the longest x5 153 us: swapped(): return lax.ppermute(x, axis, [(i, i ^ bit) for i in range(size)])]
    unnamed x11 -> x1, waiting for transfers between devices: 72.5 us -> 0.02 us
    ppermute x0 -> x11, starting transfers between devices: none -> 15.5 us  [the longest x5 7.79 us: swapped(): return lax.ppermute(x, axis, [(i, i ^ bit) for i in range(size)])]
    dot_general x16, matrix products: 15 us -> 26.5 us  [the longest x4 8.55 us: local(): lax.dot_general(inv_all[level], update.astype(jnp.bfloat16), (((0,), (0,)...]
  transfers between devices with their start and end apart: 10 -> 12, of which waited for: 10 -> 8; matrix products, arithmetic and copies ran while one was open for 0% -> 7% of each run, Pallas kernels for 0% -> 0%
where the time goes in v1:
time: 243 us; the launch traced here: 242 us
  waiting for transfers between devices  158 us (65%)
  matrix products  34.4 us (14%)
  starting transfers between devices  15.5 us (6%)
  between operations  14.3 us (6%)
  other arithmetic  9.86 us (4%)
  local copies, waits for them, and re-layouts  9.58 us (4%)
    ppermute x5, waiting for transfers between devices, swapped(): return lax.ppermute(x, axis, [(i, i ^ bit) for i in range(size)])  153 us
    dot_general x4, matrix products, local(): lax.dot_general(inv_all[level], update.astype(jnp.bfloat16), (((0,), (0,)...  8.55 us
    ppermute x5, starting transfers between devices, swapped(): return lax.ppermute(x, axis, [(i, i ^ bit) for i in range(size)])  7.79 us
    ppermute x6, starting transfers between devices, shifted(): return lax.ppermute(x, axis, [(i, (i + shift) % size) for i in range(size)])  7.69 us
    dot_general x4, matrix products, local(): jnp.dot(tiles_all[level * (level - 1) // 2 + u], top_forward[u], preferre...  5.39 us
    dot_general x3, matrix products, local(): jnp.dot(inv_all[level], residue.astype(jnp.bfloat16), preferred_element_t...  5.27 us
  transfers between devices with their start and end apart: 12, of which 8 were waited for; matrix products, arithmetic and copies ran while one was open for 7% of the time, Pallas kernels for 0%

profile of v1, /device:TPU:0, one launch (start us, length us, event | category | flops | bytes accessed | tf_op | source)
XLA Modules:
  0.0 241.9 jit_solution(12772350492322413493)
XLA Ops:
  7.2 0.0 all-gather.2.cloned.1.call-start
  7.2 2.1 pad_maximum_fusion
  9.3 0.0 all-gather.2.cloned.1.call-update
  9.4 1.4 convolution_convert_fusion.4
  10.7 0.5 collective-permute-start
  11.3 2.6 %collective-permute-start.1 = (bf16[512,128]{1,0:T(8,128)(2,1)S(1)}, bf16[512,128]{1,0:T(8,128)(2,1)S(1)}, u32[]{:S(2)}, u32[]{:S(2)}) collective-permute-start(bf16[512,128]{1,0:T(8,128)(2,1)S(1)} %convolution_convert_fusion.4), channel_id=1, source_target_pairs={{0,2},{1,3},{2,0},{3,1},{4,6},{5,7},{6,4},{7,5},{8,10},{9,11},{10,... | collective-permute-start | bytes 393224 | tf_op jit(solution)/shard_map/ppermute | solution.py:8
  13.9 1.4 collective-permute-start.2
  15.2 0.7 and_select_fusion
  16.0 0.6 iota_reduce_fusion
  16.6 1.1 broadcast_in_dim.9
  17.7 1.5 select_dynamic-update-slice_fusion
  19.3 0.6 collective-permute-done.2
  19.9 0.1 pad_maximum_fusion.1
  20.0 1.4 gather_fusion
  21.4 1.9 fusion.2
  23.3 1.3 copy.16
  24.6 2.7 %convolution_subtract_fusion = f32[4,512,128]{2,0,1:T(4,128)S(1)} fusion(f32[4,512,128]{2,0,1:T(4,128)} %select_dynamic-update-slice_fusion, f32[4,128,512]{1,0,2:T(4,128)} %copy.16, s32[4]{0:T(128)S(1)} %bitcast.151), kind=kOutput, calls=%fused_computation.6 | convolution fusion | flops 12845072 | bytes 3145744 | tf_op jit(solution)/shard_map/st,sak->tak/dot_general | solution.py:55
  27.3 0.1 collective-permute-start.3
  27.4 2.6 %collective-permute-done.3 = f32[4,512,128]{2,0,1:T(4,128)S(1)} collective-permute-done((f32[4,512,128]{2,0,1:T(4,128)S(1)}, f32[4,512,128]{2,0,1:T(4,128)S(1)}, u32[]{:S(2)}, u32[]{:S(2)}) %collective-permute-start.3) | collective-permute-done | bytes 1048608 | tf_op jit(solution)/shard_map/ppermute | solution.py:12
  30.0 0.3 add.68
  30.3 2.1 collective-permute-start.4
  32.3 23.7 %collective-permute-done.4 = f32[4,512,128]{2,0,1:T(4,128)S(1)} collective-permute-done((f32[4,512,128]{2,0,1:T(4,128)S(1)}, f32[4,512,128]{2,0,1:T(4,128)S(1)}, u32[]{:S(2)}, u32[]{:S(2)}) %collective-permute-start.4) | collective-permute-done | bytes 1048608 | tf_op jit(solution)/shard_map/ppermute | solution.py:12
  56.0 0.3 add.69
  56.3 1.8 collective-permute-start.5
  58.1 45.4 %collective-permute-done.5 = f32[4,512,128]{2,0,1:T(4,128)S(1)} collective-permute-done((f32[4,512,128]{2,0,1:T(4,128)S(1)}, f32[4,512,128]{2,0,1:T(4,128)S(1)}, u32[]{:S(2)}, u32[]{:S(2)}) %collective-permute-start.5) | collective-permute-done | bytes 1048608 | tf_op jit(solution)/shard_map/ppermute | solution.py:12
  103.5 0.3 add.70
  103.7 1.6 collective-permute-start.6
  105.3 35.8 %collective-permute-done.6 = f32[4,512,128]{2,0,1:T(4,128)S(1)} collective-permute-done((f32[4,512,128]{2,0,1:T(4,128)S(1)}, f32[4,512,128]{2,0,1:T(4,128)S(1)}, u32[]{:S(2)}, u32[]{:S(2)}) %collective-permute-start.6) | collective-permute-done | bytes 1048608 | tf_op jit(solution)/shard_map/ppermute | solution.py:12
  141.1 0.3 add.71
  141.4 2.3 collective-permute-start.7
  143.8 45.9 %collective-permute-done.7 = f32[4,512,128]{2,0,1:T(4,128)S(1)} collective-permute-done((f32[4,512,128]{2,0,1:T(4,128)S(1)}, f32[4,512,128]{2,0,1:T(4,128)S(1)}, u32[]{:S(2)}, u32[]{:S(2)}) %collective-permute-start.7) | collective-permute-done | bytes 1048608 | tf_op jit(solution)/shard_map/ppermute | solution.py:12
  189.7 0.3 add.72
  190.0 1.7 slice_negate_fusion
  191.7 1.3 convolution_convert_fusion.3
  193.0 1.3 fusion.20
  194.4 1.9 convolution_convert_fusion.2
  196.3 1.3 fusion.21
  197.6 1.3 fusion.18
  199.0 2.0 convolution_convert_fusion.1
  201.0 1.4 fusion.4
  202.4 2.6 %fusion.45 = (bf16[512,128]{1,0:T(8,128)(2,1)S(1)}, f32[512,128]{1,0:T(8,128)}) fusion(bf16[512,128]{1,0:T(8,128)(2,1)S(1)} %fusion.4, bf16[10,512,512]{2,1,0:T(8,128)(2,1)} %all-gather.2.cloned.1.call-done), kind=kOutput, calls=%fused_computation.104 | convolution fusion | flops 134348800 | bytes 1572864 | tf_op jit(solution)/shard_map/dot_general | solution.py:87
  205.0 2.0 fusion.11
  207.0 0.6 dynamic-slice_bitcast_fusion.1
  207.6 1.4 convolution_subtract_fusion.5
  209.0 1.9 fusion.10
  211.0 0.6 dynamic-slice_bitcast_fusion.2
  211.6 1.4 convolution_subtract_fusion.3
  213.0 1.4 convolution_subtract_fusion.2
  214.4 2.0 fusion.9
  216.4 1.0 pad_maximum_fusion.2
  217.4 1.4 gather_fusion.1
  218.8 1.5 fusion
  220.4 1.3 copy.17
  221.7 2.4 fusion.12
  224.1 0.1 copy.25
  224.2 0.1 collective-permute-start.10
  224.3 1.7 collective-permute-start.8
  226.0 1.4 collective-permute-start.9
  227.3 0.8 dynamic-slice_bitcast_fusion
  228.1 0.7 pad_maximum_fusion.3
  228.8 1.1 collective-permute-done.8
  229.9 3.0 %collective-permute-done.9 = bf16[512,128]{1,0:T(8,128)(2,1)S(1)} collective-permute-done((bf16[512,128]{1,0:T(8,128)(2,1)S(1)}, bf16[512,128]{1,0:T(8,128)(2,1)S(1)}, u32[]{:S(2)}, u32[]{:S(2)}) %collective-permute-start.9) | collective-permute-done | bytes 131104 | tf_op jit(solution)/shard_map/ppermute | solution.py:8
  232.8 1.3 convolution_bitcast_fusion
  234.2 0.8 copy.15
  (24 shorter events, 0.1 us)
Async XLA Ops:
  7.2 14.2 %copy-start = (bf16[1,4,512,512]{3,2,1,0:T(8,128)(2,1)S(1)}, bf16[1,4,512,512]{3,2,1,0:T(8,128)(2,1)}, u32[]{:S(2)}) copy-start(bf16[1,4,512,512]{3,2,1,0:T(8,128)(2,1)} %param.10) | copy-start | bytes 6291460
  7.2 184.5 %all-gather.2.cloned.1.call-start = ((), (), s32[]{:S(2)}) async-start(), calls=%async_computation | async-start | bytes 5898240 | tf_op jit(solution)/shard_map/all_gather | solution.py:32
  9.3 15.3 %copy-start.4 = (s32[1,4]{1,0:T(1,128)S(1)}, s32[1,4]{1,0:T(1,128)}, u32[]{:S(2)}) copy-start(s32[1,4]{1,0:T(1,128)} %param.11) | copy-start | bytes 52
  10.7 8.5 %collective-permute-start = (bf16[512,128]{1,0:T(8,128)(2,1)S(1)}, bf16[512,128]{1,0:T(8,128)(2,1)S(1)}, u32[]{:S(2)}, u32[]{:S(2)}) collective-permute-start(bf16[512,128]{1,0:T(8,128)(2,1)S(1)} %convolution_convert_fusion.4), channel_id=1, source_target_pairs={{0,1},{1,2},{2,3},{3,0},{4,5},{5,6},{6,7},{7,4},{8,9},{9,10},{10,1... | collective-permute-start | bytes 393224 | tf_op jit(solution)/shard_map/ppermute | solution.py:8
  11.3 8.0 %collective-permute-start.1 = (bf16[512,128]{1,0:T(8,128)(2,1)S(1)}, bf16[512,128]{1,0:T(8,128)(2,1)S(1)}, u32[]{:S(2)}, u32[]{:S(2)}) collective-permute-start(bf16[512,128]{1,0:T(8,128)(2,1)S(1)} %convolution_convert_fusion.4), channel_id=1, source_target_pairs={{0,2},{1,3},{2,0},{3,1},{4,6},{5,7},{6,4},{7,5},{8,10},{9,11},{10,... | collective-permute-start | bytes 393224 | tf_op jit(solution)/shard_map/ppermute | solution.py:8
  13.9 6.0 %collective-permute-start.2 = (bf16[512,128]{1,0:T(8,128)(2,1)S(1)}, bf16[512,128]{1,0:T(8,128)(2,1)S(1)}, u32[]{:S(2)}, u32[]{:S(2)}) collective-permute-start(bf16[512,128]{1,0:T(8,128)(2,1)S(1)} %convolution_convert_fusion.4), channel_id=1, source_target_pairs={{0,3},{1,0},{2,1},{3,2},{4,7},{5,4},{6,5},{7,6},{8,11},{9,8},{10,9... | collective-permute-start | bytes 393224 | tf_op jit(solution)/shard_map/ppermute | solution.py:8
  27.3 2.7 %collective-permute-start.3 = (f32[4,512,128]{2,0,1:T(4,128)S(1)}, f32[4,512,128]{2,0,1:T(4,128)S(1)}, u32[]{:S(2)}, u32[]{:S(2)}) collective-permute-start(f32[4,512,128]{2,0,1:T(4,128)S(1)} %convolution_subtract_fusion), channel_id=1, source_target_pairs={{0,1},{1,0},{2,3},{3,2},{4,5},{5,4},{6,7},{7,6},{8,9},{9,8},{10,11... | collective-permute-start | bytes 3145736 | tf_op jit(solution)/shard_map/ppermute | solution.py:12
  30.3 25.8 %collective-permute-start.4 = (f32[4,512,128]{2,0,1:T(4,128)S(1)}, f32[4,512,128]{2,0,1:T(4,128)S(1)}, u32[]{:S(2)}, u32[]{:S(2)}) collective-permute-start(f32[4,512,128]{2,0,1:T(4,128)S(1)} %add.68), channel_id=1, source_target_pairs={{0,2},{1,3},{2,0},{3,1},{4,6},{5,7},{6,4},{7,5},{8,10},{9,11},{10,... | collective-permute-start | bytes 3145736 | tf_op jit(solution)/shard_map/ppermute | solution.py:12
  56.3 47.1 %collective-permute-start.5 = (f32[4,512,128]{2,0,1:T(4,128)S(1)}, f32[4,512,128]{2,0,1:T(4,128)S(1)}, u32[]{:S(2)}, u32[]{:S(2)}) collective-permute-start(f32[4,512,128]{2,0,1:T(4,128)S(1)} %add.69), channel_id=1, source_target_pairs={{0,4},{4,0},{8,12},{12,8},{16,20},{20,16},{24,28},{28,24},{1,5},{5... | collective-permute-start | bytes 3145736 | tf_op jit(solution)/shard_map/ppermute | solution.py:12
  103.7 37.4 %collective-permute-start.6 = (f32[4,512,128]{2,0,1:T(4,128)S(1)}, f32[4,512,128]{2,0,1:T(4,128)S(1)}, u32[]{:S(2)}, u32[]{:S(2)}) collective-permute-start(f32[4,512,128]{2,0,1:T(4,128)S(1)} %add.70), channel_id=1, source_target_pairs={{0,8},{4,12},{8,0},{12,4},{16,24},{20,28},{24,16},{28,20},{1,9},{5... | collective-permute-start | bytes 3145736 | tf_op jit(solution)/shard_map/ppermute | solution.py:12
  141.4 48.3 %collective-permute-start.7 = (f32[4,512,128]{2,0,1:T(4,128)S(1)}, f32[4,512,128]{2,0,1:T(4,128)S(1)}, u32[]{:S(2)}, u32[]{:S(2)}) collective-permute-start(f32[4,512,128]{2,0,1:T(4,128)S(1)} %add.71), channel_id=1, source_target_pairs={{0,16},{4,20},{8,24},{12,28},{16,0},{20,4},{24,8},{28,12},{1,17},{... | collective-permute-start | bytes 3145736 | tf_op jit(solution)/shard_map/ppermute | solution.py:12
  205.0 6.6 %copy-start.3 = (bf16[512,128]{1,0:T(8,128)(2,1)}, bf16[512,128]{1,0:T(8,128)(2,1)S(1)}, u32[]{:S(2)}) copy-start(bf16[512,128]{1,0:T(8,128)(2,1)S(1)} %get-tuple-element.15) | copy-start | bytes 393220
  217.4 10.7 %copy-start.1 = (f32[1,64,128]{2,1,0:T(8,128)S(1)}, f32[1,64,128]{2,1,0:T(8,128)}, u32[]{:S(2)}) copy-start(f32[1,64,128]{2,1,0:T(8,128)} %dynamic-slice_bitcast_fusion.1) | copy-start | bytes 98308
  217.4 10.7 %copy-start.2 = (f32[1,64,128]{2,1,0:T(8,128)S(1)}, f32[1,64,128]{2,1,0:T(8,128)}, u32[]{:S(2)}) copy-start(f32[1,64,128]{2,1,0:T(8,128)} %dynamic-slice_bitcast_fusion.2) | copy-start | bytes 98308
  224.2 4.6 %collective-permute-start.10 = (bf16[512,128]{1,0:T(8,128)(2,1)S(1)}, bf16[512,128]{1,0:T(8,128)(2,1)S(1)}, u32[]{:S(2)}, u32[]{:S(2)}) collective-permute-start(bf16[512,128]{1,0:T(8,128)(2,1)S(1)} %get-tuple-element.13), channel_id=1, source_target_pairs={{0,1},{1,2},{2,3},{3,0},{4,5},{5,6},{6,7},{7,4},{8,9},{9,10},{10,1... | collective-permute-start | bytes 393224 | tf_op jit(solution)/shard_map/ppermute | solution.py:8
  224.3 5.6 %collective-permute-start.8 = (bf16[512,128]{1,0:T(8,128)(2,1)S(1)}, bf16[512,128]{1,0:T(8,128)(2,1)S(1)}, u32[]{:S(2)}, u32[]{:S(2)}) collective-permute-start(bf16[512,128]{1,0:T(8,128)(2,1)S(1)} %get-tuple-element.12), channel_id=1, source_target_pairs={{0,3},{1,0},{2,1},{3,2},{4,7},{5,4},{6,5},{7,6},{8,11},{9,8},{10,9... | collective-permute-start | bytes 393224 | tf_op jit(solution)/shard_map/ppermute | solution.py:8
  226.0 6.9 %collective-permute-start.9 = (bf16[512,128]{1,0:T(8,128)(2,1)S(1)}, bf16[512,128]{1,0:T(8,128)(2,1)S(1)}, u32[]{:S(2)}, u32[]{:S(2)}) collective-permute-start(bf16[512,128]{1,0:T(8,128)(2,1)S(1)} %get-tuple-element.14), channel_id=1, source_target_pairs={{0,2},{1,3},{2,0},{3,1},{4,6},{5,7},{6,4},{7,5},{8,10},{9,11},{10,... | collective-permute-start | bytes 393224 | tf_op jit(solution)/shard_map/ppermute | solution.py:8
Sparse Core Ops, SparseCore 0:
  10.2 119.7 all-gather.1

commit v2 on v1

--- a/solution.py
+++ b/solution.py
@@ -20,6 +20,31 @@
     return x
 
 
+def summed_everywhere(x, peers, rows_n, me):
+    shape = x.shape
+    chunks = x.reshape(peers, -1, shape[-1]).astype(jnp.bfloat16)
+    bit = peers // 2
+    while bit >= 1:
+        halves = chunks.reshape(2, -1, *chunks.shape[1:])
+        mine = (me // bit) % 2
+        keep = lax.dynamic_index_in_dim(halves, mine, 0, keepdims=False)
+        give = lax.dynamic_index_in_dim(halves, 1 - mine, 0, keepdims=False)
+        got = swapped(give, "col", peers, bit)
+        chunks = (keep.astype(jnp.float32) + got.astype(jnp.float32)).astype(jnp.bfloat16)
+        bit //= 2
+    part = chunks[0]
+    bit = 1
+    while bit < rows_n:
+        got = swapped(part, "row", rows_n, bit)
+        part = (part.astype(jnp.float32) + got.astype(jnp.float32)).astype(jnp.bfloat16)
+        bit *= 2
+    pieces = [part] + [shifted(part, "col", peers, s) for s in range(1, peers)]
+    stacked = jnp.stack(pieces)
+    index = (me - jnp.arange(peers)) % peers
+    ordered = jnp.zeros_like(stacked).at[index].set(stacked)
+    return ordered.reshape(shape).astype(jnp.float32)
+
+
 def local(low_rhs, low_inv, low_tiles, tile_rows, tile_cols, top_rhs, top_inv, top_tiles):
     peers = lax.axis_size("col")
     rows_n = lax.axis_size("row")
@@ -29,7 +54,13 @@
     me = lax.axis_index("col")
 
     stacked = jnp.concatenate([top_inv, top_tiles], axis=0)
-    whole = lax.all_gather(stacked, "row", axis=1, tiled=True)
+    quarter = share // peers
+    mine = lax.dynamic_slice_in_dim(stacked, me * quarter, quarter, 1)
+    pulled = lax.all_gather(mine, "row", axis=0)
+    shared = lax.all_gather(pulled, "col", axis=0)
+    whole = jnp.transpose(shared, (2, 1, 0, 3, 4)).reshape(
+        stacked.shape[0], rows_n * share, stacked.shape[2]
+    )
     inv_all = whole[:levels]
     tiles_all = whole[levels:]
 
@@ -56,8 +87,7 @@
     own_rhs = jnp.zeros((levels, share * rows_n, top_rhs.shape[2]), jnp.float32)
     own_rhs = lax.dynamic_update_slice_in_dim(own_rhs, top_rhs.astype(jnp.float32), position * share, 1)
     coupling = coupling - jnp.where(me == 0, own_rhs, 0.0)
-    coupling = butterfly_sum(coupling, "col", peers)
-    coupling = butterfly_sum(coupling, "row", rows_n)
+    coupling = summed_everywhere(coupling, peers, rows_n, me)
 
     top_forward = []
     for level in range(levels):

time: 243 us -> 178 us (0.73)
  waiting for transfers between devices: 158 us -> 89.8 us
  local copies, waits for them, and re-layouts: 9.58 us -> 20.1 us
  starting transfers between devices: 15.5 us -> 10.5 us
    ppermute x5, waiting for transfers between devices: 153 us -> 29 us  [swapped(): return lax.ppermute(x, axis, [(i, i ^ bit) for i in range(size)])]
    all_gather x1 -> x2, waiting for transfers between devices: 0.01 us -> 46.3 us  [the longest x1 46.3 us: local(): pulled = lax.all_gather(mine, 'row', axis=0)]
    ppermute x6 -> x9, waiting for transfers between devices: 4.69 us -> 14.5 us  [shifted(): return lax.ppermute(x, axis, [(i, (i + shift) % size) for i in range(size)])]
    slice x0 -> x11, local copies, waits for them, and re-layouts: none -> 8.33 us  [the longest x4 5.6 us: local(): tiles_all[k * (k - 1) // 2 + level]]
    ppermute x5, starting transfers between devices: 7.79 us -> 4.84 us  [swapped(): return lax.ppermute(x, axis, [(i, i ^ bit) for i in range(size)])]
    ppermute x6 -> x9, starting transfers between devices: 7.69 us -> 5.56 us  [shifted(): return lax.ppermute(x, axis, [(i, (i + shift) % size) for i in range(size)])]
  transfers between devices with their start and end apart: 12 -> 16, of which waited for: 8 -> 14; matrix products, arithmetic and copies ran while one was open for 7% -> 8% of each run, Pallas kernels for 0% -> 0%
where the time goes in v2:
time: 178 us; the launch traced here: 177 us
  waiting for transfers between devices  89.8 us (50%)
  matrix products  34.3 us (19%)
  local copies, waits for them, and re-layouts  20.1 us (11%)
  between operations  14.5 us (8%)
  starting transfers between devices  10.5 us (6%)
  other arithmetic  7.63 us (4%)
    all_gather x1, waiting for transfers between devices, local(): pulled = lax.all_gather(mine, 'row', axis=0)  46.3 us
    ppermute x5, waiting for transfers between devices, swapped(): return lax.ppermute(x, axis, [(i, i ^ bit) for i in range(size)])  29 us
    ppermute x9, waiting for transfers between devices, shifted(): return lax.ppermute(x, axis, [(i, (i + shift) % size) for i in range(size)])  14.5 us
    dot_general x4, matrix products, local(): lax.dot_general(inv_all[level], update.astype(jnp.bfloat16), (((0,), (0,)...  9.3 us
    dot_general x4, matrix products, local(): jnp.dot(tiles_all[level * (level - 1) // 2 + u], top_forward[u], preferre...  6.29 us
    slice x4, local copies, waits for them, and re-layouts, local(): tiles_all[k * (k - 1) // 2 + level]  5.6 us
    ppermute x9, starting transfers between devices, shifted(): return lax.ppermute(x, axis, [(i, (i + shift) % size) for i in range(size)])  5.56 us
    dot_general x3, matrix products, local(): lax.dot_general(tiles_all[k * (k - 1) // 2 + level], top_back[k], (((0,),...  5.46 us
  transfers between devices with their start and end apart: 16, of which 14 were waited for; matrix products, arithmetic and copies ran while one was open for 8% of the time, Pallas kernels for 0%

profile of v2, /device:TPU:0, one launch (start us, length us, event | category | flops | bytes accessed | tf_op | source)
XLA Modules:
  0.0 176.9 jit_solution(15640960249570937780)
XLA Ops:
  7.3 1.8 fusion.34
  9.1 46.3 %all-gather.5.cloned.1.call-done = bf16[80,16,512]{2,1,0:T(8,128)(2,1)} async-done(((bf16[10,16,512]{2,1,0:T(8,128)(2,1)}), bf16[80,16,512]{2,1,0:T(8,128)(2,1)}) %all-gather.5.cloned.1.call-update) | async-done | bytes 1310736 | tf_op jit(solution)/shard_map/all_gather | solution.py:59
  55.8 1.5 collective-permute-start.1
  57.6 0.6 iota_reduce_fusion
  58.2 1.1 broadcast_in_dim.12
  59.3 0.7 select_dynamic-update-slice_fusion
  60.0 4.3 %collective-permute-done.1 = bf16[512,128]{1,0:T(8,128)(2,1)S(1)} collective-permute-done((bf16[512,128]{1,0:T(8,128)(2,1)S(1)}, bf16[512,128]{1,0:T(8,128)(2,1)S(1)}, u32[]{:S(2)}, u32[]{:S(2)}) %collective-permute-start.1) | collective-permute-done | bytes 131104 | tf_op jit(solution)/shard_map/ppermute | solution.py:8
  64.5 1.5 gather_fusion
  66.0 1.9 %fusion.4 = f32[4,512,128]{1,2,0:T(8,128)S(1)} fusion(bf16[4,512,128]{2,1,0:T(8,128)(2,1)} %gather_fusion, bf16[1,4,512,512]{3,2,1,0:T(8,128)(2,1)S(1)} %copy-done), kind=kOutput, calls=%fused_computation.7 | convolution fusion | flops 268435456 | bytes 3670016 | tf_op jit(solution)/shard_map/sab,sbk->sak/dot_general | solution.py:80
  67.9 1.4 copy.39
  69.3 2.7 %fusion.10 = bf16[4,512,128]{2,0,1:T(4,128)(2,1)S(1)} fusion(f32[4,512,128]{2,0,1:T(4,128)} %select_dynamic-update-slice_fusion, f32[4,512,128]{2,0,1:T(4,128)} %copy.39, s32[4]{0:T(128)S(1)} %bitcast.185), kind=kOutput, calls=%fused_computation.10 | convolution fusion | flops 13107216 | bytes 2621456 | tf_op jit(solution)/shard_map/st,sak->tak/dot_general | solution.py:86
  72.0 0.4 constant_dynamic-slice_fusion.2
  72.4 0.7 collective-permute-start.3
  73.1 13.2 %collective-permute-done.3 = bf16[2,512,128]{2,1,0:T(8,128)(2,1)S(1)} collective-permute-done((bf16[2,512,128]{2,1,0:T(8,128)(2,1)S(1)}, bf16[2,512,128]{2,1,0:T(8,128)(2,1)S(1)}, u32[]{:S(2)}, u32[]{:S(2)}) %collective-permute-start.3) | collective-permute-done | bytes 262176 | tf_op jit(solution)/shard_map/ppermute | solution.py:12
  86.5 1.3 collective-permute-done.4
  87.9 0.9 collective-permute-start.5
  88.8 4.7 %collective-permute-done.5 = bf16[512,128]{1,0:T(8,128)(2,1)S(1)} collective-permute-done((bf16[512,128]{1,0:T(8,128)(2,1)S(1)}, bf16[512,128]{1,0:T(8,128)(2,1)S(1)}, u32[]{:S(2)}, u32[]{:S(2)}) %collective-permute-start.5) | collective-permute-done | bytes 131104 | tf_op jit(solution)/shard_map/ppermute | solution.py:12
  93.6 1.3 collective-permute-start.6
  94.9 3.7 %collective-permute-done.6 = bf16[512,128]{1,0:T(8,128)(2,1)S(1)} collective-permute-done((bf16[512,128]{1,0:T(8,128)(2,1)S(1)}, bf16[512,128]{1,0:T(8,128)(2,1)S(1)}, u32[]{:S(2)}, u32[]{:S(2)}) %collective-permute-start.6) | collective-permute-done | bytes 131104 | tf_op jit(solution)/shard_map/ppermute | solution.py:12
  98.6 1.8 %collective-permute-start.7 = (bf16[512,128]{1,0:T(8,128)(2,1)S(1)}, bf16[512,128]{1,0:T(8,128)(2,1)S(1)}, u32[]{:S(2)}, u32[]{:S(2)}) collective-permute-start(bf16[512,128]{1,0:T(8,128)(2,1)S(1)} %add_convert_fusion.1), channel_id=1, source_target_pairs={{0,16},{4,20},{8,24},{12,28},{16,0},{20,4},{24,8},{28,12},{1,17},{... | collective-permute-start | bytes 393224 | tf_op jit(solution)/shard_map/ppermute | solution.py:12
  100.5 6.0 %collective-permute-done.7 = bf16[512,128]{1,0:T(8,128)(2,1)S(1)} collective-permute-done((bf16[512,128]{1,0:T(8,128)(2,1)S(1)}, bf16[512,128]{1,0:T(8,128)(2,1)S(1)}, u32[]{:S(2)}, u32[]{:S(2)}) %collective-permute-start.7) | collective-permute-done | bytes 131104 | tf_op jit(solution)/shard_map/ppermute | solution.py:12
  106.6 1.1 collective-permute-start.9
  107.8 2.1 %collective-permute-done.10 = bf16[512,128]{1,0:T(8,128)(2,1)S(1)} collective-permute-done((bf16[512,128]{1,0:T(8,128)(2,1)S(1)}, bf16[512,128]{1,0:T(8,128)(2,1)S(1)}, u32[]{:S(2)}, u32[]{:S(2)}) %collective-permute-start.10) | collective-permute-done | bytes 131104 | tf_op jit(solution)/shard_map/ppermute | solution.py:8
  109.9 4.2 %collective-permute-done.9 = bf16[512,128]{1,0:T(8,128)(2,1)S(1)} collective-permute-done((bf16[512,128]{1,0:T(8,128)(2,1)S(1)}, bf16[512,128]{1,0:T(8,128)(2,1)S(1)}, u32[]{:S(2)}, u32[]{:S(2)}) %collective-permute-start.9) | collective-permute-done | bytes 131104 | tf_op jit(solution)/shard_map/ppermute | solution.py:8
  114.1 0.6 collective-permute-done.8
  114.9 0.8 scatter_fusion
  115.6 1.0 convert_element_type.167
  116.7 3.1 %fusion.56 = (bf16[1,8,4,16,512]{4,3,0,1,2:T(8,128)(2,1)S(1)}, bf16[1,8,4,16,512]{4,3,0,1,2:T(8,128)(2,1)S(1)}, bf16[1,8,4,16,512]{4,3,0,1,2:T(8,128)(2,1)S(1)},...) fusion(bf16[10,8,4,16,512]{4,3,0,1,2:T(8,128)(2,1)} %bitcast.153), kind=kLoop, calls=%fused_computation.119 | loop fusion | bytes 10485760 | tf_op jit(solution)/shard_map/slice | solution.py:112
  119.8 0.8 copy.49
  120.7 0.9 copy.51
  121.6 0.8 copy.44
  122.5 0.8 copy.43
  123.3 0.8 copy.48
  124.3 0.3 convolution_convert_fusion.3
  124.6 1.0 convolution_subtract_fusion.9
  125.6 1.0 convolution_subtract_fusion.11
  126.6 0.8 copy.45
  127.4 2.0 %convolution_convert_fusion.2 = bf16[512,128]{1,0:T(8,128)(2,1)S(1)} fusion(bf16[512,512]{1,0:T(8,128)(2,1)} %bitcast.160, bf16[512,512]{1,0:T(8,128)(2,1)} %bitcast.158, bf16[512,128]{1,0:T(8,128)(2,1)S(1)} %convolution_convert_fusion.3, f32[4,512,128]{2,1,0:T(8,128)} %convert_element_type.167), kind=kOutput, calls=%fused_computation.32 | convolution fusion | flops 134479872 | bytes 1572864 | tf_op jit(solution)/shard_map/dot_general | solution.py:102
  129.4 2.2 %convolution_subtract_fusion.8 = f32[512,128]{1,0:T(8,128)} fusion(f32[512,128]{1,0:T(8,128)} %convolution_subtract_fusion.9, bf16[512,512]{1,0:T(8,128)(2,1)} %bitcast.171, bf16[512,128]{1,0:T(8,128)(2,1)S(1)} %convolution_convert_fusion.2), kind=kOutput, calls=%fused_computation.19 | convolution fusion | flops 67174400 | bytes 1179648 | tf_op jit(solution)/shard_map/dot_general | solution.py:96
  131.6 1.8 %convolution_convert_fusion.1 = bf16[512,128]{1,0:T(8,128)(2,1)S(1)} fusion(bf16[512,512]{1,0:T(8,128)(2,1)S(1)} %bitcast.154, f32[512,128]{1,0:T(8,128)} %convolution_subtract_fusion.11, bf16[512,512]{1,0:T(8,128)(2,1)} %bitcast.165, bf16[512,128]{1,0:T(8,128)(2,1)S(1)} %convolution_convert_fusion.2), kind=kOutput, calls=%fused_computation.31 | convolution fusion | flops 134414336 | bytes 1572864 | tf_op jit(solution)/shard_map/dot_general | solution.py:102
  133.5 2.1 %fusion.13 = bf16[512,128]{1,0:T(8,128)(2,1)} fusion(f32[512,128]{1,0:T(8,128)} %convolution_subtract_fusion.8, bf16[512,512]{1,0:T(8,128)(2,1)} %bitcast.163, bf16[512,128]{1,0:T(8,128)(2,1)S(1)} %convolution_convert_fusion.1), kind=kOutput, calls=%fused_computation.26 | convolution fusion | flops 67239936 | bytes 1048576 | tf_op jit(solution)/shard_map/dot_general | solution.py:96
  135.6 2.7 %fusion.57 = (bf16[512,128]{1,0:T(8,128)(2,1)}, f32[512,128]{1,0:T(8,128)}) fusion(bf16[512,512]{1,0:T(8,128)(2,1)} %bitcast.162, bf16[512,128]{1,0:T(8,128)(2,1)} %fusion.13), kind=kOutput, calls=%fused_computation.120 | convolution fusion | flops 134348800 | bytes 1048576 | tf_op jit(solution)/shard_map/dot_general | solution.py:117
  138.3 1.9 %fusion.20 = f32[512,128]{1,0:T(8,128)S(1)} fusion(bf16[512,512]{1,0:T(8,128)(2,1)S(1)} %bitcast.155, bf16[512,512]{1,0:T(8,128)(2,1)} %bitcast.164, bf16[512,128]{1,0:T(8,128)(2,1)} %get-tuple-element.27, bf16[512,128]{1,0:T(8,128)(2,1)} %copy-done.9), kind=kOutput, calls=%fused_computation.38 | convolution fusion | flops 134414336 | bytes 1572864 | tf_op jit(solution)/shard_map/dot_general | solution.py:117
  140.2 0.7 convert_bitcast_fusion.2
  140.9 2.1 %convolution_subtract_fusion.5 = f32[512,128]{1,0:T(8,128)} fusion(bf16[512,512]{1,0:T(8,128)(2,1)} %bitcast.166, bf16[512,128]{1,0:T(8,128)(2,1)} %copy-done.6, f32[512,128]{1,0:T(8,128)S(1)} %fusion.20), kind=kOutput, calls=%fused_computation.16 | convolution fusion | flops 67305472 | bytes 1179648 | tf_op jit(solution)/shard_map/dot_general | solution.py:111
  143.0 2.8 %fusion.19 = f32[512,128]{1,0:T(8,128)} fusion(bf16[512,512]{1,0:T(8,128)(2,1)} %bitcast.161, f32[512,128]{1,0:T(8,128)} %convolution_subtract_fusion.5, bf16[512,512]{1,0:T(8,128)(2,1)} %bitcast.172, bf16[512,128]{1,0:T(8,128)(2,1)} %get-tuple-element.27), kind=kOutput, calls=%fused_computation.37 | convolution fusion | flops 134348800 | bytes 1703936 | tf_op jit(solution)/shard_map/dot_general | solution.py:117
  145.7 1.6 convert_bitcast_fusion.1
  147.4 1.3 convolution_subtract_fusion.3
  148.7 0.6 dynamic-slice_bitcast_fusion.1
  149.3 1.4 dynamic-slice_bitcast_fusion.2
  150.7 2.1 %convolution_subtract_fusion.2 = f32[512,128]{1,0:T(8,128)} fusion(f32[512,128]{1,0:T(8,128)S(1)} %convolution_subtract_fusion.3, bf16[512,512]{1,0:T(8,128)(2,1)} %bitcast.170, f32[512,128]{1,0:T(8,128)S(1)} %fusion.20), kind=kOutput, calls=%fused_computation.13 | convolution fusion | flops 67239936 | bytes 1310720 | tf_op jit(solution)/shard_map/dot_general | solution.py:111
  152.8 1.9 %fusion.18 = f32[512,128]{1,0:T(8,128)S(1)} fusion(bf16[512,512]{1,0:T(8,128)(2,1)S(1)} %bitcast.157, f32[512,128]{1,0:T(8,128)} %convolution_subtract_fusion.2, bf16[512,512]{1,0:T(8,128)(2,1)} %bitcast.168, bf16[512,128]{1,0:T(8,128)(2,1)} %get-tuple-element.27), kind=kOutput, calls=%fused_computation.36 | convolution fusion | flops 134348800 | bytes 1703936 | tf_op jit(solution)/shard_map/dot_general | solution.py:117
  154.8 1.4 gather_fusion.1
  156.3 1.5 fusion.7
  157.8 1.3 copy.53
  159.1 2.4 %fusion.43 = bf16[4,512,128]{2,0,1:T(4,128)(2,1)S(1)} fusion(f32[4,512,128]{2,0,1:T(4,128)} %copy.53, s32[4]{0:T(128)S(1)} %get-tuple-element.29, pred[4]{0:T(512)(128)(4,1)S(1)} %broadcast_compare_fusion, s32[4]{0:T(128)S(1)} %get-tuple-element.30), kind=kOutput, calls=%fused_computation.100 | convolution fusion | flops 12582944 | bytes 1572900 | tf_op jit(solution)/shard_map/sp,sbk->pbk/dot_general | solution.py:132
  161.7 1.1 collective-permute-start.12
  162.8 1.4 collective-permute-start.11
  164.2 0.8 dynamic-slice_bitcast_fusion
  165.0 0.7 pad_maximum_fusion.3
  165.7 1.2 collective-permute-done.13
  166.9 1.3 collective-permute-done.12
  168.2 0.7 collective-permute-done.11
  169.2 0.8 copy.55
  (81 shorter events, 2.3 us)
Async XLA Ops:
  7.2 58.8 %copy-start = (bf16[1,4,512,512]{3,2,1,0:T(8,128)(2,1)S(1)}, bf16[1,4,512,512]{3,2,1,0:T(8,128)(2,1)}, u32[]{:S(2)}) copy-start(bf16[1,4,512,512]{3,2,1,0:T(8,128)(2,1)} %param.10) | copy-start | bytes 6291460
  7.2 48.2 %copy-start.7 = (bf16[1,512,512]{2,1,0:T(8,128)(2,1)S(1)}, bf16[1,512,512]{2,1,0:T(8,128)(2,1)}, u32[]{:S(2)}) copy-start(bf16[1,512,512]{2,1,0:T(8,128)(2,1)} %param.9) | copy-start | bytes 1572868
  7.2 48.2 %copy-start.14 = (bf16[1,512,128]{2,1,0:T(8,128)(2,1)S(1)}, bf16[1,512,128]{2,1,0:T(8,128)(2,1)}, u32[]{:S(2)}) copy-start(bf16[1,512,128]{2,1,0:T(8,128)(2,1)} %param.8) | copy-start | bytes 393220
  7.2 50.3 %copy-start.18 = (s32[1,4]{1,0:T(1,128)S(1)}, s32[1,4]{1,0:T(1,128)}, u32[]{:S(2)}) copy-start(s32[1,4]{1,0:T(1,128)} %param.12) | copy-start | bytes 52
  7.2 48.1 %all-gather.5.cloned.1.call-start = ((), (), s32[]{:S(2)}) async-start(), calls=%async_computation | async-start | bytes 1474560 | tf_op jit(solution)/shard_map/all_gather | solution.py:59
  7.3 52.0 %copy-start.17 = (bf16[4,64,128]{2,1,0:T(8,128)(2,1)S(1)}, bf16[4,64,128]{2,1,0:T(8,128)(2,1)}, u32[]{:S(2)}) copy-start(bf16[4,64,128]{2,1,0:T(8,128)(2,1)} %param.13) | copy-start | bytes 196612
  9.1 107.6 %all-gather.7.cloned.1.call-start = ((), (), s32[]{:S(2)}) async-start(), calls=%async_computation.1 | async-start | bytes 6553600 | tf_op jit(solution)/shard_map/all_gather | solution.py:60
  55.7 8.8 %copy-start.10 = (bf16[512,128]{1,0:T(8,128)(2,1)}, bf16[512,128]{1,0:T(8,128)(2,1)S(1)}, u32[]{:S(2)}) copy-start(bf16[512,128]{1,0:T(8,128)(2,1)S(1)} %convolution_convert_fusion.4) | copy-start | bytes 393220
  55.7 4.3 %collective-permute-start.2 = (bf16[512,128]{1,0:T(8,128)(2,1)S(1)}, bf16[512,128]{1,0:T(8,128)(2,1)S(1)}, u32[]{:S(2)}, u32[]{:S(2)}) collective-permute-start(bf16[512,128]{1,0:T(8,128)(2,1)S(1)} %convolution_convert_fusion.4), channel_id=1, source_target_pairs={{0,3},{1,0},{2,1},{3,2},{4,7},{5,4},{6,5},{7,6},{8,11},{9,8},{10,9... | collective-permute-start | bytes 393224 | tf_op jit(solution)/shard_map/ppermute | solution.py:8
  55.8 8.5 %collective-permute-start.1 = (bf16[512,128]{1,0:T(8,128)(2,1)S(1)}, bf16[512,128]{1,0:T(8,128)(2,1)S(1)}, u32[]{:S(2)}, u32[]{:S(2)}) collective-permute-start(bf16[512,128]{1,0:T(8,128)(2,1)S(1)} %convolution_convert_fusion.4), channel_id=1, source_target_pairs={{0,2},{1,3},{2,0},{3,1},{4,6},{5,7},{6,4},{7,5},{8,10},{9,11},{10,... | collective-permute-start | bytes 393224 | tf_op jit(solution)/shard_map/ppermute | solution.py:8
  57.3 7.1 %collective-permute-start = (bf16[512,128]{1,0:T(8,128)(2,1)S(1)}, bf16[512,128]{1,0:T(8,128)(2,1)S(1)}, u32[]{:S(2)}, u32[]{:S(2)}) collective-permute-start(bf16[512,128]{1,0:T(8,128)(2,1)S(1)} %convolution_convert_fusion.4), channel_id=1, source_target_pairs={{0,1},{1,2},{2,3},{3,0},{4,5},{5,6},{6,7},{7,4},{8,9},{9,10},{10,1... | collective-permute-start | bytes 393224 | tf_op jit(solution)/shard_map/ppermute | solution.py:8
  66.0 3.3 %copy-start.19 = (s32[1,4]{1,0:T(1,128)S(1)}, s32[1,4]{1,0:T(1,128)}, u32[]{:S(2)}) copy-start(s32[1,4]{1,0:T(1,128)} %param.11) | copy-start | bytes 52
  72.4 14.0 %collective-permute-start.3 = (bf16[2,512,128]{2,1,0:T(8,128)(2,1)S(1)}, bf16[2,512,128]{2,1,0:T(8,128)(2,1)S(1)}, u32[]{:S(2)}, u32[]{:S(2)}) collective-permute-start(bf16[2,512,128]{2,1,0:T(8,128)(2,1)S(1)} %bitcast.178), channel_id=1, source_target_pairs={{0,2},{1,3},{2,0},{3,1},{4,6},{5,7},{6,4},{7,5},{8,10},{9,11},{10,... | collective-permute-start | bytes 786440 | tf_op jit(solution)/shard_map/ppermute | solution.py:12
  86.5 1.4 collective-permute-start.4
  87.9 5.6 %collective-permute-start.5 = (bf16[512,128]{1,0:T(8,128)(2,1)S(1)}, bf16[512,128]{1,0:T(8,128)(2,1)S(1)}, u32[]{:S(2)}, u32[]{:S(2)}) collective-permute-start(bf16[512,128]{1,0:T(8,128)(2,1)S(1)} %fusion.35), channel_id=1, source_target_pairs={{0,4},{4,0},{8,12},{12,8},{16,20},{20,16},{24,28},{28,24},{1,5},{5... | collective-permute-start | bytes 393224 | tf_op jit(solution)/shard_map/ppermute | solution.py:12
  93.6 5.0 %collective-permute-start.6 = (bf16[512,128]{1,0:T(8,128)(2,1)S(1)}, bf16[512,128]{1,0:T(8,128)(2,1)S(1)}, u32[]{:S(2)}, u32[]{:S(2)}) collective-permute-start(bf16[512,128]{1,0:T(8,128)(2,1)S(1)} %add_convert_fusion.2), channel_id=1, source_target_pairs={{0,8},{4,12},{8,0},{12,4},{16,24},{20,28},{24,16},{28,20},{1,9},{5... | collective-permute-start | bytes 393224 | tf_op jit(solution)/shard_map/ppermute | solution.py:12
  98.6 7.8 %collective-permute-start.7 = (bf16[512,128]{1,0:T(8,128)(2,1)S(1)}, bf16[512,128]{1,0:T(8,128)(2,1)S(1)}, u32[]{:S(2)}, u32[]{:S(2)}) collective-permute-start(bf16[512,128]{1,0:T(8,128)(2,1)S(1)} %add_convert_fusion.1), channel_id=1, source_target_pairs={{0,16},{4,20},{8,24},{12,28},{16,0},{20,4},{24,8},{28,12},{1,17},{... | collective-permute-start | bytes 393224 | tf_op jit(solution)/shard_map/ppermute | solution.py:12
  106.5 3.4 %collective-permute-start.10 = (bf16[512,128]{1,0:T(8,128)(2,1)S(1)}, bf16[512,128]{1,0:T(8,128)(2,1)S(1)}, u32[]{:S(2)}, u32[]{:S(2)}) collective-permute-start(bf16[512,128]{1,0:T(8,128)(2,1)S(1)} %add_convert_fusion), channel_id=1, source_target_pairs={{0,3},{1,0},{2,1},{3,2},{4,7},{5,4},{6,5},{7,6},{8,11},{9,8},{10,9... | collective-permute-start | bytes 393224 | tf_op jit(solution)/shard_map/ppermute | solution.py:8
  106.6 7.6 %collective-permute-start.9 = (bf16[512,128]{1,0:T(8,128)(2,1)S(1)}, bf16[512,128]{1,0:T(8,128)(2,1)S(1)}, u32[]{:S(2)}, u32[]{:S(2)}) collective-permute-start(bf16[512,128]{1,0:T(8,128)(2,1)S(1)} %add_convert_fusion), channel_id=1, source_target_pairs={{0,2},{1,3},{2,0},{3,1},{4,6},{5,7},{6,4},{7,5},{8,10},{9,11},{10,... | collective-permute-start | bytes 393224 | tf_op jit(solution)/shard_map/ppermute | solution.py:8
  107.6 7.1 %collective-permute-start.8 = (bf16[512,128]{1,0:T(8,128)(2,1)S(1)}, bf16[512,128]{1,0:T(8,128)(2,1)S(1)}, u32[]{:S(2)}, u32[]{:S(2)}) collective-permute-start(bf16[512,128]{1,0:T(8,128)(2,1)S(1)} %add_convert_fusion), channel_id=1, source_target_pairs={{0,1},{1,2},{2,3},{3,0},{4,5},{5,6},{6,7},{7,4},{8,9},{9,10},{10,1... | collective-permute-start | bytes 393224 | tf_op jit(solution)/shard_map/ppermute | solution.py:8
  120.7 3.9 %copy-start.2 = (bf16[1,8,4,16,512]{4,3,2,1,0:T(8,128)(2,1)}, bf16[1,8,4,16,512]{4,3,2,1,0:T(8,128)(2,1)S(1)}, u32[]{:S(2)}) copy-start(bf16[1,8,4,16,512]{4,3,2,1,0:T(8,128)(2,1)S(1)} %copy.50) | copy-start | bytes 1572868
  122.5 1.8 %copy-start.4 = (f32[4,512,128]{2,1,0:T(8,128)S(1)}, f32[4,512,128]{2,1,0:T(8,128)}, u32[]{:S(2)}) copy-start(f32[4,512,128]{2,1,0:T(8,128)} %convert_element_type.167) | copy-start | bytes 3145732
  124.2 3.2 %copy-start.3 = (bf16[1,8,4,16,512]{4,3,2,1,0:T(8,128)(2,1)}, bf16[1,8,4,16,512]{4,3,2,1,0:T(8,128)(2,1)S(1)}, u32[]{:S(2)}) copy-start(bf16[1,8,4,16,512]{4,3,2,1,0:T(8,128)(2,1)S(1)} %copy.47) | copy-start | bytes 1572868
  129.4 8.9 %copy-start.6 = (bf16[512,128]{1,0:T(8,128)(2,1)}, bf16[512,128]{1,0:T(8,128)(2,1)S(1)}, u32[]{:S(2)}) copy-start(bf16[512,128]{1,0:T(8,128)(2,1)S(1)} %convolution_convert_fusion.2) | copy-start | bytes 393220
  133.4 4.8 %copy-start.9 = (bf16[512,128]{1,0:T(8,128)(2,1)}, bf16[512,128]{1,0:T(8,128)(2,1)S(1)}, u32[]{:S(2)}) copy-start(bf16[512,128]{1,0:T(8,128)(2,1)S(1)} %convolution_convert_fusion.1) | copy-start | bytes 393220
  140.2 7.2 %copy-start.1 = (bf16[1,8,4,16,512]{4,3,2,1,0:T(8,128)(2,1)S(1)}, bf16[1,8,4,16,512]{4,3,2,1,0:T(8,128)(2,1)}, u32[]{:S(2)}) copy-start(bf16[1,8,4,16,512]{4,3,2,1,0:T(8,128)(2,1)} %copy.43) | copy-start | bytes 1572868
  148.7 6.1 %copy-start.5 = (bf16[512,128]{1,0:T(8,128)(2,1)S(1)}, bf16[512,128]{1,0:T(8,128)(2,1)}, u32[]{:S(2)}) copy-start(bf16[512,128]{1,0:T(8,128)(2,1)} %get-tuple-element.27) | copy-start | bytes 393220
  148.7 6.1 %copy-start.12 = (bf16[1,512,128]{2,1,0:T(8,128)(2,1)S(1)}, bf16[1,512,128]{2,1,0:T(8,128)(2,1)}, u32[]{:S(2)}) copy-start(bf16[1,512,128]{2,1,0:T(8,128)(2,1)} %convert_bitcast_fusion.2) | copy-start | bytes 393220
  148.7 6.1 %copy-start.13 = (bf16[1,512,128]{2,1,0:T(8,128)(2,1)S(1)}, bf16[1,512,128]{2,1,0:T(8,128)(2,1)}, u32[]{:S(2)}) copy-start(bf16[1,512,128]{2,1,0:T(8,128)(2,1)} %convert_bitcast_fusion.1) | copy-start | bytes 393220
  159.1 5.9 %copy-start.15 = (f32[1,64,128]{2,1,0:T(8,128)S(1)}, f32[1,64,128]{2,1,0:T(8,128)}, u32[]{:S(2)}) copy-start(f32[1,64,128]{2,1,0:T(8,128)} %dynamic-slice_bitcast_fusion.1) | copy-start | bytes 98308
  159.1 5.9 %copy-start.16 = (f32[1,64,128]{2,1,0:T(8,128)S(1)}, f32[1,64,128]{2,1,0:T(8,128)}, u32[]{:S(2)}) copy-start(f32[1,64,128]{2,1,0:T(8,128)} %dynamic-slice_bitcast_fusion.2) | copy-start | bytes 98308
  159.1 9.8 %copy-start.8 = (bf16[1,512,512]{2,1,0:T(8,128)(2,1)S(1)}, bf16[1,512,512]{2,1,0:T(8,128)(2,1)}, u32[]{:S(2)}) copy-start(bf16[1,512,512]{2,1,0:T(8,128)(2,1)} %param.9) | copy-start | bytes 1572868
  159.1 9.8 %copy-start.11 = (bf16[512,128]{1,0:T(8,128)(2,1)S(1)}, bf16[512,128]{1,0:T(8,128)(2,1)}, u32[]{:S(2)}) copy-start(bf16[512,128]{1,0:T(8,128)(2,1)} %copy-done.10) | copy-start | bytes 393220
  161.7 5.2 %collective-permute-start.13 = (bf16[512,128]{1,0:T(8,128)(2,1)S(1)}, bf16[512,128]{1,0:T(8,128)(2,1)S(1)}, u32[]{:S(2)}, u32[]{:S(2)}) collective-permute-start(bf16[512,128]{1,0:T(8,128)(2,1)S(1)} %get-tuple-element.23), channel_id=1, source_target_pairs={{0,1},{1,2},{2,3},{3,0},{4,5},{5,6},{6,7},{7,4},{8,9},{9,10},{10,1... | collective-permute-start | bytes 393224 | tf_op jit(solution)/shard_map/ppermute | solution.py:8
  161.7 6.4 %collective-permute-start.12 = (bf16[512,128]{1,0:T(8,128)(2,1)S(1)}, bf16[512,128]{1,0:T(8,128)(2,1)S(1)}, u32[]{:S(2)}, u32[]{:S(2)}) collective-permute-start(bf16[512,128]{1,0:T(8,128)(2,1)S(1)} %get-tuple-element.24), channel_id=1, source_target_pairs={{0,2},{1,3},{2,0},{3,1},{4,6},{5,7},{6,4},{7,5},{8,10},{9,11},{10,... | collective-permute-start | bytes 393224 | tf_op jit(solution)/shard_map/ppermute | solution.py:8
  162.8 6.0 %collective-permute-start.11 = (bf16[512,128]{1,0:T(8,128)(2,1)S(1)}, bf16[512,128]{1,0:T(8,128)(2,1)S(1)}, u32[]{:S(2)}, u32[]{:S(2)}) collective-permute-start(bf16[512,128]{1,0:T(8,128)(2,1)S(1)} %get-tuple-element.22), channel_id=1, source_target_pairs={{0,3},{1,0},{2,1},{3,2},{4,7},{5,4},{6,5},{7,6},{8,11},{9,8},{10,9... | collective-permute-start | bytes 393224 | tf_op jit(solution)/shard_map/ppermute | solution.py:8
Sparse Core Ops, SparseCore 0:
  10.8 44.5 all-gather.4
  56.9 44.8 all-gather.6

commit v3 on v2

v3 whole, which is shorter than its diff:
```python
import jax
import jax.numpy as jnp
import numpy as np
from jax import lax
from jax.sharding import PartitionSpec as P


def shifted(x, axis, size, shift):
    return lax.ppermute(x, axis, [(i, (i + shift) % size) for i in range(size)])


def swapped(x, axis, size, bit):
    return lax.ppermute(x, axis, [(i, i ^ bit) for i in range(size)])


def broadcast_from(x, owner, me, axis, size):
    got = None
    for s in range(1, size):
        part = lax.ppermute(x, axis, [(owner, (owner + s) % size)])
        got = part if got is None else got + part
    return jnp.where(me == owner, x, got)


def pair_index(t, u):
    return t * (t - 1) // 2 + u


def tile_table(levels):
    table = np.zeros((levels, levels - 1), np.int32)
    for c in range(levels):
        for j in range(levels - 1):
            table[c, j] = pair_index(c, j) if j < c else pair_index(j + 1, c)
    return table


def summed_chunks(x, peers, rows_n, me):
    chunks = x.reshape(peers, -1, x.shape[-1]).astype(jnp.bfloat16)
    bit = peers // 2
    while bit >= 1:
        halves = chunks.reshape(2, -1, *chunks.shape[1:])
        mine = (me // bit) % 2
        keep = lax.dynamic_index_in_dim(halves, mine, 0, keepdims=False)
        give = lax.dynamic_index_in_dim(halves, 1 - mine, 0, keepdims=False)
        got = swapped(give, "col", peers, bit)
        chunks = (keep.astype(jnp.float32) + got.astype(jnp.float32)).astype(jnp.bfloat16)
        bit //= 2
    part = chunks[0]
    bit = 1
    while bit < rows_n:
        got = swapped(part, "row", rows_n, bit)
        part = (part.astype(jnp.float32) + got.astype(jnp.float32)).astype(jnp.bfloat16)
        bit *= 2
    return part


def gathered_chunks(part, peers, me):
    pieces = [part] + [shifted(part, "col", peers, s) for s in range(1, peers)]
    stacked = jnp.stack(pieces)
    source = (me - jnp.arange(peers)) % peers
    return jnp.zeros_like(stacked).at[source].set(stacked)


def local(low_rhs, low_inv, low_tiles, tile_rows, tile_cols, top_rhs, top_inv, top_tiles):
    peers = lax.axis_size("col")
    rows_n = lax.axis_size("row")
    levels = top_rhs.shape[0]
    share = top_rhs.shape[1]
    width = top_rhs.shape[2]
    position = lax.axis_index("row")
    me = lax.axis_index("col")
    owned = jnp.minimum(me, levels - 1)

    picks = jnp.asarray(tile_table(levels))[owned]
    mine = jnp.concatenate(
        [lax.dynamic_index_in_dim(top_inv, owned, 0), jnp.take(top_tiles, picks, axis=0)], axis=0
    )
    mats = lax.all_gather(mine, "row", axis=1, tiled=True)
    inv = mats[0]

    slot_rows = tile_rows[0]
    slot_cols = tile_cols[0] % peers
    alive = slot_rows >= 0
    safe_rows = jnp.maximum(slot_rows, 0)
    own_tiles = low_tiles[0]
    low_forward = jnp.dot(low_inv[0], low_rhs[0], preferred_element_type=jnp.float32).astype(
        jnp.bfloat16
    )
    received = [low_forward] + [shifted(low_forward, "col", peers, s) for s in range(1, peers)]
    source_of = (me - jnp.arange(peers)) % peers
    by_source = jnp.stack(received)
    slot_pick = jnp.argmax(source_of[None, :] == slot_cols[:, None], axis=1)
    products = jnp.einsum(
        "sab,sbk->sak", own_tiles, by_source[slot_pick], preferred_element_type=jnp.float32
    )
    pick_level = (slot_rows[:, None] == jnp.arange(levels, dtype=jnp.int32)[None, :]).astype(
        jnp.float32
    )
    coupling = jnp.einsum("st,sak->tak", pick_level, products, precision=lax.Precision.HIGHEST)
    own_rhs = jnp.zeros((levels, share * rows_n, width), jnp.float32)
    own_rhs = lax.dynamic_update_slice_in_dim(own_rhs, top_rhs.astype(jnp.float32), position * share, 1)
    coupling = coupling - jnp.where(me == 0, own_rhs, 0.0)
    part = summed_chunks(coupling, peers, rows_n, me)
    if peers == levels:
        level_sum = part
    else:
        level_sum = gathered_chunks(part, peers, me).reshape(levels, -1, width)[owned]
    rhs_level = -level_sum.astype(jnp.float32)

    top_forward = [None] * levels
    for level in range(levels):
        residue = rhs_level
        for u in range(level):
            residue = residue - jnp.dot(mats[1 + u], top_forward[u], preferred_element_type=jnp.float32)
        solved = jnp.dot(inv, residue.astype(jnp.bfloat16), preferred_element_type=jnp.float32)
        solved = solved.astype(jnp.bfloat16)
        if level < levels - 1:
            solved = broadcast_from(solved, level, me, "col", peers)
        top_forward[level] = solved
    top_back = [None] * levels
    top_slices = [None] * levels
    for level in reversed(range(levels)):
        update = top_forward[level].astype(jnp.float32)
        for k in range(level + 1, levels):
            update = update - lax.dot_general(
                mats[k], top_back[k], (((0,), (0,)), ((), ())), preferred_element_type=jnp.float32
            )
        solved = lax.dot_general(
            inv, update.astype(jnp.bfloat16), (((0,), (0,)), ((), ())), preferred_element_type=jnp.float32
        )
        solved = broadcast_from(solved, level, me, "col", peers)
        top_slices[level] = lax.dynamic_slice_in_dim(solved, position * share, share, 0)
        top_back[level] = solved.astype(jnp.bfloat16)

    back_stack = jnp.stack(top_back)
    products_back = jnp.einsum(
        "sab,sak->sbk", own_tiles, back_stack[safe_rows], preferred_element_type=jnp.float32
    )
    pick_peer = ((slot_cols[:, None] == source_of[None, :]) & alive[:, None]).astype(jnp.float32)
    terms = jnp.einsum(
        "sp,sbk->pbk", pick_peer, products_back, precision=lax.Precision.HIGHEST
    ).astype(jnp.bfloat16)
    returned = terms[0].astype(jnp.float32)
    for s in range(1, peers):
        returned = returned + shifted(terms[s], "col", peers, peers - s).astype(jnp.float32)
    low_update = (low_forward.astype(jnp.float32) - returned).astype(jnp.bfloat16)
    low_solution = lax.dot_general(
        low_inv[0], low_update, (((0,), (0,)), ((), ())), preferred_element_type=jnp.float32
    )
    return (low_solution[None], jnp.stack(top_slices))


def solution(mesh):
    in_specs = (
        P(("row", "col"), None, None),
        P(("row", "col"), None, None),
        P(("row", "col"), None, None, None),
        P(("row", "col"), None),
        P(("row", "col"), None),
        P(None, "row", None),
        P(None, "row", None),
        P(None, "row", None),
    )
    out_specs = (P(("row", "col"), None, None), P(None, "row", None))
    return jax.shard_map(local, mesh=mesh, in_specs=in_specs, out_specs=out_specs, check_vma=False)
```

time: 178 us -> 177 us (level)
  starting transfers between devices: 10.5 us -> 40.1 us
  waiting for transfers between devices: 89.8 us -> 75.6 us
  local copies, waits for them, and re-layouts: 20.1 us -> 10.4 us
  matrix products: 34.3 us -> 25.4 us
  other arithmetic: 7.63 us -> 9.7 us
    all_gather x2 -> x1, waiting for transfers between devices: 46.3 us -> 2.58 us  [local(): mats = lax.all_gather(mine, 'row', axis=1, tiled=True)]
    ppermute x0 -> x21, waiting for transfers between devices: none -> 35.3 us  [broadcast_from(): part = lax.ppermute(x, axis, [(owner, (owner + s) % size)])]
    ppermute x0 -> x21, starting transfers between devices: none -> 26.7 us  [broadcast_from(): part = lax.ppermute(x, axis, [(owner, (owner + s) % size)])]
    dot_general x14 -> x12, matrix products: 25.2 us -> 15 us  [the longest x4 5.3 us: local(): lax.dot_general(inv, update.astype(jnp.bfloat16), (((0,), (0,)), ((), ())...]
    ppermute x9 -> x6, waiting for transfers between devices: 14.5 us -> 5.61 us  [shifted(): return lax.ppermute(x, axis, [(i, (i + shift) % size) for i in range(size)])]
    slice x11 -> x0, local copies, waits for them, and re-layouts: 8.33 us -> none  [the longest x4 5.6 us: local(): tiles_all[k * (k - 1) // 2 + level]]
    ppermute x5, waiting for transfers between devices: 29 us -> 32.1 us  [swapped(): return lax.ppermute(x, axis, [(i, i ^ bit) for i in range(size)])]
    ppermute x5, starting transfers between devices: 4.84 us -> 7.74 us  [swapped(): return lax.ppermute(x, axis, [(i, i ^ bit) for i in range(size)])]
  transfers between devices with their start and end apart: 16 -> 33, of which waited for: 14 -> 17; matrix products, arithmetic and copies ran while one was open for 8% -> 9% of each run, Pallas kernels for 0% -> 0%
where the time goes in v3:
time: 177 us; the launch traced here: 176 us
  waiting for transfers between devices  75.6 us (43%)
  starting transfers between devices  40.1 us (23%)
  matrix products  25.4 us (14%)
  between operations  14.7 us (8%)
  local copies, waits for them, and re-layouts  10.4 us (6%)
  other arithmetic  9.7 us (5%)
    ppermute x21, waiting for transfers between devices, broadcast_from(): part = lax.ppermute(x, axis, [(owner, (owner + s) % size)])  35.3 us
    ppermute x5, waiting for transfers between devices, swapped(): return lax.ppermute(x, axis, [(i, i ^ bit) for i in range(size)])  32.1 us
    ppermute x21, starting transfers between devices, broadcast_from(): part = lax.ppermute(x, axis, [(owner, (owner + s) % size)])  26.7 us
    ppermute x5, starting transfers between devices, swapped(): return lax.ppermute(x, axis, [(i, i ^ bit) for i in range(size)])  7.74 us
    ppermute x6, waiting for transfers between devices, shifted(): return lax.ppermute(x, axis, [(i, (i + shift) % size) for i in range(size)])  5.61 us
    ppermute x6, starting transfers between devices, shifted(): return lax.ppermute(x, axis, [(i, (i + shift) % size) for i in range(size)])  5.6 us
    dot_general x4, matrix products, local(): lax.dot_general(inv, update.astype(jnp.bfloat16), (((0,), (0,)), ((), ())...  5.3 us
    another operation x5, other arithmetic, local(): back_stack = jnp.stack(top_back)  5.17 us
  transfers between devices with their start and end apart: 33, of which 17 were waited for; matrix products, arithmetic and copies ran while one was open for 9% of the time, Pallas kernels for 0%

profile of v3, /device:TPU:0, one launch (start us, length us, event | category | flops | bytes accessed | tf_op | source)
XLA Modules:
  0.0 175.9 jit_solution(18151293830952235689)
XLA Ops:
  7.2 1.5 convolution_convert_fusion.4
  9.3 2.6 %collective-permute-start.1 = (bf16[512,128]{1,0:T(8,128)(2,1)S(1)}, bf16[512,128]{1,0:T(8,128)(2,1)S(1)}, u32[]{:S(2)}, u32[]{:S(2)}) collective-permute-start(bf16[512,128]{1,0:T(8,128)(2,1)S(1)} %convolution_convert_fusion.4), channel_id=1, source_target_pairs={{0,2},{1,3},{2,0},{3,1},{4,6},{5,7},{6,4},{7,5},{8,10},{9,11},{10,... | collective-permute-start | bytes 393224 | tf_op jit(solution)/shard_map/ppermute | solution.py:9
  11.9 1.4 collective-permute-start.2
  14.0 0.7 compare_and_fusion
  14.7 0.9 constant_dynamic-slice_fusion.4
  15.5 1.6 gather_fusion
  17.2 0.7 pad_maximum_fusion.2
  18.5 1.1 broadcast_in_dim.31
  19.7 0.7 select_dynamic-update-slice_fusion
  20.5 1.4 gather_fusion.1
  21.9 1.9 %fusion.2 = f32[4,128,512]{2,1,0:T(8,128)S(1)} fusion(bf16[4,512,128]{2,1,0:T(8,128)(2,1)} %gather_fusion.1, bf16[1,4,512,512]{3,2,1,0:T(8,128)(2,1)S(1)} %copy-done), kind=kOutput, calls=%fused_computation.5 | convolution fusion | flops 268435456 | bytes 3670016 | tf_op jit(solution)/shard_map/sab,sbk->sak/dot_general | solution.py:92
  23.8 1.3 copy.16
  25.1 2.8 %fusion.4 = bf16[4,512,128]{2,0,1:T(4,128)(2,1)S(1)} fusion(f32[4,512,128]{2,0,1:T(4,128)} %select_dynamic-update-slice_fusion, f32[4,128,512]{1,0,2:T(4,128)} %copy.16, s32[4]{0:T(128)S(1)} %bitcast.122), kind=kOutput, calls=%fused_computation.8 | convolution fusion | flops 13107216 | bytes 2621456 | tf_op jit(solution)/shard_map/st,sak->tak/dot_general | solution.py:98
  28.6 7.1 %collective-permute-done.3 = bf16[2,512,128]{2,1,0:T(8,128)(2,1)S(1)} collective-permute-done((bf16[2,512,128]{2,1,0:T(8,128)(2,1)S(1)}, bf16[2,512,128]{2,1,0:T(8,128)(2,1)S(1)}, u32[]{:S(2)}, u32[]{:S(2)}) %collective-permute-start.3) | collective-permute-done | bytes 262176 | tf_op jit(solution)/shard_map/ppermute | solution.py:13
  35.9 1.3 collective-permute-done.4
  37.2 1.5 collective-permute-start.5
  38.8 4.1 %collective-permute-done.5 = bf16[512,128]{1,0:T(8,128)(2,1)S(1)} collective-permute-done((bf16[512,128]{1,0:T(8,128)(2,1)S(1)}, bf16[512,128]{1,0:T(8,128)(2,1)S(1)}, u32[]{:S(2)}, u32[]{:S(2)}) %collective-permute-start.5) | collective-permute-done | bytes 131104 | tf_op jit(solution)/shard_map/ppermute | solution.py:13
  42.9 1.7 collective-permute-start.6
  44.6 7.4 %collective-permute-done.6 = bf16[512,128]{1,0:T(8,128)(2,1)S(1)} collective-permute-done((bf16[512,128]{1,0:T(8,128)(2,1)S(1)}, bf16[512,128]{1,0:T(8,128)(2,1)S(1)}, u32[]{:S(2)}, u32[]{:S(2)}) %collective-permute-start.6) | collective-permute-done | bytes 131104 | tf_op jit(solution)/shard_map/ppermute | solution.py:13
  52.0 4.2 %collective-permute-start.7 = (bf16[512,128]{1,0:T(8,128)(2,1)S(1)}, bf16[512,128]{1,0:T(8,128)(2,1)S(1)}, u32[]{:S(2)}, u32[]{:S(2)}) collective-permute-start(bf16[512,128]{1,0:T(8,128)(2,1)S(1)} %add_convert_fusion.1), channel_id=1, source_target_pairs={{0,16},{4,20},{8,24},{12,28},{16,0},{20,4},{24,8},{28,12},{1,17},{... | collective-permute-start | bytes 393224 | tf_op jit(solution)/shard_map/ppermute | solution.py:13
  56.2 12.2 %collective-permute-done.7 = bf16[512,128]{1,0:T(8,128)(2,1)S(1)} collective-permute-done((bf16[512,128]{1,0:T(8,128)(2,1)S(1)}, bf16[512,128]{1,0:T(8,128)(2,1)S(1)}, u32[]{:S(2)}, u32[]{:S(2)}) %collective-permute-start.7) | collective-permute-done | bytes 131104 | tf_op jit(solution)/shard_map/ppermute | solution.py:13
  68.4 2.6 %all-gather.2.cloned.1.call-done = bf16[4,512,512]{2,1,0:T(8,128)(2,1)} async-done(((bf16[4,64,512]{2,1,0:T(8,128)(2,1)}), bf16[4,512,512]{2,1,0:T(8,128)(2,1)}) %all-gather.2.cloned.1.call-update) | async-done | bytes 2097168 | tf_op jit(solution)/shard_map/all_gather | solution.py:77
  71.0 1.3 convolution_convert_fusion.3
  72.4 2.7 %collective-permute-start.10 = (bf16[512,128]{1,0:T(8,128)(2,1)S(1)}, bf16[512,128]{1,0:T(8,128)(2,1)S(1)}, u32[]{:S(2)}, u32[]{:S(2)}) collective-permute-start(bf16[512,128]{1,0:T(8,128)(2,1)S(1)} %convolution_convert_fusion.3), channel_id=1, source_target_pairs={{0,3},{4,7},{8,11},{12,15},{16,19},{20,23},{24,27},{28,31}} | collective-permute-start | bytes 393224 | tf_op jit(solution)/shard_map/ppermute | solution.py:19
  75.0 1.3 collective-permute-start.8
  76.3 1.3 collective-permute-start.9
  77.7 2.5 %collective-permute-done.9 = bf16[512,128]{1,0:T(8,128)(2,1)S(1)} collective-permute-done((bf16[512,128]{1,0:T(8,128)(2,1)S(1)}, bf16[512,128]{1,0:T(8,128)(2,1)S(1)}, u32[]{:S(2)}, u32[]{:S(2)}) %collective-permute-start.9) | collective-permute-done | bytes 131104 | tf_op jit(solution)/shard_map/ppermute | solution.py:19
  80.2 1.3 convolution_subtract_fusion.3
  81.5 1.3 convolution_convert_fusion.2
  84.2 1.3 collective-permute-start.13
  85.5 5.2 %collective-permute-done.13 = bf16[512,128]{1,0:T(8,128)(2,1)S(1)} collective-permute-done((bf16[512,128]{1,0:T(8,128)(2,1)S(1)}, bf16[512,128]{1,0:T(8,128)(2,1)S(1)}, u32[]{:S(2)}, u32[]{:S(2)}) %collective-permute-start.13) | collective-permute-done | bytes 131104 | tf_op jit(solution)/shard_map/ppermute | solution.py:19
  90.8 1.3 convolution_subtract_fusion.2
  92.1 1.3 convolution_convert_fusion.1
  94.2 1.3 collective-permute-start.15
  96.1 5.5 %collective-permute-done.15 = bf16[512,128]{1,0:T(8,128)(2,1)S(1)} collective-permute-done((bf16[512,128]{1,0:T(8,128)(2,1)S(1)}, bf16[512,128]{1,0:T(8,128)(2,1)S(1)}, u32[]{:S(2)}, u32[]{:S(2)}) %collective-permute-start.15) | collective-permute-done | bytes 131104 | tf_op jit(solution)/shard_map/ppermute | solution.py:19
  101.7 1.3 fusion.5
  103.0 1.9 %fusion.6 = f32[512,128]{1,0:T(8,128)S(1)} fusion(bf16[512,128]{1,0:T(8,128)(2,1)S(1)} %fusion.5, bf16[4,512,512]{2,1,0:T(8,128)(2,1)} %all-gather.2.cloned.1.call-done), kind=kOutput, calls=%fused_computation.19 | convolution fusion | flops 134283264 | bytes 1441792 | tf_op jit(solution)/shard_map/dot_general | solution.py:127
  105.0 1.3 collective-permute-start.17
  107.0 1.4 collective-permute-start.19
  108.3 4.3 %collective-permute-done.17 = f32[512,128]{1,0:T(8,128)S(1)} collective-permute-done((f32[512,128]{1,0:T(8,128)S(1)}, f32[512,128]{1,0:T(8,128)S(1)}, u32[]{:S(2)}, u32[]{:S(2)}) %collective-permute-start.17) | collective-permute-done | bytes 262176 | tf_op jit(solution)/shard_map/ppermute | solution.py:19
  112.7 1.7 convert_bitcast_fusion.3
  114.3 1.4 fusion.15
  116.8 1.3 collective-permute-start.21
  118.8 7.3 %collective-permute-done.21 = f32[512,128]{1,0:T(8,128)S(1)} collective-permute-done((f32[512,128]{1,0:T(8,128)S(1)}, f32[512,128]{1,0:T(8,128)S(1)}, u32[]{:S(2)}, u32[]{:S(2)}) %collective-permute-start.21) | collective-permute-done | bytes 262176 | tf_op jit(solution)/shard_map/ppermute | solution.py:19
  126.1 0.7 convert_bitcast_fusion.2
  128.9 1.3 collective-permute-start.25
  130.3 5.3 %collective-permute-done.25 = f32[512,128]{1,0:T(8,128)S(1)} collective-permute-done((f32[512,128]{1,0:T(8,128)S(1)}, f32[512,128]{1,0:T(8,128)S(1)}, u32[]{:S(2)}, u32[]{:S(2)}) %collective-permute-start.25) | collective-permute-done | bytes 262176 | tf_op jit(solution)/shard_map/ppermute | solution.py:19
  135.5 0.7 convert_bitcast_fusion.1
  136.2 2.7 %fusion.23 = f32[512,128]{1,0:T(8,128)} fusion(bf16[4,512,512]{2,1,0:T(8,128)(2,1)} %all-gather.2.cloned.1.call-done, f32[512,128]{1,0:T(8,128)S(1)} %fusion.15, f32[512,128]{1,0:T(8,128)S(1)} %fusion.14, bf16[512,128]{1,0:T(8,128)(2,1)S(1)} %add_select_fusion.6, f32[512,128]{1,0:T(8,128)S(1)} %get-tuple-element.9), kind=kOutput, calls=%fused_computation.61 | convolution fusion | flops 134610944 | bytes 2228224 | tf_op jit(solution)/shard_map/dot_general | solution.py:127
  138.9 4.4 %collective-permute-start.26 = (f32[512,128]{1,0:T(8,128)}, f32[512,128]{1,0:T(8,128)S(1)}, u32[]{:S(2)}, u32[]{:S(2)}) collective-permute-start(f32[512,128]{1,0:T(8,128)} %fusion.23), channel_id=1, source_target_pairs={{0,1},{4,5},{8,9},{12,13},{16,17},{20,21},{24,25},{28,29}} | collective-permute-start | bytes 786440 | tf_op jit(solution)/shard_map/ppermute | solution.py:19
  143.3 1.3 collective-permute-start.27
  144.6 1.8 %collective-permute-start.28 = (f32[512,128]{1,0:T(8,128)}, f32[512,128]{1,0:T(8,128)S(1)}, u32[]{:S(2)}, u32[]{:S(2)}) collective-permute-start(f32[512,128]{1,0:T(8,128)} %fusion.23), channel_id=1, source_target_pairs={{0,3},{4,7},{8,11},{12,15},{16,19},{20,23},{24,27},{28,31}} | collective-permute-start | bytes 786440 | tf_op jit(solution)/shard_map/ppermute | solution.py:19
  146.5 2.3 %collective-permute-done.27 = f32[512,128]{1,0:T(8,128)S(1)} collective-permute-done((f32[512,128]{1,0:T(8,128)}, f32[512,128]{1,0:T(8,128)S(1)}, u32[]{:S(2)}, u32[]{:S(2)}) %collective-permute-start.27) | collective-permute-done | bytes 262176 | tf_op jit(solution)/shard_map/ppermute | solution.py:19
  148.8 2.8 %collective-permute-done.28 = f32[512,128]{1,0:T(8,128)S(1)} collective-permute-done((f32[512,128]{1,0:T(8,128)}, f32[512,128]{1,0:T(8,128)S(1)}, u32[]{:S(2)}, u32[]{:S(2)}) %collective-permute-start.28) | collective-permute-done | bytes 262176 | tf_op jit(solution)/shard_map/ppermute | solution.py:19
  151.6 1.0 convert_bitcast_fusion
  152.6 1.1 pad_maximum_fusion.1
  153.7 1.4 gather_fusion.2
  155.1 1.5 fusion
  156.7 1.3 copy.17
  158.0 2.4 %fusion.7 = bf16[4,512,128]{2,0,1:T(4,128)(2,1)S(1)} fusion(f32[4,128,512]{1,0,2:T(4,128)} %copy.17, s32[4]{0:T(128)S(1)} %get-tuple-element.20, pred[4]{0:T(512)(128)(4,1)S(1)} %broadcast_compare_fusion, s32[4]{0:T(128)S(1)} %get-tuple-element.19), kind=kOutput, calls=%fused_computation.20 | convolution fusion | flops 12582944 | bytes 1572900 | tf_op jit(solution)/shard_map/sp,sbk->pbk/dot_general | solution.py:139
  160.5 0.9 collective-permute-start.29
  162.3 3.0 %collective-permute-done.29 = bf16[512,128]{1,0:T(8,128)(2,1)S(1)} collective-permute-done((bf16[512,128]{1,0:T(8,128)(2,1)S(1)}, bf16[512,128]{1,0:T(8,128)(2,1)S(1)}, u32[]{:S(2)}, u32[]{:S(2)}) %collective-permute-start.29) | collective-permute-done | bytes 131104 | tf_op jit(solution)/shard_map/ppermute | solution.py:9
  165.3 2.5 %collective-permute-done.30 = bf16[512,128]{1,0:T(8,128)(2,1)S(1)} collective-permute-done((bf16[512,128]{1,0:T(8,128)(2,1)S(1)}, bf16[512,128]{1,0:T(8,128)(2,1)S(1)}, u32[]{:S(2)}, u32[]{:S(2)}) %collective-permute-start.30) | collective-permute-done | bytes 131104 | tf_op jit(solution)/shard_map/ppermute | solution.py:9
  168.2 0.8 copy.15
  (83 shorter events, 11.7 us)
Async XLA Ops:
  7.2 14.7 %copy-start = (bf16[1,4,512,512]{3,2,1,0:T(8,128)(2,1)S(1)}, bf16[1,4,512,512]{3,2,1,0:T(8,128)(2,1)}, u32[]{:S(2)}) copy-start(bf16[1,4,512,512]{3,2,1,0:T(8,128)(2,1)} %param.11) | copy-start | bytes 6291460
  7.2 10.7 %copy-start.6 = (s32[1,4]{1,0:T(1,128)S(1)}, s32[1,4]{1,0:T(1,128)}, u32[]{:S(2)}) copy-start(s32[1,4]{1,0:T(1,128)} %param.13) | copy-start | bytes 52
  7.2 12.5 %copy-start.5 = (bf16[4,64,128]{2,1,0:T(8,128)(2,1)S(1)}, bf16[4,64,128]{2,1,0:T(8,128)(2,1)}, u32[]{:S(2)}) copy-start(bf16[4,64,128]{2,1,0:T(8,128)(2,1)} %param.14) | copy-start | bytes 196612
  7.2 63.8 %all-gather.2.cloned.1.call-start = ((), (), s32[]{:S(2)}) async-start(), calls=%async_computation | async-start | bytes 2359296 | tf_op jit(solution)/shard_map/all_gather | solution.py:77
  8.8 11.7 %copy-start.3 = (bf16[512,128]{1,0:T(8,128)(2,1)}, bf16[512,128]{1,0:T(8,128)(2,1)S(1)}, u32[]{:S(2)}) copy-start(bf16[512,128]{1,0:T(8,128)(2,1)S(1)} %convolution_convert_fusion.4) | copy-start | bytes 393220
  8.8 11.6 %collective-permute-start = (bf16[512,128]{1,0:T(8,128)(2,1)S(1)}, bf16[512,128]{1,0:T(8,128)(2,1)S(1)}, u32[]{:S(2)}, u32[]{:S(2)}) collective-permute-start(bf16[512,128]{1,0:T(8,128)(2,1)S(1)} %convolution_convert_fusion.4), channel_id=1, source_target_pairs={{0,1},{1,2},{2,3},{3,0},{4,5},{5,6},{6,7},{7,4},{8,9},{9,10},{10,1... | collective-permute-start | bytes 393224 | tf_op jit(solution)/shard_map/ppermute | solution.py:9
  9.3 11.1 %collective-permute-start.1 = (bf16[512,128]{1,0:T(8,128)(2,1)S(1)}, bf16[512,128]{1,0:T(8,128)(2,1)S(1)}, u32[]{:S(2)}, u32[]{:S(2)}) collective-permute-start(bf16[512,128]{1,0:T(8,128)(2,1)S(1)} %convolution_convert_fusion.4), channel_id=1, source_target_pairs={{0,2},{1,3},{2,0},{3,1},{4,6},{5,7},{6,4},{7,5},{8,10},{9,11},{10,... | collective-permute-start | bytes 393224 | tf_op jit(solution)/shard_map/ppermute | solution.py:9
  11.9 8.5 %collective-permute-start.2 = (bf16[512,128]{1,0:T(8,128)(2,1)S(1)}, bf16[512,128]{1,0:T(8,128)(2,1)S(1)}, u32[]{:S(2)}, u32[]{:S(2)}) collective-permute-start(bf16[512,128]{1,0:T(8,128)(2,1)S(1)} %convolution_convert_fusion.4), channel_id=1, source_target_pairs={{0,3},{1,0},{2,1},{3,2},{4,7},{5,4},{6,5},{7,6},{8,11},{9,8},{10,9... | collective-permute-start | bytes 393224 | tf_op jit(solution)/shard_map/ppermute | solution.py:9
  21.9 3.2 %copy-start.7 = (s32[1,4]{1,0:T(1,128)S(1)}, s32[1,4]{1,0:T(1,128)}, u32[]{:S(2)}) copy-start(s32[1,4]{1,0:T(1,128)} %param.12) | copy-start | bytes 52
  28.4 7.3 %collective-permute-start.3 = (bf16[2,512,128]{2,1,0:T(8,128)(2,1)S(1)}, bf16[2,512,128]{2,1,0:T(8,128)(2,1)S(1)}, u32[]{:S(2)}, u32[]{:S(2)}) collective-permute-start(bf16[2,512,128]{2,1,0:T(8,128)(2,1)S(1)} %bitcast.118), channel_id=1, source_target_pairs={{0,2},{1,3},{2,0},{3,1},{4,6},{5,7},{6,4},{7,5},{8,10},{9,11},{10,... | collective-permute-start | bytes 786440 | tf_op jit(solution)/shard_map/ppermute | solution.py:13
  35.8 1.4 collective-permute-start.4
  37.2 5.6 %collective-permute-start.5 = (bf16[512,128]{1,0:T(8,128)(2,1)S(1)}, bf16[512,128]{1,0:T(8,128)(2,1)S(1)}, u32[]{:S(2)}, u32[]{:S(2)}) collective-permute-start(bf16[512,128]{1,0:T(8,128)(2,1)S(1)} %fusion.24), channel_id=1, source_target_pairs={{0,4},{4,0},{8,12},{12,8},{16,20},{20,16},{24,28},{28,24},{1,5},{5... | collective-permute-start | bytes 393224 | tf_op jit(solution)/shard_map/ppermute | solution.py:13
  42.9 9.1 %collective-permute-start.6 = (bf16[512,128]{1,0:T(8,128)(2,1)S(1)}, bf16[512,128]{1,0:T(8,128)(2,1)S(1)}, u32[]{:S(2)}, u32[]{:S(2)}) collective-permute-start(bf16[512,128]{1,0:T(8,128)(2,1)S(1)} %add_convert_fusion.2), channel_id=1, source_target_pairs={{0,8},{4,12},{8,0},{12,4},{16,24},{20,28},{24,16},{28,20},{1,9},{5... | collective-permute-start | bytes 393224 | tf_op jit(solution)/shard_map/ppermute | solution.py:13
  52.0 16.4 %collective-permute-start.7 = (bf16[512,128]{1,0:T(8,128)(2,1)S(1)}, bf16[512,128]{1,0:T(8,128)(2,1)S(1)}, u32[]{:S(2)}, u32[]{:S(2)}) collective-permute-start(bf16[512,128]{1,0:T(8,128)(2,1)S(1)} %add_convert_fusion.1), channel_id=1, source_target_pairs={{0,16},{4,20},{8,24},{12,28},{16,0},{20,4},{24,8},{28,12},{1,17},{... | collective-permute-start | bytes 393224 | tf_op jit(solution)/shard_map/ppermute | solution.py:13
  72.4 5.3 %collective-permute-start.10 = (bf16[512,128]{1,0:T(8,128)(2,1)S(1)}, bf16[512,128]{1,0:T(8,128)(2,1)S(1)}, u32[]{:S(2)}, u32[]{:S(2)}) collective-permute-start(bf16[512,128]{1,0:T(8,128)(2,1)S(1)} %convolution_convert_fusion.3), channel_id=1, source_target_pairs={{0,3},{4,7},{8,11},{12,15},{16,19},{20,23},{24,27},{28,31}} | collective-permute-start | bytes 393224 | tf_op jit(solution)/shard_map/ppermute | solution.py:19
  75.0 2.6 %collective-permute-start.8 = (bf16[512,128]{1,0:T(8,128)(2,1)S(1)}, bf16[512,128]{1,0:T(8,128)(2,1)S(1)}, u32[]{:S(2)}, u32[]{:S(2)}) collective-permute-start(bf16[512,128]{1,0:T(8,128)(2,1)S(1)} %convolution_convert_fusion.3), channel_id=1, source_target_pairs={{0,1},{4,5},{8,9},{12,13},{16,17},{20,21},{24,25},{28,29}} | collective-permute-start | bytes 393224 | tf_op jit(solution)/shard_map/ppermute | solution.py:19
  76.3 3.8 %collective-permute-start.9 = (bf16[512,128]{1,0:T(8,128)(2,1)S(1)}, bf16[512,128]{1,0:T(8,128)(2,1)S(1)}, u32[]{:S(2)}, u32[]{:S(2)}) collective-permute-start(bf16[512,128]{1,0:T(8,128)(2,1)S(1)} %convolution_convert_fusion.3), channel_id=1, source_target_pairs={{0,2},{4,6},{8,10},{12,14},{16,18},{20,22},{24,26},{28,30}} | collective-permute-start | bytes 393224 | tf_op jit(solution)/shard_map/ppermute | solution.py:19
  82.8 2.7 %collective-permute-start.11 = (bf16[512,128]{1,0:T(8,128)(2,1)S(1)}, bf16[512,128]{1,0:T(8,128)(2,1)S(1)}, u32[]{:S(2)}, u32[]{:S(2)}) collective-permute-start(bf16[512,128]{1,0:T(8,128)(2,1)S(1)} %convolution_convert_fusion.2), channel_id=1, source_target_pairs={{1,2},{5,6},{9,10},{13,14},{17,18},{21,22},{25,26},{29,30}} | collective-permute-start | bytes 393224 | tf_op jit(solution)/shard_map/ppermute | solution.py:19
  83.5 2.0 %collective-permute-start.12 = (bf16[512,128]{1,0:T(8,128)(2,1)S(1)}, bf16[512,128]{1,0:T(8,128)(2,1)S(1)}, u32[]{:S(2)}, u32[]{:S(2)}) collective-permute-start(bf16[512,128]{1,0:T(8,128)(2,1)S(1)} %convolution_convert_fusion.2), channel_id=1, source_target_pairs={{1,3},{5,7},{9,11},{13,15},{17,19},{21,23},{25,27},{29,31}} | collective-permute-start | bytes 393224 | tf_op jit(solution)/shard_map/ppermute | solution.py:19
  84.2 6.6 %collective-permute-start.13 = (bf16[512,128]{1,0:T(8,128)(2,1)S(1)}, bf16[512,128]{1,0:T(8,128)(2,1)S(1)}, u32[]{:S(2)}, u32[]{:S(2)}) collective-permute-start(bf16[512,128]{1,0:T(8,128)(2,1)S(1)} %convolution_convert_fusion.2), channel_id=1, source_target_pairs={{1,0},{5,4},{9,8},{13,12},{17,16},{21,20},{25,24},{29,28}} | collective-permute-start | bytes 393224 | tf_op jit(solution)/shard_map/ppermute | solution.py:19
  93.5 2.7 %collective-permute-start.14 = (bf16[512,128]{1,0:T(8,128)(2,1)S(1)}, bf16[512,128]{1,0:T(8,128)(2,1)S(1)}, u32[]{:S(2)}, u32[]{:S(2)}) collective-permute-start(bf16[512,128]{1,0:T(8,128)(2,1)S(1)} %convolution_convert_fusion.1), channel_id=1, source_target_pairs={{2,3},{6,7},{10,11},{14,15},{18,19},{22,23},{26,27},{30,31}} | collective-permute-start | bytes 393224 | tf_op jit(solution)/shard_map/ppermute | solution.py:19
  94.2 7.5 %collective-permute-start.15 = (bf16[512,128]{1,0:T(8,128)(2,1)S(1)}, bf16[512,128]{1,0:T(8,128)(2,1)S(1)}, u32[]{:S(2)}, u32[]{:S(2)}) collective-permute-start(bf16[512,128]{1,0:T(8,128)(2,1)S(1)} %convolution_convert_fusion.1), channel_id=1, source_target_pairs={{2,0},{6,4},{10,8},{14,12},{18,16},{22,20},{26,24},{30,28}} | collective-permute-start | bytes 393224 | tf_op jit(solution)/shard_map/ppermute | solution.py:19
  95.5 6.2 %collective-permute-start.16 = (bf16[512,128]{1,0:T(8,128)(2,1)S(1)}, bf16[512,128]{1,0:T(8,128)(2,1)S(1)}, u32[]{:S(2)}, u32[]{:S(2)}) collective-permute-start(bf16[512,128]{1,0:T(8,128)(2,1)S(1)} %convolution_convert_fusion.1), channel_id=1, source_target_pairs={{2,1},{6,5},{10,9},{14,13},{18,17},{22,21},{26,25},{30,29}} | collective-permute-start | bytes 393224 | tf_op jit(solution)/shard_map/ppermute | solution.py:19
  105.0 7.7 %collective-permute-start.17 = (f32[512,128]{1,0:T(8,128)S(1)}, f32[512,128]{1,0:T(8,128)S(1)}, u32[]{:S(2)}, u32[]{:S(2)}) collective-permute-start(f32[512,128]{1,0:T(8,128)S(1)} %fusion.6), channel_id=1, source_target_pairs={{3,0},{7,4},{11,8},{15,12},{19,16},{23,20},{27,24},{31,28}} | collective-permute-start | bytes 786440 | tf_op jit(solution)/shard_map/ppermute | solution.py:19
  106.3 6.4 %collective-permute-start.18 = (f32[512,128]{1,0:T(8,128)S(1)}, f32[512,128]{1,0:T(8,128)S(1)}, u32[]{:S(2)}, u32[]{:S(2)}) collective-permute-start(f32[512,128]{1,0:T(8,128)S(1)} %fusion.6), channel_id=1, source_target_pairs={{3,1},{7,5},{11,9},{15,13},{19,17},{23,21},{27,25},{31,29}} | collective-permute-start | bytes 786440 | tf_op jit(solution)/shard_map/ppermute | solution.py:19
  107.0 5.7 %collective-permute-start.19 = (f32[512,128]{1,0:T(8,128)S(1)}, f32[512,128]{1,0:T(8,128)}, u32[]{:S(2)}, u32[]{:S(2)}) collective-permute-start(f32[512,128]{1,0:T(8,128)S(1)} %fusion.6), channel_id=1, source_target_pairs={{3,2},{7,6},{11,10},{15,14},{19,18},{23,22},{27,26},{31,30}} | collective-permute-start | bytes 786440 | tf_op jit(solution)/shard_map/ppermute | solution.py:19
  108.3 7.4 %copy-start.1 = (bf16[4,512,512]{2,1,0:T(8,128)(2,1)S(1)}, bf16[4,512,512]{2,1,0:T(8,128)(2,1)}, u32[]{:S(2)}) copy-start(bf16[4,512,512]{2,1,0:T(8,128)(2,1)} %all-gather.2.cloned.1.call-done) | copy-start | bytes 6291460
  116.1 14.1 %copy-start.8 = (s32[1,4]{1,0:T(1,128)S(1)}, s32[1,4]{1,0:T(1,128)}, u32[]{:S(2)}) copy-start(s32[1,4]{1,0:T(1,128)} %param.12) | copy-start | bytes 52
  116.1 2.7 %collective-permute-start.20 = (f32[512,128]{1,0:T(8,128)S(1)}, f32[512,128]{1,0:T(8,128)S(1)}, u32[]{:S(2)}, u32[]{:S(2)}) collective-permute-start(f32[512,128]{1,0:T(8,128)S(1)} %fusion.22), channel_id=1, source_target_pairs={{2,3},{6,7},{10,11},{14,15},{18,19},{22,23},{26,27},{30,31}} | collective-permute-start | bytes 786440 | tf_op jit(solution)/shard_map/ppermute | solution.py:19
  116.8 9.3 %collective-permute-start.21 = (f32[512,128]{1,0:T(8,128)S(1)}, f32[512,128]{1,0:T(8,128)S(1)}, u32[]{:S(2)}, u32[]{:S(2)}) collective-permute-start(f32[512,128]{1,0:T(8,128)S(1)} %fusion.22), channel_id=1, source_target_pairs={{2,0},{6,4},{10,8},{14,12},{18,16},{22,20},{26,24},{30,28}} | collective-permute-start | bytes 786440 | tf_op jit(solution)/shard_map/ppermute | solution.py:19
  118.1 8.0 %collective-permute-start.22 = (f32[512,128]{1,0:T(8,128)S(1)}, f32[512,128]{1,0:T(8,128)S(1)}, u32[]{:S(2)}, u32[]{:S(2)}) collective-permute-start(f32[512,128]{1,0:T(8,128)S(1)} %fusion.22), channel_id=1, source_target_pairs={{2,1},{6,5},{10,9},{14,13},{18,17},{22,21},{26,25},{30,29}} | collective-permute-start | bytes 786440 | tf_op jit(solution)/shard_map/ppermute | solution.py:19
  127.5 2.7 %collective-permute-start.23 = (f32[512,128]{1,0:T(8,128)S(1)}, f32[512,128]{1,0:T(8,128)S(1)}, u32[]{:S(2)}, u32[]{:S(2)}) collective-permute-start(f32[512,128]{1,0:T(8,128)S(1)} %fusion.21), channel_id=1, source_target_pairs={{1,2},{5,6},{9,10},{13,14},{17,18},{21,22},{25,26},{29,30}} | collective-permute-start | bytes 786440 | tf_op jit(solution)/shard_map/ppermute | solution.py:19
  128.2 2.0 %collective-permute-start.24 = (f32[512,128]{1,0:T(8,128)S(1)}, f32[512,128]{1,0:T(8,128)S(1)}, u32[]{:S(2)}, u32[]{:S(2)}) collective-permute-start(f32[512,128]{1,0:T(8,128)S(1)} %fusion.21), channel_id=1, source_target_pairs={{1,3},{5,7},{9,11},{13,15},{17,19},{21,23},{25,27},{29,31}} | collective-permute-start | bytes 786440 | tf_op jit(solution)/shard_map/ppermute | solution.py:19
  128.9 6.6 %collective-permute-start.25 = (f32[512,128]{1,0:T(8,128)S(1)}, f32[512,128]{1,0:T(8,128)S(1)}, u32[]{:S(2)}, u32[]{:S(2)}) collective-permute-start(f32[512,128]{1,0:T(8,128)S(1)} %fusion.21), channel_id=1, source_target_pairs={{1,0},{5,4},{9,8},{13,12},{17,16},{21,20},{25,24},{29,28}} | collective-permute-start | bytes 786440 | tf_op jit(solution)/shard_map/ppermute | solution.py:19
  138.9 7.6 %collective-permute-start.26 = (f32[512,128]{1,0:T(8,128)}, f32[512,128]{1,0:T(8,128)S(1)}, u32[]{:S(2)}, u32[]{:S(2)}) collective-permute-start(f32[512,128]{1,0:T(8,128)} %fusion.23), channel_id=1, source_target_pairs={{0,1},{4,5},{8,9},{12,13},{16,17},{20,21},{24,25},{28,29}} | collective-permute-start | bytes 786440 | tf_op jit(solution)/shard_map/ppermute | solution.py:19
  143.3 5.5 %collective-permute-start.27 = (f32[512,128]{1,0:T(8,128)}, f32[512,128]{1,0:T(8,128)S(1)}, u32[]{:S(2)}, u32[]{:S(2)}) collective-permute-start(f32[512,128]{1,0:T(8,128)} %fusion.23), channel_id=1, source_target_pairs={{0,2},{4,6},{8,10},{12,14},{16,18},{20,22},{24,26},{28,30}} | collective-permute-start | bytes 786440 | tf_op jit(solution)/shard_map/ppermute | solution.py:19
  144.6 7.0 %collective-permute-start.28 = (f32[512,128]{1,0:T(8,128)}, f32[512,128]{1,0:T(8,128)S(1)}, u32[]{:S(2)}, u32[]{:S(2)}) collective-permute-start(f32[512,128]{1,0:T(8,128)} %fusion.23), channel_id=1, source_target_pairs={{0,3},{4,7},{8,11},{12,15},{16,19},{20,23},{24,27},{28,31}} | collective-permute-start | bytes 786440 | tf_op jit(solution)/shard_map/ppermute | solution.py:19
  158.0 9.9 %copy-start.2 = (bf16[1,512,512]{2,1,0:T(8,128)(2,1)S(1)}, bf16[1,512,512]{2,1,0:T(8,128)(2,1)}, u32[]{:S(2)}) copy-start(bf16[1,512,512]{2,1,0:T(8,128)(2,1)} %param.10) | copy-start | bytes 1572868
  158.0 9.9 %copy-start.4 = (bf16[512,128]{1,0:T(8,128)(2,1)S(1)}, bf16[512,128]{1,0:T(8,128)(2,1)}, u32[]{:S(2)}) copy-start(bf16[512,128]{1,0:T(8,128)(2,1)} %copy-done.3) | copy-start | bytes 393220
  160.5 4.8 %collective-permute-start.29 = (bf16[512,128]{1,0:T(8,128)(2,1)S(1)}, bf16[512,128]{1,0:T(8,128)(2,1)S(1)}, u32[]{:S(2)}, u32[]{:S(2)}) collective-permute-start(bf16[512,128]{1,0:T(8,128)(2,1)S(1)} %get-tuple-element.14), channel_id=1, source_target_pairs={{0,3},{1,0},{2,1},{3,2},{4,7},{5,4},{6,5},{7,6},{8,11},{9,8},{10,9... | collective-permute-start | bytes 393224 | tf_op jit(solution)/shard_map/ppermute | solution.py:9
  161.4 6.4 %collective-permute-start.30 = (bf16[512,128]{1,0:T(8,128)(2,1)S(1)}, bf16[512,128]{1,0:T(8,128)(2,1)S(1)}, u32[]{:S(2)}, u32[]{:S(2)}) collective-permute-start(bf16[512,128]{1,0:T(8,128)(2,1)S(1)} %get-tuple-element.16), channel_id=1, source_target_pairs={{0,2},{1,3},{2,0},{3,1},{4,6},{5,7},{6,4},{7,5},{8,10},{9,11},{10,... | collective-permute-start | bytes 393224 | tf_op jit(solution)/shard_map/ppermute | solution.py:9
  161.4 6.5 %collective-permute-start.31 = (bf16[512,128]{1,0:T(8,128)(2,1)S(1)}, bf16[512,128]{1,0:T(8,128)(2,1)S(1)}, u32[]{:S(2)}, u32[]{:S(2)}) collective-permute-start(bf16[512,128]{1,0:T(8,128)(2,1)S(1)} %get-tuple-element.15), channel_id=1, source_target_pairs={{0,1},{1,2},{2,3},{3,0},{4,5},{5,6},{6,7},{7,4},{8,9},{9,10},{10,1... | collective-permute-start | bytes 393224 | tf_op jit(solution)/shard_map/ppermute | solution.py:9
Sparse Core Ops, SparseCore 0:
  18.0 52.9 all-gather.1

commit v4 on v3

--- a/solution.py
+++ b/solution.py
@@ -107,29 +107,37 @@
     rhs_level = -level_sum.astype(jnp.float32)
 
     top_forward = [None] * levels
+    pushed = None
     for level in range(levels):
         residue = rhs_level
-        for u in range(level):
-            residue = residue - jnp.dot(mats[1 + u], top_forward[u], preferred_element_type=jnp.float32)
+        if level > 0:
+            pushed = lax.ppermute(pushed, "col", [(level - 1, level)])
+            residue = residue - pushed[0]
         solved = jnp.dot(inv, residue.astype(jnp.bfloat16), preferred_element_type=jnp.float32)
-        solved = solved.astype(jnp.bfloat16)
+        top_forward[level] = solved.astype(jnp.bfloat16)
         if level < levels - 1:
-            solved = broadcast_from(solved, level, me, "col", peers)
-        top_forward[level] = solved
-    top_back = [None] * levels
-    top_slices = [None] * levels
+            later = jnp.einsum(
+                "kab,bc->kac", mats[level + 1 : levels], top_forward[level], preferred_element_type=jnp.float32
+            )
+            pushed = later if level == 0 else pushed[1:] + later
+    own_solution = None
     for level in reversed(range(levels)):
         update = top_forward[level].astype(jnp.float32)
-        for k in range(level + 1, levels):
-            update = update - lax.dot_general(
-                mats[k], top_back[k], (((0,), (0,)), ((), ())), preferred_element_type=jnp.float32
-            )
+        if level < levels - 1:
+            pushed = lax.ppermute(pushed, "col", [(level + 1, level)])
+            update = update - pushed[level]
         solved = lax.dot_general(
             inv, update.astype(jnp.bfloat16), (((0,), (0,)), ((), ())), preferred_element_type=jnp.float32
         )
-        solved = broadcast_from(solved, level, me, "col", peers)
-        top_slices[level] = lax.dynamic_slice_in_dim(solved, position * share, share, 0)
-        top_back[level] = solved.astype(jnp.bfloat16)
+        own_solution = solved if own_solution is None else jnp.where(me == level, solved, own_solution)
+        if level > 0:
+            earlier = jnp.einsum(
+                "uab,ac->ubc", mats[1 : level + 1], solved.astype(jnp.bfloat16), preferred_element_type=jnp.float32
+            )
+            pushed = earlier if level == levels - 1 else pushed[:level] + earlier
+    solutions = gathered_chunks(own_solution, peers, me)[:levels]
+    top_slices = [lax.dynamic_slice_in_dim(solutions[t], position * share, share, 0) for t in range(levels)]
+    top_back = [solutions[t].astype(jnp.bfloat16) for t in range(levels)]
 
     back_stack = jnp.stack(top_back)
     products_back = jnp.einsum(

time: 177 us -> 160 us (0.904)
  starting transfers between devices: 40.1 us -> 23.9 us
  other arithmetic: 9.7 us -> 5.65 us
  local copies, waits for them, and re-layouts: 10.4 us -> 14.4 us
    ppermute x21 -> x6, starting transfers between devices: 26.7 us -> 6.55 us  [the longest x3 3.45 us: local(): pushed = lax.ppermute(pushed, 'col', [(level + 1, level)])]
    ppermute x21 -> x6, waiting for transfers between devices: 35.3 us -> 24.5 us  [the longest x3 22.7 us: local(): pushed = lax.ppermute(pushed, 'col', [(level + 1, level)])]
    ppermute x6 -> x9, waiting for transfers between devices: 5.61 us -> 16 us  [shifted(): return lax.ppermute(x, axis, [(i, (i + shift) % size) for i in range(size)])]
    another operation x5 -> x1, other arithmetic: 5.17 us -> 0.07 us  [local(): back_stack = jnp.stack(top_back)]
    ppermute x6 -> x9, starting transfers between devices: 5.6 us -> 10.3 us  [shifted(): return lax.ppermute(x, axis, [(i, (i + shift) % size) for i in range(size)])]
    scatter x0 -> x1, local copies, waits for them, and re-layouts: none -> 1.94 us  [gathered_chunks(): return jnp.zeros_like(stacked).at[source].set(stacked)]
    dot_general x3, matrix products: 4.01 us -> 2.1 us  [local(): jnp.dot(inv, residue.astype(jnp.bfloat16), preferred_element_type=jnp.flo...]
    dot_general x5 -> x6, matrix products: 5.71 us -> 7.6 us  [the longest x3 4.9 us: local(): jnp.einsum('uab,ac->ubc', mats[1:level + 1], solved.astype(jnp.bfloat16),...]
  transfers between devices with their start and end apart: 33 -> 21, of which waited for: 17 -> 13; matrix products, arithmetic and copies ran while one was open for 9% -> 10% of each run, Pallas kernels for 0% -> 0%
where the time goes in v4:
time: 160 us
  waiting for transfers between devices  75.9 us (47%)
  matrix products  25.2 us (16%)
  starting transfers between devices  23.9 us (15%)
  between operations  14.5 us (9%)
  local copies, waits for them, and re-layouts  14.4 us (9%)
  other arithmetic  5.65 us (4%)
    ppermute x5, waiting for transfers between devices, swapped(): return lax.ppermute(x, axis, [(i, i ^ bit) for i in range(size)])  32.1 us
    ppermute x3, waiting for transfers between devices, local(): pushed = lax.ppermute(pushed, 'col', [(level + 1, level)])  22.7 us
    ppermute x9, waiting for transfers between devices, shifted(): return lax.ppermute(x, axis, [(i, (i + shift) % size) for i in range(size)])  16 us
    ppermute x9, starting transfers between devices, shifted(): return lax.ppermute(x, axis, [(i, (i + shift) % size) for i in range(size)])  10.3 us
    ppermute x5, starting transfers between devices, swapped(): return lax.ppermute(x, axis, [(i, i ^ bit) for i in range(size)])  7.07 us
    dot_general x4, matrix products, local(): lax.dot_general(inv, update.astype(jnp.bfloat16), (((0,), (0,)), ((), ())...  5.15 us
    dot_general x3, matrix products, local(): jnp.einsum('uab,ac->ubc', mats[1:level + 1], solved.astype(jnp.bfloat16),...  4.9 us
    ppermute x3, starting transfers between devices, local(): pushed = lax.ppermute(pushed, 'col', [(level + 1, level)])  3.45 us
  transfers between devices with their start and end apart: 21, of which 13 were waited for; matrix products, arithmetic and copies ran while one was open for 10% of the time, Pallas kernels for 0%

profile of v4, /device:TPU:0, one launch (start us, length us, event | category | flops | bytes accessed | tf_op | source)
XLA Modules:
  0.0 159.6 jit_solution(3893351087223600638)
XLA Ops:
  7.2 1.5 convolution_convert_fusion.4
  8.7 0.6 collective-permute-start
  9.3 2.6 %collective-permute-start.1 = (bf16[512,128]{1,0:T(8,128)(2,1)S(1)}, bf16[512,128]{1,0:T(8,128)(2,1)S(1)}, u32[]{:S(2)}, u32[]{:S(2)}) collective-permute-start(bf16[512,128]{1,0:T(8,128)(2,1)S(1)} %convolution_convert_fusion.4), channel_id=1, source_target_pairs={{0,2},{1,3},{2,0},{3,1},{4,6},{5,7},{6,4},{7,5},{8,10},{9,11},{10,... | collective-permute-start | bytes 393224 | tf_op jit(solution)/shard_map/ppermute | solution.py:9
  11.9 1.4 collective-permute-start.2
  13.3 0.7 fusion.70
  13.9 0.7 compare_and_fusion
  14.6 0.9 constant_dynamic-slice_fusion.8
  15.5 1.6 gather_fusion
  17.1 0.7 pad_maximum_fusion.3
  17.9 0.6 iota_reduce_fusion
  18.5 1.1 broadcast.173
  19.7 0.7 select_dynamic-update-slice_fusion
  20.5 1.4 gather_fusion.1
  21.9 1.9 %fusion.2 = f32[4,128,512]{2,1,0:T(8,128)S(1)} fusion(bf16[4,512,128]{2,1,0:T(8,128)(2,1)} %gather_fusion.1, bf16[1,4,512,512]{3,2,1,0:T(8,128)(2,1)S(1)} %copy-done), kind=kOutput, calls=%fused_computation.6 | convolution fusion | flops 268435456 | bytes 3670016 | tf_op jit(solution)/shard_map/sab,sbk->sak/dot_general | solution.py:92
  23.8 1.3 copy.30
  25.1 2.8 %fusion.4 = bf16[4,512,128]{2,0,1:T(4,128)(2,1)S(1)} fusion(f32[4,512,128]{2,0,1:T(4,128)} %select_dynamic-update-slice_fusion, f32[4,128,512]{1,0,2:T(4,128)} %copy.30, s32[4]{0:T(128)S(1)} %bitcast.172), kind=kOutput, calls=%fused_computation.9 | convolution fusion | flops 13107216 | bytes 2621456 | tf_op jit(solution)/shard_map/st,sak->tak/dot_general | solution.py:98
  27.9 0.4 constant_dynamic-slice_fusion.6
  28.6 7.1 %collective-permute-done.3 = bf16[2,512,128]{2,1,0:T(8,128)(2,1)S(1)} collective-permute-done((bf16[2,512,128]{2,1,0:T(8,128)(2,1)S(1)}, bf16[2,512,128]{2,1,0:T(8,128)(2,1)S(1)}, u32[]{:S(2)}, u32[]{:S(2)}) %collective-permute-start.3) | collective-permute-done | bytes 262176 | tf_op jit(solution)/shard_map/ppermute | solution.py:13
  35.8 1.3 collective-permute-done.4
  37.2 1.5 collective-permute-start.5
  38.7 4.1 %collective-permute-done.5 = bf16[512,128]{1,0:T(8,128)(2,1)S(1)} collective-permute-done((bf16[512,128]{1,0:T(8,128)(2,1)S(1)}, bf16[512,128]{1,0:T(8,128)(2,1)S(1)}, u32[]{:S(2)}, u32[]{:S(2)}) %collective-permute-start.5) | collective-permute-done | bytes 131104 | tf_op jit(solution)/shard_map/ppermute | solution.py:13
  42.9 1.6 %collective-permute-start.6 = (bf16[512,128]{1,0:T(8,128)(2,1)S(1)}, bf16[512,128]{1,0:T(8,128)(2,1)S(1)}, u32[]{:S(2)}, u32[]{:S(2)}) collective-permute-start(bf16[512,128]{1,0:T(8,128)(2,1)S(1)} %add_convert_fusion.2), channel_id=1, source_target_pairs={{0,8},{4,12},{8,0},{12,4},{16,24},{20,28},{24,16},{28,20},{1,9},{5... | collective-permute-start | bytes 393224 | tf_op jit(solution)/shard_map/ppermute | solution.py:13
  44.5 7.3 %collective-permute-done.6 = bf16[512,128]{1,0:T(8,128)(2,1)S(1)} collective-permute-done((bf16[512,128]{1,0:T(8,128)(2,1)S(1)}, bf16[512,128]{1,0:T(8,128)(2,1)S(1)}, u32[]{:S(2)}, u32[]{:S(2)}) %collective-permute-start.6) | collective-permute-done | bytes 131104 | tf_op jit(solution)/shard_map/ppermute | solution.py:13
  51.9 3.6 %collective-permute-start.7 = (bf16[512,128]{1,0:T(8,128)(2,1)S(1)}, bf16[512,128]{1,0:T(8,128)(2,1)S(1)}, u32[]{:S(2)}, u32[]{:S(2)}) collective-permute-start(bf16[512,128]{1,0:T(8,128)(2,1)S(1)} %add_convert_fusion.1), channel_id=1, source_target_pairs={{0,16},{4,20},{8,24},{12,28},{16,0},{20,4},{24,8},{28,12},{1,17},{... | collective-permute-start | bytes 393224 | tf_op jit(solution)/shard_map/ppermute | solution.py:13
  55.5 12.3 %collective-permute-done.7 = bf16[512,128]{1,0:T(8,128)(2,1)S(1)} collective-permute-done((bf16[512,128]{1,0:T(8,128)(2,1)S(1)}, bf16[512,128]{1,0:T(8,128)(2,1)S(1)}, u32[]{:S(2)}, u32[]{:S(2)}) %collective-permute-start.7) | collective-permute-done | bytes 131104 | tf_op jit(solution)/shard_map/ppermute | solution.py:13
  67.8 3.2 %all-gather.2.cloned.1.call-done = bf16[4,512,512]{2,1,0:T(8,128)(2,1)} async-done(((bf16[4,64,512]{2,1,0:T(8,128)(2,1)}), bf16[4,512,512]{2,1,0:T(8,128)(2,1)}) %all-gather.2.cloned.1.call-update) | async-done | bytes 2097168 | tf_op jit(solution)/shard_map/all_gather | solution.py:77
  71.0 1.5 convolution_convert_fusion.3
  72.5 2.0 %fusion.49 = f32[3,512,128]{2,1,0:T(8,128)S(1)} fusion(bf16[4,512,512]{2,1,0:T(8,128)(2,1)} %all-gather.2.cloned.1.call-done, bf16[512,128]{1,0:T(8,128)(2,1)S(1)} %convolution_convert_fusion.3), kind=kOutput, calls=%fused_computation.83 | convolution fusion | flops 201326592 | bytes 3014656 | tf_op jit(solution)/shard_map/kab,bc->kac/dot_general | solution.py:119
  74.5 1.7 %collective-permute-start.8 = (f32[3,512,128]{2,1,0:T(8,128)S(1)}, f32[3,512,128]{2,1,0:T(8,128)S(1)}, u32[]{:S(2)}, u32[]{:S(2)}) collective-permute-start(f32[3,512,128]{2,1,0:T(8,128)S(1)} %fusion.49), channel_id=1, source_target_pairs={{0,1},{4,5},{8,9},{12,13},{16,17},{20,21},{24,25},{28,29}} | collective-permute-start | bytes 2359304 | tf_op jit(solution)/shard_map/ppermute | solution.py:114
  76.2 1.8 %collective-permute-done.8 = f32[3,512,128]{2,1,0:T(8,128)S(1)} collective-permute-done((f32[3,512,128]{2,1,0:T(8,128)S(1)}, f32[3,512,128]{2,1,0:T(8,128)S(1)}, u32[]{:S(2)}, u32[]{:S(2)}) %collective-permute-start.8) | collective-permute-done | bytes 786464 | tf_op jit(solution)/shard_map/ppermute | solution.py:114
  78.4 0.4 slice_add_fusion.1
  78.8 0.7 collective-permute-start.9
  79.5 0.3 convolution_convert_fusion.1
  80.1 0.7 collective-permute-start.10
  80.8 2.0 %fusion.5 = f32[512,128]{1,0:T(8,128)S(1)} fusion(bf16[4,512,512]{2,1,0:T(8,128)(2,1)} %all-gather.2.cloned.1.call-done, f32[1,512,128]{2,1,0:T(8,128)S(1)} %collective-permute-done.10, bf16[512,128]{1,0:T(8,128)(2,1)S(1)} %add_convert_fusion), kind=kOutput, calls=%fused_computation.19 | convolution fusion | flops 134545408 | bytes 1703936 | tf_op jit(solution)/shard_map/dot_general | solution.py:129
  82.8 2.2 %fusion.43 = f32[3,512,128]{2,1,0:T(8,128)S(1)} fusion(bf16[4,512,512]{2,1,0:T(8,128)(2,1)} %all-gather.2.cloned.1.call-done, f32[512,128]{1,0:T(8,128)S(1)} %fusion.5), kind=kOutput, calls=%fused_computation.79 | convolution fusion | flops 201392128 | bytes 3145728 | tf_op jit(solution)/shard_map/uab,ac->ubc/dot_general | solution.py:134
  85.0 0.7 collective-permute-start.11
  85.7 0.3 fusion.28
  86.1 1.3 slice_add_fusion
  87.4 1.5 collective-permute-start.12
  88.8 1.4 fusion.27
  90.3 1.5 slice_add_fusion.2
  91.7 1.3 collective-permute-start.13
  93.0 22.7 %collective-permute-done.13 = f32[1,512,128]{2,1,0:T(8,128)S(1)} collective-permute-done((f32[1,512,128]{2,1,0:T(8,128)S(1)}, f32[1,512,128]{2,1,0:T(8,128)S(1)}, u32[]{:S(2)}, u32[]{:S(2)}) %collective-permute-start.13) | collective-permute-done | bytes 262176 | tf_op jit(solution)/shard_map/ppermute | solution.py:127
  115.7 1.4 convolution_select_fusion
  117.3 1.6 %collective-permute-start.16 = (f32[512,128]{1,0:T(8,128)S(1)}, f32[512,128]{1,0:T(8,128)S(1)}, u32[]{:S(2)}, u32[]{:S(2)}) collective-permute-start(f32[512,128]{1,0:T(8,128)S(1)} %convolution_select_fusion), channel_id=1, source_target_pairs={{0,3},{1,0},{2,1},{3,2},{4,7},{5,4},{6,5},{7,6},{8,11},{9,8},{10,9... | collective-permute-start | bytes 786440 | tf_op jit(solution)/shard_map/ppermute | solution.py:9
  119.0 6.1 %collective-permute-done.14 = f32[512,128]{1,0:T(8,128)S(1)} collective-permute-done((f32[512,128]{1,0:T(8,128)S(1)}, f32[512,128]{1,0:T(8,128)S(1)}, u32[]{:S(2)}, u32[]{:S(2)}) %collective-permute-start.14) | collective-permute-done | bytes 262176 | tf_op jit(solution)/shard_map/ppermute | solution.py:9
  125.1 1.4 collective-permute-done.15
  126.5 2.5 %collective-permute-done.16 = f32[512,128]{1,0:T(8,128)S(1)} collective-permute-done((f32[512,128]{1,0:T(8,128)S(1)}, f32[512,128]{1,0:T(8,128)S(1)}, u32[]{:S(2)}, u32[]{:S(2)}) %collective-permute-start.16) | collective-permute-done | bytes 262176 | tf_op jit(solution)/shard_map/ppermute | solution.py:9
  129.0 1.1 pad_maximum_fusion
  130.1 1.9 %scatter_fusion = f32[4,512,128]{2,1,0:T(8,128)S(1)} fusion(f32[4,512,128]{2,1,0:T(8,128)S(1)} %broadcast.173.clone, s32[4]{0:T(128)S(1)} %fusion.69, f32[4,512,128]{2,1,0:T(8,128)} %pad_maximum_fusion), kind=kCustom, calls=%fused_computation.3 | custom fusion | bytes 3145744 | tf_op jit(solution)/shard_map/scatter | solution.py:60
  132.2 0.6 constant_dynamic-slice_fusion
  132.8 0.6 constant_dynamic-slice_fusion.1
  133.4 0.6 constant_dynamic-slice_fusion.2
  134.1 1.4 gather_fusion.2
  135.5 1.5 fusion
  137.1 1.3 copy.33
  138.4 2.4 %fusion.6 = bf16[4,512,128]{2,0,1:T(4,128)(2,1)S(1)} fusion(f32[4,128,512]{1,0,2:T(4,128)} %copy.33, s32[4]{0:T(128)S(1)} %get-tuple-element.22, pred[4]{0:T(512)(128)(4,1)S(1)} %broadcast_compare_fusion, s32[4]{0:T(128)S(1)} %get-tuple-element.21), kind=kOutput, calls=%fused_computation.21 | convolution fusion | flops 12582944 | bytes 1572900 | tf_op jit(solution)/shard_map/sp,sbk->pbk/dot_general | solution.py:147
  141.0 2.0 %collective-permute-start.17 = (bf16[512,128]{1,0:T(8,128)(2,1)S(1)}, bf16[512,128]{1,0:T(8,128)(2,1)S(1)}, u32[]{:S(2)}, u32[]{:S(2)}) collective-permute-start(bf16[512,128]{1,0:T(8,128)(2,1)S(1)} %get-tuple-element.16), channel_id=1, source_target_pairs={{0,3},{1,0},{2,1},{3,2},{4,7},{5,4},{6,5},{7,6},{8,11},{9,8},{10,9... | collective-permute-start | bytes 393224 | tf_op jit(solution)/shard_map/ppermute | solution.py:9
  142.9 2.0 %collective-permute-start.18 = (bf16[512,128]{1,0:T(8,128)(2,1)S(1)}, bf16[512,128]{1,0:T(8,128)(2,1)S(1)}, u32[]{:S(2)}, u32[]{:S(2)}) collective-permute-start(bf16[512,128]{1,0:T(8,128)(2,1)S(1)} %get-tuple-element.18), channel_id=1, source_target_pairs={{0,2},{1,3},{2,0},{3,1},{4,6},{5,7},{6,4},{7,5},{8,10},{9,11},{10,... | collective-permute-start | bytes 393224 | tf_op jit(solution)/shard_map/ppermute | solution.py:9
  145.0 0.7 pad_maximum_fusion.4
  145.6 1.2 collective-permute-done.17
  146.8 4.8 %collective-permute-done.18 = bf16[512,128]{1,0:T(8,128)(2,1)S(1)} collective-permute-done((bf16[512,128]{1,0:T(8,128)(2,1)S(1)}, bf16[512,128]{1,0:T(8,128)(2,1)S(1)}, u32[]{:S(2)}, u32[]{:S(2)}) %collective-permute-start.18) | collective-permute-done | bytes 131104 | tf_op jit(solution)/shard_map/ppermute | solution.py:9
  151.9 0.8 copy.29
  (62 shorter events, 2.4 us)
Async XLA Ops:
  7.2 14.7 %copy-start = (bf16[1,4,512,512]{3,2,1,0:T(8,128)(2,1)S(1)}, bf16[1,4,512,512]{3,2,1,0:T(8,128)(2,1)}, u32[]{:S(2)}) copy-start(bf16[1,4,512,512]{3,2,1,0:T(8,128)(2,1)} %param.11) | copy-start | bytes 6291460
  7.2 10.7 %copy-start.8 = (s32[1,4]{1,0:T(1,128)S(1)}, s32[1,4]{1,0:T(1,128)}, u32[]{:S(2)}) copy-start(s32[1,4]{1,0:T(1,128)} %param.13) | copy-start | bytes 52
  7.2 12.5 %copy-start.7 = (bf16[4,64,128]{2,1,0:T(8,128)(2,1)S(1)}, bf16[4,64,128]{2,1,0:T(8,128)(2,1)}, u32[]{:S(2)}) copy-start(bf16[4,64,128]{2,1,0:T(8,128)(2,1)} %param.14) | copy-start | bytes 196612
  7.2 63.8 %all-gather.2.cloned.1.call-start = ((), (), s32[]{:S(2)}) async-start(), calls=%async_computation | async-start | bytes 2359296 | tf_op jit(solution)/shard_map/all_gather | solution.py:77
  8.7 11.7 %collective-permute-start = (bf16[512,128]{1,0:T(8,128)(2,1)S(1)}, bf16[512,128]{1,0:T(8,128)(2,1)S(1)}, u32[]{:S(2)}, u32[]{:S(2)}) collective-permute-start(bf16[512,128]{1,0:T(8,128)(2,1)S(1)} %convolution_convert_fusion.4), channel_id=1, source_target_pairs={{0,1},{1,2},{2,3},{3,0},{4,5},{5,6},{6,7},{7,4},{8,9},{9,10},{10,1... | collective-permute-start | bytes 393224 | tf_op jit(solution)/shard_map/ppermute | solution.py:9
  9.3 11.1 %collective-permute-start.1 = (bf16[512,128]{1,0:T(8,128)(2,1)S(1)}, bf16[512,128]{1,0:T(8,128)(2,1)S(1)}, u32[]{:S(2)}, u32[]{:S(2)}) collective-permute-start(bf16[512,128]{1,0:T(8,128)(2,1)S(1)} %convolution_convert_fusion.4), channel_id=1, source_target_pairs={{0,2},{1,3},{2,0},{3,1},{4,6},{5,7},{6,4},{7,5},{8,10},{9,11},{10,... | collective-permute-start | bytes 393224 | tf_op jit(solution)/shard_map/ppermute | solution.py:9
  11.9 8.6 %collective-permute-start.2 = (bf16[512,128]{1,0:T(8,128)(2,1)S(1)}, bf16[512,128]{1,0:T(8,128)(2,1)S(1)}, u32[]{:S(2)}, u32[]{:S(2)}) collective-permute-start(bf16[512,128]{1,0:T(8,128)(2,1)S(1)} %convolution_convert_fusion.4), channel_id=1, source_target_pairs={{0,3},{1,0},{2,1},{3,2},{4,7},{5,4},{6,5},{7,6},{8,11},{9,8},{10,9... | collective-permute-start | bytes 393224 | tf_op jit(solution)/shard_map/ppermute | solution.py:9
  21.9 3.2 %copy-start.9 = (s32[1,4]{1,0:T(1,128)S(1)}, s32[1,4]{1,0:T(1,128)}, u32[]{:S(2)}) copy-start(s32[1,4]{1,0:T(1,128)} %param.12) | copy-start | bytes 52
  28.3 7.3 %collective-permute-start.3 = (bf16[2,512,128]{2,1,0:T(8,128)(2,1)S(1)}, bf16[2,512,128]{2,1,0:T(8,128)(2,1)S(1)}, u32[]{:S(2)}, u32[]{:S(2)}) collective-permute-start(bf16[2,512,128]{2,1,0:T(8,128)(2,1)S(1)} %bitcast.165), channel_id=1, source_target_pairs={{0,2},{1,3},{2,0},{3,1},{4,6},{5,7},{6,4},{7,5},{8,10},{9,11},{10,... | collective-permute-start | bytes 786440 | tf_op jit(solution)/shard_map/ppermute | solution.py:13
  35.7 1.4 collective-permute-start.4
  37.2 5.6 %collective-permute-start.5 = (bf16[512,128]{1,0:T(8,128)(2,1)S(1)}, bf16[512,128]{1,0:T(8,128)(2,1)S(1)}, u32[]{:S(2)}, u32[]{:S(2)}) collective-permute-start(bf16[512,128]{1,0:T(8,128)(2,1)S(1)} %fusion.29), channel_id=1, source_target_pairs={{0,4},{4,0},{8,12},{12,8},{16,20},{20,16},{24,28},{28,24},{1,5},{5... | collective-permute-start | bytes 393224 | tf_op jit(solution)/shard_map/ppermute | solution.py:13
  42.9 9.0 %collective-permute-start.6 = (bf16[512,128]{1,0:T(8,128)(2,1)S(1)}, bf16[512,128]{1,0:T(8,128)(2,1)S(1)}, u32[]{:S(2)}, u32[]{:S(2)}) collective-permute-start(bf16[512,128]{1,0:T(8,128)(2,1)S(1)} %add_convert_fusion.2), channel_id=1, source_target_pairs={{0,8},{4,12},{8,0},{12,4},{16,24},{20,28},{24,16},{28,20},{1,9},{5... | collective-permute-start | bytes 393224 | tf_op jit(solution)/shard_map/ppermute | solution.py:13
  51.9 15.9 %collective-permute-start.7 = (bf16[512,128]{1,0:T(8,128)(2,1)S(1)}, bf16[512,128]{1,0:T(8,128)(2,1)S(1)}, u32[]{:S(2)}, u32[]{:S(2)}) collective-permute-start(bf16[512,128]{1,0:T(8,128)(2,1)S(1)} %add_convert_fusion.1), channel_id=1, source_target_pairs={{0,16},{4,20},{8,24},{12,28},{16,0},{20,4},{24,8},{28,12},{1,17},{... | collective-permute-start | bytes 393224 | tf_op jit(solution)/shard_map/ppermute | solution.py:13
  71.0 7.0 %copy-start.1 = (bf16[4,512,512]{2,1,0:T(8,128)(2,1)S(1)}, bf16[4,512,512]{2,1,0:T(8,128)(2,1)}, u32[]{:S(2)}) copy-start(bf16[4,512,512]{2,1,0:T(8,128)(2,1)} %all-gather.2.cloned.1.call-done) | copy-start | bytes 6291460
  74.5 3.6 %collective-permute-start.8 = (f32[3,512,128]{2,1,0:T(8,128)S(1)}, f32[3,512,128]{2,1,0:T(8,128)S(1)}, u32[]{:S(2)}, u32[]{:S(2)}) collective-permute-start(f32[3,512,128]{2,1,0:T(8,128)S(1)} %fusion.49), channel_id=1, source_target_pairs={{0,1},{4,5},{8,9},{12,13},{16,17},{20,21},{24,25},{28,29}} | collective-permute-start | bytes 2359304 | tf_op jit(solution)/shard_map/ppermute | solution.py:114
  78.8 0.7 collective-permute-start.9
  80.1 0.7 collective-permute-start.10
  82.8 2.9 %copy-start.2 = (bf16[4,512,512]{2,1,0:T(8,128)(2,1)S(1)}, bf16[4,512,512]{2,1,0:T(8,128)(2,1)}, u32[]{:S(2)}) copy-start(bf16[4,512,512]{2,1,0:T(8,128)(2,1)} %all-gather.2.cloned.1.call-done) | copy-start | bytes 6291460
  85.0 0.7 collective-permute-start.11
  87.4 1.5 collective-permute-start.12
  91.7 24.0 %collective-permute-start.13 = (f32[1,512,128]{2,1,0:T(8,128)S(1)}, f32[1,512,128]{2,1,0:T(8,128)S(1)}, u32[]{:S(2)}, u32[]{:S(2)}) collective-permute-start(f32[1,512,128]{2,1,0:T(8,128)S(1)} %slice_add_fusion.2), channel_id=1, source_target_pairs={{1,0},{5,4},{9,8},{13,12},{17,16},{21,20},{25,24},{29,28}} | collective-permute-start | bytes 786440 | tf_op jit(solution)/shard_map/ppermute | solution.py:127
  117.1 7.9 %collective-permute-start.14 = (f32[512,128]{1,0:T(8,128)S(1)}, f32[512,128]{1,0:T(8,128)S(1)}, u32[]{:S(2)}, u32[]{:S(2)}) collective-permute-start(f32[512,128]{1,0:T(8,128)S(1)} %convolution_select_fusion), channel_id=1, source_target_pairs={{0,1},{1,2},{2,3},{3,0},{4,5},{5,6},{6,7},{7,4},{8,9},{9,10},{10,1... | collective-permute-start | bytes 786440 | tf_op jit(solution)/shard_map/ppermute | solution.py:9
  117.3 9.2 %collective-permute-start.15 = (f32[512,128]{1,0:T(8,128)S(1)}, f32[512,128]{1,0:T(8,128)S(1)}, u32[]{:S(2)}, u32[]{:S(2)}) collective-permute-start(f32[512,128]{1,0:T(8,128)S(1)} %convolution_select_fusion), channel_id=1, source_target_pairs={{0,2},{1,3},{2,0},{3,1},{4,6},{5,7},{6,4},{7,5},{8,10},{9,11},{10,... | collective-permute-start | bytes 786440 | tf_op jit(solution)/shard_map/ppermute | solution.py:9
  117.3 11.6 %collective-permute-start.16 = (f32[512,128]{1,0:T(8,128)S(1)}, f32[512,128]{1,0:T(8,128)S(1)}, u32[]{:S(2)}, u32[]{:S(2)}) collective-permute-start(f32[512,128]{1,0:T(8,128)S(1)} %convolution_select_fusion), channel_id=1, source_target_pairs={{0,3},{1,0},{2,1},{3,2},{4,7},{5,4},{6,5},{7,6},{8,11},{9,8},{10,9... | collective-permute-start | bytes 786440 | tf_op jit(solution)/shard_map/ppermute | solution.py:9
  138.4 6.5 %copy-start.4 = (f32[1,64,128]{2,1,0:T(8,128)S(1)}, f32[1,64,128]{2,1,0:T(8,128)}, u32[]{:S(2)}) copy-start(f32[1,64,128]{2,1,0:T(8,128)} %constant_dynamic-slice_fusion) | copy-start | bytes 98308
  138.4 6.5 %copy-start.5 = (f32[1,64,128]{2,1,0:T(8,128)S(1)}, f32[1,64,128]{2,1,0:T(8,128)}, u32[]{:S(2)}) copy-start(f32[1,64,128]{2,1,0:T(8,128)} %constant_dynamic-slice_fusion.1) | copy-start | bytes 98308
  138.4 6.5 %copy-start.6 = (f32[1,64,128]{2,1,0:T(8,128)S(1)}, f32[1,64,128]{2,1,0:T(8,128)}, u32[]{:S(2)}) copy-start(f32[1,64,128]{2,1,0:T(8,128)} %constant_dynamic-slice_fusion.2) | copy-start | bytes 98308
  138.4 13.2 %copy-start.3 = (bf16[1,512,512]{2,1,0:T(8,128)(2,1)S(1)}, bf16[1,512,512]{2,1,0:T(8,128)(2,1)}, u32[]{:S(2)}) copy-start(bf16[1,512,512]{2,1,0:T(8,128)(2,1)} %param.10) | copy-start | bytes 1572868
  141.0 5.8 %collective-permute-start.17 = (bf16[512,128]{1,0:T(8,128)(2,1)S(1)}, bf16[512,128]{1,0:T(8,128)(2,1)S(1)}, u32[]{:S(2)}, u32[]{:S(2)}) collective-permute-start(bf16[512,128]{1,0:T(8,128)(2,1)S(1)} %get-tuple-element.16), channel_id=1, source_target_pairs={{0,3},{1,0},{2,1},{3,2},{4,7},{5,4},{6,5},{7,6},{8,11},{9,8},{10,9... | collective-permute-start | bytes 393224 | tf_op jit(solution)/shard_map/ppermute | solution.py:9
  142.9 8.7 %collective-permute-start.18 = (bf16[512,128]{1,0:T(8,128)(2,1)S(1)}, bf16[512,128]{1,0:T(8,128)(2,1)S(1)}, u32[]{:S(2)}, u32[]{:S(2)}) collective-permute-start(bf16[512,128]{1,0:T(8,128)(2,1)S(1)} %get-tuple-element.18), channel_id=1, source_target_pairs={{0,2},{1,3},{2,0},{3,1},{4,6},{5,7},{6,4},{7,5},{8,10},{9,11},{10,... | collective-permute-start | bytes 393224 | tf_op jit(solution)/shard_map/ppermute | solution.py:9
  144.9 6.7 %collective-permute-start.19 = (bf16[512,128]{1,0:T(8,128)(2,1)S(1)}, bf16[512,128]{1,0:T(8,128)(2,1)S(1)}, u32[]{:S(2)}, u32[]{:S(2)}) collective-permute-start(bf16[512,128]{1,0:T(8,128)(2,1)S(1)} %get-tuple-element.17), channel_id=1, source_target_pairs={{0,1},{1,2},{2,3},{3,0},{4,5},{5,6},{6,7},{7,4},{8,9},{9,10},{10,1... | collective-permute-start | bytes 393224 | tf_op jit(solution)/shard_map/ppermute | solution.py:9
Sparse Core Ops, SparseCore 0:
  18.0 52.9 all-gather.1

commit v5 on v4

--- a/solution.py
+++ b/solution.py
@@ -2,7 +2,65 @@
 import jax.numpy as jnp
 import numpy as np
 from jax import lax
+from jax.experimental import pallas as pl
+from jax.experimental.pallas import tpu as pltpu
 from jax.sharding import PartitionSpec as P
+
+SMEM = pl.BlockSpec(memory_space=pltpu.SMEM)
+VMEM = pl.BlockSpec(memory_space=pltpu.VMEM)
+
+
+def coupling_kernel(rows_ref, picks_ref, fold_ref, tiles_ref, panels_ref, rhs_ref, out_ref):
+    out_ref[...] = jnp.zeros_like(out_ref)
+    share = rhs_ref.shape[1]
+
+    @pl.when(fold_ref[1] == 0)
+    def _():
+        start = pl.multiple_of(fold_ref[0], 8)
+        out_ref[:, pl.ds(start, share), :] = -rhs_ref[...].astype(jnp.float32)
+
+    for s in range(tiles_ref.shape[0]):
+        level = rows_ref[s]
+
+        @pl.when(level >= 0)
+        def _():
+            prod = jnp.dot(tiles_ref[s], panels_ref[picks_ref[s]], preferred_element_type=jnp.float32)
+            out_ref[level] += prod
+
+
+def coupling_terms(slot_rows, picks, fold, tiles, panels, rhs, levels):
+    return pl.pallas_call(
+        coupling_kernel,
+        out_shape=jax.ShapeDtypeStruct((levels, panels.shape[1], panels.shape[2]), jnp.float32),
+        in_specs=[SMEM, SMEM, SMEM, VMEM, VMEM, VMEM],
+        out_specs=VMEM,
+    )(slot_rows, picks, fold, tiles, panels, rhs)
+
+
+def back_kernel(rows_ref, dests_ref, tiles_ref, back_ref, out_ref, acc_ref):
+    acc_ref[...] = jnp.zeros_like(acc_ref)
+    for s in range(tiles_ref.shape[0]):
+        level = rows_ref[s]
+
+        @pl.when(level >= 0)
+        def _():
+            prod = lax.dot_general(
+                tiles_ref[s], back_ref[level], (((0,), (0,)), ((), ())), preferred_element_type=jnp.float32
+            )
+            acc_ref[dests_ref[s]] += prod
+
+    out_ref[...] = acc_ref[...].astype(out_ref.dtype)
+
+
+def back_terms(slot_rows, dests, tiles, back, peers):
+    shape = (peers, tiles.shape[2], back.shape[2])
+    return pl.pallas_call(
+        back_kernel,
+        out_shape=jax.ShapeDtypeStruct(shape, jnp.bfloat16),
+        in_specs=[SMEM, SMEM, VMEM, VMEM],
+        out_specs=VMEM,
+        scratch_shapes=[pltpu.VMEM(shape, jnp.float32)],
+    )(slot_rows, dests, tiles, back)
 
 
 def shifted(x, axis, size, shift):
@@ -79,8 +137,6 @@
 
     slot_rows = tile_rows[0]
     slot_cols = tile_cols[0] % peers
-    alive = slot_rows >= 0
-    safe_rows = jnp.maximum(slot_rows, 0)
     own_tiles = low_tiles[0]
     low_forward = jnp.dot(low_inv[0], low_rhs[0], preferred_element_type=jnp.float32).astype(
         jnp.bfloat16
@@ -88,17 +144,9 @@
     received = [low_forward] + [shifted(low_forward, "col", peers, s) for s in range(1, peers)]
     source_of = (me - jnp.arange(peers)) % peers
     by_source = jnp.stack(received)
-    slot_pick = jnp.argmax(source_of[None, :] == slot_cols[:, None], axis=1)
-    products = jnp.einsum(
-        "sab,sbk->sak", own_tiles, by_source[slot_pick], preferred_element_type=jnp.float32
-    )
-    pick_level = (slot_rows[:, None] == jnp.arange(levels, dtype=jnp.int32)[None, :]).astype(
-        jnp.float32
-    )
-    coupling = jnp.einsum("st,sak->tak", pick_level, products, precision=lax.Precision.HIGHEST)
-    own_rhs = jnp.zeros((levels, share * rows_n, width), jnp.float32)
-    own_rhs = lax.dynamic_update_slice_in_dim(own_rhs, top_rhs.astype(jnp.float32), position * share, 1)
-    coupling = coupling - jnp.where(me == 0, own_rhs, 0.0)
+    slot_pick = jnp.argmax(source_of[None, :] == slot_cols[:, None], axis=1).astype(jnp.int32)
+    fold = jnp.stack([position * share, me]).astype(jnp.int32)
+    coupling = coupling_terms(slot_rows, slot_pick, fold, own_tiles, by_source, top_rhs, levels)
     part = summed_chunks(coupling, peers, rows_n, me)
     if peers == levels:
         level_sum = part
@@ -140,13 +188,8 @@
     top_back = [solutions[t].astype(jnp.bfloat16) for t in range(levels)]
 
     back_stack = jnp.stack(top_back)
-    products_back = jnp.einsum(
-        "sab,sak->sbk", own_tiles, back_stack[safe_rows], preferred_element_type=jnp.float32
-    )
-    pick_peer = ((slot_cols[:, None] == source_of[None, :]) & alive[:, None]).astype(jnp.float32)
-    terms = jnp.einsum(
-        "sp,sbk->pbk", pick_peer, products_back, precision=lax.Precision.HIGHEST
-    ).astype(jnp.bfloat16)
+    dests = ((me - slot_cols) % peers).astype(jnp.int32)
+    terms = back_terms(slot_rows, dests, own_tiles, back_stack, peers)
     returned = terms[0].astype(jnp.float32)
     for s in range(1, peers):
         returned = returned + shifted(terms[s], "col", peers, peers - s).astype(jnp.float32)

time: 160 us -> 153 us (0.956)
  matrix products: 25.2 us -> 13.8 us
  local copies, waits for them, and re-layouts: 14.4 us -> 5.43 us
  waiting for transfers between devices: 75.9 us -> 82.1 us
  Pallas kernels: 0 us -> 6.09 us
  other arithmetic: 5.65 us -> 9.12 us
  starting transfers between devices: 23.9 us -> 20.9 us
    dot_general x4 -> x0, matrix products: 8.61 us -> none  [the longest x1 2.79 us: local(): jnp.einsum('st,sak->tak', pick_level, products, precision=lax.Precision.H...]
    pallas_call x0 -> x2, Pallas kernels: none -> 6.09 us  [the longest x1 3.17 us: coupling_terms(): pl.pallas_call(coupling_kernel, out_shape=jax.ShapeDtypeStruct((levels, p...]
    ppermute x5, waiting for transfers between devices: 32.1 us -> 38 us  [swapped(): return lax.ppermute(x, axis, [(i, i ^ bit) for i in range(size)])]
    ppermute x9, waiting for transfers between devices: 16 us -> 19 us  [shifted(): return lax.ppermute(x, axis, [(i, (i + shift) % size) for i in range(size)])]
    all_gather x1, waiting for transfers between devices: 3.22 us -> 0.26 us  [local(): mats = lax.all_gather(mine, 'row', axis=1, tiled=True)]
    gather x2 -> x0, local copies, waits for them, and re-layouts: 2.82 us -> none  [the longest x1 1.42 us: local(): back_stack[safe_rows]]
    dot_general x3, matrix products: 4.9 us -> 2.14 us  [local(): jnp.einsum('uab,ac->ubc', mats[1:level + 1], solved.astype(jnp.bfloat16),...]
    dot_general x3 -> x0, local copies, waits for them, and re-layouts: 2.71 us -> none  [the longest x1 1.34 us: local(): jnp.einsum('sab,sak->sbk', own_tiles, back_stack[safe_rows], preferred_el...]
  transfers between devices with their start and end apart: 21 -> 21, of which waited for: 13 -> 15; matrix products, arithmetic and copies ran while one was open for 10% -> 4% of each run, Pallas kernels for 0% -> 2%
where the time goes in v5:
time: 153 us; the launch traced here: 152 us
  waiting for transfers between devices  82.1 us (54%)
  starting transfers between devices  20.9 us (14%)
  between operations  14.4 us (9%)
  matrix products  13.8 us (9%)
  other arithmetic  9.12 us (6%)
  Pallas kernels  6.09 us (4%)
  local copies, waits for them, and re-layouts  5.43 us (4%)
    ppermute x5, waiting for transfers between devices, swapped(): return lax.ppermute(x, axis, [(i, i ^ bit) for i in range(size)])  38 us
    ppermute x3, waiting for transfers between devices, local(): pushed = lax.ppermute(pushed, 'col', [(level + 1, level)])  23 us
    ppermute x9, waiting for transfers between devices, shifted(): return lax.ppermute(x, axis, [(i, (i + shift) % size) for i in range(size)])  19 us
    ppermute x9, starting transfers between devices, shifted(): return lax.ppermute(x, axis, [(i, (i + shift) % size) for i in range(size)])  10.1 us
    ppermute x5, starting transfers between devices, swapped(): return lax.ppermute(x, axis, [(i, i ^ bit) for i in range(size)])  4.41 us
    dot_general x4, matrix products, local(): lax.dot_general(inv, update.astype(jnp.bfloat16), (((0,), (0,)), ((), ())...  4.4 us
    ppermute x3, starting transfers between devices, local(): pushed = lax.ppermute(pushed, 'col', [(level - 1, level)])  3.53 us
    pallas_call x1, Pallas kernels, coupling_terms(): pl.pallas_call(coupling_kernel, out_shape=jax.ShapeDtypeStruct((levels, p...  3.17 us
  transfers between devices with their start and end apart: 21, of which 15 were waited for; matrix products, arithmetic and copies ran while one was open for 4% of the time, Pallas kernels for 2%

profile of v5, /device:TPU:0, one launch (start us, length us, event | category | flops | bytes accessed | tf_op | source)
XLA Modules:
  0.0 151.8 jit_solution(15497029773957324538)
XLA Ops:
  7.2 0.7 fusion.54
  8.0 0.7 compare_and_fusion
  8.7 0.9 constant_dynamic-slice_fusion.6
  9.5 1.6 %gather_fusion = bf16[3,64,512]{2,1,0:T(8,128)(2,1)S(1)} fusion(bf16[6,64,512]{2,1,0:T(8,128)(2,1)} %param.16, s32[1024]{0:T(1024)S(1)} %pad_clamp_fusion), kind=kCustom, calls=%fused_computation | custom fusion | bytes 393228 | tf_op jit(solution)/shard_map/jit(_take)/gather | solution.py:133
  11.2 0.7 pad_maximum_fusion.3
  11.9 1.2 convolution_convert_fusion.4
  13.2 0.5 collective-permute-start
  13.7 2.6 %collective-permute-start.1 = (bf16[512,128]{1,0:T(8,128)(2,1)S(1)}, bf16[512,128]{1,0:T(8,128)(2,1)S(1)}, u32[]{:S(2)}, u32[]{:S(2)}) collective-permute-start(bf16[512,128]{1,0:T(8,128)(2,1)S(1)} %convolution_convert_fusion.4), channel_id=1, source_target_pairs={{0,2},{1,3},{2,0},{3,1},{4,6},{5,7},{6,4},{7,5},{8,10},{9,11},{10,... | collective-permute-start | bytes 393224 | tf_op jit(solution)/shard_map/ppermute | solution.py:67
  16.3 1.4 collective-permute-start.2
  17.7 0.6 and_select_fusion.2
  18.2 0.8 iota_reduce_fusion
  19.0 0.6 pad_add_fusion.fold_ref
  19.6 0.9 collective-permute-done.1
  20.5 1.8 %collective-permute-done.2 = bf16[512,128]{1,0:T(8,128)(2,1)S(1)} collective-permute-done((bf16[512,128]{1,0:T(8,128)(2,1)S(1)}, bf16[512,128]{1,0:T(8,128)(2,1)S(1)}, u32[]{:S(2)}, u32[]{:S(2)}) %collective-permute-start.2) | collective-permute-done | bytes 131104 | tf_op jit(solution)/shard_map/ppermute | solution.py:67
  22.3 0.9 pad_maximum_fusion.1.panels_ref
  23.2 3.2 %shard_map.104 = f32[4,512,128]{2,1,0:T(8,128)} custom-call(s32[4]{0:T(128)} %bitcast.152, s32[4]{0:T(128)} %get-tuple-element.3.picks_ref, s32[2]{0:T(128)} %pad_add_fusion.fold_ref, bf16[4,512,512]{2,1,0:T(8,128)(2,1)} %bitcast.141, bf16[4,512,128]{2,1,0:T(8,128)(2,1)} %pad_maximum_fusion.1.panels_ref, bf16[4,64,128]{2,1,0:T(8,128)(2,1)} %rhs_ref.1), custom_call_target="tpu_custom_call" | custom-call | tf_op jit(solution)/shard_map/pallas_call | solution.py:32
  26.4 1.3 convert_element_type.151
  27.7 0.8 collective-permute-start.3
  28.4 8.3 %collective-permute-done.3 = bf16[2,512,128]{2,1,0:T(8,128)(2,1)S(1)} collective-permute-done((bf16[2,512,128]{2,1,0:T(8,128)(2,1)S(1)}, bf16[2,512,128]{2,1,0:T(8,128)(2,1)S(1)}, u32[]{:S(2)}, u32[]{:S(2)}) %collective-permute-start.3) | collective-permute-done | bytes 262176 | tf_op jit(solution)/shard_map/ppermute | solution.py:71
  36.9 0.4 collective-permute-start.4
  37.3 1.0 collective-permute-done.4
  38.3 1.4 collective-permute-start.5
  39.8 5.4 %collective-permute-done.5 = bf16[512,128]{1,0:T(8,128)(2,1)S(1)} collective-permute-done((bf16[512,128]{1,0:T(8,128)(2,1)S(1)}, bf16[512,128]{1,0:T(8,128)(2,1)S(1)}, u32[]{:S(2)}, u32[]{:S(2)}) %collective-permute-start.5) | collective-permute-done | bytes 131104 | tf_op jit(solution)/shard_map/ppermute | solution.py:71
  45.2 1.4 collective-permute-start.6
  46.6 10.2 %collective-permute-done.6 = bf16[512,128]{1,0:T(8,128)(2,1)S(1)} collective-permute-done((bf16[512,128]{1,0:T(8,128)(2,1)S(1)}, bf16[512,128]{1,0:T(8,128)(2,1)S(1)}, u32[]{:S(2)}, u32[]{:S(2)}) %collective-permute-start.6) | collective-permute-done | bytes 131104 | tf_op jit(solution)/shard_map/ppermute | solution.py:71
  56.9 0.3 collective-permute-start.7
  57.2 13.1 %collective-permute-done.7 = bf16[512,128]{1,0:T(8,128)(2,1)S(1)} collective-permute-done((bf16[512,128]{1,0:T(8,128)(2,1)S(1)}, bf16[512,128]{1,0:T(8,128)(2,1)S(1)}, u32[]{:S(2)}, u32[]{:S(2)}) %collective-permute-start.7) | collective-permute-done | bytes 131104 | tf_op jit(solution)/shard_map/ppermute | solution.py:71
  70.6 1.5 convolution_convert_fusion.3
  72.1 2.0 %fusion.41 = f32[3,512,128]{2,1,0:T(8,128)S(1)} fusion(bf16[4,512,512]{2,1,0:T(8,128)(2,1)} %all-gather.2.cloned.1.call-done, bf16[512,128]{1,0:T(8,128)(2,1)S(1)} %convolution_convert_fusion.3), kind=kOutput, calls=%fused_computation.70 | convolution fusion | flops 201326592 | bytes 3014656 | tf_op jit(solution)/shard_map/kab,bc->kac/dot_general | solution.py:167
  74.1 1.5 collective-permute-start.8
  75.6 1.8 %collective-permute-done.8 = f32[3,512,128]{2,1,0:T(8,128)S(1)} collective-permute-done((f32[3,512,128]{2,1,0:T(8,128)S(1)}, f32[3,512,128]{2,1,0:T(8,128)S(1)}, u32[]{:S(2)}, u32[]{:S(2)}) %collective-permute-start.8) | collective-permute-done | bytes 786464 | tf_op jit(solution)/shard_map/ppermute | solution.py:162
  77.4 0.3 convolution_convert_fusion.2
  77.7 0.4 slice_add_fusion.1
  78.2 0.7 collective-permute-start.9
  78.9 0.3 convolution_convert_fusion.1
  79.2 0.3 slice_add_fusion.3
  79.5 1.4 collective-permute-start.10
  80.9 1.7 %fusion = f32[512,128]{1,0:T(8,128)S(1)} fusion(bf16[4,512,512]{2,1,0:T(8,128)(2,1)S(1)} %copy-done.1, f32[1,512,128]{2,1,0:T(8,128)} %collective-permute-done.10, bf16[512,128]{1,0:T(8,128)(2,1)S(1)} %add_convert_fusion), kind=kOutput, calls=%fused_computation.11 | convolution fusion | flops 134545408 | bytes 1703936 | tf_op jit(solution)/shard_map/dot_general | solution.py:177
  82.6 0.6 fusion.35
  83.2 0.8 collective-permute-start.11
  84.1 0.3 fusion.20
  84.4 0.5 slice_add_fusion
  84.9 0.7 collective-permute-start.12
  85.6 0.3 fusion.19
  86.0 1.0 slice_add_fusion.2
  87.0 1.3 collective-permute-start.13
  88.3 23.0 %collective-permute-done.13 = f32[1,512,128]{2,1,0:T(8,128)} collective-permute-done((f32[1,512,128]{2,1,0:T(8,128)}, f32[1,512,128]{2,1,0:T(8,128)}, u32[]{:S(2)}, u32[]{:S(2)}) %collective-permute-start.13) | collective-permute-done | bytes 262176 | tf_op jit(solution)/shard_map/ppermute | solution.py:175
  111.3 2.0 %convolution_select_fusion = f32[512,128]{1,0:T(8,128)} fusion(f32[512,128]{1,0:T(8,128)S(1)} %fusion.19, f32[512,128]{1,0:T(8,128)S(1)} %fusion.20, f32[512,128]{1,0:T(8,128)S(1)} %fusion, bf16[4,512,512]{2,1,0:T(8,128)(2,1)S(1)} %copy-done.1, f32[1,512,128]{2,1,0:T(8,128)} %collective-permute-done.13, bf16[512,128]{1,0:T(8,128)(2,1)} %copy-done.2, ...), kind=kOutput, calls=%fused_computation.3 | convolution fusion | flops 67502080 | bytes 1966083 | tf_op jit(solution)/shard_map/dot_general | solution.py:177
  113.5 1.6 %collective-permute-start.16 = (f32[512,128]{1,0:T(8,128)}, f32[512,128]{1,0:T(8,128)S(1)}, u32[]{:S(2)}, u32[]{:S(2)}) collective-permute-start(f32[512,128]{1,0:T(8,128)} %convolution_select_fusion), channel_id=1, source_target_pairs={{0,3},{1,0},{2,1},{3,2},{4,7},{5,4},{6,5},{7,6},{8,11},{9,8},{10,9... | collective-permute-start | bytes 786440 | tf_op jit(solution)/shard_map/ppermute | solution.py:67
  115.1 6.3 %collective-permute-done.14 = f32[512,128]{1,0:T(8,128)S(1)} collective-permute-done((f32[512,128]{1,0:T(8,128)}, f32[512,128]{1,0:T(8,128)S(1)}, u32[]{:S(2)}, u32[]{:S(2)}) %collective-permute-start.14) | collective-permute-done | bytes 262176 | tf_op jit(solution)/shard_map/ppermute | solution.py:67
  121.4 1.4 collective-permute-done.15
  122.8 2.6 %collective-permute-done.16 = f32[512,128]{1,0:T(8,128)S(1)} collective-permute-done((f32[512,128]{1,0:T(8,128)}, f32[512,128]{1,0:T(8,128)S(1)}, u32[]{:S(2)}, u32[]{:S(2)}) %collective-permute-start.16) | collective-permute-done | bytes 262176 | tf_op jit(solution)/shard_map/ppermute | solution.py:67
  125.4 1.0 pad_maximum_fusion
  126.5 0.8 scatter_fusion
  127.5 0.9 pad_maximum_fusion.2.back_ref
  128.4 2.9 %shard_map.105 = bf16[4,512,128]{2,1,0:T(8,128)(2,1)} custom-call(s32[4]{0:T(128)} %bitcast.153, s32[4]{0:T(128)} %get-tuple-element.8.dests_ref, bf16[4,512,512]{2,1,0:T(8,128)(2,1)} %bitcast.142, bf16[4,512,128]{2,1,0:T(8,128)(2,1)} %pad_maximum_fusion.2.back_ref), custom_call_target="tpu_custom_call" | custom-call | tf_op jit(solution)/shard_map/pallas_call | solution.py:57
  131.3 1.1 slice_bitcast_fusion.19
  132.4 2.5 %collective-permute-start.17 = (bf16[512,128]{1,0:T(8,128)(2,1)S(1)}, bf16[512,128]{1,0:T(8,128)(2,1)S(1)}, u32[]{:S(2)}, u32[]{:S(2)}) collective-permute-start(bf16[512,128]{1,0:T(8,128)(2,1)S(1)} %get-tuple-element.18), channel_id=1, source_target_pairs={{0,3},{1,0},{2,1},{3,2},{4,7},{5,4},{6,5},{7,6},{8,11},{9,8},{10,9... | collective-permute-start | bytes 393224 | tf_op jit(solution)/shard_map/ppermute | solution.py:67
  134.9 1.3 collective-permute-start.18
  136.2 0.7 pad_maximum_fusion.4
  136.9 1.9 %collective-permute-done.17 = bf16[512,128]{1,0:T(8,128)(2,1)S(1)} collective-permute-done((bf16[512,128]{1,0:T(8,128)(2,1)S(1)}, bf16[512,128]{1,0:T(8,128)(2,1)S(1)}, u32[]{:S(2)}, u32[]{:S(2)}) %collective-permute-start.17) | collective-permute-done | bytes 131104 | tf_op jit(solution)/shard_map/ppermute | solution.py:67
  138.8 4.1 %collective-permute-done.18 = bf16[512,128]{1,0:T(8,128)(2,1)S(1)} collective-permute-done((bf16[512,128]{1,0:T(8,128)(2,1)S(1)}, bf16[512,128]{1,0:T(8,128)(2,1)S(1)}, u32[]{:S(2)}, u32[]{:S(2)}) %collective-permute-start.18) | collective-permute-done | bytes 131104 | tf_op jit(solution)/shard_map/ppermute | solution.py:67
  142.9 1.2 convolution_bitcast_fusion
  144.1 0.8 copy.16
  (41 shorter events, 1.1 us)
Async XLA Ops:
  7.2 4.8 %copy-start = (bf16[1,512,512]{2,1,0:T(8,128)(2,1)S(1)}, bf16[1,512,512]{2,1,0:T(8,128)(2,1)}, u32[]{:S(2)}) copy-start(bf16[1,512,512]{2,1,0:T(8,128)(2,1)} %param.10) | copy-start | bytes 1572868
  7.2 10.5 %copy-start.5 = (s32[1,4]{1,0:T(1,128)S(1)}, s32[1,4]{1,0:T(1,128)}, u32[]{:S(2)}) copy-start(s32[1,4]{1,0:T(1,128)} %param.13) | copy-start | bytes 52
  7.2 63.4 %all-gather.2.cloned.1.call-start = ((), (), s32[]{:S(2)}) async-start(), calls=%async_computation | async-start | bytes 2359296 | tf_op jit(solution)/shard_map/all_gather | solution.py:135
  13.2 6.4 %collective-permute-start = (bf16[512,128]{1,0:T(8,128)(2,1)S(1)}, bf16[512,128]{1,0:T(8,128)(2,1)S(1)}, u32[]{:S(2)}, u32[]{:S(2)}) collective-permute-start(bf16[512,128]{1,0:T(8,128)(2,1)S(1)} %convolution_convert_fusion.4), channel_id=1, source_target_pairs={{0,1},{1,2},{2,3},{3,0},{4,5},{5,6},{6,7},{7,4},{8,9},{9,10},{10,1... | collective-permute-start | bytes 393224 | tf_op jit(solution)/shard_map/ppermute | solution.py:67
  13.7 6.8 %collective-permute-start.1 = (bf16[512,128]{1,0:T(8,128)(2,1)S(1)}, bf16[512,128]{1,0:T(8,128)(2,1)S(1)}, u32[]{:S(2)}, u32[]{:S(2)}) collective-permute-start(bf16[512,128]{1,0:T(8,128)(2,1)S(1)} %convolution_convert_fusion.4), channel_id=1, source_target_pairs={{0,2},{1,3},{2,0},{3,1},{4,6},{5,7},{6,4},{7,5},{8,10},{9,11},{10,... | collective-permute-start | bytes 393224 | tf_op jit(solution)/shard_map/ppermute | solution.py:67
  16.3 6.0 %collective-permute-start.2 = (bf16[512,128]{1,0:T(8,128)(2,1)S(1)}, bf16[512,128]{1,0:T(8,128)(2,1)S(1)}, u32[]{:S(2)}, u32[]{:S(2)}) collective-permute-start(bf16[512,128]{1,0:T(8,128)(2,1)S(1)} %convolution_convert_fusion.4), channel_id=1, source_target_pairs={{0,3},{1,0},{2,1},{3,2},{4,7},{5,4},{6,5},{7,6},{8,11},{9,8},{10,9... | collective-permute-start | bytes 393224 | tf_op jit(solution)/shard_map/ppermute | solution.py:67
  27.7 9.1 %collective-permute-start.3 = (bf16[2,512,128]{2,1,0:T(8,128)(2,1)S(1)}, bf16[2,512,128]{2,1,0:T(8,128)(2,1)S(1)}, u32[]{:S(2)}, u32[]{:S(2)}) collective-permute-start(bf16[2,512,128]{2,1,0:T(8,128)(2,1)S(1)} %dynamic-slice_bitcast_fusion), channel_id=1, source_target_pairs={{0,2},{1,3},{2,0},{3,1},{4,6},{5,7},{6,4},{7,5},{8,10},{9,11},{10,... | collective-permute-start | bytes 786440 | tf_op jit(solution)/shard_map/ppermute | solution.py:71
  36.9 1.4 collective-permute-start.4
  38.3 6.8 %collective-permute-start.5 = (bf16[512,128]{1,0:T(8,128)(2,1)S(1)}, bf16[512,128]{1,0:T(8,128)(2,1)S(1)}, u32[]{:S(2)}, u32[]{:S(2)}) collective-permute-start(bf16[512,128]{1,0:T(8,128)(2,1)S(1)} %fusion.21), channel_id=1, source_target_pairs={{0,4},{4,0},{8,12},{12,8},{16,20},{20,16},{24,28},{28,24},{1,5},{5... | collective-permute-start | bytes 393224 | tf_op jit(solution)/shard_map/ppermute | solution.py:71
  45.2 11.7 %collective-permute-start.6 = (bf16[512,128]{1,0:T(8,128)(2,1)S(1)}, bf16[512,128]{1,0:T(8,128)(2,1)S(1)}, u32[]{:S(2)}, u32[]{:S(2)}) collective-permute-start(bf16[512,128]{1,0:T(8,128)(2,1)S(1)} %add_convert_fusion.2), channel_id=1, source_target_pairs={{0,8},{4,12},{8,0},{12,4},{16,24},{20,28},{24,16},{28,20},{1,9},{5... | collective-permute-start | bytes 393224 | tf_op jit(solution)/shard_map/ppermute | solution.py:71
  56.9 13.4 %collective-permute-start.7 = (bf16[512,128]{1,0:T(8,128)(2,1)S(1)}, bf16[512,128]{1,0:T(8,128)(2,1)S(1)}, u32[]{:S(2)}, u32[]{:S(2)}) collective-permute-start(bf16[512,128]{1,0:T(8,128)(2,1)S(1)} %add_convert_fusion.1), channel_id=1, source_target_pairs={{0,16},{4,20},{8,24},{12,28},{16,0},{20,4},{24,8},{28,12},{1,17},{... | collective-permute-start | bytes 393224 | tf_op jit(solution)/shard_map/ppermute | solution.py:71
  70.6 6.8 %copy-start.1 = (bf16[4,512,512]{2,1,0:T(8,128)(2,1)S(1)}, bf16[4,512,512]{2,1,0:T(8,128)(2,1)}, u32[]{:S(2)}) copy-start(bf16[4,512,512]{2,1,0:T(8,128)(2,1)} %all-gather.2.cloned.1.call-done) | copy-start | bytes 6291460
  72.1 6.1 %copy-start.2 = (bf16[512,128]{1,0:T(8,128)(2,1)}, bf16[512,128]{1,0:T(8,128)(2,1)S(1)}, u32[]{:S(2)}) copy-start(bf16[512,128]{1,0:T(8,128)(2,1)S(1)} %convolution_convert_fusion.3) | copy-start | bytes 393220
  74.1 3.3 %collective-permute-start.8 = (f32[3,512,128]{2,1,0:T(8,128)S(1)}, f32[3,512,128]{2,1,0:T(8,128)S(1)}, u32[]{:S(2)}, u32[]{:S(2)}) collective-permute-start(f32[3,512,128]{2,1,0:T(8,128)S(1)} %fusion.41), channel_id=1, source_target_pairs={{0,1},{4,5},{8,9},{12,13},{16,17},{20,21},{24,25},{28,29}} | collective-permute-start | bytes 2359304 | tf_op jit(solution)/shard_map/ppermute | solution.py:162
  77.7 1.8 %copy-start.3 = (bf16[512,128]{1,0:T(8,128)(2,1)}, bf16[512,128]{1,0:T(8,128)(2,1)S(1)}, u32[]{:S(2)}) copy-start(bf16[512,128]{1,0:T(8,128)(2,1)S(1)} %convolution_convert_fusion.2) | copy-start | bytes 393220
  78.2 0.7 collective-permute-start.9
  79.5 1.4 collective-permute-start.10
  83.2 2.4 %copy-start.4 = (bf16[512,128]{1,0:T(8,128)(2,1)S(1)}, bf16[512,128]{1,0:T(8,128)(2,1)}, u32[]{:S(2)}) copy-start(bf16[512,128]{1,0:T(8,128)(2,1)} %copy-done.3) | copy-start | bytes 393220
  83.2 0.9 collective-permute-start.11
  84.9 0.7 collective-permute-start.12
  87.0 24.2 %collective-permute-start.13 = (f32[1,512,128]{2,1,0:T(8,128)}, f32[1,512,128]{2,1,0:T(8,128)}, u32[]{:S(2)}, u32[]{:S(2)}) collective-permute-start(f32[1,512,128]{2,1,0:T(8,128)} %slice_add_fusion.2), channel_id=1, source_target_pairs={{1,0},{5,4},{9,8},{13,12},{17,16},{21,20},{25,24},{29,28}} | collective-permute-start | bytes 786440 | tf_op jit(solution)/shard_map/ppermute | solution.py:175
  113.3 8.1 %collective-permute-start.14 = (f32[512,128]{1,0:T(8,128)}, f32[512,128]{1,0:T(8,128)S(1)}, u32[]{:S(2)}, u32[]{:S(2)}) collective-permute-start(f32[512,128]{1,0:T(8,128)} %convolution_select_fusion), channel_id=1, source_target_pairs={{0,1},{1,2},{2,3},{3,0},{4,5},{5,6},{6,7},{7,4},{8,9},{9,10},{10,1... | collective-permute-start | bytes 786440 | tf_op jit(solution)/shard_map/ppermute | solution.py:67
  113.5 9.4 %collective-permute-start.15 = (f32[512,128]{1,0:T(8,128)}, f32[512,128]{1,0:T(8,128)S(1)}, u32[]{:S(2)}, u32[]{:S(2)}) collective-permute-start(f32[512,128]{1,0:T(8,128)} %convolution_select_fusion), channel_id=1, source_target_pairs={{0,2},{1,3},{2,0},{3,1},{4,6},{5,7},{6,4},{7,5},{8,10},{9,11},{10,... | collective-permute-start | bytes 786440 | tf_op jit(solution)/shard_map/ppermute | solution.py:67
  113.5 11.9 %collective-permute-start.16 = (f32[512,128]{1,0:T(8,128)}, f32[512,128]{1,0:T(8,128)S(1)}, u32[]{:S(2)}, u32[]{:S(2)}) collective-permute-start(f32[512,128]{1,0:T(8,128)} %convolution_select_fusion), channel_id=1, source_target_pairs={{0,3},{1,0},{2,1},{3,2},{4,7},{5,4},{6,5},{7,6},{8,11},{9,8},{10,9... | collective-permute-start | bytes 786440 | tf_op jit(solution)/shard_map/ppermute | solution.py:67
  132.4 6.4 %collective-permute-start.17 = (bf16[512,128]{1,0:T(8,128)(2,1)S(1)}, bf16[512,128]{1,0:T(8,128)(2,1)S(1)}, u32[]{:S(2)}, u32[]{:S(2)}) collective-permute-start(bf16[512,128]{1,0:T(8,128)(2,1)S(1)} %get-tuple-element.18), channel_id=1, source_target_pairs={{0,3},{1,0},{2,1},{3,2},{4,7},{5,4},{6,5},{7,6},{8,11},{9,8},{10,9... | collective-permute-start | bytes 393224 | tf_op jit(solution)/shard_map/ppermute | solution.py:67
  134.9 8.0 %collective-permute-start.18 = (bf16[512,128]{1,0:T(8,128)(2,1)S(1)}, bf16[512,128]{1,0:T(8,128)(2,1)S(1)}, u32[]{:S(2)}, u32[]{:S(2)}) collective-permute-start(bf16[512,128]{1,0:T(8,128)(2,1)S(1)} %get-tuple-element.20), channel_id=1, source_target_pairs={{0,2},{1,3},{2,0},{3,1},{4,6},{5,7},{6,4},{7,5},{8,10},{9,11},{10,... | collective-permute-start | bytes 393224 | tf_op jit(solution)/shard_map/ppermute | solution.py:67
  136.2 6.7 %collective-permute-start.19 = (bf16[512,128]{1,0:T(8,128)(2,1)S(1)}, bf16[512,128]{1,0:T(8,128)(2,1)S(1)}, u32[]{:S(2)}, u32[]{:S(2)}) collective-permute-start(bf16[512,128]{1,0:T(8,128)(2,1)S(1)} %get-tuple-element.19), channel_id=1, source_target_pairs={{0,1},{1,2},{2,3},{3,0},{4,5},{5,6},{6,7},{7,4},{8,9},{9,10},{10,1... | collective-permute-start | bytes 393224 | tf_op jit(solution)/shard_map/ppermute | solution.py:67
Sparse Core Ops, SparseCore 0:
  12.1 58.4 all-gather.1

commit v6 on v5

--- a/solution.py
+++ b/solution.py
@@ -37,30 +37,52 @@
     )(slot_rows, picks, fold, tiles, panels, rhs)
 
 
-def back_kernel(rows_ref, dests_ref, tiles_ref, back_ref, out_ref, acc_ref):
-    acc_ref[...] = jnp.zeros_like(acc_ref)
+def back_upper_kernel(rows_ref, dests_ref, tiles_ref, back_ref, out_ref):
+    out_ref[...] = jnp.zeros_like(out_ref)
     for s in range(tiles_ref.shape[0]):
         level = rows_ref[s]
 
-        @pl.when(level >= 0)
+        @pl.when(level >= 1)
         def _():
             prod = lax.dot_general(
-                tiles_ref[s], back_ref[level], (((0,), (0,)), ((), ())), preferred_element_type=jnp.float32
+                tiles_ref[s], back_ref[level - 1], (((0,), (0,)), ((), ())), preferred_element_type=jnp.float32
+            )
+            out_ref[dests_ref[s]] += prod
+
+
+def back_first_kernel(rows_ref, dests_ref, tiles_ref, back_ref, upper_ref, out_ref, acc_ref):
+    acc_ref[...] = upper_ref[...]
+    for s in range(tiles_ref.shape[0]):
+        level = rows_ref[s]
+
+        @pl.when(level == 0)
+        def _():
+            prod = lax.dot_general(
+                tiles_ref[s], back_ref[...], (((0,), (0,)), ((), ())), preferred_element_type=jnp.float32
             )
             acc_ref[dests_ref[s]] += prod
 
     out_ref[...] = acc_ref[...].astype(out_ref.dtype)
 
 
-def back_terms(slot_rows, dests, tiles, back, peers):
+def back_upper(slot_rows, dests, tiles, back, peers):
     shape = (peers, tiles.shape[2], back.shape[2])
     return pl.pallas_call(
-        back_kernel,
-        out_shape=jax.ShapeDtypeStruct(shape, jnp.bfloat16),
+        back_upper_kernel,
+        out_shape=jax.ShapeDtypeStruct(shape, jnp.float32),
         in_specs=[SMEM, SMEM, VMEM, VMEM],
         out_specs=VMEM,
-        scratch_shapes=[pltpu.VMEM(shape, jnp.float32)],
     )(slot_rows, dests, tiles, back)
+
+
+def back_first(slot_rows, dests, tiles, back, upper):
+    return pl.pallas_call(
+        back_first_kernel,
+        out_shape=jax.ShapeDtypeStruct(upper.shape, jnp.bfloat16),
+        in_specs=[SMEM, SMEM, VMEM, VMEM, VMEM],
+        out_specs=VMEM,
+        scratch_shapes=[pltpu.VMEM(upper.shape, jnp.float32)],
+    )(slot_rows, dests, tiles, back, upper)
 
 
 def shifted(x, axis, size, shift):
@@ -168,7 +190,7 @@
                 "kab,bc->kac", mats[level + 1 : levels], top_forward[level], preferred_element_type=jnp.float32
             )
             pushed = later if level == 0 else pushed[1:] + later
-    own_solution = None
+    solutions = [None] * levels
     for level in reversed(range(levels)):
         update = top_forward[level].astype(jnp.float32)
         if level < levels - 1:
@@ -177,19 +199,18 @@
         solved = lax.dot_general(
             inv, update.astype(jnp.bfloat16), (((0,), (0,)), ((), ())), preferred_element_type=jnp.float32
         )
-        own_solution = solved if own_solution is None else jnp.where(me == level, solved, own_solution)
         if level > 0:
             earlier = jnp.einsum(
                 "uab,ac->ubc", mats[1 : level + 1], solved.astype(jnp.bfloat16), preferred_element_type=jnp.float32
             )
             pushed = earlier if level == levels - 1 else pushed[:level] + earlier
-    solutions = gathered_chunks(own_solution, peers, me)[:levels]
+        solutions[level] = broadcast_from(solved, level, me, "col", peers)
     top_slices = [lax.dynamic_slice_in_dim(solutions[t], position * share, share, 0) for t in range(levels)]
     top_back = [solutions[t].astype(jnp.bfloat16) for t in range(levels)]
 
-    back_stack = jnp.stack(top_back)
     dests = ((me - slot_cols) % peers).astype(jnp.int32)
-    terms = back_terms(slot_rows, dests, own_tiles, back_stack, peers)
+    upper = back_upper(slot_rows, dests, own_tiles, jnp.stack(top_back[1:]), peers)
+    terms = back_first(slot_rows, dests, own_tiles, top_back[0], upper)
     returned = terms[0].astype(jnp.float32)
     for s in range(1, peers):
         returned = returned + shifted(terms[s], "col", peers, peers - s).astype(jnp.float32)

time: 153 us -> 167 us (1.092)
  starting transfers between devices: 20.9 us -> 37.5 us
  waiting for transfers between devices: 82.1 us -> 75.1 us
  Pallas kernels: 6.09 us -> 9.07 us
    ppermute x0 -> x12, waiting for transfers between devices: none -> 28.9 us  [broadcast_from(): part = lax.ppermute(x, axis, [(owner, (owner + s) % size)])]
    ppermute x3, waiting for transfers between devices: 23 us -> 0.01 us  [local(): pushed = lax.ppermute(pushed, 'col', [(level + 1, level)])]
    ppermute x0 -> x12, starting transfers between devices: none -> 15.6 us  [broadcast_from(): part = lax.ppermute(x, axis, [(owner, (owner + s) % size)])]
    ppermute x9 -> x6, waiting for transfers between devices: 19 us -> 8.62 us  [shifted(): return lax.ppermute(x, axis, [(i, (i + shift) % size) for i in range(size)])]
    pallas_call x1 -> x2, Pallas kernels: 2.92 us -> 5.9 us  [the longest x1 3.01 us: back_upper(): pl.pallas_call(back_upper_kernel, out_shape=jax.ShapeDtypeStruct(shape, j...]
    ppermute x5, waiting for transfers between devices: 38 us -> 35.5 us  [swapped(): return lax.ppermute(x, axis, [(i, i ^ bit) for i in range(size)])]
    ppermute x9 -> x6, starting transfers between devices: 10.1 us -> 8.85 us  [shifted(): return lax.ppermute(x, axis, [(i, (i + shift) % size) for i in range(size)])]
  transfers between devices with their start and end apart: 21 -> 30, of which waited for: 15 -> 15; matrix products, arithmetic and copies ran while one was open for 4% -> 7% of each run, Pallas kernels for 2% -> 4%
where the time goes in v6:
time: 167 us; the launch traced here: 165 us
  waiting for transfers between devices  75.1 us (45%)
  starting transfers between devices  37.5 us (22%)
  between operations  14.5 us (9%)
  matrix products  14 us (8%)
  other arithmetic  9.95 us (6%)
  Pallas kernels  9.07 us (5%)
  local copies, waits for them, and re-layouts  4.4 us (3%)
    ppermute x5, waiting for transfers between devices, swapped(): return lax.ppermute(x, axis, [(i, i ^ bit) for i in range(size)])  35.5 us
    ppermute x12, waiting for transfers between devices, broadcast_from(): part = lax.ppermute(x, axis, [(owner, (owner + s) % size)])  28.9 us
    ppermute x12, starting transfers between devices, broadcast_from(): part = lax.ppermute(x, axis, [(owner, (owner + s) % size)])  15.6 us
    ppermute x6, starting transfers between devices, shifted(): return lax.ppermute(x, axis, [(i, (i + shift) % size) for i in range(size)])  8.85 us
    ppermute x6, waiting for transfers between devices, shifted(): return lax.ppermute(x, axis, [(i, (i + shift) % size) for i in range(size)])  8.62 us
    ppermute x5, starting transfers between devices, swapped(): return lax.ppermute(x, axis, [(i, i ^ bit) for i in range(size)])  5.85 us
    ppermute x3, starting transfers between devices, local(): pushed = lax.ppermute(pushed, 'col', [(level - 1, level)])  3.68 us
    dot_general x4, matrix products, local(): lax.dot_general(inv, update.astype(jnp.bfloat16), (((0,), (0,)), ((), ())...  3.65 us
  transfers between devices with their start and end apart: 30, of which 15 were waited for; matrix products, arithmetic and copies ran while one was open for 7% of the time, Pallas kernels for 4%

profile of v6, /device:TPU:0, one launch (start us, length us, event | category | flops | bytes accessed | tf_op | source)
XLA Modules:
  0.0 164.5 jit_solution(2891297831395183170)
XLA Ops:
  7.2 0.7 fusion.53
  8.0 0.7 compare_and_fusion
  8.7 0.9 constant_dynamic-slice_fusion.2
  9.5 1.6 gather_fusion
  11.2 0.7 pad_maximum_fusion.2
  11.9 1.2 convolution_convert_fusion.4
  13.2 2.5 %collective-permute-start.2 = (bf16[512,128]{1,0:T(8,128)(2,1)S(1)}, bf16[512,128]{1,0:T(8,128)(2,1)S(1)}, u32[]{:S(2)}, u32[]{:S(2)}) collective-permute-start(bf16[512,128]{1,0:T(8,128)(2,1)S(1)} %convolution_convert_fusion.4), channel_id=1, source_target_pairs={{0,3},{1,0},{2,1},{3,2},{4,7},{5,4},{6,5},{7,6},{8,11},{9,8},{10,9... | collective-permute-start | bytes 393224 | tf_op jit(solution)/shard_map/ppermute | solution.py:89
  15.6 0.6 collective-permute-start.1
  17.0 0.7 iota_reduce_fusion
  18.3 1.1 collective-permute-done.2
  19.4 3.8 %collective-permute-done.1 = bf16[512,128]{1,0:T(8,128)(2,1)S(1)} collective-permute-done((bf16[512,128]{1,0:T(8,128)(2,1)S(1)}, bf16[512,128]{1,0:T(8,128)(2,1)S(1)}, u32[]{:S(2)}, u32[]{:S(2)}) %collective-permute-start.1) | collective-permute-done | bytes 131104 | tf_op jit(solution)/shard_map/ppermute | solution.py:89
  23.2 0.9 pad_maximum_fusion.panels_ref
  24.0 3.2 %shard_map.104 = f32[4,512,128]{2,1,0:T(8,128)} custom-call(s32[4]{0:T(128)} %bitcast.158, s32[4]{0:T(128)} %get-tuple-element.3.picks_ref, s32[2]{0:T(128)} %pad_add_fusion.fold_ref, bf16[4,512,512]{2,1,0:T(8,128)(2,1)} %bitcast.149, bf16[4,512,128]{2,1,0:T(8,128)(2,1)} %pad_maximum_fusion.panels_ref, bf16[4,64,128]{2,1,0:T(8,128)(2,1)} %rhs_ref.1), custom_call_target="tpu_custom_call" | custom-call | tf_op jit(solution)/shard_map/pallas_call | solution.py:32
  27.2 1.3 convert_element_type.147
  28.6 1.7 %collective-permute-start.3 = (bf16[2,512,128]{2,1,0:T(8,128)(2,1)S(1)}, bf16[2,512,128]{2,1,0:T(8,128)(2,1)S(1)}, u32[]{:S(2)}, u32[]{:S(2)}) collective-permute-start(bf16[2,512,128]{2,1,0:T(8,128)(2,1)S(1)} %dynamic-slice_bitcast_fusion), channel_id=1, source_target_pairs={{0,2},{1,3},{2,0},{3,1},{4,6},{5,7},{6,4},{7,5},{8,10},{9,11},{10,... | collective-permute-start | bytes 786440 | tf_op jit(solution)/shard_map/ppermute | solution.py:93
  30.3 6.0 %collective-permute-done.3 = bf16[2,512,128]{2,1,0:T(8,128)(2,1)S(1)} collective-permute-done((bf16[2,512,128]{2,1,0:T(8,128)(2,1)S(1)}, bf16[2,512,128]{2,1,0:T(8,128)(2,1)S(1)}, u32[]{:S(2)}, u32[]{:S(2)}) %collective-permute-start.3) | collective-permute-done | bytes 262176 | tf_op jit(solution)/shard_map/ppermute | solution.py:93
  36.4 1.3 collective-permute-done.4
  37.8 1.9 %collective-permute-start.5 = (bf16[512,128]{1,0:T(8,128)(2,1)S(1)}, bf16[512,128]{1,0:T(8,128)(2,1)S(1)}, u32[]{:S(2)}, u32[]{:S(2)}) collective-permute-start(bf16[512,128]{1,0:T(8,128)(2,1)S(1)} %fusion.22), channel_id=1, source_target_pairs={{0,4},{4,0},{8,12},{12,8},{16,20},{20,16},{24,28},{28,24},{1,5},{5... | collective-permute-start | bytes 393224 | tf_op jit(solution)/shard_map/ppermute | solution.py:93
  39.7 5.2 %collective-permute-done.5 = bf16[512,128]{1,0:T(8,128)(2,1)S(1)} collective-permute-done((bf16[512,128]{1,0:T(8,128)(2,1)S(1)}, bf16[512,128]{1,0:T(8,128)(2,1)S(1)}, u32[]{:S(2)}, u32[]{:S(2)}) %collective-permute-start.5) | collective-permute-done | bytes 131104 | tf_op jit(solution)/shard_map/ppermute | solution.py:93
  44.9 1.7 %collective-permute-start.6 = (bf16[512,128]{1,0:T(8,128)(2,1)S(1)}, bf16[512,128]{1,0:T(8,128)(2,1)S(1)}, u32[]{:S(2)}, u32[]{:S(2)}) collective-permute-start(bf16[512,128]{1,0:T(8,128)(2,1)S(1)} %add_convert_fusion.2), channel_id=1, source_target_pairs={{0,8},{4,12},{8,0},{12,4},{16,24},{20,28},{24,16},{28,20},{1,9},{5... | collective-permute-start | bytes 393224 | tf_op jit(solution)/shard_map/ppermute | solution.py:93
  46.6 10.1 %collective-permute-done.6 = bf16[512,128]{1,0:T(8,128)(2,1)S(1)} collective-permute-done((bf16[512,128]{1,0:T(8,128)(2,1)S(1)}, bf16[512,128]{1,0:T(8,128)(2,1)S(1)}, u32[]{:S(2)}, u32[]{:S(2)}) %collective-permute-start.6) | collective-permute-done | bytes 131104 | tf_op jit(solution)/shard_map/ppermute | solution.py:93
  57.2 13.0 %collective-permute-done.7 = bf16[512,128]{1,0:T(8,128)(2,1)S(1)} collective-permute-done((bf16[512,128]{1,0:T(8,128)(2,1)S(1)}, bf16[512,128]{1,0:T(8,128)(2,1)S(1)}, u32[]{:S(2)}, u32[]{:S(2)}) %collective-permute-start.7) | collective-permute-done | bytes 131104 | tf_op jit(solution)/shard_map/ppermute | solution.py:93
  70.4 1.5 convolution_convert_fusion.3
  71.9 2.0 %fusion.42 = f32[3,512,128]{2,1,0:T(8,128)S(1)} fusion(bf16[4,512,512]{2,1,0:T(8,128)(2,1)} %all-gather.2.cloned.1.call-done, bf16[512,128]{1,0:T(8,128)(2,1)S(1)} %convolution_convert_fusion.3), kind=kOutput, calls=%fused_computation.72 | convolution fusion | flops 201326592 | bytes 3014656 | tf_op jit(solution)/shard_map/kab,bc->kac/dot_general | solution.py:189
  73.9 1.6 collective-permute-start.8
  75.5 1.8 %collective-permute-done.8 = f32[3,512,128]{2,1,0:T(8,128)S(1)} collective-permute-done((f32[3,512,128]{2,1,0:T(8,128)S(1)}, f32[3,512,128]{2,1,0:T(8,128)S(1)}, u32[]{:S(2)}, u32[]{:S(2)}) %collective-permute-start.8) | collective-permute-done | bytes 786464 | tf_op jit(solution)/shard_map/ppermute | solution.py:184
  78.1 0.7 collective-permute-start.9
  79.5 1.4 collective-permute-start.10
  80.8 1.7 %fusion = f32[512,128]{1,0:T(8,128)S(1)} fusion(bf16[4,512,512]{2,1,0:T(8,128)(2,1)S(1)} %copy-done.1, f32[1,512,128]{2,1,0:T(8,128)} %collective-permute-done.10, bf16[512,128]{1,0:T(8,128)(2,1)S(1)} %add_convert_fusion), kind=kOutput, calls=%fused_computation.9 | convolution fusion | flops 134545408 | bytes 1703936 | tf_op jit(solution)/shard_map/dot_general | solution.py:199
  82.5 0.6 fusion.36
  83.1 0.7 collective-permute-start.11
  84.2 1.3 slice_add_fusion
  85.5 1.5 collective-permute-start.12
  87.0 1.4 collective-permute-start.25
  88.3 1.3 collective-permute-start.23
  89.6 1.4 collective-permute-start.24
  91.0 20.1 %collective-permute-done.23 = f32[512,128]{1,0:T(8,128)} collective-permute-done((f32[512,128]{1,0:T(8,128)S(1)}, f32[512,128]{1,0:T(8,128)}, u32[]{:S(2)}, u32[]{:S(2)}) %collective-permute-start.23) | collective-permute-done | bytes 262176 | tf_op jit(solution)/shard_map/ppermute | solution.py:99
  111.1 1.2 convert_bitcast_fusion
  112.3 0.7 collective-permute-start.22
  113.0 0.7 collective-permute-start.20
  113.7 1.3 collective-permute-start.21
  115.0 1.3 fusion.19
  116.3 1.3 slice_add_fusion.2
  117.6 1.3 collective-permute-start.13
  118.9 6.7 %collective-permute-done.21 = f32[512,128]{1,0:T(8,128)S(1)} collective-permute-done((f32[512,128]{1,0:T(8,128)S(1)}, f32[512,128]{1,0:T(8,128)S(1)}, u32[]{:S(2)}, u32[]{:S(2)}) %collective-permute-start.21) | collective-permute-done | bytes 262176 | tf_op jit(solution)/shard_map/ppermute | solution.py:99
  125.7 1.3 collective-permute-start.19
  127.0 0.7 collective-permute-start.17
  127.7 0.7 collective-permute-start.18
  128.7 1.3 collective-permute-start.16
  130.0 3.7 %collective-permute-start.14 = (f32[512,128]{1,0:T(8,128)S(1)}, f32[512,128]{1,0:T(8,128)S(1)}, u32[]{:S(2)}, u32[]{:S(2)}) collective-permute-start(f32[512,128]{1,0:T(8,128)S(1)} %fusion.21), channel_id=1, source_target_pairs={{0,1},{4,5},{8,9},{12,13},{16,17},{20,21},{24,25},{28,29}} | collective-permute-start | bytes 786440 | tf_op jit(solution)/shard_map/ppermute | solution.py:99
  133.7 1.3 collective-permute-start.15
  135.1 0.8 pad_maximum_fusion.1.back_ref
  136.0 3.0 %shard_map.105.upper_ref = f32[4,512,128]{2,1,0:T(8,128)} custom-call(s32[4]{0:T(128)} %bitcast.159, s32[4]{0:T(128)} %get-tuple-element.16.dests_ref, bf16[4,512,512]{2,1,0:T(8,128)(2,1)} %bitcast.150, bf16[3,512,128]{2,1,0:T(8,128)(2,1)} %pad_maximum_fusion.1.back_ref), custom_call_target="tpu_custom_call" | custom-call | tf_op jit(solution)/shard_map/pallas_call | solution.py:70
  139.0 2.0 %collective-permute-done.15 = f32[512,128]{1,0:T(8,128)S(1)} collective-permute-done((f32[512,128]{1,0:T(8,128)S(1)}, f32[512,128]{1,0:T(8,128)S(1)}, u32[]{:S(2)}, u32[]{:S(2)}) %collective-permute-start.15) | collective-permute-done | bytes 262176 | tf_op jit(solution)/shard_map/ppermute | solution.py:99
  141.0 0.7 fusion.54
  141.7 2.9 %shard_map.106 = bf16[4,512,128]{2,1,0:T(8,128)(2,1)} custom-call(s32[4]{0:T(128)} %bitcast.160, s32[4]{0:T(128)} %get-tuple-element.16.dests_ref, bf16[4,512,512]{2,1,0:T(8,128)(2,1)} %bitcast.151, bf16[512,128]{1,0:T(8,128)(2,1)} %get-tuple-element.14.back_ref, f32[4,512,128]{2,1,0:T(8,128)} %shard_map.105.upper_ref), custom_call_target="tpu_custom_call" | custom-call | tf_op jit(solution)/shard_map/pallas_call | solution.py:79
  144.6 1.1 slice_bitcast_fusion.19
  145.7 2.8 %collective-permute-start.28 = (bf16[512,128]{1,0:T(8,128)(2,1)S(1)}, bf16[512,128]{1,0:T(8,128)(2,1)S(1)}, u32[]{:S(2)}, u32[]{:S(2)}) collective-permute-start(bf16[512,128]{1,0:T(8,128)(2,1)S(1)} %get-tuple-element.19), channel_id=1, source_target_pairs={{0,1},{1,2},{2,3},{3,0},{4,5},{5,6},{6,7},{7,4},{8,9},{9,10},{10,1... | collective-permute-start | bytes 393224 | tf_op jit(solution)/shard_map/ppermute | solution.py:89
  148.5 2.8 %collective-permute-start.27 = (bf16[512,128]{1,0:T(8,128)(2,1)S(1)}, bf16[512,128]{1,0:T(8,128)(2,1)S(1)}, u32[]{:S(2)}, u32[]{:S(2)}) collective-permute-start(bf16[512,128]{1,0:T(8,128)(2,1)S(1)} %get-tuple-element.20), channel_id=1, source_target_pairs={{0,2},{1,3},{2,0},{3,1},{4,6},{5,7},{6,4},{7,5},{8,10},{9,11},{10,... | collective-permute-start | bytes 393224 | tf_op jit(solution)/shard_map/ppermute | solution.py:89
  151.3 0.7 pad_maximum_fusion.3
  151.9 2.3 %collective-permute-done.28 = bf16[512,128]{1,0:T(8,128)(2,1)S(1)} collective-permute-done((bf16[512,128]{1,0:T(8,128)(2,1)S(1)}, bf16[512,128]{1,0:T(8,128)(2,1)S(1)}, u32[]{:S(2)}, u32[]{:S(2)}) %collective-permute-start.28) | collective-permute-done | bytes 131104 | tf_op jit(solution)/shard_map/ppermute | solution.py:89
  154.2 1.4 collective-permute-done.27
  155.7 1.2 convolution_bitcast_fusion
  156.8 0.8 copy.16
  (55 shorter events, 4.8 us)
Async XLA Ops:
  7.2 4.8 %copy-start = (bf16[1,512,512]{2,1,0:T(8,128)(2,1)S(1)}, bf16[1,512,512]{2,1,0:T(8,128)(2,1)}, u32[]{:S(2)}) copy-start(bf16[1,512,512]{2,1,0:T(8,128)(2,1)} %param.10) | copy-start | bytes 1572868
  7.2 9.3 %copy-start.4 = (s32[1,4]{1,0:T(1,128)S(1)}, s32[1,4]{1,0:T(1,128)}, u32[]{:S(2)}) copy-start(s32[1,4]{1,0:T(1,128)} %param.13) | copy-start | bytes 52
  7.2 63.2 %all-gather.2.cloned.1.call-start = ((), (), s32[]{:S(2)}) async-start(), calls=%async_computation | async-start | bytes 2359296 | tf_op jit(solution)/shard_map/all_gather | solution.py:157
  13.2 6.3 %collective-permute-start.2 = (bf16[512,128]{1,0:T(8,128)(2,1)S(1)}, bf16[512,128]{1,0:T(8,128)(2,1)S(1)}, u32[]{:S(2)}, u32[]{:S(2)}) collective-permute-start(bf16[512,128]{1,0:T(8,128)(2,1)S(1)} %convolution_convert_fusion.4), channel_id=1, source_target_pairs={{0,3},{1,0},{2,1},{3,2},{4,7},{5,4},{6,5},{7,6},{8,11},{9,8},{10,9... | collective-permute-start | bytes 393224 | tf_op jit(solution)/shard_map/ppermute | solution.py:89
  15.6 7.5 %collective-permute-start.1 = (bf16[512,128]{1,0:T(8,128)(2,1)S(1)}, bf16[512,128]{1,0:T(8,128)(2,1)S(1)}, u32[]{:S(2)}, u32[]{:S(2)}) collective-permute-start(bf16[512,128]{1,0:T(8,128)(2,1)S(1)} %convolution_convert_fusion.4), channel_id=1, source_target_pairs={{0,2},{1,3},{2,0},{3,1},{4,6},{5,7},{6,4},{7,5},{8,10},{9,11},{10,... | collective-permute-start | bytes 393224 | tf_op jit(solution)/shard_map/ppermute | solution.py:89
  16.3 6.9 %collective-permute-start = (bf16[512,128]{1,0:T(8,128)(2,1)S(1)}, bf16[512,128]{1,0:T(8,128)(2,1)S(1)}, u32[]{:S(2)}, u32[]{:S(2)}) collective-permute-start(bf16[512,128]{1,0:T(8,128)(2,1)S(1)} %convolution_convert_fusion.4), channel_id=1, source_target_pairs={{0,1},{1,2},{2,3},{3,0},{4,5},{5,6},{6,7},{7,4},{8,9},{9,10},{10,1... | collective-permute-start | bytes 393224 | tf_op jit(solution)/shard_map/ppermute | solution.py:89
  28.6 7.7 %collective-permute-start.3 = (bf16[2,512,128]{2,1,0:T(8,128)(2,1)S(1)}, bf16[2,512,128]{2,1,0:T(8,128)(2,1)S(1)}, u32[]{:S(2)}, u32[]{:S(2)}) collective-permute-start(bf16[2,512,128]{2,1,0:T(8,128)(2,1)S(1)} %dynamic-slice_bitcast_fusion), channel_id=1, source_target_pairs={{0,2},{1,3},{2,0},{3,1},{4,6},{5,7},{6,4},{7,5},{8,10},{9,11},{10,... | collective-permute-start | bytes 786440 | tf_op jit(solution)/shard_map/ppermute | solution.py:93
  36.3 1.4 collective-permute-start.4
  37.8 7.1 %collective-permute-start.5 = (bf16[512,128]{1,0:T(8,128)(2,1)S(1)}, bf16[512,128]{1,0:T(8,128)(2,1)S(1)}, u32[]{:S(2)}, u32[]{:S(2)}) collective-permute-start(bf16[512,128]{1,0:T(8,128)(2,1)S(1)} %fusion.22), channel_id=1, source_target_pairs={{0,4},{4,0},{8,12},{12,8},{16,20},{20,16},{24,28},{28,24},{1,5},{5... | collective-permute-start | bytes 393224 | tf_op jit(solution)/shard_map/ppermute | solution.py:93
  44.9 11.7 %collective-permute-start.6 = (bf16[512,128]{1,0:T(8,128)(2,1)S(1)}, bf16[512,128]{1,0:T(8,128)(2,1)S(1)}, u32[]{:S(2)}, u32[]{:S(2)}) collective-permute-start(bf16[512,128]{1,0:T(8,128)(2,1)S(1)} %add_convert_fusion.2), channel_id=1, source_target_pairs={{0,8},{4,12},{8,0},{12,4},{16,24},{20,28},{24,16},{28,20},{1,9},{5... | collective-permute-start | bytes 393224 | tf_op jit(solution)/shard_map/ppermute | solution.py:93
  56.7 13.5 %collective-permute-start.7 = (bf16[512,128]{1,0:T(8,128)(2,1)S(1)}, bf16[512,128]{1,0:T(8,128)(2,1)S(1)}, u32[]{:S(2)}, u32[]{:S(2)}) collective-permute-start(bf16[512,128]{1,0:T(8,128)(2,1)S(1)} %add_convert_fusion.1), channel_id=1, source_target_pairs={{0,16},{4,20},{8,24},{12,28},{16,0},{20,4},{24,8},{28,12},{1,17},{... | collective-permute-start | bytes 393224 | tf_op jit(solution)/shard_map/ppermute | solution.py:93
  70.4 6.9 %copy-start.1 = (bf16[4,512,512]{2,1,0:T(8,128)(2,1)S(1)}, bf16[4,512,512]{2,1,0:T(8,128)(2,1)}, u32[]{:S(2)}) copy-start(bf16[4,512,512]{2,1,0:T(8,128)(2,1)} %all-gather.2.cloned.1.call-done) | copy-start | bytes 6291460
  73.9 3.5 %collective-permute-start.8 = (f32[3,512,128]{2,1,0:T(8,128)S(1)}, f32[3,512,128]{2,1,0:T(8,128)S(1)}, u32[]{:S(2)}, u32[]{:S(2)}) collective-permute-start(f32[3,512,128]{2,1,0:T(8,128)S(1)} %fusion.42), channel_id=1, source_target_pairs={{0,1},{4,5},{8,9},{12,13},{16,17},{20,21},{24,25},{28,29}} | collective-permute-start | bytes 2359304 | tf_op jit(solution)/shard_map/ppermute | solution.py:184
  77.7 1.8 %copy-start.2 = (bf16[512,128]{1,0:T(8,128)(2,1)}, bf16[512,128]{1,0:T(8,128)(2,1)S(1)}, u32[]{:S(2)}) copy-start(bf16[512,128]{1,0:T(8,128)(2,1)S(1)} %convolution_convert_fusion.2) | copy-start | bytes 393220
  78.1 0.7 collective-permute-start.9
  79.5 1.4 collective-permute-start.10
  83.1 0.7 collective-permute-start.11
  84.2 30.8 %copy-start.3 = (bf16[512,128]{1,0:T(8,128)(2,1)S(1)}, bf16[512,128]{1,0:T(8,128)(2,1)}, u32[]{:S(2)}) copy-start(bf16[512,128]{1,0:T(8,128)(2,1)} %copy-done.2) | copy-start | bytes 393220
  85.5 29.5 %collective-permute-start.12 = (f32[2,512,128]{2,1,0:T(8,128)}, f32[2,512,128]{2,1,0:T(8,128)}, u32[]{:S(2)}, u32[]{:S(2)}) collective-permute-start(f32[2,512,128]{2,1,0:T(8,128)} %slice_add_fusion), channel_id=1, source_target_pairs={{2,1},{6,5},{10,9},{14,13},{18,17},{22,21},{26,25},{30,29}} | collective-permute-start | bytes 1572872 | tf_op jit(solution)/shard_map/ppermute | solution.py:197
  87.0 4.0 %collective-permute-start.25 = (f32[512,128]{1,0:T(8,128)S(1)}, f32[512,128]{1,0:T(8,128)}, u32[]{:S(2)}, u32[]{:S(2)}) collective-permute-start(f32[512,128]{1,0:T(8,128)S(1)} %fusion), channel_id=1, source_target_pairs={{3,2},{7,6},{11,10},{15,14},{19,18},{23,22},{27,26},{31,30}} | collective-permute-start | bytes 786440 | tf_op jit(solution)/shard_map/ppermute | solution.py:99
  88.3 22.8 %collective-permute-start.23 = (f32[512,128]{1,0:T(8,128)S(1)}, f32[512,128]{1,0:T(8,128)}, u32[]{:S(2)}, u32[]{:S(2)}) collective-permute-start(f32[512,128]{1,0:T(8,128)S(1)} %fusion), channel_id=1, source_target_pairs={{3,0},{7,4},{11,8},{15,12},{19,16},{23,20},{27,24},{31,28}} | collective-permute-start | bytes 786440 | tf_op jit(solution)/shard_map/ppermute | solution.py:99
  89.6 21.5 %collective-permute-start.24 = (f32[512,128]{1,0:T(8,128)S(1)}, f32[512,128]{1,0:T(8,128)}, u32[]{:S(2)}, u32[]{:S(2)}) collective-permute-start(f32[512,128]{1,0:T(8,128)S(1)} %fusion), channel_id=1, source_target_pairs={{3,1},{7,5},{11,9},{15,13},{19,17},{23,21},{27,25},{31,29}} | collective-permute-start | bytes 786440 | tf_op jit(solution)/shard_map/ppermute | solution.py:99
  112.3 6.6 %collective-permute-start.22 = (f32[512,128]{1,0:T(8,128)S(1)}, f32[512,128]{1,0:T(8,128)S(1)}, u32[]{:S(2)}, u32[]{:S(2)}) collective-permute-start(f32[512,128]{1,0:T(8,128)S(1)} %fusion.20), channel_id=1, source_target_pairs={{2,1},{6,5},{10,9},{14,13},{18,17},{22,21},{26,25},{30,29}} | collective-permute-start | bytes 786440 | tf_op jit(solution)/shard_map/ppermute | solution.py:99
  113.0 5.9 %collective-permute-start.20 = (f32[512,128]{1,0:T(8,128)S(1)}, f32[512,128]{1,0:T(8,128)S(1)}, u32[]{:S(2)}, u32[]{:S(2)}) collective-permute-start(f32[512,128]{1,0:T(8,128)S(1)} %fusion.20), channel_id=1, source_target_pairs={{2,3},{6,7},{10,11},{14,15},{18,19},{22,23},{26,27},{30,31}} | collective-permute-start | bytes 786440 | tf_op jit(solution)/shard_map/ppermute | solution.py:99
  113.7 11.9 %collective-permute-start.21 = (f32[512,128]{1,0:T(8,128)S(1)}, f32[512,128]{1,0:T(8,128)S(1)}, u32[]{:S(2)}, u32[]{:S(2)}) collective-permute-start(f32[512,128]{1,0:T(8,128)S(1)} %fusion.20), channel_id=1, source_target_pairs={{2,0},{6,4},{10,8},{14,12},{18,16},{22,20},{26,24},{30,28}} | collective-permute-start | bytes 786440 | tf_op jit(solution)/shard_map/ppermute | solution.py:99
  117.6 10.8 %collective-permute-start.13 = (f32[1,512,128]{2,1,0:T(8,128)S(1)}, f32[1,512,128]{2,1,0:T(8,128)S(1)}, u32[]{:S(2)}, u32[]{:S(2)}) collective-permute-start(f32[1,512,128]{2,1,0:T(8,128)S(1)} %slice_add_fusion.2), channel_id=1, source_target_pairs={{1,0},{5,4},{9,8},{13,12},{17,16},{21,20},{25,24},{29,28}} | collective-permute-start | bytes 786440 | tf_op jit(solution)/shard_map/ppermute | solution.py:197
  125.7 8.1 %collective-permute-start.19 = (f32[512,128]{1,0:T(8,128)S(1)}, f32[512,128]{1,0:T(8,128)S(1)}, u32[]{:S(2)}, u32[]{:S(2)}) collective-permute-start(f32[512,128]{1,0:T(8,128)S(1)} %fusion.19), channel_id=1, source_target_pairs={{1,0},{5,4},{9,8},{13,12},{17,16},{21,20},{25,24},{29,28}} | collective-permute-start | bytes 786440 | tf_op jit(solution)/shard_map/ppermute | solution.py:99
  127.0 8.1 %collective-permute-start.17 = (f32[512,128]{1,0:T(8,128)S(1)}, f32[512,128]{1,0:T(8,128)S(1)}, u32[]{:S(2)}, u32[]{:S(2)}) collective-permute-start(f32[512,128]{1,0:T(8,128)S(1)} %fusion.19), channel_id=1, source_target_pairs={{1,2},{5,6},{9,10},{13,14},{17,18},{21,22},{25,26},{29,30}} | collective-permute-start | bytes 786440 | tf_op jit(solution)/shard_map/ppermute | solution.py:99
  127.7 7.4 %collective-permute-start.18 = (f32[512,128]{1,0:T(8,128)S(1)}, f32[512,128]{1,0:T(8,128)S(1)}, u32[]{:S(2)}, u32[]{:S(2)}) collective-permute-start(f32[512,128]{1,0:T(8,128)S(1)} %fusion.19), channel_id=1, source_target_pairs={{1,3},{5,7},{9,11},{13,15},{17,19},{21,23},{25,27},{29,31}} | collective-permute-start | bytes 786440 | tf_op jit(solution)/shard_map/ppermute | solution.py:99
  128.7 10.2 %collective-permute-start.16 = (f32[512,128]{1,0:T(8,128)S(1)}, f32[512,128]{1,0:T(8,128)S(1)}, u32[]{:S(2)}, u32[]{:S(2)}) collective-permute-start(f32[512,128]{1,0:T(8,128)S(1)} %fusion.21), channel_id=1, source_target_pairs={{0,3},{4,7},{8,11},{12,15},{16,19},{20,23},{24,27},{28,31}} | collective-permute-start | bytes 786440 | tf_op jit(solution)/shard_map/ppermute | solution.py:99
  130.0 8.9 %collective-permute-start.14 = (f32[512,128]{1,0:T(8,128)S(1)}, f32[512,128]{1,0:T(8,128)S(1)}, u32[]{:S(2)}, u32[]{:S(2)}) collective-permute-start(f32[512,128]{1,0:T(8,128)S(1)} %fusion.21), channel_id=1, source_target_pairs={{0,1},{4,5},{8,9},{12,13},{16,17},{20,21},{24,25},{28,29}} | collective-permute-start | bytes 786440 | tf_op jit(solution)/shard_map/ppermute | solution.py:99
  133.7 7.3 %collective-permute-start.15 = (f32[512,128]{1,0:T(8,128)S(1)}, f32[512,128]{1,0:T(8,128)S(1)}, u32[]{:S(2)}, u32[]{:S(2)}) collective-permute-start(f32[512,128]{1,0:T(8,128)S(1)} %fusion.21), channel_id=1, source_target_pairs={{0,2},{4,6},{8,10},{12,14},{16,18},{20,22},{24,26},{28,30}} | collective-permute-start | bytes 786440 | tf_op jit(solution)/shard_map/ppermute | solution.py:99
  145.7 8.5 %collective-permute-start.28 = (bf16[512,128]{1,0:T(8,128)(2,1)S(1)}, bf16[512,128]{1,0:T(8,128)(2,1)S(1)}, u32[]{:S(2)}, u32[]{:S(2)}) collective-permute-start(bf16[512,128]{1,0:T(8,128)(2,1)S(1)} %get-tuple-element.19), channel_id=1, source_target_pairs={{0,1},{1,2},{2,3},{3,0},{4,5},{5,6},{6,7},{7,4},{8,9},{9,10},{10,1... | collective-permute-start | bytes 393224 | tf_op jit(solution)/shard_map/ppermute | solution.py:89
  148.5 7.1 %collective-permute-start.27 = (bf16[512,128]{1,0:T(8,128)(2,1)S(1)}, bf16[512,128]{1,0:T(8,128)(2,1)S(1)}, u32[]{:S(2)}, u32[]{:S(2)}) collective-permute-start(bf16[512,128]{1,0:T(8,128)(2,1)S(1)} %get-tuple-element.20), channel_id=1, source_target_pairs={{0,2},{1,3},{2,0},{3,1},{4,6},{5,7},{6,4},{7,5},{8,10},{9,11},{10,... | collective-permute-start | bytes 393224 | tf_op jit(solution)/shard_map/ppermute | solution.py:89
  151.2 4.4 %collective-permute-start.26 = (bf16[512,128]{1,0:T(8,128)(2,1)S(1)}, bf16[512,128]{1,0:T(8,128)(2,1)S(1)}, u32[]{:S(2)}, u32[]{:S(2)}) collective-permute-start(bf16[512,128]{1,0:T(8,128)(2,1)S(1)} %get-tuple-element.18), channel_id=1, source_target_pairs={{0,3},{1,0},{2,1},{3,2},{4,7},{5,4},{6,5},{7,6},{8,11},{9,8},{10,9... | collective-permute-start | bytes 393224 | tf_op jit(solution)/shard_map/ppermute | solution.py:89
Sparse Core Ops, SparseCore 0:
  12.1 58.3 all-gather.1

commit v7 on v5

--- a/solution.py
+++ b/solution.py
@@ -83,12 +83,33 @@
     return t * (t - 1) // 2 + u
 
 
+def holdings(levels):
+    hold = [[] for _ in range(levels)]
+    for t in range(1, levels):
+        for u in range(t):
+            keeper = t if (levels > 2 and t == levels - 1 and u == 0) else u
+            hold[keeper].append((t, u))
+    return hold
+
+
 def tile_table(levels):
-    table = np.zeros((levels, levels - 1), np.int32)
+    hold = holdings(levels)
+    width = max(len(h) for h in hold)
+    table = np.zeros((levels, width), np.int32)
     for c in range(levels):
-        for j in range(levels - 1):
-            table[c, j] = pair_index(c, j) if j < c else pair_index(j + 1, c)
+        for j, (t, u) in enumerate(hold[c]):
+            table[c, j] = pair_index(t, u)
     return table
+
+
+def plus(a, b):
+    return b if a is None else a + b
+
+
+def held_slice(mats, positions):
+    if positions == list(range(positions[0], positions[0] + len(positions))):
+        return mats[1 + positions[0] : 1 + positions[0] + len(positions)]
+    return jnp.stack([mats[1 + p] for p in positions])
 
 
 def summed_chunks(x, peers, rows_n, me):
@@ -154,35 +175,70 @@
         level_sum = gathered_chunks(part, peers, me).reshape(levels, -1, width)[owned]
     rhs_level = -level_sum.astype(jnp.float32)
 
+    hold = holdings(levels)
     top_forward = [None] * levels
-    pushed = None
+    pushed = {}
+    direct = {}
     for level in range(levels):
         residue = rhs_level
         if level > 0:
-            pushed = lax.ppermute(pushed, "col", [(level - 1, level)])
-            residue = residue - pushed[0]
+            keys = [k for k in range(level, levels) if pushed.get(k) is not None]
+            message = lax.ppermute(jnp.stack([pushed[k] for k in keys]), "col", [(level - 1, level)])
+            pushed = {k: message[i] for i, k in enumerate(keys)}
+            if pushed.get(level) is not None:
+                residue = residue - pushed[level]
+        for j, (t, u) in enumerate(hold[level]):
+            if t == level:
+                residue = residue - jnp.dot(mats[1 + j], direct[(t, u)], preferred_element_type=jnp.float32)
         solved = jnp.dot(inv, residue.astype(jnp.bfloat16), preferred_element_type=jnp.float32)
         top_forward[level] = solved.astype(jnp.bfloat16)
-        if level < levels - 1:
+        for k in range(level + 1, levels):
+            if (k, level) in hold[k]:
+                direct[(k, level)] = lax.ppermute(top_forward[level], "col", [(level, k)])
+        positions = [j for j, (t, u) in enumerate(hold[level]) if u == level]
+        if positions and level < levels - 1:
             later = jnp.einsum(
-                "kab,bc->kac", mats[level + 1 : levels], top_forward[level], preferred_element_type=jnp.float32
+                "kab,bc->kac", held_slice(mats, positions), top_forward[level], preferred_element_type=jnp.float32
             )
-            pushed = later if level == 0 else pushed[1:] + later
+            for i, j in enumerate(positions):
+                k = hold[level][j][0]
+                pushed[k] = plus(pushed.get(k), later[i])
     own_solution = None
+    carried = {}
     for level in reversed(range(levels)):
         update = top_forward[level].astype(jnp.float32)
         if level < levels - 1:
-            pushed = lax.ppermute(pushed, "col", [(level + 1, level)])
-            update = update - pushed[level]
+            keys = sorted(carried)
+            message = lax.ppermute(jnp.stack([carried[k] for k in keys]), "col", [(level + 1, level)])
+            carried = {k: message[i] for i, k in enumerate(keys)}
+            if carried.get(("q", level)) is not None:
+                update = update - carried.pop(("q", level))
+        for j, (t, u) in enumerate(hold[level]):
+            if u == level:
+                update = update - lax.dot_general(
+                    mats[1 + j],
+                    carried[("x", t)].astype(jnp.bfloat16),
+                    (((0,), (0,)), ((), ())),
+                    preferred_element_type=jnp.float32,
+                )
         solved = lax.dot_general(
             inv, update.astype(jnp.bfloat16), (((0,), (0,)), ((), ())), preferred_element_type=jnp.float32
         )
         own_solution = solved if own_solution is None else jnp.where(me == level, solved, own_solution)
-        if level > 0:
-            earlier = jnp.einsum(
-                "uab,ac->ubc", mats[1 : level + 1], solved.astype(jnp.bfloat16), preferred_element_type=jnp.float32
-            )
-            pushed = earlier if level == levels - 1 else pushed[:level] + earlier
+        if level == 0:
+            break
+        for j, (t, u) in enumerate(hold[level]):
+            if t == level:
+                term = lax.dot_general(
+                    mats[1 + j],
+                    solved.astype(jnp.bfloat16),
+                    (((0,), (0,)), ((), ())),
+                    preferred_element_type=jnp.float32,
+                )
+                carried[("q", u)] = plus(carried.get(("q", u)), term)
+        carried[("x", level)] = solved
+        below = {t for c in range(level) for (t, u) in hold[c] if u == c}
+        carried = {k: v for k, v in carried.items() if k[0] == "q" or k[1] in below}
     solutions = gathered_chunks(own_solution, peers, me)[:levels]
     top_slices = [lax.dynamic_slice_in_dim(solutions[t], position * share, share, 0) for t in range(levels)]
     top_back = [solutions[t].astype(jnp.bfloat16) for t in range(levels)]

time: 153 us -> 157 us (1.026)
  waiting for transfers between devices: 82.1 us -> 77.6 us
  local copies, waits for them, and re-layouts: 5.43 us -> 8.65 us
  starting transfers between devices: 20.9 us -> 23.3 us
  other arithmetic: 9.12 us -> 11.2 us
    ppermute x5, waiting for transfers between devices: 38 us -> 29.5 us  [swapped(): return lax.ppermute(x, axis, [(i, i ^ bit) for i in range(size)])]
    ppermute x5, starting transfers between devices: 4.41 us -> 10.4 us  [swapped(): return lax.ppermute(x, axis, [(i, i ^ bit) for i in range(size)])]
    ppermute x9, starting transfers between devices: 10.1 us -> 5.89 us  [shifted(): return lax.ppermute(x, axis, [(i, (i + shift) % size) for i in range(size)])]
    ppermute x6 -> x7, waiting for transfers between devices: 24.8 us -> 28.2 us  [the longest x3 22.8 us: local(): lax.ppermute(jnp.stack([carried[k] for k in keys]), 'col', [(level + 1, l...]
    unnamed x13 -> x15, local copies, waits for them, and re-layouts: 0.88 us -> 3.23 us
    another operation x0 -> x5, other arithmetic: none -> 2.16 us  [the longest x3 2.07 us: local(): jnp.stack([carried[k] for k in keys])]
    ppermute x6 -> x7, starting transfers between devices: 6.34 us -> 6.96 us  [the longest x3 2.98 us: local(): lax.ppermute(jnp.stack([pushed[k] for k in keys]), 'col', [(level - 1, le...]
    dot_general x6 -> x7, matrix products: 4.88 us -> 5.15 us  [the longest x3 2.42 us: local(): jnp.einsum('kab,bc->kac', held_slice(mats, positions), top_forward[level]...]
  transfers between devices with their start and end apart: 21 -> 22, of which waited for: 15 -> 15; matrix products, arithmetic and copies ran while one was open for 4% -> 6% of each run, Pallas kernels for 2% -> 2%
where the time goes in v7:
time: 157 us
  waiting for transfers between devices  77.6 us (49%)
  starting transfers between devices  23.3 us (15%)
  matrix products  15.3 us (10%)
  between operations  14.4 us (9%)
  other arithmetic  11.2 us (7%)
  local copies, waits for them, and re-layouts  8.65 us (6%)
  Pallas kernels  6.07 us (4%)
    ppermute x5, waiting for transfers between devices, swapped(): return lax.ppermute(x, axis, [(i, i ^ bit) for i in range(size)])  29.5 us
    ppermute x3, waiting for transfers between devices, local(): lax.ppermute(jnp.stack([carried[k] for k in keys]), 'col', [(level + 1, l...  22.8 us
    ppermute x9, waiting for transfers between devices, shifted(): return lax.ppermute(x, axis, [(i, (i + shift) % size) for i in range(size)])  18.5 us
    ppermute x5, starting transfers between devices, swapped(): return lax.ppermute(x, axis, [(i, i ^ bit) for i in range(size)])  10.4 us
    ppermute x9, starting transfers between devices, shifted(): return lax.ppermute(x, axis, [(i, (i + shift) % size) for i in range(size)])  5.89 us
    dot_general x4, matrix products, local(): lax.dot_general(inv, update.astype(jnp.bfloat16), (((0,), (0,)), ((), ())...  5.72 us
    ppermute x1, waiting for transfers between devices, local(): direct[k, level] = lax.ppermute(top_forward[level], 'col', [(level, k)])  3.86 us
    unnamed x15, local copies, waits for them, and re-layouts  3.23 us
  transfers between devices with their start and end apart: 22, of which 15 were waited for; matrix products, arithmetic and copies ran while one was open for 6% of the time, Pallas kernels for 2%

profile of v7, /device:TPU:0, one launch (start us, length us, event | category | flops | bytes accessed | tf_op | source)
XLA Modules:
  0.0 156.5 jit_solution(9680454567663405386)
XLA Ops:
  7.2 1.0 copy-done
  8.2 1.2 convolution_convert_fusion.4
  9.4 2.5 %collective-permute-start.2 = (bf16[512,128]{1,0:T(8,128)(2,1)S(1)}, bf16[512,128]{1,0:T(8,128)(2,1)S(1)}, u32[]{:S(2)}, u32[]{:S(2)}) collective-permute-start(bf16[512,128]{1,0:T(8,128)(2,1)S(1)} %convolution_convert_fusion.4), channel_id=1, source_target_pairs={{0,3},{1,0},{2,1},{3,2},{4,7},{5,4},{6,5},{7,6},{8,11},{9,8},{10,9... | collective-permute-start | bytes 393224 | tf_op jit(solution)/shard_map/ppermute | solution.py:67
  11.9 0.6 collective-permute-start.1
  12.7 0.7 fusion.57
  13.4 0.7 compare_and_fusion
  14.1 0.9 constant_dynamic-slice_fusion.6
  14.9 1.5 gather_fusion
  16.6 0.7 pad_maximum_fusion.7
  17.3 0.5 and_select_fusion.2
  17.8 0.8 iota_reduce_fusion
  18.6 0.6 pad_add_fusion.fold_ref
  19.4 0.9 pad_maximum_fusion.3.panels_ref
  20.3 3.2 %shard_map.104 = f32[4,512,128]{2,1,0:T(8,128)} custom-call(s32[4]{0:T(128)} %bitcast.172, s32[4]{0:T(128)} %get-tuple-element.3.picks_ref, s32[2]{0:T(128)} %pad_add_fusion.fold_ref, bf16[4,512,512]{2,1,0:T(8,128)(2,1)} %bitcast.157, bf16[4,512,128]{2,1,0:T(8,128)(2,1)} %pad_maximum_fusion.3.panels_ref, bf16[4,64,128]{2,1,0:T(8,128)(2,1)} %rhs_ref.1), custom_call_target="tpu_custom_call" | custom-call | tf_op jit(solution)/shard_map/pallas_call | solution.py:32
  23.5 1.3 convert_element_type.169
  24.8 1.7 %collective-permute-start.3 = (bf16[2,512,128]{2,1,0:T(8,128)(2,1)S(1)}, bf16[2,512,128]{2,1,0:T(8,128)(2,1)S(1)}, u32[]{:S(2)}, u32[]{:S(2)}) collective-permute-start(bf16[2,512,128]{2,1,0:T(8,128)(2,1)S(1)} %dynamic-slice_bitcast_fusion), channel_id=1, source_target_pairs={{0,2},{1,3},{2,0},{3,1},{4,6},{5,7},{6,4},{7,5},{8,10},{9,11},{10,... | collective-permute-start | bytes 786440 | tf_op jit(solution)/shard_map/ppermute | solution.py:71
  26.5 7.2 %collective-permute-done.3 = bf16[2,512,128]{2,1,0:T(8,128)(2,1)S(1)} collective-permute-done((bf16[2,512,128]{2,1,0:T(8,128)(2,1)S(1)}, bf16[2,512,128]{2,1,0:T(8,128)(2,1)S(1)}, u32[]{:S(2)}, u32[]{:S(2)}) %collective-permute-start.3) | collective-permute-done | bytes 262176 | tf_op jit(solution)/shard_map/ppermute | solution.py:71
  34.0 1.1 collective-permute-done.4
  35.2 1.7 %collective-permute-start.5 = (bf16[512,128]{1,0:T(8,128)(2,1)S(1)}, bf16[512,128]{1,0:T(8,128)(2,1)S(1)}, u32[]{:S(2)}, u32[]{:S(2)}) collective-permute-start(bf16[512,128]{1,0:T(8,128)(2,1)S(1)} %fusion.30), channel_id=1, source_target_pairs={{0,4},{4,0},{8,12},{12,8},{16,20},{20,16},{24,28},{28,24},{1,5},{5... | collective-permute-start | bytes 393224 | tf_op jit(solution)/shard_map/ppermute | solution.py:71
  36.9 4.0 %collective-permute-done.5 = bf16[512,128]{1,0:T(8,128)(2,1)S(1)} collective-permute-done((bf16[512,128]{1,0:T(8,128)(2,1)S(1)}, bf16[512,128]{1,0:T(8,128)(2,1)S(1)}, u32[]{:S(2)}, u32[]{:S(2)}) %collective-permute-start.5) | collective-permute-done | bytes 131104 | tf_op jit(solution)/shard_map/ppermute | solution.py:71
  40.9 2.5 %collective-permute-start.6 = (bf16[512,128]{1,0:T(8,128)(2,1)S(1)}, bf16[512,128]{1,0:T(8,128)(2,1)S(1)}, u32[]{:S(2)}, u32[]{:S(2)}) collective-permute-start(bf16[512,128]{1,0:T(8,128)(2,1)S(1)} %add_convert_fusion.2), channel_id=1, source_target_pairs={{0,8},{4,12},{8,0},{12,4},{16,24},{20,28},{24,16},{28,20},{1,9},{5... | collective-permute-start | bytes 393224 | tf_op jit(solution)/shard_map/ppermute | solution.py:71
  43.4 5.4 %collective-permute-done.6 = bf16[512,128]{1,0:T(8,128)(2,1)S(1)} collective-permute-done((bf16[512,128]{1,0:T(8,128)(2,1)S(1)}, bf16[512,128]{1,0:T(8,128)(2,1)S(1)}, u32[]{:S(2)}, u32[]{:S(2)}) %collective-permute-start.6) | collective-permute-done | bytes 131104 | tf_op jit(solution)/shard_map/ppermute | solution.py:71
  48.9 4.2 %collective-permute-start.7 = (bf16[512,128]{1,0:T(8,128)(2,1)S(1)}, bf16[512,128]{1,0:T(8,128)(2,1)S(1)}, u32[]{:S(2)}, u32[]{:S(2)}) collective-permute-start(bf16[512,128]{1,0:T(8,128)(2,1)S(1)} %add_convert_fusion.1), channel_id=1, source_target_pairs={{0,16},{4,20},{8,24},{12,28},{16,0},{20,4},{24,8},{28,12},{1,17},{... | collective-permute-start | bytes 393224 | tf_op jit(solution)/shard_map/ppermute | solution.py:71
  53.1 11.8 %collective-permute-done.7 = bf16[512,128]{1,0:T(8,128)(2,1)S(1)} collective-permute-done((bf16[512,128]{1,0:T(8,128)(2,1)S(1)}, bf16[512,128]{1,0:T(8,128)(2,1)S(1)}, u32[]{:S(2)}, u32[]{:S(2)}) %collective-permute-start.7) | collective-permute-done | bytes 131104 | tf_op jit(solution)/shard_map/ppermute | solution.py:71
  64.9 1.5 all-gather.2.cloned.1.call-done
  66.4 1.5 convolution_convert_fusion.3
  67.9 1.7 %fusion.44 = f32[2,512,128]{2,1,0:T(8,128)S(1)} fusion(bf16[3,512,512]{2,1,0:T(8,128)(2,1)} %all-gather.2.cloned.1.call-done, bf16[512,128]{1,0:T(8,128)(2,1)S(1)} %convolution_convert_fusion.3), kind=kOutput, calls=%fused_computation.82 | convolution fusion | flops 134217728 | bytes 2228224 | tf_op jit(solution)/shard_map/kab,bc->kac/dot_general | solution.py:200
  69.6 1.6 %collective-permute-start.8 = (f32[2,512,128]{2,1,0:T(8,128)S(1)}, f32[2,512,128]{2,1,0:T(8,128)S(1)}, u32[]{:S(2)}, u32[]{:S(2)}) collective-permute-start(f32[2,512,128]{2,1,0:T(8,128)S(1)} %fusion.44), channel_id=1, source_target_pairs={{0,1},{4,5},{8,9},{12,13},{16,17},{20,21},{24,25},{28,29}} | collective-permute-start | bytes 1572872 | tf_op jit(solution)/shard_map/ppermute | solution.py:186
  71.2 1.5 collective-permute-done.8
  73.0 0.6 copy-done.5
  73.7 0.4 fusion.42
  74.2 0.7 collective-permute-start.9
  75.5 0.7 collective-permute-start.10
  76.2 1.3 collective-permute-start.11
  77.5 3.9 %collective-permute-done.11 = bf16[512,128]{1,0:T(8,128)(2,1)S(1)} collective-permute-done((bf16[512,128]{1,0:T(8,128)(2,1)S(1)}, bf16[512,128]{1,0:T(8,128)(2,1)S(1)}, u32[]{:S(2)}, u32[]{:S(2)}) %collective-permute-start.11) | collective-permute-done | bytes 131104 | tf_op jit(solution)/shard_map/ppermute | solution.py:197
  81.7 0.7 fusion.3
  82.4 0.3 convolution_bitcast_fusion.1
  82.8 0.7 collective-permute-start.12
  83.5 0.7 fusion.5
  84.4 0.7 collective-permute-start.13
  85.1 1.0 fusion.10
  86.2 0.8 fusion.64
  87.0 1.7 %fusion.4 = f32[512,128]{1,0:T(8,128)S(1)} fusion(f32[512,128]{1,0:T(8,128)} %fusion.10, bf16[512,128]{1,0:T(8,128)(2,1)} %copy-done.5, bf16[3,512,512]{2,1,0:T(8,128)(2,1)S(1)} %copy-done.1, f32[3,512,128]{2,1,0:T(8,128)S(1)} %collective-permute-done.13), kind=kOutput, calls=%fused_computation.17 | convolution fusion | flops 134479872 | bytes 1835008 | tf_op jit(solution)/shard_map/dot_general | solution.py:224
  88.8 2.0 %pad_maximum_fusion.2 = f32[3,512,128]{2,1,0:T(8,128)} fusion(f32[1,512,128]{2,1,0:T(8,128)} %get-tuple-element.19, f32[1,512,128]{2,1,0:T(8,128)S(1)} %bitcast.159, f32[1,512,128]{2,1,0:T(8,128)} %get-tuple-element.18), kind=kLoop, calls=%fused_computation.21 | loop fusion | flops 393216 | bytes 1572864 | tf_op jit(solution)/shard_map/stack | solution.py:212
  90.7 1.3 collective-permute-start.14
  92.0 22.8 %collective-permute-done.14 = f32[3,512,128]{2,1,0:T(8,128)S(1)} collective-permute-done((f32[3,512,128]{2,1,0:T(8,128)}, f32[3,512,128]{2,1,0:T(8,128)S(1)}, u32[]{:S(2)}, u32[]{:S(2)}) %collective-permute-start.14) | collective-permute-done | bytes 786464 | tf_op jit(solution)/shard_map/ppermute | solution.py:212
  114.9 0.7 copy-done.3
  115.6 1.0 fusion.9
  116.7 2.5 %convolution_select_fusion = f32[512,128]{1,0:T(8,128)} fusion(f32[512,128]{1,0:T(8,128)S(1)} %fusion.4, f32[512,128]{1,0:T(8,128)} %copy-done.2, f32[512,128]{1,0:T(8,128)S(1)} %fusion.3, bf16[3,512,512]{2,1,0:T(8,128)(2,1)S(1)} %copy-done.1, f32[512,128]{1,0:T(8,128)} %fusion.9, f32[3,512,128]{2,1,0:T(8,128)S(1)} %collective-permute-done.14, ...), kind=kOutput, calls=%fused_computation.3 | convolution fusion | flops 134742016 | bytes 2883587 | tf_op jit(solution)/shard_map/dot_general | solution.py:224
  119.2 1.8 %collective-permute-start.16 = (f32[512,128]{1,0:T(8,128)}, f32[512,128]{1,0:T(8,128)S(1)}, u32[]{:S(2)}, u32[]{:S(2)}) collective-permute-start(f32[512,128]{1,0:T(8,128)} %convolution_select_fusion), channel_id=1, source_target_pairs={{0,2},{1,3},{2,0},{3,1},{4,6},{5,7},{6,4},{7,5},{8,10},{9,11},{10,... | collective-permute-start | bytes 786440 | tf_op jit(solution)/shard_map/ppermute | solution.py:67
  121.0 5.2 %collective-permute-done.17 = f32[512,128]{1,0:T(8,128)S(1)} collective-permute-done((f32[512,128]{1,0:T(8,128)}, f32[512,128]{1,0:T(8,128)S(1)}, u32[]{:S(2)}, u32[]{:S(2)}) %collective-permute-start.17) | collective-permute-done | bytes 262176 | tf_op jit(solution)/shard_map/ppermute | solution.py:67
  126.2 7.5 %collective-permute-done.16 = f32[512,128]{1,0:T(8,128)S(1)} collective-permute-done((f32[512,128]{1,0:T(8,128)}, f32[512,128]{1,0:T(8,128)S(1)}, u32[]{:S(2)}, u32[]{:S(2)}) %collective-permute-start.16) | collective-permute-done | bytes 262176 | tf_op jit(solution)/shard_map/ppermute | solution.py:67
  133.7 1.0 pad_maximum_fusion
  134.8 0.8 scatter_fusion
  135.8 0.9 pad_maximum_fusion.6.back_ref
  136.7 2.9 %shard_map.105 = bf16[4,512,128]{2,1,0:T(8,128)(2,1)} custom-call(s32[4]{0:T(128)} %bitcast.173, s32[4]{0:T(128)} %get-tuple-element.8.dests_ref, bf16[4,512,512]{2,1,0:T(8,128)(2,1)} %bitcast.158, bf16[4,512,128]{2,1,0:T(8,128)(2,1)} %pad_maximum_fusion.6.back_ref), custom_call_target="tpu_custom_call" | custom-call | tf_op jit(solution)/shard_map/pallas_call | solution.py:57
  139.6 1.1 slice_bitcast_fusion.34
  140.8 0.5 collective-permute-start.20
  141.6 0.7 pad_maximum_fusion.8
  142.2 2.4 %collective-permute-done.18 = bf16[512,128]{1,0:T(8,128)(2,1)S(1)} collective-permute-done((bf16[512,128]{1,0:T(8,128)(2,1)S(1)}, bf16[512,128]{1,0:T(8,128)(2,1)S(1)}, u32[]{:S(2)}, u32[]{:S(2)}) %collective-permute-start.18) | collective-permute-done | bytes 131104 | tf_op jit(solution)/shard_map/ppermute | solution.py:67
  144.6 1.3 collective-permute-done.20
  145.9 1.7 %collective-permute-done.19 = bf16[512,128]{1,0:T(8,128)(2,1)S(1)} collective-permute-done((bf16[512,128]{1,0:T(8,128)(2,1)S(1)}, bf16[512,128]{1,0:T(8,128)(2,1)S(1)}, u32[]{:S(2)}, u32[]{:S(2)}) %collective-permute-start.19) | collective-permute-done | bytes 131104 | tf_op jit(solution)/shard_map/ppermute | solution.py:67
  147.6 1.2 convolution_bitcast_fusion
  148.8 0.8 copy.12
  (54 shorter events, 3.3 us)
Async XLA Ops:
  7.2 1.0 copy-start
  7.2 10.1 %copy-start.6 = (s32[1,4]{1,0:T(1,128)S(1)}, s32[1,4]{1,0:T(1,128)}, u32[]{:S(2)}) copy-start(s32[1,4]{1,0:T(1,128)} %param.13) | copy-start | bytes 52
  7.2 59.2 %all-gather.2.cloned.1.call-start = ((), (), s32[]{:S(2)}) async-start(), calls=%async_computation | async-start | bytes 1769472 | tf_op jit(solution)/shard_map/all_gather | solution.py:156
  9.4 9.7 %collective-permute-start.2 = (bf16[512,128]{1,0:T(8,128)(2,1)S(1)}, bf16[512,128]{1,0:T(8,128)(2,1)S(1)}, u32[]{:S(2)}, u32[]{:S(2)}) collective-permute-start(bf16[512,128]{1,0:T(8,128)(2,1)S(1)} %convolution_convert_fusion.4), channel_id=1, source_target_pairs={{0,3},{1,0},{2,1},{3,2},{4,7},{5,4},{6,5},{7,6},{8,11},{9,8},{10,9... | collective-permute-start | bytes 393224 | tf_op jit(solution)/shard_map/ppermute | solution.py:67
  11.9 7.5 %collective-permute-start.1 = (bf16[512,128]{1,0:T(8,128)(2,1)S(1)}, bf16[512,128]{1,0:T(8,128)(2,1)S(1)}, u32[]{:S(2)}, u32[]{:S(2)}) collective-permute-start(bf16[512,128]{1,0:T(8,128)(2,1)S(1)} %convolution_convert_fusion.4), channel_id=1, source_target_pairs={{0,2},{1,3},{2,0},{3,1},{4,6},{5,7},{6,4},{7,5},{8,10},{9,11},{10,... | collective-permute-start | bytes 393224 | tf_op jit(solution)/shard_map/ppermute | solution.py:67
  12.5 6.9 %collective-permute-start = (bf16[512,128]{1,0:T(8,128)(2,1)S(1)}, bf16[512,128]{1,0:T(8,128)(2,1)S(1)}, u32[]{:S(2)}, u32[]{:S(2)}) collective-permute-start(bf16[512,128]{1,0:T(8,128)(2,1)S(1)} %convolution_convert_fusion.4), channel_id=1, source_target_pairs={{0,1},{1,2},{2,3},{3,0},{4,5},{5,6},{6,7},{7,4},{8,9},{9,10},{10,1... | collective-permute-start | bytes 393224 | tf_op jit(solution)/shard_map/ppermute | solution.py:67
  24.8 8.9 %collective-permute-start.3 = (bf16[2,512,128]{2,1,0:T(8,128)(2,1)S(1)}, bf16[2,512,128]{2,1,0:T(8,128)(2,1)S(1)}, u32[]{:S(2)}, u32[]{:S(2)}) collective-permute-start(bf16[2,512,128]{2,1,0:T(8,128)(2,1)S(1)} %dynamic-slice_bitcast_fusion), channel_id=1, source_target_pairs={{0,2},{1,3},{2,0},{3,1},{4,6},{5,7},{6,4},{7,5},{8,10},{9,11},{10,... | collective-permute-start | bytes 786440 | tf_op jit(solution)/shard_map/ppermute | solution.py:71
  33.7 1.4 collective-permute-start.4
  35.2 5.7 %collective-permute-start.5 = (bf16[512,128]{1,0:T(8,128)(2,1)S(1)}, bf16[512,128]{1,0:T(8,128)(2,1)S(1)}, u32[]{:S(2)}, u32[]{:S(2)}) collective-permute-start(bf16[512,128]{1,0:T(8,128)(2,1)S(1)} %fusion.30), channel_id=1, source_target_pairs={{0,4},{4,0},{8,12},{12,8},{16,20},{20,16},{24,28},{28,24},{1,5},{5... | collective-permute-start | bytes 393224 | tf_op jit(solution)/shard_map/ppermute | solution.py:71
  40.9 7.9 %collective-permute-start.6 = (bf16[512,128]{1,0:T(8,128)(2,1)S(1)}, bf16[512,128]{1,0:T(8,128)(2,1)S(1)}, u32[]{:S(2)}, u32[]{:S(2)}) collective-permute-start(bf16[512,128]{1,0:T(8,128)(2,1)S(1)} %add_convert_fusion.2), channel_id=1, source_target_pairs={{0,8},{4,12},{8,0},{12,4},{16,24},{20,28},{24,16},{28,20},{1,9},{5... | collective-permute-start | bytes 393224 | tf_op jit(solution)/shard_map/ppermute | solution.py:71
  48.9 16.0 %collective-permute-start.7 = (bf16[512,128]{1,0:T(8,128)(2,1)S(1)}, bf16[512,128]{1,0:T(8,128)(2,1)S(1)}, u32[]{:S(2)}, u32[]{:S(2)}) collective-permute-start(bf16[512,128]{1,0:T(8,128)(2,1)S(1)} %add_convert_fusion.1), channel_id=1, source_target_pairs={{0,16},{4,20},{8,24},{12,28},{16,0},{20,4},{24,8},{28,12},{1,17},{... | collective-permute-start | bytes 393224 | tf_op jit(solution)/shard_map/ppermute | solution.py:71
  66.4 6.3 %copy-start.1 = (bf16[3,512,512]{2,1,0:T(8,128)(2,1)S(1)}, bf16[3,512,512]{2,1,0:T(8,128)(2,1)}, u32[]{:S(2)}) copy-start(bf16[3,512,512]{2,1,0:T(8,128)(2,1)} %all-gather.2.cloned.1.call-done) | copy-start | bytes 4718596
  67.9 8.3 %copy-start.4 = (bf16[512,128]{1,0:T(8,128)(2,1)}, bf16[512,128]{1,0:T(8,128)(2,1)S(1)}, u32[]{:S(2)}) copy-start(bf16[512,128]{1,0:T(8,128)(2,1)S(1)} %convolution_convert_fusion.3) | copy-start | bytes 393220
  69.6 3.1 %collective-permute-start.8 = (f32[2,512,128]{2,1,0:T(8,128)S(1)}, f32[2,512,128]{2,1,0:T(8,128)S(1)}, u32[]{:S(2)}, u32[]{:S(2)}) collective-permute-start(f32[2,512,128]{2,1,0:T(8,128)S(1)} %fusion.44), channel_id=1, source_target_pairs={{0,1},{4,5},{8,9},{12,13},{16,17},{20,21},{24,25},{28,29}} | collective-permute-start | bytes 1572872 | tf_op jit(solution)/shard_map/ppermute | solution.py:186
  73.0 0.7 copy-start.5
  74.2 0.7 collective-permute-start.9
  75.5 5.9 %collective-permute-start.10 = (f32[1,512,128]{2,1,0:T(8,128)S(1)}, f32[1,512,128]{2,1,0:T(8,128)S(1)}, u32[]{:S(2)}, u32[]{:S(2)}) collective-permute-start(f32[1,512,128]{2,1,0:T(8,128)S(1)} %slice_add_fusion), channel_id=1, source_target_pairs={{2,3},{6,7},{10,11},{14,15},{18,19},{22,23},{26,27},{30,31}} | collective-permute-start | bytes 786440 | tf_op jit(solution)/shard_map/ppermute | solution.py:186
  76.2 5.2 %collective-permute-start.11 = (bf16[512,128]{1,0:T(8,128)(2,1)S(1)}, bf16[512,128]{1,0:T(8,128)(2,1)S(1)}, u32[]{:S(2)}, u32[]{:S(2)}) collective-permute-start(bf16[512,128]{1,0:T(8,128)(2,1)S(1)} %convolution_convert_fusion.3), channel_id=1, source_target_pairs={{0,3},{4,7},{8,11},{12,15},{16,19},{20,23},{24,27},{28,31}} | collective-permute-start | bytes 393224 | tf_op jit(solution)/shard_map/ppermute | solution.py:197
  82.8 0.7 collective-permute-start.12
  84.3 1.9 %copy-start.2 = (f32[512,128]{1,0:T(8,128)}, f32[512,128]{1,0:T(8,128)S(1)}, u32[]{:S(2)}) copy-start(f32[512,128]{1,0:T(8,128)S(1)} %fusion.5) | copy-start | bytes 786436
  84.4 0.7 collective-permute-start.13
  90.7 24.1 %collective-permute-start.14 = (f32[3,512,128]{2,1,0:T(8,128)}, f32[3,512,128]{2,1,0:T(8,128)S(1)}, u32[]{:S(2)}, u32[]{:S(2)}) collective-permute-start(f32[3,512,128]{2,1,0:T(8,128)} %pad_maximum_fusion.2), channel_id=1, source_target_pairs={{1,0},{5,4},{9,8},{13,12},{17,16},{21,20},{25,24},{29,28}} | collective-permute-start | bytes 2359304 | tf_op jit(solution)/shard_map/ppermute | solution.py:212
  114.9 0.7 copy-start.3
  119.2 7.0 %collective-permute-start.17 = (f32[512,128]{1,0:T(8,128)}, f32[512,128]{1,0:T(8,128)S(1)}, u32[]{:S(2)}, u32[]{:S(2)}) collective-permute-start(f32[512,128]{1,0:T(8,128)} %convolution_select_fusion), channel_id=1, source_target_pairs={{0,3},{1,0},{2,1},{3,2},{4,7},{5,4},{6,5},{7,6},{8,11},{9,8},{10,9... | collective-permute-start | bytes 786440 | tf_op jit(solution)/shard_map/ppermute | solution.py:67
  119.2 14.5 %collective-permute-start.16 = (f32[512,128]{1,0:T(8,128)}, f32[512,128]{1,0:T(8,128)S(1)}, u32[]{:S(2)}, u32[]{:S(2)}) collective-permute-start(f32[512,128]{1,0:T(8,128)} %convolution_select_fusion), channel_id=1, source_target_pairs={{0,2},{1,3},{2,0},{3,1},{4,6},{5,7},{6,4},{7,5},{8,10},{9,11},{10,... | collective-permute-start | bytes 786440 | tf_op jit(solution)/shard_map/ppermute | solution.py:67
  120.9 12.8 %collective-permute-start.15 = (f32[512,128]{1,0:T(8,128)}, f32[512,128]{1,0:T(8,128)S(1)}, u32[]{:S(2)}, u32[]{:S(2)}) collective-permute-start(f32[512,128]{1,0:T(8,128)} %convolution_select_fusion), channel_id=1, source_target_pairs={{0,1},{1,2},{2,3},{3,0},{4,5},{5,6},{6,7},{7,4},{8,9},{9,10},{10,1... | collective-permute-start | bytes 786440 | tf_op jit(solution)/shard_map/ppermute | solution.py:67
  140.7 3.9 %collective-permute-start.18 = (bf16[512,128]{1,0:T(8,128)(2,1)S(1)}, bf16[512,128]{1,0:T(8,128)(2,1)S(1)}, u32[]{:S(2)}, u32[]{:S(2)}) collective-permute-start(bf16[512,128]{1,0:T(8,128)(2,1)S(1)} %get-tuple-element.20), channel_id=1, source_target_pairs={{0,3},{1,0},{2,1},{3,2},{4,7},{5,4},{6,5},{7,6},{8,11},{9,8},{10,9... | collective-permute-start | bytes 393224 | tf_op jit(solution)/shard_map/ppermute | solution.py:67
  140.8 5.2 %collective-permute-start.20 = (bf16[512,128]{1,0:T(8,128)(2,1)S(1)}, bf16[512,128]{1,0:T(8,128)(2,1)S(1)}, u32[]{:S(2)}, u32[]{:S(2)}) collective-permute-start(bf16[512,128]{1,0:T(8,128)(2,1)S(1)} %get-tuple-element.21), channel_id=1, source_target_pairs={{0,1},{1,2},{2,3},{3,0},{4,5},{5,6},{6,7},{7,4},{8,9},{9,10},{10,1... | collective-permute-start | bytes 393224 | tf_op jit(solution)/shard_map/ppermute | solution.py:67
  141.3 6.4 %collective-permute-start.19 = (bf16[512,128]{1,0:T(8,128)(2,1)S(1)}, bf16[512,128]{1,0:T(8,128)(2,1)S(1)}, u32[]{:S(2)}, u32[]{:S(2)}) collective-permute-start(bf16[512,128]{1,0:T(8,128)(2,1)S(1)} %get-tuple-element.22), channel_id=1, source_target_pairs={{0,2},{1,3},{2,0},{3,1},{4,6},{5,7},{6,4},{7,5},{8,10},{9,11},{10,... | collective-permute-start | bytes 393224 | tf_op jit(solution)/shard_map/ppermute | solution.py:67
Sparse Core Ops, SparseCore 0:
  17.4 48.9 all-gather.1

commit v8 on v5

--- a/solution.py
+++ b/solution.py
@@ -79,16 +79,117 @@
     return jnp.where(me == owner, x, got)
 
 
+def forward_hop(level, rhs, pushed_in, in_keys, direct, row_pos, mats, pushes, out_keys):
+    def kernel(*refs):
+        refs = list(refs)
+        rhs_ref = refs.pop(0)
+        pin_ref = refs.pop(0) if in_keys else None
+        direct_ref = refs.pop(0) if row_pos else None
+        mats_ref = refs.pop(0)
+        f_ref = refs.pop(0)
+        out_ref = refs.pop(0) if out_keys else None
+        residue = rhs_ref[...]
+        if level in in_keys:
+            residue = residue - pin_ref[in_keys.index(level)]
+        for pos in row_pos:
+            residue = residue - jnp.dot(mats_ref[pos], direct_ref[...], preferred_element_type=jnp.float32)
+        f = jnp.dot(mats_ref[0], residue.astype(jnp.bfloat16), preferred_element_type=jnp.float32)
+        f = f.astype(jnp.bfloat16)
+        f_ref[...] = f
+        for i, k in enumerate(out_keys):
+            value = pin_ref[in_keys.index(k)] if k in in_keys else None
+            if k in pushes:
+                value = plus(value, jnp.dot(mats_ref[pushes[k]], f, preferred_element_type=jnp.float32))
+            out_ref[i] = value
+
+    args = [rhs] + ([pushed_in] if in_keys else []) + ([direct] if row_pos else []) + [mats]
+    shape = rhs.shape
+    outs = [jax.ShapeDtypeStruct(shape, jnp.bfloat16)]
+    if out_keys:
+        outs.append(jax.ShapeDtypeStruct((len(out_keys),) + shape, jnp.float32))
+    result = pl.pallas_call(
+        kernel, out_shape=outs, in_specs=[VMEM] * len(args), out_specs=[VMEM] * len(outs)
+    )(*args)
+    return result[0], (result[1] if out_keys else None)
+
+
+def backward_hop(level, forward, carried_in, in_keys, mats, pulls, pushes, out_keys):
+    def kernel(*refs):
+        refs = list(refs)
+        f_ref = refs.pop(0)
+        cin_ref = refs.pop(0) if in_keys else None
+        mats_ref = refs.pop(0)
+        x_ref = refs.pop(0)
+        out_ref = refs.pop(0) if out_keys else None
+        update = f_ref[...].astype(jnp.float32)
+        if ("q", level) in in_keys:
+            update = update - cin_ref[in_keys.index(("q", level))]
+        for pos, k in pulls:
+            update = update - lax.dot_general(
+                mats_ref[pos],
+                cin_ref[in_keys.index(("x", k))].astype(jnp.bfloat16),
+                (((0,), (0,)), ((), ())),
+                preferred_element_type=jnp.float32,
+            )
+        x = lax.dot_general(
+            mats_ref[0], update.astype(jnp.bfloat16), (((0,), (0,)), ((), ())), preferred_element_type=jnp.float32
+        )
+        x_ref[...] = x
+        xb = x.astype(jnp.bfloat16)
+        for i, key in enumerate(out_keys):
+            if key == ("x", level):
+                out_ref[i] = x
+                continue
+            value = cin_ref[in_keys.index(key)] if key in in_keys else None
+            if key[0] == "q" and key[1] in pushes:
+                term = lax.dot_general(
+                    mats_ref[pushes[key[1]]], xb, (((0,), (0,)), ((), ())), preferred_element_type=jnp.float32
+                )
+                value = plus(value, term)
+            out_ref[i] = value
+
+    args = [forward] + ([carried_in] if in_keys else []) + [mats]
+    shape = forward.shape
+    outs = [jax.ShapeDtypeStruct(shape, jnp.float32)]
+    if out_keys:
+        outs.append(jax.ShapeDtypeStruct((len(out_keys),) + shape, jnp.float32))
+    result = pl.pallas_call(
+        kernel, out_shape=outs, in_specs=[VMEM] * len(args), out_specs=[VMEM] * len(outs)
+    )(*args)
+    return result[0], (result[1] if out_keys else None)
+
+
 def pair_index(t, u):
     return t * (t - 1) // 2 + u
 
 
+def holdings(levels):
+    hold = [[] for _ in range(levels)]
+    for t in range(1, levels):
+        for u in range(t):
+            keeper = t if (levels > 2 and t == levels - 1 and u == 0) else u
+            hold[keeper].append((t, u))
+    return hold
+
+
 def tile_table(levels):
-    table = np.zeros((levels, levels - 1), np.int32)
+    hold = holdings(levels)
+    width = max(len(h) for h in hold)
+    table = np.zeros((levels, width), np.int32)
     for c in range(levels):
-        for j in range(levels - 1):
-            table[c, j] = pair_index(c, j) if j < c else pair_index(j + 1, c)
+        for j, (t, u) in enumerate(hold[c]):
+            table[c, j] = pair_index(t, u)
     return table
+
+
+def plus(a, b):
+    return b if a is None else a + b
+
+
+def held_slice(mats, positions):
+    if positions == list(range(positions[0], positions[0] + len(positions))):
+        return mats[1 + positions[0] : 1 + positions[0] + len(positions)]
+    return jnp.stack([mats[1 + p] for p in positions])
 
 
 def summed_chunks(x, peers, rows_n, me):
@@ -154,35 +255,54 @@
         level_sum = gathered_chunks(part, peers, me).reshape(levels, -1, width)[owned]
     rhs_level = -level_sum.astype(jnp.float32)
 
+    hold = holdings(levels)
     top_forward = [None] * levels
-    pushed = None
+    message, in_keys = None, []
+    pending = set()
+    direct = {}
     for level in range(levels):
-        residue = rhs_level
         if level > 0:
-            pushed = lax.ppermute(pushed, "col", [(level - 1, level)])
-            residue = residue - pushed[0]
-        solved = jnp.dot(inv, residue.astype(jnp.bfloat16), preferred_element_type=jnp.float32)
-        top_forward[level] = solved.astype(jnp.bfloat16)
+            message = lax.ppermute(message, "col", [(level - 1, level)])
+        row_pos = [1 + j for j, (t, u) in enumerate(hold[level]) if t == level]
+        pushes = {t: 1 + j for j, (t, u) in enumerate(hold[level]) if u == level}
+        pending = (pending | set(pushes)) - {level}
+        out_keys = sorted(k for k in pending if k > level) if level < levels - 1 else []
+        sources = [u for (t, u) in hold[level] if t == level]
+        solved, sent = forward_hop(
+            level,
+            rhs_level,
+            message,
+            in_keys,
+            direct[(level, sources[0])] if sources else None,
+            row_pos,
+            mats,
+            pushes,
+            out_keys,
+        )
+        top_forward[level] = solved
+        for k in range(level + 1, levels):
+            if (k, level) in hold[k]:
+                direct[(k, level)] = lax.ppermute(solved, "col", [(level, k)])
+        message, in_keys = sent, out_keys
+    own_solution = None
+    message, in_keys = None, []
+    for level in reversed(range(levels)):
         if level < levels - 1:
-            later = jnp.einsum(
-                "kab,bc->kac", mats[level + 1 : levels], top_forward[level], preferred_element_type=jnp.float32
-            )
-            pushed = later if level == 0 else pushed[1:] + later
-    own_solution = None
-    for level in reversed(range(levels)):
-        update = top_forward[level].astype(jnp.float32)
-        if level < levels - 1:
-            pushed = lax.ppermute(pushed, "col", [(level + 1, level)])
-            update = update - pushed[level]
-        solved = lax.dot_general(
-            inv, update.astype(jnp.bfloat16), (((0,), (0,)), ((), ())), preferred_element_type=jnp.float32
+            message = lax.ppermute(message, "col", [(level + 1, level)])
+        pulls = [(1 + j, t) for j, (t, u) in enumerate(hold[level]) if u == level]
+        pushes = {u: 1 + j for j, (t, u) in enumerate(hold[level]) if t == level}
+        below = {t for c in range(level) for (t, u) in hold[c] if u == c}
+        out_keys = []
+        if level > 0:
+            qs = {k[1] for k in in_keys if k[0] == "q"} | set(pushes)
+            out_keys = [("q", u) for u in sorted(qs) if u < level]
+            xs = {k[1] for k in in_keys if k[0] == "x"} | {level}
+            out_keys += [("x", k) for k in sorted(xs) if k in below]
+        solved, sent = backward_hop(
+            level, top_forward[level], message, in_keys, mats, pulls, pushes, out_keys
         )
         own_solution = solved if own_solution is None else jnp.where(me == level, solved, own_solution)
-        if level > 0:
-            earlier = jnp.einsum(
-                "uab,ac->ubc", mats[1 : level + 1], solved.astype(jnp.bfloat16), preferred_element_type=jnp.float32
-            )
-            pushed = earlier if level == levels - 1 else pushed[:level] + earlier
+        message, in_keys = sent, out_keys
     solutions = gathered_chunks(own_solution, peers, me)[:levels]
     top_slices = [lax.dynamic_slice_in_dim(solutions[t], position * share, share, 0) for t in range(levels)]
     top_back = [solutions[t].astype(jnp.bfloat16) for t in range(levels)]

time: 153 us -> 172 us (1.12)
  Pallas kernels: 6.09 us -> 31.6 us
  matrix products: 13.8 us -> 2.38 us
  waiting for transfers between devices: 82.1 us -> 74.7 us
  local copies, waits for them, and re-layouts: 5.43 us -> 12 us
  starting transfers between devices: 20.9 us -> 26.1 us
    pallas_call x0 -> x8, Pallas kernels: none -> 25.5 us  [the longest x4 13.3 us: backward_hop(): pl.pallas_call(kernel, out_shape=outs, in_specs=[VMEM] * len(args), out_s...]
    dot_general x13 -> x0, matrix products: 11.4 us -> none  [the longest x4 4.4 us: local(): lax.dot_general(inv, update.astype(jnp.bfloat16), (((0,), (0,)), ((), ())...]
    unnamed x13 -> x25, local copies, waits for them, and re-layouts: 0.88 us -> 7.41 us
    ppermute x5, waiting for transfers between devices: 38 us -> 32.3 us  [swapped(): return lax.ppermute(x, axis, [(i, i ^ bit) for i in range(size)])]
    ppermute x9, waiting for transfers between devices: 19 us -> 15.1 us  [shifted(): return lax.ppermute(x, axis, [(i, (i + shift) % size) for i in range(size)])]
    ppermute x5, starting transfers between devices: 4.41 us -> 8.23 us  [swapped(): return lax.ppermute(x, axis, [(i, i ^ bit) for i in range(size)])]
    ppermute x6 -> x7, waiting for transfers between devices: 24.8 us -> 27.4 us  [the longest x3 23 us: local(): message = lax.ppermute(message, 'col', [(level + 1, level)])]
    ppermute x6 -> x7, starting transfers between devices: 6.34 us -> 7.24 us  [the longest x3 3.15 us: local(): message = lax.ppermute(message, 'col', [(level - 1, level)])]
  transfers between devices with their start and end apart: 21 -> 22, of which waited for: 15 -> 12; matrix products, arithmetic and copies ran while one was open for 4% -> 6% of each run, Pallas kernels for 2% -> 2%
where the time goes in v8:
time: 172 us; the launch traced here: 171 us
  waiting for transfers between devices  74.7 us (43%)
  Pallas kernels  31.6 us (18%)
  starting transfers between devices  26.1 us (15%)
  between operations  14.3 us (8%)
  local copies, waits for them, and re-layouts  12 us (7%)
  other arithmetic  10.4 us (6%)
  matrix products  2.38 us (1%)
    ppermute x5, waiting for transfers between devices, swapped(): return lax.ppermute(x, axis, [(i, i ^ bit) for i in range(size)])  32.3 us
    ppermute x3, waiting for transfers between devices, local(): message = lax.ppermute(message, 'col', [(level + 1, level)])  23 us
    ppermute x9, waiting for transfers between devices, shifted(): return lax.ppermute(x, axis, [(i, (i + shift) % size) for i in range(size)])  15.1 us
    pallas_call x4, Pallas kernels, backward_hop(): pl.pallas_call(kernel, out_shape=outs, in_specs=[VMEM] * len(args), out_s...  13.3 us
    pallas_call x4, Pallas kernels, forward_hop(): pl.pallas_call(kernel, out_shape=outs, in_specs=[VMEM] * len(args), out_s...  12.2 us
    ppermute x9, starting transfers between devices, shifted(): return lax.ppermute(x, axis, [(i, (i + shift) % size) for i in range(size)])  10.6 us
    ppermute x5, starting transfers between devices, swapped(): return lax.ppermute(x, axis, [(i, i ^ bit) for i in range(size)])  8.23 us
    unnamed x25, local copies, waits for them, and re-layouts  7.41 us
  transfers between devices with their start and end apart: 22, of which 12 were waited for; matrix products, arithmetic and copies ran while one was open for 6% of the time, Pallas kernels for 2%

profile of v8, /device:TPU:0, one launch (start us, length us, event | category | flops | bytes accessed | tf_op | source)
XLA Modules:
  0.0 171.5 jit_solution(7018247003041610365)
XLA Ops:
  7.2 1.0 copy-done
  8.2 1.2 convolution_convert_fusion
  9.4 3.1 %collective-permute-start.1 = (bf16[512,128]{1,0:T(8,128)(2,1)S(1)}, bf16[512,128]{1,0:T(8,128)(2,1)S(1)}, u32[]{:S(2)}, u32[]{:S(2)}) collective-permute-start(bf16[512,128]{1,0:T(8,128)(2,1)S(1)} %convolution_convert_fusion), channel_id=1, source_target_pairs={{0,2},{1,3},{2,0},{3,1},{4,6},{5,7},{6,4},{7,5},{8,10},{9,11},{10,... | collective-permute-start | bytes 393224 | tf_op jit(solution)/shard_map/ppermute | solution.py:67
  13.0 0.7 fusion.15
  13.7 0.7 compare_and_fusion
  14.4 0.9 constant_dynamic-slice_fusion.5
  15.2 1.5 gather_fusion
  16.9 0.7 pad_maximum_fusion.3
  17.6 1.2 and_select_fusion.2
  18.8 0.7 iota_reduce_fusion
  19.5 0.6 pad_add_fusion.fold_ref
  20.1 0.9 pad_maximum_fusion.1.panels_ref
  21.0 3.2 %shard_map.104 = f32[4,512,128]{2,1,0:T(8,128)} custom-call(s32[4]{0:T(128)} %bitcast.67, s32[4]{0:T(128)} %get-tuple-element.15.picks_ref, s32[2]{0:T(128)} %pad_add_fusion.fold_ref, bf16[4,512,512]{2,1,0:T(8,128)(2,1)} %bitcast.55, bf16[4,512,128]{2,1,0:T(8,128)(2,1)} %pad_maximum_fusion.1.panels_ref, bf16[4,64,128]{2,1,0:T(8,128)(2,1)} %rhs_ref.1), custom_call_target="tpu_custom_call" | custom-call | tf_op jit(solution)/shard_map/pallas_call | solution.py:32
  24.2 1.3 convert_element_type.98
  25.5 1.6 collective-permute-start.3
  27.1 7.5 %collective-permute-done.3 = bf16[2,512,128]{2,1,0:T(8,128)(2,1)S(1)} collective-permute-done((bf16[2,512,128]{2,1,0:T(8,128)(2,1)S(1)}, bf16[2,512,128]{2,1,0:T(8,128)(2,1)S(1)}, u32[]{:S(2)}, u32[]{:S(2)}) %collective-permute-start.3) | collective-permute-done | bytes 262176 | tf_op jit(solution)/shard_map/ppermute | solution.py:71
  35.1 1.0 collective-permute-done.4
  36.2 2.1 %collective-permute-start.5 = (bf16[512,128]{1,0:T(8,128)(2,1)S(1)}, bf16[512,128]{1,0:T(8,128)(2,1)S(1)}, u32[]{:S(2)}, u32[]{:S(2)}) collective-permute-start(bf16[512,128]{1,0:T(8,128)(2,1)S(1)} %fusion.7), channel_id=1, source_target_pairs={{0,4},{4,0},{8,12},{12,8},{16,20},{20,16},{24,28},{28,24},{1,5},{5... | collective-permute-start | bytes 393224 | tf_op jit(solution)/shard_map/ppermute | solution.py:71
  38.3 4.0 %collective-permute-done.5 = bf16[512,128]{1,0:T(8,128)(2,1)S(1)} collective-permute-done((bf16[512,128]{1,0:T(8,128)(2,1)S(1)}, bf16[512,128]{1,0:T(8,128)(2,1)S(1)}, u32[]{:S(2)}, u32[]{:S(2)}) %collective-permute-start.5) | collective-permute-done | bytes 131104 | tf_op jit(solution)/shard_map/ppermute | solution.py:71
  42.4 1.0 collective-permute-start.6
  43.4 8.2 %collective-permute-done.6 = bf16[512,128]{1,0:T(8,128)(2,1)S(1)} collective-permute-done((bf16[512,128]{1,0:T(8,128)(2,1)S(1)}, bf16[512,128]{1,0:T(8,128)(2,1)S(1)}, u32[]{:S(2)}, u32[]{:S(2)}) %collective-permute-start.6) | collective-permute-done | bytes 131104 | tf_op jit(solution)/shard_map/ppermute | solution.py:71
  51.6 3.0 %collective-permute-start.7 = (bf16[512,128]{1,0:T(8,128)(2,1)S(1)}, bf16[512,128]{1,0:T(8,128)(2,1)S(1)}, u32[]{:S(2)}, u32[]{:S(2)}) collective-permute-start(bf16[512,128]{1,0:T(8,128)(2,1)S(1)} %add_convert_fusion.1), channel_id=1, source_target_pairs={{0,16},{4,20},{8,24},{12,28},{16,0},{20,4},{24,8},{28,12},{1,17},{... | collective-permute-start | bytes 393224 | tf_op jit(solution)/shard_map/ppermute | solution.py:71
  54.6 11.6 %collective-permute-done.7 = bf16[512,128]{1,0:T(8,128)(2,1)S(1)} collective-permute-done((bf16[512,128]{1,0:T(8,128)(2,1)S(1)}, bf16[512,128]{1,0:T(8,128)(2,1)S(1)}, u32[]{:S(2)}, u32[]{:S(2)}) %collective-permute-start.7) | collective-permute-done | bytes 131104 | tf_op jit(solution)/shard_map/ppermute | solution.py:71
  66.2 0.7 convert_negate_fusion.refs_0_
  67.0 2.9 %shard_map.105 = (bf16[512,128]{1,0:T(8,128)(2,1)}, f32[2,512,128]{2,1,0:T(8,128)}) custom-call(f32[512,128]{1,0:T(8,128)} %convert_negate_fusion.refs_0_, bf16[3,512,512]{2,1,0:T(8,128)(2,1)} %all-gather.2.cloned.1.call-done.refs_1_.refs_2_.refs_3_), custom_call_target="tpu_custom_call" | custom-call | tf_op jit(solution)/shard_map/pallas_call | solution.py:110
  69.9 1.8 %collective-permute-start.8 = (f32[2,512,128]{2,1,0:T(8,128)}, f32[2,512,128]{2,1,0:T(8,128)S(1)}, u32[]{:S(2)}, u32[]{:S(2)}) collective-permute-start(f32[2,512,128]{2,1,0:T(8,128)} %get-tuple-element.17), channel_id=1, source_target_pairs={{0,1},{4,5},{8,9},{12,13},{16,17},{20,21},{24,25},{28,29}} | collective-permute-start | bytes 1572872 | tf_op jit(solution)/shard_map/ppermute | solution.py:265
  71.7 1.7 collective-permute-done.8.refs_1_
  73.4 0.8 copy-done.4
  74.2 3.1 %shard_map.106 = (bf16[512,128]{1,0:T(8,128)(2,1)}, f32[2,512,128]{2,1,0:T(8,128)}) custom-call(f32[512,128]{1,0:T(8,128)} %convert_negate_fusion.refs_0_, f32[2,512,128]{2,1,0:T(8,128)} %copy-done.4, bf16[3,512,512]{2,1,0:T(8,128)(2,1)} %all-gather.2.cloned.1.call-done.refs_1_.refs_2_.refs_3_), custom_call_target="tpu_custom_call" | custom-call | tf_op jit(solution)/shard_map/pallas_call | solution.py:110
  77.3 0.7 collective-permute-start.9
  78.0 0.8 copy-done.5
  78.8 3.1 %shard_map.107 = (bf16[512,128]{1,0:T(8,128)(2,1)}, f32[1,512,128]{2,1,0:T(8,128)}) custom-call(f32[512,128]{1,0:T(8,128)} %convert_negate_fusion.refs_0_, f32[2,512,128]{2,1,0:T(8,128)} %copy-done.5, bf16[3,512,512]{2,1,0:T(8,128)(2,1)} %all-gather.2.cloned.1.call-done.refs_1_.refs_2_.refs_3_), custom_call_target="tpu_custom_call" | custom-call | tf_op jit(solution)/shard_map/pallas_call | solution.py:110
  81.9 0.7 collective-permute-start.10
  82.6 1.3 collective-permute-start.11
  83.9 2.7 %collective-permute-done.11.refs_2_ = bf16[512,128]{1,0:T(8,128)(2,1)S(1)} collective-permute-done((bf16[512,128]{1,0:T(8,128)(2,1)S(1)}, bf16[512,128]{1,0:T(8,128)(2,1)S(1)}, u32[]{:S(2)}, u32[]{:S(2)}) %collective-permute-start.11) | collective-permute-done | bytes 131104 | tf_op jit(solution)/shard_map/ppermute | solution.py:285
  86.6 0.6 copy-done.10
  87.2 0.7 copy-done.6
  88.0 3.0 %shard_map.108.refs_0_ = bf16[512,128]{1,0:T(8,128)(2,1)} custom-call(f32[512,128]{1,0:T(8,128)} %convert_negate_fusion.refs_0_, f32[1,512,128]{2,1,0:T(8,128)} %copy-done.6, bf16[512,128]{1,0:T(8,128)(2,1)} %copy-done.10, bf16[3,512,512]{2,1,0:T(8,128)(2,1)} %all-gather.2.cloned.1.call-done.refs_1_.refs_2_.refs_3_), custom_call_target="tpu_custom_call" | custom-call | tf_op jit(solution)/shard_map/pallas_call | solution.py:110
  91.0 3.0 %shard_map.109 = (f32[512,128]{1,0:T(8,128)}, f32[2,512,128]{2,1,0:T(8,128)}) custom-call(bf16[512,128]{1,0:T(8,128)(2,1)} %shard_map.108.refs_0_, bf16[3,512,512]{2,1,0:T(8,128)(2,1)} %all-gather.2.cloned.1.call-done.refs_1_.refs_2_.refs_3_), custom_call_target="tpu_custom_call" | custom-call | tf_op jit(solution)/shard_map/pallas_call | solution.py:156
  94.0 0.7 collective-permute-start.12
  94.7 0.8 copy-done.3
  95.5 3.4 %shard_map.110 = (f32[512,128]{1,0:T(8,128)}, f32[3,512,128]{2,1,0:T(8,128)}) custom-call(bf16[512,128]{1,0:T(8,128)(2,1)} %get-tuple-element.20.refs_0_, f32[2,512,128]{2,1,0:T(8,128)} %copy-done.3, bf16[3,512,512]{2,1,0:T(8,128)(2,1)} %all-gather.2.cloned.1.call-done.refs_1_.refs_2_.refs_3_), custom_call_target="tpu_custom_call" | custom-call | tf_op jit(solution)/shard_map/pallas_call | solution.py:156
  98.9 0.7 collective-permute-start.13
  99.6 0.9 copy-done.1
  100.5 3.6 %shard_map.111 = (f32[512,128]{1,0:T(8,128)}, f32[3,512,128]{2,1,0:T(8,128)}) custom-call(bf16[512,128]{1,0:T(8,128)(2,1)} %get-tuple-element.18.refs_0_, f32[3,512,128]{2,1,0:T(8,128)} %copy-done.1, bf16[3,512,512]{2,1,0:T(8,128)(2,1)} %all-gather.2.cloned.1.call-done.refs_1_.refs_2_.refs_3_), custom_call_target="tpu_custom_call" | custom-call | tf_op jit(solution)/shard_map/pallas_call | solution.py:156
  104.1 1.4 collective-permute-start.14
  105.6 23.0 %collective-permute-done.14.refs_1_ = f32[3,512,128]{2,1,0:T(8,128)S(1)} collective-permute-done((f32[3,512,128]{2,1,0:T(8,128)}, f32[3,512,128]{2,1,0:T(8,128)S(1)}, u32[]{:S(2)}, u32[]{:S(2)}) %collective-permute-start.14) | collective-permute-done | bytes 786464 | tf_op jit(solution)/shard_map/ppermute | solution.py:291
  128.5 0.9 copy-done.2
  129.5 3.3 %shard_map.112 = f32[512,128]{1,0:T(8,128)} custom-call(bf16[512,128]{1,0:T(8,128)(2,1)} %get-tuple-element.16.refs_0_, f32[3,512,128]{2,1,0:T(8,128)} %copy-done.2, bf16[3,512,512]{2,1,0:T(8,128)(2,1)} %all-gather.2.cloned.1.call-done.refs_1_.refs_2_.refs_3_), custom_call_target="tpu_custom_call" | custom-call | tf_op jit(solution)/shard_map/pallas_call | solution.py:156
  132.8 1.0 select_select_fusion
  133.9 1.7 collective-permute-start.17
  135.6 6.2 %collective-permute-done.15 = f32[512,128]{1,0:T(8,128)S(1)} collective-permute-done((f32[512,128]{1,0:T(8,128)S(1)}, f32[512,128]{1,0:T(8,128)S(1)}, u32[]{:S(2)}, u32[]{:S(2)}) %collective-permute-start.15) | collective-permute-done | bytes 262176 | tf_op jit(solution)/shard_map/ppermute | solution.py:67
  141.8 1.3 collective-permute-done.16
  143.1 1.6 collective-permute-done.17
  144.8 0.8 scatter_fusion
  145.8 0.9 pad_maximum_fusion.2.back_ref
  146.7 2.9 %shard_map.113 = bf16[4,512,128]{2,1,0:T(8,128)(2,1)} custom-call(s32[4]{0:T(128)} %bitcast.68, s32[4]{0:T(128)} %get-tuple-element.32.dests_ref, bf16[4,512,512]{2,1,0:T(8,128)(2,1)} %bitcast.56, bf16[4,512,128]{2,1,0:T(8,128)(2,1)} %pad_maximum_fusion.2.back_ref), custom_call_target="tpu_custom_call" | custom-call | tf_op jit(solution)/shard_map/pallas_call | solution.py:57
  149.6 1.1 slice_bitcast_fusion.2
  150.7 2.4 %collective-permute-start.18 = (bf16[512,128]{1,0:T(8,128)(2,1)S(1)}, bf16[512,128]{1,0:T(8,128)(2,1)S(1)}, u32[]{:S(2)}, u32[]{:S(2)}) collective-permute-start(bf16[512,128]{1,0:T(8,128)(2,1)S(1)} %get-tuple-element.42), channel_id=1, source_target_pairs={{0,3},{1,0},{2,1},{3,2},{4,7},{5,4},{6,5},{7,6},{8,11},{9,8},{10,9... | collective-permute-start | bytes 393224 | tf_op jit(solution)/shard_map/ppermute | solution.py:67
  153.1 2.8 %collective-permute-start.19 = (bf16[512,128]{1,0:T(8,128)(2,1)S(1)}, bf16[512,128]{1,0:T(8,128)(2,1)S(1)}, u32[]{:S(2)}, u32[]{:S(2)}) collective-permute-start(bf16[512,128]{1,0:T(8,128)(2,1)S(1)} %get-tuple-element.44), channel_id=1, source_target_pairs={{0,2},{1,3},{2,0},{3,1},{4,6},{5,7},{6,4},{7,5},{8,10},{9,11},{10,... | collective-permute-start | bytes 393224 | tf_op jit(solution)/shard_map/ppermute | solution.py:67
  155.9 0.7 pad_maximum_fusion.4
  156.6 6.0 %collective-permute-done.19 = bf16[512,128]{1,0:T(8,128)(2,1)S(1)} collective-permute-done((bf16[512,128]{1,0:T(8,128)(2,1)S(1)}, bf16[512,128]{1,0:T(8,128)(2,1)S(1)}, u32[]{:S(2)}, u32[]{:S(2)}) %collective-permute-start.19) | collective-permute-done | bytes 131104 | tf_op jit(solution)/shard_map/ppermute | solution.py:67
  162.6 1.2 convolution_bitcast_fusion
  163.8 0.8 copy.12
  (51 shorter events, 1.8 us)
Async XLA Ops:
  7.2 1.0 copy-start
  7.2 59.8 %all-gather.2.cloned.1.call-start = ((), (), s32[]{:S(2)}) async-start(), calls=%async_computation | async-start | bytes 1769472 | tf_op jit(solution)/shard_map/all_gather | solution.py:236
  9.4 10.7 %collective-permute-start.1 = (bf16[512,128]{1,0:T(8,128)(2,1)S(1)}, bf16[512,128]{1,0:T(8,128)(2,1)S(1)}, u32[]{:S(2)}, u32[]{:S(2)}) collective-permute-start(bf16[512,128]{1,0:T(8,128)(2,1)S(1)} %convolution_convert_fusion), channel_id=1, source_target_pairs={{0,2},{1,3},{2,0},{3,1},{4,6},{5,7},{6,4},{7,5},{8,10},{9,11},{10,... | collective-permute-start | bytes 393224 | tf_op jit(solution)/shard_map/ppermute | solution.py:67
  12.5 7.6 %collective-permute-start.2 = (bf16[512,128]{1,0:T(8,128)(2,1)S(1)}, bf16[512,128]{1,0:T(8,128)(2,1)S(1)}, u32[]{:S(2)}, u32[]{:S(2)}) collective-permute-start(bf16[512,128]{1,0:T(8,128)(2,1)S(1)} %convolution_convert_fusion), channel_id=1, source_target_pairs={{0,3},{1,0},{2,1},{3,2},{4,7},{5,4},{6,5},{7,6},{8,11},{9,8},{10,9... | collective-permute-start | bytes 393224 | tf_op jit(solution)/shard_map/ppermute | solution.py:67
  12.5 7.6 %collective-permute-start = (bf16[512,128]{1,0:T(8,128)(2,1)S(1)}, bf16[512,128]{1,0:T(8,128)(2,1)S(1)}, u32[]{:S(2)}, u32[]{:S(2)}) collective-permute-start(bf16[512,128]{1,0:T(8,128)(2,1)S(1)} %convolution_convert_fusion), channel_id=1, source_target_pairs={{0,1},{1,2},{2,3},{3,0},{4,5},{5,6},{6,7},{7,4},{8,9},{9,10},{10,1... | collective-permute-start | bytes 393224 | tf_op jit(solution)/shard_map/ppermute | solution.py:67
  25.5 9.1 %collective-permute-start.3 = (bf16[2,512,128]{2,1,0:T(8,128)(2,1)S(1)}, bf16[2,512,128]{2,1,0:T(8,128)(2,1)S(1)}, u32[]{:S(2)}, u32[]{:S(2)}) collective-permute-start(bf16[2,512,128]{2,1,0:T(8,128)(2,1)S(1)} %dynamic-slice_bitcast_fusion), channel_id=1, source_target_pairs={{0,2},{1,3},{2,0},{3,1},{4,6},{5,7},{6,4},{7,5},{8,10},{9,11},{10,... | collective-permute-start | bytes 786440 | tf_op jit(solution)/shard_map/ppermute | solution.py:71
  34.7 1.4 collective-permute-start.4
  36.2 6.2 %collective-permute-start.5 = (bf16[512,128]{1,0:T(8,128)(2,1)S(1)}, bf16[512,128]{1,0:T(8,128)(2,1)S(1)}, u32[]{:S(2)}, u32[]{:S(2)}) collective-permute-start(bf16[512,128]{1,0:T(8,128)(2,1)S(1)} %fusion.7), channel_id=1, source_target_pairs={{0,4},{4,0},{8,12},{12,8},{16,20},{20,16},{24,28},{28,24},{1,5},{5... | collective-permute-start | bytes 393224 | tf_op jit(solution)/shard_map/ppermute | solution.py:71
  42.4 9.2 %collective-permute-start.6 = (bf16[512,128]{1,0:T(8,128)(2,1)S(1)}, bf16[512,128]{1,0:T(8,128)(2,1)S(1)}, u32[]{:S(2)}, u32[]{:S(2)}) collective-permute-start(bf16[512,128]{1,0:T(8,128)(2,1)S(1)} %add_convert_fusion.2), channel_id=1, source_target_pairs={{0,8},{4,12},{8,0},{12,4},{16,24},{20,28},{24,16},{28,20},{1,9},{5... | collective-permute-start | bytes 393224 | tf_op jit(solution)/shard_map/ppermute | solution.py:71
  51.6 14.6 %collective-permute-start.7 = (bf16[512,128]{1,0:T(8,128)(2,1)S(1)}, bf16[512,128]{1,0:T(8,128)(2,1)S(1)}, u32[]{:S(2)}, u32[]{:S(2)}) collective-permute-start(bf16[512,128]{1,0:T(8,128)(2,1)S(1)} %add_convert_fusion.1), channel_id=1, source_target_pairs={{0,16},{4,20},{8,24},{12,28},{16,0},{20,4},{24,8},{28,12},{1,17},{... | collective-permute-start | bytes 393224 | tf_op jit(solution)/shard_map/ppermute | solution.py:71
  69.9 12.7 %copy-start.11 = (bf16[512,128]{1,0:T(8,128)(2,1)S(1)}, bf16[512,128]{1,0:T(8,128)(2,1)}, u32[]{:S(2)}) copy-start(bf16[512,128]{1,0:T(8,128)(2,1)} %get-tuple-element.16.refs_0_) | copy-start | bytes 393220
  69.9 3.5 %collective-permute-start.8 = (f32[2,512,128]{2,1,0:T(8,128)}, f32[2,512,128]{2,1,0:T(8,128)S(1)}, u32[]{:S(2)}, u32[]{:S(2)}) collective-permute-start(f32[2,512,128]{2,1,0:T(8,128)} %get-tuple-element.17), channel_id=1, source_target_pairs={{0,1},{4,5},{8,9},{12,13},{16,17},{20,21},{24,25},{28,29}} | collective-permute-start | bytes 1572872 | tf_op jit(solution)/shard_map/ppermute | solution.py:265
  73.4 0.8 copy-start.4
  77.3 0.7 collective-permute-start.9
  78.0 0.8 copy-start.5
  81.9 4.7 %collective-permute-start.10 = (f32[1,512,128]{2,1,0:T(8,128)}, f32[1,512,128]{2,1,0:T(8,128)S(1)}, u32[]{:S(2)}, u32[]{:S(2)}) collective-permute-start(f32[1,512,128]{2,1,0:T(8,128)} %get-tuple-element.21), channel_id=1, source_target_pairs={{2,3},{6,7},{10,11},{14,15},{18,19},{22,23},{26,27},{30,31}} | collective-permute-start | bytes 786440 | tf_op jit(solution)/shard_map/ppermute | solution.py:265
  82.6 4.0 %collective-permute-start.11 = (bf16[512,128]{1,0:T(8,128)(2,1)S(1)}, bf16[512,128]{1,0:T(8,128)(2,1)S(1)}, u32[]{:S(2)}, u32[]{:S(2)}) collective-permute-start(bf16[512,128]{1,0:T(8,128)(2,1)S(1)} %copy-done.11), channel_id=1, source_target_pairs={{0,3},{4,7},{8,11},{12,15},{16,19},{20,23},{24,27},{28,31}} | collective-permute-start | bytes 393224 | tf_op jit(solution)/shard_map/ppermute | solution.py:285
  86.6 0.6 copy-start.10
  87.2 0.7 copy-start.6
  94.0 0.7 collective-permute-start.12
  94.7 0.8 copy-start.3
  98.9 0.7 collective-permute-start.13
  99.6 0.9 copy-start.1
  100.5 32.3 %copy-start.7 = (f32[512,128]{1,0:T(8,128)S(1)}, f32[512,128]{1,0:T(8,128)}, u32[]{:S(2)}) copy-start(f32[512,128]{1,0:T(8,128)} %get-tuple-element.27) | copy-start | bytes 786436
  100.5 32.3 %copy-start.8 = (f32[512,128]{1,0:T(8,128)S(1)}, f32[512,128]{1,0:T(8,128)}, u32[]{:S(2)}) copy-start(f32[512,128]{1,0:T(8,128)} %get-tuple-element.26) | copy-start | bytes 786436
  104.1 28.7 %copy-start.9 = (f32[512,128]{1,0:T(8,128)S(1)}, f32[512,128]{1,0:T(8,128)}, u32[]{:S(2)}) copy-start(f32[512,128]{1,0:T(8,128)} %get-tuple-element.25) | copy-start | bytes 786436
  104.1 24.4 %collective-permute-start.14 = (f32[3,512,128]{2,1,0:T(8,128)}, f32[3,512,128]{2,1,0:T(8,128)S(1)}, u32[]{:S(2)}, u32[]{:S(2)}) collective-permute-start(f32[3,512,128]{2,1,0:T(8,128)} %get-tuple-element.24), channel_id=1, source_target_pairs={{1,0},{5,4},{9,8},{13,12},{17,16},{21,20},{25,24},{29,28}} | collective-permute-start | bytes 2359304 | tf_op jit(solution)/shard_map/ppermute | solution.py:291
  128.5 0.9 copy-start.2
  133.8 8.0 %collective-permute-start.15 = (f32[512,128]{1,0:T(8,128)S(1)}, f32[512,128]{1,0:T(8,128)S(1)}, u32[]{:S(2)}, u32[]{:S(2)}) collective-permute-start(f32[512,128]{1,0:T(8,128)S(1)} %select_select_fusion), channel_id=1, source_target_pairs={{0,1},{1,2},{2,3},{3,0},{4,5},{5,6},{6,7},{7,4},{8,9},{9,10},{10,1... | collective-permute-start | bytes 786440 | tf_op jit(solution)/shard_map/ppermute | solution.py:67
  133.9 9.2 %collective-permute-start.16 = (f32[512,128]{1,0:T(8,128)S(1)}, f32[512,128]{1,0:T(8,128)S(1)}, u32[]{:S(2)}, u32[]{:S(2)}) collective-permute-start(f32[512,128]{1,0:T(8,128)S(1)} %select_select_fusion), channel_id=1, source_target_pairs={{0,2},{1,3},{2,0},{3,1},{4,6},{5,7},{6,4},{7,5},{8,10},{9,11},{10,... | collective-permute-start | bytes 786440 | tf_op jit(solution)/shard_map/ppermute | solution.py:67
  133.9 10.7 %collective-permute-start.17 = (f32[512,128]{1,0:T(8,128)S(1)}, f32[512,128]{1,0:T(8,128)S(1)}, u32[]{:S(2)}, u32[]{:S(2)}) collective-permute-start(f32[512,128]{1,0:T(8,128)S(1)} %select_select_fusion), channel_id=1, source_target_pairs={{0,3},{1,0},{2,1},{3,2},{4,7},{5,4},{6,5},{7,6},{8,11},{9,8},{10,9... | collective-permute-start | bytes 786440 | tf_op jit(solution)/shard_map/ppermute | solution.py:67
  150.7 5.9 %collective-permute-start.18 = (bf16[512,128]{1,0:T(8,128)(2,1)S(1)}, bf16[512,128]{1,0:T(8,128)(2,1)S(1)}, u32[]{:S(2)}, u32[]{:S(2)}) collective-permute-start(bf16[512,128]{1,0:T(8,128)(2,1)S(1)} %get-tuple-element.42), channel_id=1, source_target_pairs={{0,3},{1,0},{2,1},{3,2},{4,7},{5,4},{6,5},{7,6},{8,11},{9,8},{10,9... | collective-permute-start | bytes 393224 | tf_op jit(solution)/shard_map/ppermute | solution.py:67
  153.1 9.5 %collective-permute-start.19 = (bf16[512,128]{1,0:T(8,128)(2,1)S(1)}, bf16[512,128]{1,0:T(8,128)(2,1)S(1)}, u32[]{:S(2)}, u32[]{:S(2)}) collective-permute-start(bf16[512,128]{1,0:T(8,128)(2,1)S(1)} %get-tuple-element.44), channel_id=1, source_target_pairs={{0,2},{1,3},{2,0},{3,1},{4,6},{5,7},{6,4},{7,5},{8,10},{9,11},{10,... | collective-permute-start | bytes 393224 | tf_op jit(solution)/shard_map/ppermute | solution.py:67
  155.9 6.7 %collective-permute-start.20 = (bf16[512,128]{1,0:T(8,128)(2,1)S(1)}, bf16[512,128]{1,0:T(8,128)(2,1)S(1)}, u32[]{:S(2)}, u32[]{:S(2)}) collective-permute-start(bf16[512,128]{1,0:T(8,128)(2,1)S(1)} %get-tuple-element.43), channel_id=1, source_target_pairs={{0,1},{1,2},{2,3},{3,0},{4,5},{5,6},{6,7},{7,4},{8,9},{9,10},{10,1... | collective-permute-start | bytes 393224 | tf_op jit(solution)/shard_map/ppermute | solution.py:67
Sparse Core Ops, SparseCore 0:
  17.7 49.2 all-gather.1

commit v9 on v5

--- a/solution.py
+++ b/solution.py
@@ -10,14 +10,14 @@
 VMEM = pl.BlockSpec(memory_space=pltpu.VMEM)
 
 
-def coupling_kernel(rows_ref, picks_ref, fold_ref, tiles_ref, panels_ref, rhs_ref, out_ref):
-    out_ref[...] = jnp.zeros_like(out_ref)
+def coupling_kernel(rows_ref, picks_ref, fold_ref, tiles_ref, panels_ref, rhs_ref, out_ref, acc_ref):
+    acc_ref[...] = jnp.zeros_like(acc_ref)
     share = rhs_ref.shape[1]
 
     @pl.when(fold_ref[1] == 0)
     def _():
         start = pl.multiple_of(fold_ref[0], 8)
-        out_ref[:, pl.ds(start, share), :] = -rhs_ref[...].astype(jnp.float32)
+        acc_ref[:, pl.ds(start, share), :] = -rhs_ref[...].astype(jnp.float32)
 
     for s in range(tiles_ref.shape[0]):
         level = rows_ref[s]
@@ -25,15 +25,19 @@
         @pl.when(level >= 0)
         def _():
             prod = jnp.dot(tiles_ref[s], panels_ref[picks_ref[s]], preferred_element_type=jnp.float32)
-            out_ref[level] += prod
+            acc_ref[level] += prod
+
+    out_ref[...] = acc_ref[...].astype(out_ref.dtype)
 
 
 def coupling_terms(slot_rows, picks, fold, tiles, panels, rhs, levels):
+    shape = (levels, panels.shape[1], panels.shape[2])
     return pl.pallas_call(
         coupling_kernel,
-        out_shape=jax.ShapeDtypeStruct((levels, panels.shape[1], panels.shape[2]), jnp.float32),
+        out_shape=jax.ShapeDtypeStruct(shape, jnp.bfloat16),
         in_specs=[SMEM, SMEM, SMEM, VMEM, VMEM, VMEM],
         out_specs=VMEM,
+        scratch_shapes=[pltpu.VMEM(shape, jnp.float32)],
     )(slot_rows, picks, fold, tiles, panels, rhs)
 
 
@@ -93,15 +97,15 @@
 
 def summed_chunks(x, peers, rows_n, me):
     chunks = x.reshape(peers, -1, x.shape[-1]).astype(jnp.bfloat16)
-    bit = peers // 2
-    while bit >= 1:
-        halves = chunks.reshape(2, -1, *chunks.shape[1:])
+    bit = 1
+    while bit < peers:
+        pairs = chunks.reshape(-1, 2, *chunks.shape[1:])
         mine = (me // bit) % 2
-        keep = lax.dynamic_index_in_dim(halves, mine, 0, keepdims=False)
-        give = lax.dynamic_index_in_dim(halves, 1 - mine, 0, keepdims=False)
+        keep = lax.dynamic_index_in_dim(pairs, mine, 1, keepdims=False)
+        give = lax.dynamic_index_in_dim(pairs, 1 - mine, 1, keepdims=False)
         got = swapped(give, "col", peers, bit)
         chunks = (keep.astype(jnp.float32) + got.astype(jnp.float32)).astype(jnp.bfloat16)
-        bit //= 2
+        bit *= 2
     part = chunks[0]
     bit = 1
     while bit < rows_n:

time: 153 us -> 153 us (level)
  waiting for transfers between devices: 82.1 us -> 76.9 us
  starting transfers between devices: 20.9 us -> 25.7 us
    ppermute x5, waiting for transfers between devices: 38 us -> 32.5 us  [swapped(): return lax.ppermute(x, axis, [(i, i ^ bit) for i in range(size)])]
    ppermute x5, starting transfers between devices: 4.41 us -> 8.03 us  [swapped(): return lax.ppermute(x, axis, [(i, i ^ bit) for i in range(size)])]
where the time goes in v9:
time: 153 us; the launch traced here: 152 us
  waiting for transfers between devices  76.9 us (50%)
  starting transfers between devices  25.7 us (17%)
  between operations  14.4 us (9%)
  matrix products  13.8 us (9%)
  other arithmetic  8.73 us (6%)
  local copies, waits for them, and re-layouts  6.37 us (4%)
  Pallas kernels  5.96 us (4%)
    ppermute x5, waiting for transfers between devices, swapped(): return lax.ppermute(x, axis, [(i, i ^ bit) for i in range(size)])  32.5 us
    ppermute x3, waiting for transfers between devices, local(): pushed = lax.ppermute(pushed, 'col', [(level + 1, level)])  23 us
    ppermute x9, waiting for transfers between devices, shifted(): return lax.ppermute(x, axis, [(i, (i + shift) % size) for i in range(size)])  19.1 us
    ppermute x9, starting transfers between devices, shifted(): return lax.ppermute(x, axis, [(i, (i + shift) % size) for i in range(size)])  10.8 us
    ppermute x5, starting transfers between devices, swapped(): return lax.ppermute(x, axis, [(i, i ^ bit) for i in range(size)])  8.03 us
    dot_general x4, matrix products, local(): lax.dot_general(inv, update.astype(jnp.bfloat16), (((0,), (0,)), ((), ())...  4.4 us
    ppermute x3, starting transfers between devices, local(): pushed = lax.ppermute(pushed, 'col', [(level - 1, level)])  3.99 us
  transfers between devices with their start and end apart: 21, of which 15 were waited for; matrix products, arithmetic and copies ran while one was open for 4% of the time, Pallas kernels for 2%

profile of v9, /device:TPU:0, one launch (start us, length us, event | category | flops | bytes accessed | tf_op | source)
XLA Modules:
  0.0 151.7 jit_solution(8984369646170048039)
XLA Ops:
  7.2 0.7 fusion.54
  8.0 0.7 compare_and_fusion
  8.7 0.9 constant_dynamic-slice_fusion.6
  9.5 1.6 %gather_fusion = bf16[3,64,512]{2,1,0:T(8,128)(2,1)S(1)} fusion(bf16[6,64,512]{2,1,0:T(8,128)(2,1)} %param.16, s32[1024]{0:T(1024)S(1)} %pad_clamp_fusion), kind=kCustom, calls=%fused_computation | custom fusion | bytes 393228 | tf_op jit(solution)/shard_map/jit(_take)/gather | solution.py:137
  11.2 0.7 pad_maximum_fusion.3
  11.9 1.2 convolution_convert_fusion.4
  13.2 0.5 collective-permute-start
  13.7 2.6 %collective-permute-start.1 = (bf16[512,128]{1,0:T(8,128)(2,1)S(1)}, bf16[512,128]{1,0:T(8,128)(2,1)S(1)}, u32[]{:S(2)}, u32[]{:S(2)}) collective-permute-start(bf16[512,128]{1,0:T(8,128)(2,1)S(1)} %convolution_convert_fusion.4), channel_id=1, source_target_pairs={{0,2},{1,3},{2,0},{3,1},{4,6},{5,7},{6,4},{7,5},{8,10},{9,11},{10,... | collective-permute-start | bytes 393224 | tf_op jit(solution)/shard_map/ppermute | solution.py:71
  16.3 1.4 collective-permute-start.2
  17.7 0.6 and_select_fusion.2
  18.3 0.7 iota_reduce_fusion
  19.0 0.6 pad_add_fusion.fold_ref
  19.6 0.9 collective-permute-done.1
  20.5 1.8 %collective-permute-done.2 = bf16[512,128]{1,0:T(8,128)(2,1)S(1)} collective-permute-done((bf16[512,128]{1,0:T(8,128)(2,1)S(1)}, bf16[512,128]{1,0:T(8,128)(2,1)S(1)}, u32[]{:S(2)}, u32[]{:S(2)}) %collective-permute-start.2) | collective-permute-done | bytes 131104 | tf_op jit(solution)/shard_map/ppermute | solution.py:71
  22.3 0.9 pad_maximum_fusion.1.panels_ref
  23.2 3.0 %shard_map.104 = bf16[4,512,128]{2,1,0:T(8,128)(2,1)} custom-call(s32[4]{0:T(128)} %bitcast.154, s32[4]{0:T(128)} %get-tuple-element.3.picks_ref, s32[2]{0:T(128)} %pad_add_fusion.fold_ref, bf16[4,512,512]{2,1,0:T(8,128)(2,1)} %bitcast.143, bf16[4,512,128]{2,1,0:T(8,128)(2,1)} %pad_maximum_fusion.1.panels_ref, bf16[4,64,128]{2,1,0:T(8,128)(2,1)} %rhs_ref.1), custom_call_target="tpu_custom_call" | custom-call | tf_op jit(solution)/shard_map/pallas_call | solution.py:35
  26.2 1.0 dynamic-slice_bitcast_fusion
  27.2 0.7 collective-permute-start.3
  27.9 1.2 collective-permute-done.3
  29.1 1.0 fusion.1
  30.1 1.7 %collective-permute-start.4 = (bf16[1,512,128]{2,1,0:T(8,128)(2,1)S(1)}, bf16[1,512,128]{2,1,0:T(8,128)(2,1)S(1)}, u32[]{:S(2)}, u32[]{:S(2)}) collective-permute-start(bf16[1,512,128]{2,1,0:T(8,128)(2,1)S(1)} %constant_dynamic-slice_fusion.4), channel_id=1, source_target_pairs={{0,2},{1,3},{2,0},{3,1},{4,6},{5,7},{6,4},{7,5},{8,10},{9,11},{10,... | collective-permute-start | bytes 393224 | tf_op jit(solution)/shard_map/ppermute | solution.py:75
  31.8 4.1 %collective-permute-done.4 = bf16[1,512,128]{2,1,0:T(8,128)(2,1)S(1)} collective-permute-done((bf16[1,512,128]{2,1,0:T(8,128)(2,1)S(1)}, bf16[1,512,128]{2,1,0:T(8,128)(2,1)S(1)}, u32[]{:S(2)}, u32[]{:S(2)}) %collective-permute-start.4) | collective-permute-done | bytes 131104 | tf_op jit(solution)/shard_map/ppermute | solution.py:75
  36.0 2.0 %collective-permute-start.5 = (bf16[512,128]{1,0:T(8,128)(2,1)S(1)}, bf16[512,128]{1,0:T(8,128)(2,1)S(1)}, u32[]{:S(2)}, u32[]{:S(2)}) collective-permute-start(bf16[512,128]{1,0:T(8,128)(2,1)S(1)} %fusion.21), channel_id=1, source_target_pairs={{0,4},{4,0},{8,12},{12,8},{16,20},{20,16},{24,28},{28,24},{1,5},{5... | collective-permute-start | bytes 393224 | tf_op jit(solution)/shard_map/ppermute | solution.py:75
  38.0 3.4 %collective-permute-done.5 = bf16[512,128]{1,0:T(8,128)(2,1)S(1)} collective-permute-done((bf16[512,128]{1,0:T(8,128)(2,1)S(1)}, bf16[512,128]{1,0:T(8,128)(2,1)S(1)}, u32[]{:S(2)}, u32[]{:S(2)}) %collective-permute-start.5) | collective-permute-done | bytes 131104 | tf_op jit(solution)/shard_map/ppermute | solution.py:75
  41.5 2.0 %collective-permute-start.6 = (bf16[512,128]{1,0:T(8,128)(2,1)S(1)}, bf16[512,128]{1,0:T(8,128)(2,1)S(1)}, u32[]{:S(2)}, u32[]{:S(2)}) collective-permute-start(bf16[512,128]{1,0:T(8,128)(2,1)S(1)} %add_convert_fusion.2), channel_id=1, source_target_pairs={{0,8},{4,12},{8,0},{12,4},{16,24},{20,28},{24,16},{28,20},{1,9},{5... | collective-permute-start | bytes 393224 | tf_op jit(solution)/shard_map/ppermute | solution.py:75
  43.5 10.2 %collective-permute-done.6 = bf16[512,128]{1,0:T(8,128)(2,1)S(1)} collective-permute-done((bf16[512,128]{1,0:T(8,128)(2,1)S(1)}, bf16[512,128]{1,0:T(8,128)(2,1)S(1)}, u32[]{:S(2)}, u32[]{:S(2)}) %collective-permute-start.6) | collective-permute-done | bytes 131104 | tf_op jit(solution)/shard_map/ppermute | solution.py:75
  53.8 1.6 %collective-permute-start.7 = (bf16[512,128]{1,0:T(8,128)(2,1)S(1)}, bf16[512,128]{1,0:T(8,128)(2,1)S(1)}, u32[]{:S(2)}, u32[]{:S(2)}) collective-permute-start(bf16[512,128]{1,0:T(8,128)(2,1)S(1)} %add_convert_fusion.1), channel_id=1, source_target_pairs={{0,16},{4,20},{8,24},{12,28},{16,0},{20,4},{24,8},{28,12},{1,17},{... | collective-permute-start | bytes 393224 | tf_op jit(solution)/shard_map/ppermute | solution.py:75
  55.3 13.6 %collective-permute-done.7 = bf16[512,128]{1,0:T(8,128)(2,1)S(1)} collective-permute-done((bf16[512,128]{1,0:T(8,128)(2,1)S(1)}, bf16[512,128]{1,0:T(8,128)(2,1)S(1)}, u32[]{:S(2)}, u32[]{:S(2)}) %collective-permute-start.7) | collective-permute-done | bytes 131104 | tf_op jit(solution)/shard_map/ppermute | solution.py:75
  68.9 0.5 all-gather.2.cloned.1.call-done
  69.4 1.5 convolution_convert_fusion.3
  70.9 2.0 %fusion.41 = f32[3,512,128]{2,1,0:T(8,128)S(1)} fusion(bf16[4,512,512]{2,1,0:T(8,128)(2,1)} %all-gather.2.cloned.1.call-done, bf16[512,128]{1,0:T(8,128)(2,1)S(1)} %convolution_convert_fusion.3), kind=kOutput, calls=%fused_computation.70 | convolution fusion | flops 201326592 | bytes 3014656 | tf_op jit(solution)/shard_map/kab,bc->kac/dot_general | solution.py:171
  72.9 1.9 %collective-permute-start.8 = (f32[3,512,128]{2,1,0:T(8,128)S(1)}, f32[3,512,128]{2,1,0:T(8,128)S(1)}, u32[]{:S(2)}, u32[]{:S(2)}) collective-permute-start(f32[3,512,128]{2,1,0:T(8,128)S(1)} %fusion.41), channel_id=1, source_target_pairs={{0,1},{4,5},{8,9},{12,13},{16,17},{20,21},{24,25},{28,29}} | collective-permute-start | bytes 2359304 | tf_op jit(solution)/shard_map/ppermute | solution.py:166
  74.9 1.8 %collective-permute-done.8 = f32[3,512,128]{2,1,0:T(8,128)S(1)} collective-permute-done((f32[3,512,128]{2,1,0:T(8,128)S(1)}, f32[3,512,128]{2,1,0:T(8,128)S(1)}, u32[]{:S(2)}, u32[]{:S(2)}) %collective-permute-start.8) | collective-permute-done | bytes 786464 | tf_op jit(solution)/shard_map/ppermute | solution.py:166
  76.7 0.3 convolution_convert_fusion.2
  77.0 0.4 slice_add_fusion.1
  77.5 0.7 collective-permute-start.9
  78.2 0.3 convolution_convert_fusion.1
  78.8 1.4 collective-permute-start.10
  80.2 1.7 %fusion = f32[512,128]{1,0:T(8,128)S(1)} fusion(bf16[4,512,512]{2,1,0:T(8,128)(2,1)S(1)} %copy-done.1, f32[1,512,128]{2,1,0:T(8,128)} %collective-permute-done.10, bf16[512,128]{1,0:T(8,128)(2,1)S(1)} %add_convert_fusion), kind=kOutput, calls=%fused_computation.11 | convolution fusion | flops 134545408 | bytes 1703936 | tf_op jit(solution)/shard_map/dot_general | solution.py:181
  81.9 0.6 fusion.35
  82.5 0.8 collective-permute-start.11
  83.4 0.3 fusion.20
  83.7 0.5 slice_add_fusion
  84.2 0.7 collective-permute-start.12
  84.9 0.3 fusion.19
  85.3 1.0 slice_add_fusion.2
  86.3 1.3 collective-permute-start.13
  87.6 23.0 %collective-permute-done.13 = f32[1,512,128]{2,1,0:T(8,128)} collective-permute-done((f32[1,512,128]{2,1,0:T(8,128)}, f32[1,512,128]{2,1,0:T(8,128)}, u32[]{:S(2)}, u32[]{:S(2)}) %collective-permute-start.13) | collective-permute-done | bytes 262176 | tf_op jit(solution)/shard_map/ppermute | solution.py:179
  110.6 2.0 %convolution_select_fusion = f32[512,128]{1,0:T(8,128)} fusion(f32[512,128]{1,0:T(8,128)S(1)} %fusion.19, f32[512,128]{1,0:T(8,128)S(1)} %fusion.20, f32[512,128]{1,0:T(8,128)S(1)} %fusion, bf16[4,512,512]{2,1,0:T(8,128)(2,1)S(1)} %copy-done.1, f32[1,512,128]{2,1,0:T(8,128)} %collective-permute-done.13, bf16[512,128]{1,0:T(8,128)(2,1)} %copy-done.2, ...), kind=kOutput, calls=%fused_computation.3 | convolution fusion | flops 67502080 | bytes 1966083 | tf_op jit(solution)/shard_map/dot_general | solution.py:181
  112.8 1.6 %collective-permute-start.16 = (f32[512,128]{1,0:T(8,128)}, f32[512,128]{1,0:T(8,128)S(1)}, u32[]{:S(2)}, u32[]{:S(2)}) collective-permute-start(f32[512,128]{1,0:T(8,128)} %convolution_select_fusion), channel_id=1, source_target_pairs={{0,3},{1,0},{2,1},{3,2},{4,7},{5,4},{6,5},{7,6},{8,11},{9,8},{10,9... | collective-permute-start | bytes 786440 | tf_op jit(solution)/shard_map/ppermute | solution.py:71
  114.4 6.3 %collective-permute-done.14 = f32[512,128]{1,0:T(8,128)S(1)} collective-permute-done((f32[512,128]{1,0:T(8,128)}, f32[512,128]{1,0:T(8,128)S(1)}, u32[]{:S(2)}, u32[]{:S(2)}) %collective-permute-start.14) | collective-permute-done | bytes 262176 | tf_op jit(solution)/shard_map/ppermute | solution.py:71
  120.7 1.4 collective-permute-done.15
  122.1 2.6 %collective-permute-done.16 = f32[512,128]{1,0:T(8,128)S(1)} collective-permute-done((f32[512,128]{1,0:T(8,128)}, f32[512,128]{1,0:T(8,128)S(1)}, u32[]{:S(2)}, u32[]{:S(2)}) %collective-permute-start.16) | collective-permute-done | bytes 262176 | tf_op jit(solution)/shard_map/ppermute | solution.py:71
  124.7 1.0 pad_maximum_fusion
  125.8 0.8 scatter_fusion
  126.8 0.9 pad_maximum_fusion.2.back_ref
  127.7 2.9 %shard_map.105 = bf16[4,512,128]{2,1,0:T(8,128)(2,1)} custom-call(s32[4]{0:T(128)} %bitcast.155, s32[4]{0:T(128)} %get-tuple-element.8.dests_ref, bf16[4,512,512]{2,1,0:T(8,128)(2,1)} %bitcast.144, bf16[4,512,128]{2,1,0:T(8,128)(2,1)} %pad_maximum_fusion.2.back_ref), custom_call_target="tpu_custom_call" | custom-call | tf_op jit(solution)/shard_map/pallas_call | solution.py:61
  130.6 1.1 slice_bitcast_fusion.19
  131.7 1.9 %collective-permute-start.17 = (bf16[512,128]{1,0:T(8,128)(2,1)S(1)}, bf16[512,128]{1,0:T(8,128)(2,1)S(1)}, u32[]{:S(2)}, u32[]{:S(2)}) collective-permute-start(bf16[512,128]{1,0:T(8,128)(2,1)S(1)} %get-tuple-element.18), channel_id=1, source_target_pairs={{0,3},{1,0},{2,1},{3,2},{4,7},{5,4},{6,5},{7,6},{8,11},{9,8},{10,9... | collective-permute-start | bytes 393224 | tf_op jit(solution)/shard_map/ppermute | solution.py:71
  133.5 2.7 %collective-permute-start.18 = (bf16[512,128]{1,0:T(8,128)(2,1)S(1)}, bf16[512,128]{1,0:T(8,128)(2,1)S(1)}, u32[]{:S(2)}, u32[]{:S(2)}) collective-permute-start(bf16[512,128]{1,0:T(8,128)(2,1)S(1)} %get-tuple-element.20), channel_id=1, source_target_pairs={{0,2},{1,3},{2,0},{3,1},{4,6},{5,7},{6,4},{7,5},{8,10},{9,11},{10,... | collective-permute-start | bytes 393224 | tf_op jit(solution)/shard_map/ppermute | solution.py:71
  136.2 0.7 pad_maximum_fusion.4
  137.0 5.9 %collective-permute-done.18 = bf16[512,128]{1,0:T(8,128)(2,1)S(1)} collective-permute-done((bf16[512,128]{1,0:T(8,128)(2,1)S(1)}, bf16[512,128]{1,0:T(8,128)(2,1)S(1)}, u32[]{:S(2)}, u32[]{:S(2)}) %collective-permute-start.18) | collective-permute-done | bytes 131104 | tf_op jit(solution)/shard_map/ppermute | solution.py:71
  142.9 1.2 convolution_bitcast_fusion
  144.0 0.8 copy.18
  (40 shorter events, 1.2 us)
Async XLA Ops:
  7.2 4.8 %copy-start = (bf16[1,512,512]{2,1,0:T(8,128)(2,1)S(1)}, bf16[1,512,512]{2,1,0:T(8,128)(2,1)}, u32[]{:S(2)}) copy-start(bf16[1,512,512]{2,1,0:T(8,128)(2,1)} %param.10) | copy-start | bytes 1572868
  7.2 10.5 %copy-start.5 = (s32[1,4]{1,0:T(1,128)S(1)}, s32[1,4]{1,0:T(1,128)}, u32[]{:S(2)}) copy-start(s32[1,4]{1,0:T(1,128)} %param.13) | copy-start | bytes 52
  7.2 62.2 %all-gather.2.cloned.1.call-start = ((), (), s32[]{:S(2)}) async-start(), calls=%async_computation | async-start | bytes 2359296 | tf_op jit(solution)/shard_map/all_gather | solution.py:139
  13.2 6.4 %collective-permute-start = (bf16[512,128]{1,0:T(8,128)(2,1)S(1)}, bf16[512,128]{1,0:T(8,128)(2,1)S(1)}, u32[]{:S(2)}, u32[]{:S(2)}) collective-permute-start(bf16[512,128]{1,0:T(8,128)(2,1)S(1)} %convolution_convert_fusion.4), channel_id=1, source_target_pairs={{0,1},{1,2},{2,3},{3,0},{4,5},{5,6},{6,7},{7,4},{8,9},{9,10},{10,1... | collective-permute-start | bytes 393224 | tf_op jit(solution)/shard_map/ppermute | solution.py:71
  13.7 6.8 %collective-permute-start.1 = (bf16[512,128]{1,0:T(8,128)(2,1)S(1)}, bf16[512,128]{1,0:T(8,128)(2,1)S(1)}, u32[]{:S(2)}, u32[]{:S(2)}) collective-permute-start(bf16[512,128]{1,0:T(8,128)(2,1)S(1)} %convolution_convert_fusion.4), channel_id=1, source_target_pairs={{0,2},{1,3},{2,0},{3,1},{4,6},{5,7},{6,4},{7,5},{8,10},{9,11},{10,... | collective-permute-start | bytes 393224 | tf_op jit(solution)/shard_map/ppermute | solution.py:71
  16.3 6.0 %collective-permute-start.2 = (bf16[512,128]{1,0:T(8,128)(2,1)S(1)}, bf16[512,128]{1,0:T(8,128)(2,1)S(1)}, u32[]{:S(2)}, u32[]{:S(2)}) collective-permute-start(bf16[512,128]{1,0:T(8,128)(2,1)S(1)} %convolution_convert_fusion.4), channel_id=1, source_target_pairs={{0,3},{1,0},{2,1},{3,2},{4,7},{5,4},{6,5},{7,6},{8,11},{9,8},{10,9... | collective-permute-start | bytes 393224 | tf_op jit(solution)/shard_map/ppermute | solution.py:71
  27.2 1.9 %collective-permute-start.3 = (bf16[2,512,128]{2,1,0:T(8,128)(2,1)S(1)}, bf16[2,512,128]{2,1,0:T(8,128)(2,1)S(1)}, u32[]{:S(2)}, u32[]{:S(2)}) collective-permute-start(bf16[2,512,128]{2,1,0:T(8,128)(2,1)S(1)} %dynamic-slice_bitcast_fusion), channel_id=1, source_target_pairs={{0,1},{1,0},{2,3},{3,2},{4,5},{5,4},{6,7},{7,6},{8,9},{9,8},{10,11... | collective-permute-start | bytes 786440 | tf_op jit(solution)/shard_map/ppermute | solution.py:75
  30.1 5.8 %collective-permute-start.4 = (bf16[1,512,128]{2,1,0:T(8,128)(2,1)S(1)}, bf16[1,512,128]{2,1,0:T(8,128)(2,1)S(1)}, u32[]{:S(2)}, u32[]{:S(2)}) collective-permute-start(bf16[1,512,128]{2,1,0:T(8,128)(2,1)S(1)} %constant_dynamic-slice_fusion.4), channel_id=1, source_target_pairs={{0,2},{1,3},{2,0},{3,1},{4,6},{5,7},{6,4},{7,5},{8,10},{9,11},{10,... | collective-permute-start | bytes 393224 | tf_op jit(solution)/shard_map/ppermute | solution.py:75
  36.0 5.4 %collective-permute-start.5 = (bf16[512,128]{1,0:T(8,128)(2,1)S(1)}, bf16[512,128]{1,0:T(8,128)(2,1)S(1)}, u32[]{:S(2)}, u32[]{:S(2)}) collective-permute-start(bf16[512,128]{1,0:T(8,128)(2,1)S(1)} %fusion.21), channel_id=1, source_target_pairs={{0,4},{4,0},{8,12},{12,8},{16,20},{20,16},{24,28},{28,24},{1,5},{5... | collective-permute-start | bytes 393224 | tf_op jit(solution)/shard_map/ppermute | solution.py:75
  41.5 12.2 %collective-permute-start.6 = (bf16[512,128]{1,0:T(8,128)(2,1)S(1)}, bf16[512,128]{1,0:T(8,128)(2,1)S(1)}, u32[]{:S(2)}, u32[]{:S(2)}) collective-permute-start(bf16[512,128]{1,0:T(8,128)(2,1)S(1)} %add_convert_fusion.2), channel_id=1, source_target_pairs={{0,8},{4,12},{8,0},{12,4},{16,24},{20,28},{24,16},{28,20},{1,9},{5... | collective-permute-start | bytes 393224 | tf_op jit(solution)/shard_map/ppermute | solution.py:75
  53.8 15.1 %collective-permute-start.7 = (bf16[512,128]{1,0:T(8,128)(2,1)S(1)}, bf16[512,128]{1,0:T(8,128)(2,1)S(1)}, u32[]{:S(2)}, u32[]{:S(2)}) collective-permute-start(bf16[512,128]{1,0:T(8,128)(2,1)S(1)} %add_convert_fusion.1), channel_id=1, source_target_pairs={{0,16},{4,20},{8,24},{12,28},{16,0},{20,4},{24,8},{28,12},{1,17},{... | collective-permute-start | bytes 393224 | tf_op jit(solution)/shard_map/ppermute | solution.py:75
  69.4 7.3 %copy-start.1 = (bf16[4,512,512]{2,1,0:T(8,128)(2,1)S(1)}, bf16[4,512,512]{2,1,0:T(8,128)(2,1)}, u32[]{:S(2)}) copy-start(bf16[4,512,512]{2,1,0:T(8,128)(2,1)} %all-gather.2.cloned.1.call-done) | copy-start | bytes 6291460
  70.9 6.6 %copy-start.2 = (bf16[512,128]{1,0:T(8,128)(2,1)}, bf16[512,128]{1,0:T(8,128)(2,1)S(1)}, u32[]{:S(2)}) copy-start(bf16[512,128]{1,0:T(8,128)(2,1)S(1)} %convolution_convert_fusion.3) | copy-start | bytes 393220
  72.9 3.8 %collective-permute-start.8 = (f32[3,512,128]{2,1,0:T(8,128)S(1)}, f32[3,512,128]{2,1,0:T(8,128)S(1)}, u32[]{:S(2)}, u32[]{:S(2)}) collective-permute-start(f32[3,512,128]{2,1,0:T(8,128)S(1)} %fusion.41), channel_id=1, source_target_pairs={{0,1},{4,5},{8,9},{12,13},{16,17},{20,21},{24,25},{28,29}} | collective-permute-start | bytes 2359304 | tf_op jit(solution)/shard_map/ppermute | solution.py:166
  77.0 1.8 %copy-start.3 = (bf16[512,128]{1,0:T(8,128)(2,1)}, bf16[512,128]{1,0:T(8,128)(2,1)S(1)}, u32[]{:S(2)}) copy-start(bf16[512,128]{1,0:T(8,128)(2,1)S(1)} %convolution_convert_fusion.2) | copy-start | bytes 393220
  77.5 0.7 collective-permute-start.9
  78.8 1.4 collective-permute-start.10
  82.5 2.4 %copy-start.4 = (bf16[512,128]{1,0:T(8,128)(2,1)S(1)}, bf16[512,128]{1,0:T(8,128)(2,1)}, u32[]{:S(2)}) copy-start(bf16[512,128]{1,0:T(8,128)(2,1)} %copy-done.3) | copy-start | bytes 393220
  82.5 0.9 collective-permute-start.11
  84.2 0.7 collective-permute-start.12
  86.3 24.3 %collective-permute-start.13 = (f32[1,512,128]{2,1,0:T(8,128)}, f32[1,512,128]{2,1,0:T(8,128)}, u32[]{:S(2)}, u32[]{:S(2)}) collective-permute-start(f32[1,512,128]{2,1,0:T(8,128)} %slice_add_fusion.2), channel_id=1, source_target_pairs={{1,0},{5,4},{9,8},{13,12},{17,16},{21,20},{25,24},{29,28}} | collective-permute-start | bytes 786440 | tf_op jit(solution)/shard_map/ppermute | solution.py:179
  112.6 8.1 %collective-permute-start.14 = (f32[512,128]{1,0:T(8,128)}, f32[512,128]{1,0:T(8,128)S(1)}, u32[]{:S(2)}, u32[]{:S(2)}) collective-permute-start(f32[512,128]{1,0:T(8,128)} %convolution_select_fusion), channel_id=1, source_target_pairs={{0,1},{1,2},{2,3},{3,0},{4,5},{5,6},{6,7},{7,4},{8,9},{9,10},{10,1... | collective-permute-start | bytes 786440 | tf_op jit(solution)/shard_map/ppermute | solution.py:71
  112.8 9.4 %collective-permute-start.15 = (f32[512,128]{1,0:T(8,128)}, f32[512,128]{1,0:T(8,128)S(1)}, u32[]{:S(2)}, u32[]{:S(2)}) collective-permute-start(f32[512,128]{1,0:T(8,128)} %convolution_select_fusion), channel_id=1, source_target_pairs={{0,2},{1,3},{2,0},{3,1},{4,6},{5,7},{6,4},{7,5},{8,10},{9,11},{10,... | collective-permute-start | bytes 786440 | tf_op jit(solution)/shard_map/ppermute | solution.py:71
  112.8 11.9 %collective-permute-start.16 = (f32[512,128]{1,0:T(8,128)}, f32[512,128]{1,0:T(8,128)S(1)}, u32[]{:S(2)}, u32[]{:S(2)}) collective-permute-start(f32[512,128]{1,0:T(8,128)} %convolution_select_fusion), channel_id=1, source_target_pairs={{0,3},{1,0},{2,1},{3,2},{4,7},{5,4},{6,5},{7,6},{8,11},{9,8},{10,9... | collective-permute-start | bytes 786440 | tf_op jit(solution)/shard_map/ppermute | solution.py:71
  131.7 5.3 %collective-permute-start.17 = (bf16[512,128]{1,0:T(8,128)(2,1)S(1)}, bf16[512,128]{1,0:T(8,128)(2,1)S(1)}, u32[]{:S(2)}, u32[]{:S(2)}) collective-permute-start(bf16[512,128]{1,0:T(8,128)(2,1)S(1)} %get-tuple-element.18), channel_id=1, source_target_pairs={{0,3},{1,0},{2,1},{3,2},{4,7},{5,4},{6,5},{7,6},{8,11},{9,8},{10,9... | collective-permute-start | bytes 393224 | tf_op jit(solution)/shard_map/ppermute | solution.py:71
  133.5 9.3 %collective-permute-start.18 = (bf16[512,128]{1,0:T(8,128)(2,1)S(1)}, bf16[512,128]{1,0:T(8,128)(2,1)S(1)}, u32[]{:S(2)}, u32[]{:S(2)}) collective-permute-start(bf16[512,128]{1,0:T(8,128)(2,1)S(1)} %get-tuple-element.20), channel_id=1, source_target_pairs={{0,2},{1,3},{2,0},{3,1},{4,6},{5,7},{6,4},{7,5},{8,10},{9,11},{10,... | collective-permute-start | bytes 393224 | tf_op jit(solution)/shard_map/ppermute | solution.py:71
  136.2 6.7 %collective-permute-start.19 = (bf16[512,128]{1,0:T(8,128)(2,1)S(1)}, bf16[512,128]{1,0:T(8,128)(2,1)S(1)}, u32[]{:S(2)}, u32[]{:S(2)}) collective-permute-start(bf16[512,128]{1,0:T(8,128)(2,1)S(1)} %get-tuple-element.19), channel_id=1, source_target_pairs={{0,1},{1,2},{2,3},{3,0},{4,5},{5,6},{6,7},{7,4},{8,9},{9,10},{10,1... | collective-permute-start | bytes 393224 | tf_op jit(solution)/shard_map/ppermute | solution.py:71
Sparse Core Ops, SparseCore 0:
  12.1 57.3 all-gather.1

commit v10 on v9

--- a/solution.py
+++ b/solution.py
@@ -1,3 +1,5 @@
+import functools
+
 import jax
 import jax.numpy as jnp
 import numpy as np
@@ -81,6 +83,76 @@
         part = lax.ppermute(x, axis, [(owner, (owner + s) % size)])
         got = part if got is None else got + part
     return jnp.where(me == owner, x, got)
+
+
+def tail_kernel(levels, peers, rows_ref, dests_ref, table_ref, start_ref, tiles_ref, *refs):
+    x_refs = refs[:peers]
+    term_refs = refs[peers : 2 * peers]
+    slices_ref = refs[2 * peers]
+    acc_ref = refs[2 * peers + 1]
+    share = slices_ref.shape[1]
+    start = pl.multiple_of(start_ref[0], 8)
+    for t in range(levels):
+        for p in range(peers):
+
+            @pl.when(table_ref[t] == p)
+            def _():
+                slices_ref[t] = x_refs[p][pl.ds(start, share), :]
+
+    acc_ref[...] = jnp.zeros_like(acc_ref)
+    for s in range(tiles_ref.shape[0]):
+        level = rows_ref[s]
+        piece = table_ref[jnp.maximum(level, 0)]
+        for p in range(peers):
+
+            @pl.when((level >= 0) & (piece == p))
+            def _():
+                prod = lax.dot_general(
+                    tiles_ref[s],
+                    x_refs[p][...].astype(jnp.bfloat16),
+                    (((0,), (0,)), ((), ())),
+                    preferred_element_type=jnp.float32,
+                )
+                acc_ref[dests_ref[s]] += prod
+
+    for p in range(peers):
+        term_refs[p][...] = acc_ref[p].astype(jnp.bfloat16)
+
+
+def tail_terms(slot_rows, dests, table, start, tiles, pieces, levels, share):
+    peers = len(pieces)
+    shape = pieces[0].shape
+    outs = [jax.ShapeDtypeStruct(shape, jnp.bfloat16) for _ in range(peers)]
+    outs.append(jax.ShapeDtypeStruct((levels, share, shape[1]), jnp.float32))
+    result = pl.pallas_call(
+        functools.partial(tail_kernel, levels, peers),
+        out_shape=outs,
+        in_specs=[SMEM] * 4 + [VMEM] * (1 + peers),
+        out_specs=[VMEM] * (peers + 1),
+        scratch_shapes=[pltpu.VMEM((peers,) + shape, jnp.float32)],
+    )(slot_rows, dests, table, start, tiles, *pieces)
+    return result[:peers], result[peers]
+
+
+def last_kernel(forward_ref, inv_ref, *refs):
+    term_refs = refs[:-1]
+    out_ref = refs[-1]
+    returned = term_refs[0][...].astype(jnp.float32)
+    for ref in term_refs[1:]:
+        returned = returned + ref[...].astype(jnp.float32)
+    update = (forward_ref[...].astype(jnp.float32) - returned).astype(jnp.bfloat16)
+    out_ref[0] = lax.dot_general(
+        inv_ref[0], update, (((0,), (0,)), ((), ())), preferred_element_type=jnp.float32
+    )
+
+
+def last_solve(forward, inv, terms):
+    return pl.pallas_call(
+        last_kernel,
+        out_shape=jax.ShapeDtypeStruct((1,) + forward.shape, jnp.float32),
+        in_specs=[VMEM] * (2 + len(terms)),
+        out_specs=VMEM,
+    )(forward, inv, *terms)
 
 
 def pair_index(t, u):
@@ -187,21 +259,14 @@
                 "uab,ac->ubc", mats[1 : level + 1], solved.astype(jnp.bfloat16), preferred_element_type=jnp.float32
             )
             pushed = earlier if level == levels - 1 else pushed[:level] + earlier
-    solutions = gathered_chunks(own_solution, peers, me)[:levels]
-    top_slices = [lax.dynamic_slice_in_dim(solutions[t], position * share, share, 0) for t in range(levels)]
-    top_back = [solutions[t].astype(jnp.bfloat16) for t in range(levels)]
-
-    back_stack = jnp.stack(top_back)
+    pieces = [own_solution] + [shifted(own_solution, "col", peers, s) for s in range(1, peers)]
+    table = ((me - jnp.arange(levels)) % peers).astype(jnp.int32)
     dests = ((me - slot_cols) % peers).astype(jnp.int32)
-    terms = back_terms(slot_rows, dests, own_tiles, back_stack, peers)
-    returned = terms[0].astype(jnp.float32)
-    for s in range(1, peers):
-        returned = returned + shifted(terms[s], "col", peers, peers - s).astype(jnp.float32)
-    low_update = (low_forward.astype(jnp.float32) - returned).astype(jnp.bfloat16)
-    low_solution = lax.dot_general(
-        low_inv[0], low_update, (((0,), (0,)), ((), ())), preferred_element_type=jnp.float32
-    )
-    return (low_solution[None], jnp.stack(top_slices))
+    start = (position * share)[None].astype(jnp.int32)
+    terms, top_rows = tail_terms(slot_rows, dests, table, start, own_tiles, pieces, levels, share)
+    returned = [terms[0]] + [shifted(terms[s], "col", peers, peers - s) for s in range(1, peers)]
+    low_solution = last_solve(low_forward, low_inv, returned)
+    return (low_solution, top_rows)
 
 
 def solution(mesh):

time: 153 us -> 146 us (0.954)
  matrix products: 13.8 us -> 10.4 us
  starting transfers between devices: 25.7 us -> 22.8 us
  Pallas kernels: 5.96 us -> 8.63 us
  local copies, waits for them, and re-layouts: 6.37 us -> 3.81 us
  other arithmetic: 8.73 us -> 6.23 us
  waiting for transfers between devices: 76.9 us -> 79.3 us
    pallas_call x1 -> x2, Pallas kernels: 2.92 us -> 5.6 us  [the longest x1 3.31 us: tail_terms(): pl.pallas_call(functools.partial(tail_kernel, levels, peers), out_shape=o...]
    ppermute x9, waiting for transfers between devices: 19.1 us -> 21.7 us  [shifted(): return lax.ppermute(x, axis, [(i, (i + shift) % size) for i in range(size)])]
    another operation x3 -> x0, other arithmetic: 2.54 us -> none  [the longest x1 1.02 us: gathered_chunks(): stacked = jnp.stack(pieces)]
    dot_general x4, matrix products: 4.4 us -> 2.74 us  [local(): lax.dot_general(inv, update.astype(jnp.bfloat16), (((0,), (0,)), ((), ())...]
    ppermute x9, starting transfers between devices: 10.8 us -> 9.26 us  [shifted(): return lax.ppermute(x, axis, [(i, (i + shift) % size) for i in range(size)])]
where the time goes in v10:
time: 146 us
  waiting for transfers between devices  79.3 us (54%)
  starting transfers between devices  22.8 us (16%)
  between operations  14.4 us (10%)
  matrix products  10.4 us (7%)
  Pallas kernels  8.63 us (6%)
  other arithmetic  6.23 us (4%)
  local copies, waits for them, and re-layouts  3.81 us (3%)
    ppermute x5, waiting for transfers between devices, swapped(): return lax.ppermute(x, axis, [(i, i ^ bit) for i in range(size)])  32 us
    ppermute x3, waiting for transfers between devices, local(): pushed = lax.ppermute(pushed, 'col', [(level + 1, level)])  23.3 us
    ppermute x9, waiting for transfers between devices, shifted(): return lax.ppermute(x, axis, [(i, (i + shift) % size) for i in range(size)])  21.7 us
    ppermute x9, starting transfers between devices, shifted(): return lax.ppermute(x, axis, [(i, (i + shift) % size) for i in range(size)])  9.26 us
    ppermute x5, starting transfers between devices, swapped(): return lax.ppermute(x, axis, [(i, i ^ bit) for i in range(size)])  7.56 us
    pallas_call x1, Pallas kernels, tail_terms(): pl.pallas_call(functools.partial(tail_kernel, levels, peers), out_shape=o...  3.31 us
    ppermute x3, starting transfers between devices, local(): pushed = lax.ppermute(pushed, 'col', [(level - 1, level)])  3.28 us
    pallas_call x1, Pallas kernels, coupling_terms(): pl.pallas_call(coupling_kernel, out_shape=jax.ShapeDtypeStruct(shape, jnp...  3.03 us
  transfers between devices with their start and end apart: 21, of which 15 were waited for; matrix products, arithmetic and copies ran while one was open for 4% of the time, Pallas kernels for 2%

profile of v10, /device:TPU:0, one launch (start us, length us, event | category | flops | bytes accessed | tf_op | source)
XLA Modules:
  0.0 145.6 jit_solution(15690143337460190695)
XLA Ops:
  7.2 0.7 fusion.46
  8.0 0.7 compare_and_fusion
  8.7 0.9 constant_dynamic-slice_fusion.2
  9.5 0.6 gather_fusion
  10.1 0.1 broadcast_select_fusion
  10.2 0.7 pad_maximum_fusion.1
  11.0 1.4 convolution_convert_fusion.4.forward_ref
  12.3 2.5 %collective-permute-start.2 = (bf16[512,128]{1,0:T(8,128)(2,1)S(1)}, bf16[512,128]{1,0:T(8,128)(2,1)S(1)}, u32[]{:S(2)}, u32[]{:S(2)}) collective-permute-start(bf16[512,128]{1,0:T(8,128)(2,1)S(1)} %convolution_convert_fusion.4.forward_ref), channel_id=1, source_target_pairs={{0,3},{1,0},{2,1},{3,2},{4,7},{5,4},{6,5},{7,6},{8,11},{9,8},{10,9... | collective-permute-start | bytes 393224 | tf_op jit(solution)/shard_map/ppermute | solution.py:73
  14.8 0.6 collective-permute-start.1
  15.4 0.2 collective-permute-start
  15.6 0.6 and_select_fusion.1
  16.2 0.8 iota_reduce_fusion
  17.0 0.6 pad_add_fusion.fold_ref
  17.5 1.1 collective-permute-done.2
  18.6 3.8 %collective-permute-done.1 = bf16[512,128]{1,0:T(8,128)(2,1)S(1)} collective-permute-done((bf16[512,128]{1,0:T(8,128)(2,1)S(1)}, bf16[512,128]{1,0:T(8,128)(2,1)S(1)}, u32[]{:S(2)}, u32[]{:S(2)}) %collective-permute-start.1) | collective-permute-done | bytes 131104 | tf_op jit(solution)/shard_map/ppermute | solution.py:73
  22.4 0.9 pad_maximum_fusion.panels_ref
  23.2 3.0 %shard_map.104 = bf16[4,512,128]{2,1,0:T(8,128)(2,1)} custom-call(s32[4]{0:T(128)} %bitcast.127, s32[4]{0:T(128)} %get-tuple-element.8.picks_ref, s32[2]{0:T(128)} %pad_add_fusion.fold_ref, bf16[4,512,512]{2,1,0:T(8,128)(2,1)} %bitcast.119, bf16[4,512,128]{2,1,0:T(8,128)(2,1)} %pad_maximum_fusion.panels_ref, bf16[4,64,128]{2,1,0:T(8,128)(2,1)} %rhs_ref.1), custom_call_target="tpu_custom_call" | custom-call | tf_op jit(solution)/shard_map/pallas_call | solution.py:37
  26.3 1.0 dynamic-slice_bitcast_fusion
  27.2 0.1 collective-permute-start.3
  27.3 1.5 %collective-permute-done.3 = bf16[2,512,128]{2,1,0:T(8,128)(2,1)S(1)} collective-permute-done((bf16[2,512,128]{2,1,0:T(8,128)(2,1)S(1)}, bf16[2,512,128]{2,1,0:T(8,128)(2,1)S(1)}, u32[]{:S(2)}, u32[]{:S(2)}) %collective-permute-start.3) | collective-permute-done | bytes 262176 | tf_op jit(solution)/shard_map/ppermute | solution.py:77
  28.8 1.0 fusion.1
  29.9 2.0 %collective-permute-start.4 = (bf16[1,512,128]{2,1,0:T(8,128)(2,1)S(1)}, bf16[1,512,128]{2,1,0:T(8,128)(2,1)S(1)}, u32[]{:S(2)}, u32[]{:S(2)}) collective-permute-start(bf16[1,512,128]{2,1,0:T(8,128)(2,1)S(1)} %constant_dynamic-slice_fusion), channel_id=1, source_target_pairs={{0,2},{1,3},{2,0},{3,1},{4,6},{5,7},{6,4},{7,5},{8,10},{9,11},{10,... | collective-permute-start | bytes 393224 | tf_op jit(solution)/shard_map/ppermute | solution.py:77
  31.9 3.8 %collective-permute-done.4 = bf16[1,512,128]{2,1,0:T(8,128)(2,1)S(1)} collective-permute-done((bf16[1,512,128]{2,1,0:T(8,128)(2,1)S(1)}, bf16[1,512,128]{2,1,0:T(8,128)(2,1)S(1)}, u32[]{:S(2)}, u32[]{:S(2)}) %collective-permute-start.4) | collective-permute-done | bytes 131104 | tf_op jit(solution)/shard_map/ppermute | solution.py:77
  35.7 2.4 %collective-permute-start.5 = (bf16[512,128]{1,0:T(8,128)(2,1)S(1)}, bf16[512,128]{1,0:T(8,128)(2,1)S(1)}, u32[]{:S(2)}, u32[]{:S(2)}) collective-permute-start(bf16[512,128]{1,0:T(8,128)(2,1)S(1)} %fusion.16), channel_id=1, source_target_pairs={{0,4},{4,0},{8,12},{12,8},{16,20},{20,16},{24,28},{28,24},{1,5},{5... | collective-permute-start | bytes 393224 | tf_op jit(solution)/shard_map/ppermute | solution.py:77
  38.2 2.9 %collective-permute-done.5 = bf16[512,128]{1,0:T(8,128)(2,1)S(1)} collective-permute-done((bf16[512,128]{1,0:T(8,128)(2,1)S(1)}, bf16[512,128]{1,0:T(8,128)(2,1)S(1)}, u32[]{:S(2)}, u32[]{:S(2)}) %collective-permute-start.5) | collective-permute-done | bytes 131104 | tf_op jit(solution)/shard_map/ppermute | solution.py:77
  41.1 1.6 %collective-permute-start.6 = (bf16[512,128]{1,0:T(8,128)(2,1)S(1)}, bf16[512,128]{1,0:T(8,128)(2,1)S(1)}, u32[]{:S(2)}, u32[]{:S(2)}) collective-permute-start(bf16[512,128]{1,0:T(8,128)(2,1)S(1)} %add_convert_fusion.2), channel_id=1, source_target_pairs={{0,8},{4,12},{8,0},{12,4},{16,24},{20,28},{24,16},{28,20},{1,9},{5... | collective-permute-start | bytes 393224 | tf_op jit(solution)/shard_map/ppermute | solution.py:77
  42.7 10.0 %collective-permute-done.6 = bf16[512,128]{1,0:T(8,128)(2,1)S(1)} collective-permute-done((bf16[512,128]{1,0:T(8,128)(2,1)S(1)}, bf16[512,128]{1,0:T(8,128)(2,1)S(1)}, u32[]{:S(2)}, u32[]{:S(2)}) %collective-permute-start.6) | collective-permute-done | bytes 131104 | tf_op jit(solution)/shard_map/ppermute | solution.py:77
  52.8 1.5 %collective-permute-start.7 = (bf16[512,128]{1,0:T(8,128)(2,1)S(1)}, bf16[512,128]{1,0:T(8,128)(2,1)S(1)}, u32[]{:S(2)}, u32[]{:S(2)}) collective-permute-start(bf16[512,128]{1,0:T(8,128)(2,1)S(1)} %add_convert_fusion.1), channel_id=1, source_target_pairs={{0,16},{4,20},{8,24},{12,28},{16,0},{20,4},{24,8},{28,12},{1,17},{... | collective-permute-start | bytes 393224 | tf_op jit(solution)/shard_map/ppermute | solution.py:77
  54.3 13.7 %collective-permute-done.7 = bf16[512,128]{1,0:T(8,128)(2,1)S(1)} collective-permute-done((bf16[512,128]{1,0:T(8,128)(2,1)S(1)}, bf16[512,128]{1,0:T(8,128)(2,1)S(1)}, u32[]{:S(2)}, u32[]{:S(2)}) %collective-permute-start.7) | collective-permute-done | bytes 131104 | tf_op jit(solution)/shard_map/ppermute | solution.py:77
  68.0 0.5 all-gather.2.cloned.1.call-done
  68.5 1.5 %convolution_convert_fusion.3 = bf16[512,128]{1,0:T(8,128)(2,1)S(1)} fusion(bf16[4,512,512]{2,1,0:T(8,128)(2,1)} %all-gather.2.cloned.1.call-done, bf16[512,128]{1,0:T(8,128)(2,1)S(1)} %add_convert_fusion), kind=kOutput, calls=%fused_computation.7 | convolution fusion | flops 67371008 | bytes 786432 | tf_op jit(solution)/shard_map/dot_general | solution.py:240
  70.0 2.0 %fusion.35 = f32[3,512,128]{2,1,0:T(8,128)S(1)} fusion(bf16[4,512,512]{2,1,0:T(8,128)(2,1)} %all-gather.2.cloned.1.call-done, bf16[512,128]{1,0:T(8,128)(2,1)S(1)} %convolution_convert_fusion.3), kind=kOutput, calls=%fused_computation.55 | convolution fusion | flops 201326592 | bytes 3014656 | tf_op jit(solution)/shard_map/kab,bc->kac/dot_general | solution.py:243
  72.1 1.9 %collective-permute-start.8 = (f32[3,512,128]{2,1,0:T(8,128)S(1)}, f32[3,512,128]{2,1,0:T(8,128)S(1)}, u32[]{:S(2)}, u32[]{:S(2)}) collective-permute-start(f32[3,512,128]{2,1,0:T(8,128)S(1)} %fusion.35), channel_id=1, source_target_pairs={{0,1},{4,5},{8,9},{12,13},{16,17},{20,21},{24,25},{28,29}} | collective-permute-start | bytes 2359304 | tf_op jit(solution)/shard_map/ppermute | solution.py:238
  74.0 1.8 %collective-permute-done.8 = f32[3,512,128]{2,1,0:T(8,128)S(1)} collective-permute-done((f32[3,512,128]{2,1,0:T(8,128)S(1)}, f32[3,512,128]{2,1,0:T(8,128)S(1)}, u32[]{:S(2)}, u32[]{:S(2)}) %collective-permute-start.8) | collective-permute-done | bytes 786464 | tf_op jit(solution)/shard_map/ppermute | solution.py:238
  75.8 0.3 convolution_convert_fusion.2
  76.1 0.4 slice_add_fusion.1
  76.6 0.7 collective-permute-start.9
  77.3 0.3 convolution_convert_fusion.1
  77.6 0.3 slice_add_fusion.3
  77.9 0.7 collective-permute-start.10
  78.6 0.7 fusion
  79.3 0.6 fusion.29
  80.0 0.7 collective-permute-start.11
  80.7 0.3 fusion.15
  81.0 0.5 slice_add_fusion
  81.5 0.7 collective-permute-start.12
  82.2 0.3 fusion.14
  82.6 0.3 slice_add_fusion.2
  82.9 1.3 collective-permute-start.13
  84.2 23.3 %collective-permute-done.13 = f32[1,512,128]{2,1,0:T(8,128)} collective-permute-done((f32[1,512,128]{2,1,0:T(8,128)S(1)}, f32[1,512,128]{2,1,0:T(8,128)}, u32[]{:S(2)}, u32[]{:S(2)}) %collective-permute-start.13) | collective-permute-done | bytes 262176 | tf_op jit(solution)/shard_map/ppermute | solution.py:251
  107.5 1.3 convolution_select_fusion.refs_0_
  108.9 0.2 collective-permute-start.14
  109.1 1.6 %collective-permute-start.16 = (f32[512,128]{1,0:T(8,128)S(1)}, f32[512,128]{1,0:T(8,128)S(1)}, u32[]{:S(2)}, u32[]{:S(2)}) collective-permute-start(f32[512,128]{1,0:T(8,128)S(1)} %convolution_select_fusion.refs_0_), channel_id=1, source_target_pairs={{0,3},{1,0},{2,1},{3,2},{4,7},{5,4},{6,5},{7,6},{8,11},{9,8},{10,9... | collective-permute-start | bytes 786440 | tf_op jit(solution)/shard_map/ppermute | solution.py:73
  110.7 6.1 %collective-permute-done.14.refs_1_ = f32[512,128]{1,0:T(8,128)S(1)} collective-permute-done((f32[512,128]{1,0:T(8,128)S(1)}, f32[512,128]{1,0:T(8,128)S(1)}, u32[]{:S(2)}, u32[]{:S(2)}) %collective-permute-start.14) | collective-permute-done | bytes 262176 | tf_op jit(solution)/shard_map/ppermute | solution.py:73
  116.8 1.4 collective-permute-done.15.refs_2_
  118.2 2.5 %collective-permute-done.16.refs_3_ = f32[512,128]{1,0:T(8,128)S(1)} collective-permute-done((f32[512,128]{1,0:T(8,128)S(1)}, f32[512,128]{1,0:T(8,128)S(1)}, u32[]{:S(2)}, u32[]{:S(2)}) %collective-permute-start.16) | collective-permute-done | bytes 262176 | tf_op jit(solution)/shard_map/ppermute | solution.py:73
  120.7 0.7 copy-done.7
  121.4 3.3 %shard_map.105 = (bf16[512,128]{1,0:T(8,128)(2,1)}, bf16[512,128]{1,0:T(8,128)(2,1)}, bf16[512,128]{1,0:T(8,128)(2,1)}, bf16[512,128]{1,0:T(8,128)(2,1)}, f32[4,64,128]{2,1,0:T(8,128)}) custom-call(s32[4]{0:T(128)} %bitcast.128, s32[4]{0:T(128)} %get-tuple-element.14.dests_ref, s32[4]{0:T(128)} %copy-done.11, s32[1]{0:T(128)} %bitcast.4.start_ref, ...), custom_call_target="tpu_custom_call" | custom-call | tf_op jit(solution)/shard_map/pallas_call | solution.py:127
  124.7 1.9 %collective-permute-start.17 = (bf16[512,128]{1,0:T(8,128)(2,1)}, bf16[512,128]{1,0:T(8,128)(2,1)S(1)}, u32[]{:S(2)}, u32[]{:S(2)}) collective-permute-start(bf16[512,128]{1,0:T(8,128)(2,1)} %get-tuple-element.10), channel_id=1, source_target_pairs={{0,3},{1,0},{2,1},{3,2},{4,7},{5,4},{6,5},{7,6},{8,11},{9,8},{10,9... | collective-permute-start | bytes 393224 | tf_op jit(solution)/shard_map/ppermute | solution.py:73
  126.6 2.3 %collective-permute-start.18 = (bf16[512,128]{1,0:T(8,128)(2,1)}, bf16[512,128]{1,0:T(8,128)(2,1)S(1)}, u32[]{:S(2)}, u32[]{:S(2)}) collective-permute-start(bf16[512,128]{1,0:T(8,128)(2,1)} %get-tuple-element.11), channel_id=1, source_target_pairs={{0,2},{1,3},{2,0},{3,1},{4,6},{5,7},{6,4},{7,5},{8,10},{9,11},{10,... | collective-permute-start | bytes 393224 | tf_op jit(solution)/shard_map/ppermute | solution.py:73
  128.9 1.8 %collective-permute-done.17.refs_1_ = bf16[512,128]{1,0:T(8,128)(2,1)S(1)} collective-permute-done((bf16[512,128]{1,0:T(8,128)(2,1)}, bf16[512,128]{1,0:T(8,128)(2,1)S(1)}, u32[]{:S(2)}, u32[]{:S(2)}) %collective-permute-start.17) | collective-permute-done | bytes 131104 | tf_op jit(solution)/shard_map/ppermute | solution.py:73
  130.7 5.1 %collective-permute-done.18.refs_2_ = bf16[512,128]{1,0:T(8,128)(2,1)S(1)} collective-permute-done((bf16[512,128]{1,0:T(8,128)(2,1)}, bf16[512,128]{1,0:T(8,128)(2,1)S(1)}, u32[]{:S(2)}, u32[]{:S(2)}) %collective-permute-start.18) | collective-permute-done | bytes 131104 | tf_op jit(solution)/shard_map/ppermute | solution.py:73
  135.8 0.6 copy-done.9
  136.4 2.3 %shard_map.106 = f32[1,512,128]{2,1,0:T(8,128)} custom-call(bf16[512,128]{1,0:T(8,128)(2,1)} %copy-done.2, bf16[1,512,512]{2,1,0:T(8,128)(2,1)} %inv_ref.1, bf16[512,128]{1,0:T(8,128)(2,1)} %get-tuple-element.9.refs_0_, bf16[512,128]{1,0:T(8,128)(2,1)} %copy-done.8, bf16[512,128]{1,0:T(8,128)(2,1)} %copy-done.9, bf16[512,128]{1,0:T(8,128)(2,1)} %copy-done.10), custom_call_target="tpu_custom_call" | custom-call | tf_op jit(solution)/shard_map/pallas_call | solution.py:150
  (40 shorter events, 0.4 us)
Async XLA Ops:
  7.2 2.4 %copy-start = (bf16[6,64,512]{2,1,0:T(8,128)(2,1)S(1)}, bf16[6,64,512]{2,1,0:T(8,128)(2,1)}, u32[]{:S(2)}) copy-start(bf16[6,64,512]{2,1,0:T(8,128)(2,1)} %param.16) | copy-start | bytes 1179652
  7.2 8.4 %copy-start.12 = (s32[1,4]{1,0:T(1,128)S(1)}, s32[1,4]{1,0:T(1,128)}, u32[]{:S(2)}) copy-start(s32[1,4]{1,0:T(1,128)} %param.13) | copy-start | bytes 52
  7.2 61.3 %all-gather.2.cloned.1.call-start = ((), (), s32[]{:S(2)}) async-start(), calls=%async_computation | async-start | bytes 2359296 | tf_op jit(solution)/shard_map/all_gather | solution.py:211
  12.3 13.9 %copy-start.2 = (bf16[512,128]{1,0:T(8,128)(2,1)}, bf16[512,128]{1,0:T(8,128)(2,1)S(1)}, u32[]{:S(2)}) copy-start(bf16[512,128]{1,0:T(8,128)(2,1)S(1)} %convolution_convert_fusion.4.forward_ref) | copy-start | bytes 393220
  12.3 6.3 %collective-permute-start.2 = (bf16[512,128]{1,0:T(8,128)(2,1)S(1)}, bf16[512,128]{1,0:T(8,128)(2,1)S(1)}, u32[]{:S(2)}, u32[]{:S(2)}) collective-permute-start(bf16[512,128]{1,0:T(8,128)(2,1)S(1)} %convolution_convert_fusion.4.forward_ref), channel_id=1, source_target_pairs={{0,3},{1,0},{2,1},{3,2},{4,7},{5,4},{6,5},{7,6},{8,11},{9,8},{10,9... | collective-permute-start | bytes 393224 | tf_op jit(solution)/shard_map/ppermute | solution.py:73
  14.8 7.5 %collective-permute-start.1 = (bf16[512,128]{1,0:T(8,128)(2,1)S(1)}, bf16[512,128]{1,0:T(8,128)(2,1)S(1)}, u32[]{:S(2)}, u32[]{:S(2)}) collective-permute-start(bf16[512,128]{1,0:T(8,128)(2,1)S(1)} %convolution_convert_fusion.4.forward_ref), channel_id=1, source_target_pairs={{0,2},{1,3},{2,0},{3,1},{4,6},{5,7},{6,4},{7,5},{8,10},{9,11},{10,... | collective-permute-start | bytes 393224 | tf_op jit(solution)/shard_map/ppermute | solution.py:73
  15.4 6.9 %collective-permute-start = (bf16[512,128]{1,0:T(8,128)(2,1)S(1)}, bf16[512,128]{1,0:T(8,128)(2,1)S(1)}, u32[]{:S(2)}, u32[]{:S(2)}) collective-permute-start(bf16[512,128]{1,0:T(8,128)(2,1)S(1)} %convolution_convert_fusion.4.forward_ref), channel_id=1, source_target_pairs={{0,1},{1,2},{2,3},{3,0},{4,5},{5,6},{6,7},{7,4},{8,9},{9,10},{10,1... | collective-permute-start | bytes 393224 | tf_op jit(solution)/shard_map/ppermute | solution.py:73
  16.2 10.1 %copy-start.11 = (s32[4]{0:T(128)}, s32[4]{0:T(128)S(1)}, u32[]{:S(2)}) copy-start(s32[4]{0:T(128)S(1)} %get-tuple-element.16.table_ref) | copy-start | bytes 52
  27.2 1.6 %collective-permute-start.3 = (bf16[2,512,128]{2,1,0:T(8,128)(2,1)S(1)}, bf16[2,512,128]{2,1,0:T(8,128)(2,1)S(1)}, u32[]{:S(2)}, u32[]{:S(2)}) collective-permute-start(bf16[2,512,128]{2,1,0:T(8,128)(2,1)S(1)} %dynamic-slice_bitcast_fusion), channel_id=1, source_target_pairs={{0,1},{1,0},{2,3},{3,2},{4,5},{5,4},{6,7},{7,6},{8,9},{9,8},{10,11... | collective-permute-start | bytes 786440 | tf_op jit(solution)/shard_map/ppermute | solution.py:77
  29.9 5.8 %collective-permute-start.4 = (bf16[1,512,128]{2,1,0:T(8,128)(2,1)S(1)}, bf16[1,512,128]{2,1,0:T(8,128)(2,1)S(1)}, u32[]{:S(2)}, u32[]{:S(2)}) collective-permute-start(bf16[1,512,128]{2,1,0:T(8,128)(2,1)S(1)} %constant_dynamic-slice_fusion), channel_id=1, source_target_pairs={{0,2},{1,3},{2,0},{3,1},{4,6},{5,7},{6,4},{7,5},{8,10},{9,11},{10,... | collective-permute-start | bytes 393224 | tf_op jit(solution)/shard_map/ppermute | solution.py:77
  35.7 5.4 %collective-permute-start.5 = (bf16[512,128]{1,0:T(8,128)(2,1)S(1)}, bf16[512,128]{1,0:T(8,128)(2,1)S(1)}, u32[]{:S(2)}, u32[]{:S(2)}) collective-permute-start(bf16[512,128]{1,0:T(8,128)(2,1)S(1)} %fusion.16), channel_id=1, source_target_pairs={{0,4},{4,0},{8,12},{12,8},{16,20},{20,16},{24,28},{28,24},{1,5},{5... | collective-permute-start | bytes 393224 | tf_op jit(solution)/shard_map/ppermute | solution.py:77
  41.1 11.6 %collective-permute-start.6 = (bf16[512,128]{1,0:T(8,128)(2,1)S(1)}, bf16[512,128]{1,0:T(8,128)(2,1)S(1)}, u32[]{:S(2)}, u32[]{:S(2)}) collective-permute-start(bf16[512,128]{1,0:T(8,128)(2,1)S(1)} %add_convert_fusion.2), channel_id=1, source_target_pairs={{0,8},{4,12},{8,0},{12,4},{16,24},{20,28},{24,16},{28,20},{1,9},{5... | collective-permute-start | bytes 393224 | tf_op jit(solution)/shard_map/ppermute | solution.py:77
  52.8 15.2 %collective-permute-start.7 = (bf16[512,128]{1,0:T(8,128)(2,1)S(1)}, bf16[512,128]{1,0:T(8,128)(2,1)S(1)}, u32[]{:S(2)}, u32[]{:S(2)}) collective-permute-start(bf16[512,128]{1,0:T(8,128)(2,1)S(1)} %add_convert_fusion.1), channel_id=1, source_target_pairs={{0,16},{4,20},{8,24},{12,28},{16,0},{20,4},{24,8},{28,12},{1,17},{... | collective-permute-start | bytes 393224 | tf_op jit(solution)/shard_map/ppermute | solution.py:77
  68.5 7.3 %copy-start.1 = (bf16[4,512,512]{2,1,0:T(8,128)(2,1)S(1)}, bf16[4,512,512]{2,1,0:T(8,128)(2,1)}, u32[]{:S(2)}) copy-start(bf16[4,512,512]{2,1,0:T(8,128)(2,1)} %all-gather.2.cloned.1.call-done) | copy-start | bytes 6291460
  70.0 6.6 %copy-start.4 = (bf16[512,128]{1,0:T(8,128)(2,1)}, bf16[512,128]{1,0:T(8,128)(2,1)S(1)}, u32[]{:S(2)}) copy-start(bf16[512,128]{1,0:T(8,128)(2,1)S(1)} %convolution_convert_fusion.3) | copy-start | bytes 393220
  72.1 3.8 %collective-permute-start.8 = (f32[3,512,128]{2,1,0:T(8,128)S(1)}, f32[3,512,128]{2,1,0:T(8,128)S(1)}, u32[]{:S(2)}, u32[]{:S(2)}) collective-permute-start(f32[3,512,128]{2,1,0:T(8,128)S(1)} %fusion.35), channel_id=1, source_target_pairs={{0,1},{4,5},{8,9},{12,13},{16,17},{20,21},{24,25},{28,29}} | collective-permute-start | bytes 2359304 | tf_op jit(solution)/shard_map/ppermute | solution.py:238
  76.6 0.7 collective-permute-start.9
  77.9 0.7 collective-permute-start.10
  80.0 0.7 collective-permute-start.11
  81.5 0.7 collective-permute-start.12
  82.9 24.6 %collective-permute-start.13 = (f32[1,512,128]{2,1,0:T(8,128)S(1)}, f32[1,512,128]{2,1,0:T(8,128)}, u32[]{:S(2)}, u32[]{:S(2)}) collective-permute-start(f32[1,512,128]{2,1,0:T(8,128)S(1)} %slice_add_fusion.2), channel_id=1, source_target_pairs={{1,0},{5,4},{9,8},{13,12},{17,16},{21,20},{25,24},{29,28}} | collective-permute-start | bytes 786440 | tf_op jit(solution)/shard_map/ppermute | solution.py:251
  108.9 11.8 %copy-start.3 = (f32[512,128]{1,0:T(8,128)}, f32[512,128]{1,0:T(8,128)S(1)}, u32[]{:S(2)}) copy-start(f32[512,128]{1,0:T(8,128)S(1)} %convolution_select_fusion.refs_0_) | copy-start | bytes 786436
  108.9 7.9 %collective-permute-start.14 = (f32[512,128]{1,0:T(8,128)S(1)}, f32[512,128]{1,0:T(8,128)S(1)}, u32[]{:S(2)}, u32[]{:S(2)}) collective-permute-start(f32[512,128]{1,0:T(8,128)S(1)} %convolution_select_fusion.refs_0_), channel_id=1, source_target_pairs={{0,1},{1,2},{2,3},{3,0},{4,5},{5,6},{6,7},{7,4},{8,9},{9,10},{10,1... | collective-permute-start | bytes 786440 | tf_op jit(solution)/shard_map/ppermute | solution.py:73
  109.1 9.2 %collective-permute-start.15 = (f32[512,128]{1,0:T(8,128)S(1)}, f32[512,128]{1,0:T(8,128)S(1)}, u32[]{:S(2)}, u32[]{:S(2)}) collective-permute-start(f32[512,128]{1,0:T(8,128)S(1)} %convolution_select_fusion.refs_0_), channel_id=1, source_target_pairs={{0,2},{1,3},{2,0},{3,1},{4,6},{5,7},{6,4},{7,5},{8,10},{9,11},{10,... | collective-permute-start | bytes 786440 | tf_op jit(solution)/shard_map/ppermute | solution.py:73
  109.1 11.6 %collective-permute-start.16 = (f32[512,128]{1,0:T(8,128)S(1)}, f32[512,128]{1,0:T(8,128)S(1)}, u32[]{:S(2)}, u32[]{:S(2)}) collective-permute-start(f32[512,128]{1,0:T(8,128)S(1)} %convolution_select_fusion.refs_0_), channel_id=1, source_target_pairs={{0,3},{1,0},{2,1},{3,2},{4,7},{5,4},{6,5},{7,6},{8,11},{9,8},{10,9... | collective-permute-start | bytes 786440 | tf_op jit(solution)/shard_map/ppermute | solution.py:73
  116.8 3.9 %copy-start.5 = (f32[512,128]{1,0:T(8,128)}, f32[512,128]{1,0:T(8,128)S(1)}, u32[]{:S(2)}) copy-start(f32[512,128]{1,0:T(8,128)S(1)} %collective-permute-done.14.refs_1_) | copy-start | bytes 786436
  118.2 2.5 %copy-start.6 = (f32[512,128]{1,0:T(8,128)}, f32[512,128]{1,0:T(8,128)S(1)}, u32[]{:S(2)}) copy-start(f32[512,128]{1,0:T(8,128)S(1)} %collective-permute-done.15.refs_2_) | copy-start | bytes 786436
  120.7 0.7 copy-start.7
  124.7 6.0 %collective-permute-start.17 = (bf16[512,128]{1,0:T(8,128)(2,1)}, bf16[512,128]{1,0:T(8,128)(2,1)S(1)}, u32[]{:S(2)}, u32[]{:S(2)}) collective-permute-start(bf16[512,128]{1,0:T(8,128)(2,1)} %get-tuple-element.10), channel_id=1, source_target_pairs={{0,3},{1,0},{2,1},{3,2},{4,7},{5,4},{6,5},{7,6},{8,11},{9,8},{10,9... | collective-permute-start | bytes 393224 | tf_op jit(solution)/shard_map/ppermute | solution.py:73
  126.6 9.2 %collective-permute-start.18 = (bf16[512,128]{1,0:T(8,128)(2,1)}, bf16[512,128]{1,0:T(8,128)(2,1)S(1)}, u32[]{:S(2)}, u32[]{:S(2)}) collective-permute-start(bf16[512,128]{1,0:T(8,128)(2,1)} %get-tuple-element.11), channel_id=1, source_target_pairs={{0,2},{1,3},{2,0},{3,1},{4,6},{5,7},{6,4},{7,5},{8,10},{9,11},{10,... | collective-permute-start | bytes 393224 | tf_op jit(solution)/shard_map/ppermute | solution.py:73
  128.9 6.9 %collective-permute-start.19 = (bf16[512,128]{1,0:T(8,128)(2,1)}, bf16[512,128]{1,0:T(8,128)(2,1)S(1)}, u32[]{:S(2)}, u32[]{:S(2)}) collective-permute-start(bf16[512,128]{1,0:T(8,128)(2,1)} %get-tuple-element.12), channel_id=1, source_target_pairs={{0,1},{1,2},{2,3},{3,0},{4,5},{5,6},{6,7},{7,4},{8,9},{9,10},{10,1... | collective-permute-start | bytes 393224 | tf_op jit(solution)/shard_map/ppermute | solution.py:73
  130.7 5.1 %copy-start.8 = (bf16[512,128]{1,0:T(8,128)(2,1)}, bf16[512,128]{1,0:T(8,128)(2,1)S(1)}, u32[]{:S(2)}) copy-start(bf16[512,128]{1,0:T(8,128)(2,1)S(1)} %collective-permute-done.17.refs_1_) | copy-start | bytes 393220
  135.8 0.6 copy-start.9
  135.8 0.7 copy-start.10
Sparse Core Ops, SparseCore 0:
  11.1 57.3 all-gather.1

commit v11 on v10

--- a/solution.py
+++ b/solution.py
@@ -208,7 +208,10 @@
     mine = jnp.concatenate(
         [lax.dynamic_index_in_dim(top_inv, owned, 0), jnp.take(top_tiles, picks, axis=0)], axis=0
     )
-    mats = lax.all_gather(mine, "row", axis=1, tiled=True)
+    mats = jnp.zeros((mine.shape[0], share * rows_n, mine.shape[2]), mine.dtype)
+    for s in range(rows_n):
+        piece = mine if s == 0 else shifted(mine, "row", rows_n, s)
+        mats = lax.dynamic_update_slice_in_dim(mats, piece, ((position - s) % rows_n) * share, 1)
     inv = mats[0]
 
     slot_rows = tile_rows[0]

time: 146 us -> 151 us (1.034)
  starting transfers between devices: 22.8 us -> 47.8 us
  between operations: 14.4 us -> 1.02 us
  waiting for transfers between devices: 79.3 us -> 71.5 us
  local copies, waits for them, and re-layouts: 3.81 us -> 6.54 us
  matrix products: 10.4 us -> 7.78 us
    ppermute x5, waiting for transfers between devices: 32 us -> 9.3 us  [swapped(): return lax.ppermute(x, axis, [(i, i ^ bit) for i in range(size)])]
    ppermute x5, starting transfers between devices: 7.56 us -> 23.4 us  [swapped(): return lax.ppermute(x, axis, [(i, i ^ bit) for i in range(size)])]
    ppermute x9 -> x16, waiting for transfers between devices: 21.7 us -> 37 us  [shifted(): return lax.ppermute(x, axis, [(i, (i + shift) % size) for i in range(size)])]
    ppermute x9 -> x16, starting transfers between devices: 9.26 us -> 19 us  [shifted(): return lax.ppermute(x, axis, [(i, (i + shift) % size) for i in range(size)])]
  transfers between devices with their start and end apart: 21 -> 27, of which waited for: 15 -> 13; matrix products, arithmetic and copies ran while one was open for 4% -> 7% of each run, Pallas kernels for 2% -> 0%
where the time goes in v11:
time: 151 us
  waiting for transfers between devices  71.5 us (47%)
  starting transfers between devices  47.8 us (32%)
  Pallas kernels  8.82 us (6%)
  matrix products  7.78 us (5%)
  other arithmetic  7.7 us (5%)
  local copies, waits for them, and re-layouts  6.54 us (4%)
    ppermute x16, waiting for transfers between devices, shifted(): return lax.ppermute(x, axis, [(i, (i + shift) % size) for i in range(size)])  37 us
    ppermute x5, starting transfers between devices, swapped(): return lax.ppermute(x, axis, [(i, i ^ bit) for i in range(size)])  23.4 us
    ppermute x3, waiting for transfers between devices, local(): pushed = lax.ppermute(pushed, 'col', [(level + 1, level)])  23.3 us
    ppermute x16, starting transfers between devices, shifted(): return lax.ppermute(x, axis, [(i, (i + shift) % size) for i in range(size)])  19 us
    ppermute x5, waiting for transfers between devices, swapped(): return lax.ppermute(x, axis, [(i, i ^ bit) for i in range(size)])  9.3 us
    pallas_call x1, Pallas kernels, tail_terms(): pl.pallas_call(functools.partial(tail_kernel, levels, peers), out_shape=o...  3.5 us
    pallas_call x1, Pallas kernels, coupling_terms(): pl.pallas_call(coupling_kernel, out_shape=jax.ShapeDtypeStruct(shape, jnp...  3.04 us
  transfers between devices with their start and end apart: 27, of which 13 were waited for; matrix products, arithmetic and copies ran while one was open for 7% of the time, Pallas kernels for 0%

profile of v11, /device:TPU:0, one launch (start us, length us, event | category | flops | bytes accessed | tf_op | source)
XLA Modules:
  0.0 151.1 jit_solution(4381501747123329059)
XLA Ops:
  0.6 1.4 convolution_convert_fusion.4.forward_ref
  2.1 2.5 %collective-permute-start.9 = (bf16[512,128]{1,0:T(8,128)(2,1)S(1)}, bf16[512,128]{1,0:T(8,128)(2,1)S(1)}, u32[]{:S(2)}, u32[]{:S(2)}) collective-permute-start(bf16[512,128]{1,0:T(8,128)(2,1)S(1)} %convolution_convert_fusion.4.forward_ref), channel_id=1, source_target_pairs={{0,3},{1,0},{2,1},{3,2},{4,7},{5,4},{6,5},{7,6},{8,11},{9,8},{10,9... | collective-permute-start | bytes 393224 | tf_op jit(solution)/shard_map/ppermute | solution.py:73
  4.6 0.6 collective-permute-start.8
  5.4 1.2 and_select_fusion.1
  6.6 0.7 fusion.46
  7.3 0.7 iota_reduce_fusion
  8.0 0.7 compare_and_fusion
  8.7 0.6 gather_fusion
  9.2 0.6 pad_add_fusion.fold_ref
  9.8 2.3 %collective-permute-done.8 = bf16[512,128]{1,0:T(8,128)(2,1)S(1)} collective-permute-done((bf16[512,128]{1,0:T(8,128)(2,1)S(1)}, bf16[512,128]{1,0:T(8,128)(2,1)S(1)}, u32[]{:S(2)}, u32[]{:S(2)}) %collective-permute-start.8) | collective-permute-done | bytes 131104 | tf_op jit(solution)/shard_map/ppermute | solution.py:73
  12.1 0.9 pad_maximum_fusion.panels_ref
  13.0 3.0 %shard_map.104 = bf16[4,512,128]{2,1,0:T(8,128)(2,1)} custom-call(s32[4]{0:T(128)} %bitcast.127, s32[4]{0:T(128)} %get-tuple-element.8.picks_ref, s32[2]{0:T(128)} %pad_add_fusion.fold_ref, bf16[4,512,512]{2,1,0:T(8,128)(2,1)} %bitcast.119, bf16[4,512,128]{2,1,0:T(8,128)(2,1)} %pad_maximum_fusion.panels_ref, bf16[4,64,128]{2,1,0:T(8,128)(2,1)} %rhs_ref.1), custom_call_target="tpu_custom_call" | custom-call | tf_op jit(solution)/shard_map/pallas_call | solution.py:37
  16.0 1.8 %dynamic-slice_bitcast_fusion = bf16[2,512,128]{2,1,0:T(8,128)(2,1)} fusion(bf16[2,2,512,128]{3,2,1,0:T(8,128)(2,1)} %bitcast.121, s32[]{:T(128)S(6)} %select_n.181), kind=kLoop, calls=%fused_computation.44 | loop fusion | bytes 524292 | tf_op jit(solution)/shard_map/jit(dynamic_index_in_dim)/squeeze | solution.py:177
  17.9 0.9 constant_dynamic-slice_fusion.2
  18.9 0.8 pad_maximum_fusion.1
  19.7 1.7 %collective-permute-start = (bf16[4,64,512]{2,1,0:T(8,128)(2,1)}, bf16[4,64,512]{2,1,0:T(8,128)(2,1)S(1)}, u32[]{:S(2)}, u32[]{:S(2)}) collective-permute-start(bf16[4,64,512]{2,1,0:T(8,128)(2,1)} %get-tuple-element.16), channel_id=1, source_target_pairs={{0,4},{4,8},{8,12},{12,16},{16,20},{20,24},{24,28},{28,0},{1,5},{5... | collective-permute-start | bytes 786440 | tf_op jit(solution)/shard_map/ppermute | solution.py:73
  21.3 1.0 fusion.1
  22.4 0.7 constant_dynamic-slice_fusion
  23.0 2.0 %collective-permute-start.11 = (bf16[1,512,128]{2,1,0:T(8,128)(2,1)}, bf16[1,512,128]{2,1,0:T(8,128)(2,1)}, u32[]{:S(2)}, u32[]{:S(2)}) collective-permute-start(bf16[1,512,128]{2,1,0:T(8,128)(2,1)} %constant_dynamic-slice_fusion), channel_id=1, source_target_pairs={{0,2},{1,3},{2,0},{3,1},{4,6},{5,7},{6,4},{7,5},{8,10},{9,11},{10,... | collective-permute-start | bytes 393224 | tf_op jit(solution)/shard_map/ppermute | solution.py:77
  25.1 1.6 %collective-permute-start.1 = (bf16[4,64,512]{2,1,0:T(8,128)(2,1)}, bf16[4,64,512]{2,1,0:T(8,128)(2,1)}, u32[]{:S(2)}, u32[]{:S(2)}) collective-permute-start(bf16[4,64,512]{2,1,0:T(8,128)(2,1)} %get-tuple-element.16), channel_id=1, source_target_pairs={{0,8},{4,12},{8,16},{12,20},{16,24},{20,28},{24,0},{28,4},{1,9},{5... | collective-permute-start | bytes 786440 | tf_op jit(solution)/shard_map/ppermute | solution.py:73
  26.7 2.0 %collective-permute-start.2 = (bf16[4,64,512]{2,1,0:T(8,128)(2,1)}, bf16[4,64,512]{2,1,0:T(8,128)(2,1)S(1)}, u32[]{:S(2)}, u32[]{:S(2)}) collective-permute-start(bf16[4,64,512]{2,1,0:T(8,128)(2,1)} %get-tuple-element.16), channel_id=1, source_target_pairs={{0,12},{4,16},{8,20},{12,24},{16,28},{20,0},{24,4},{28,8},{1,13},{... | collective-permute-start | bytes 786440 | tf_op jit(solution)/shard_map/ppermute | solution.py:73
  28.6 1.2 collective-permute-start.3
  29.9 2.0 %collective-permute-done = bf16[4,64,512]{2,1,0:T(8,128)(2,1)S(1)} collective-permute-done((bf16[4,64,512]{2,1,0:T(8,128)(2,1)}, bf16[4,64,512]{2,1,0:T(8,128)(2,1)S(1)}, u32[]{:S(2)}, u32[]{:S(2)}) %collective-permute-start) | collective-permute-done | bytes 262176 | tf_op jit(solution)/shard_map/ppermute | solution.py:73
  31.8 1.0 collective-permute-start.4
  32.9 1.9 %collective-permute-start.5 = (bf16[4,64,512]{2,1,0:T(8,128)(2,1)}, bf16[4,64,512]{2,1,0:T(8,128)(2,1)S(1)}, u32[]{:S(2)}, u32[]{:S(2)}) collective-permute-start(bf16[4,64,512]{2,1,0:T(8,128)(2,1)} %get-tuple-element.16), channel_id=1, source_target_pairs={{0,24},{4,28},{8,0},{12,4},{16,8},{20,12},{24,16},{28,20},{1,25},{... | collective-permute-start | bytes 786440 | tf_op jit(solution)/shard_map/ppermute | solution.py:73
  34.7 0.9 fusion.16
  35.7 0.9 collective-permute-done.1
  36.6 1.6 %collective-permute-start.12 = (bf16[512,128]{1,0:T(8,128)(2,1)S(1)}, bf16[512,128]{1,0:T(8,128)(2,1)S(1)}, u32[]{:S(2)}, u32[]{:S(2)}) collective-permute-start(bf16[512,128]{1,0:T(8,128)(2,1)S(1)} %fusion.16), channel_id=1, source_target_pairs={{0,4},{4,0},{8,12},{12,8},{16,20},{20,16},{24,28},{28,24},{1,5},{5... | collective-permute-start | bytes 393224 | tf_op jit(solution)/shard_map/ppermute | solution.py:77
  38.2 1.0 constant_dynamic-update-slice_fusion.5
  39.1 15.0 %collective-permute-done.2 = bf16[4,64,512]{2,1,0:T(8,128)(2,1)S(1)} collective-permute-done((bf16[4,64,512]{2,1,0:T(8,128)(2,1)}, bf16[4,64,512]{2,1,0:T(8,128)(2,1)S(1)}, u32[]{:S(2)}, u32[]{:S(2)}) %collective-permute-start.2) | collective-permute-done | bytes 262176 | tf_op jit(solution)/shard_map/ppermute | solution.py:73
  54.3 14.4 %collective-permute-start.13 = (bf16[512,128]{1,0:T(8,128)(2,1)S(1)}, bf16[512,128]{1,0:T(8,128)(2,1)S(1)}, u32[]{:S(2)}, u32[]{:S(2)}) collective-permute-start(bf16[512,128]{1,0:T(8,128)(2,1)S(1)} %add_convert_fusion.2), channel_id=1, source_target_pairs={{0,8},{4,12},{8,0},{12,4},{16,24},{20,28},{24,16},{28,20},{1,9},{5... | collective-permute-start | bytes 393224 | tf_op jit(solution)/shard_map/ppermute | solution.py:77
  68.8 2.9 %collective-permute-done.13 = bf16[512,128]{1,0:T(8,128)(2,1)S(1)} collective-permute-done((bf16[512,128]{1,0:T(8,128)(2,1)S(1)}, bf16[512,128]{1,0:T(8,128)(2,1)S(1)}, u32[]{:S(2)}, u32[]{:S(2)}) %collective-permute-start.13) | collective-permute-done | bytes 131104 | tf_op jit(solution)/shard_map/ppermute | solution.py:77
  71.7 5.3 %collective-permute-start.14 = (bf16[512,128]{1,0:T(8,128)(2,1)S(1)}, bf16[512,128]{1,0:T(8,128)(2,1)S(1)}, u32[]{:S(2)}, u32[]{:S(2)}) collective-permute-start(bf16[512,128]{1,0:T(8,128)(2,1)S(1)} %add_convert_fusion.1), channel_id=1, source_target_pairs={{0,16},{4,20},{8,24},{12,28},{16,0},{20,4},{24,8},{28,12},{1,17},{... | collective-permute-start | bytes 393224 | tf_op jit(solution)/shard_map/ppermute | solution.py:77
  77.0 6.4 %collective-permute-done.14 = bf16[512,128]{1,0:T(8,128)(2,1)S(1)} collective-permute-done((bf16[512,128]{1,0:T(8,128)(2,1)S(1)}, bf16[512,128]{1,0:T(8,128)(2,1)S(1)}, u32[]{:S(2)}, u32[]{:S(2)}) %collective-permute-start.14) | collective-permute-done | bytes 131104 | tf_op jit(solution)/shard_map/ppermute | solution.py:77
  83.8 0.6 fusion.35
  84.4 1.4 collective-permute-start.15
  85.8 1.8 %collective-permute-done.15 = f32[3,512,128]{2,1,0:T(8,128)S(1)} collective-permute-done((f32[3,512,128]{2,1,0:T(8,128)S(1)}, f32[3,512,128]{2,1,0:T(8,128)S(1)}, u32[]{:S(2)}, u32[]{:S(2)}) %collective-permute-start.15) | collective-permute-done | bytes 786464 | tf_op jit(solution)/shard_map/ppermute | solution.py:241
  87.6 0.3 convolution_convert_fusion.2
  87.9 0.4 slice_add_fusion.1
  88.4 0.7 collective-permute-start.16
  89.7 0.7 collective-permute-start.17
  90.4 0.7 fusion
  91.2 0.6 fusion.29
  91.8 0.7 collective-permute-start.18
  92.5 0.3 fusion.15
  92.9 0.5 slice_add_fusion
  93.3 0.7 collective-permute-start.19
  94.0 0.3 fusion.14
  94.4 0.3 slice_add_fusion.2
  94.7 1.3 collective-permute-start.20
  96.1 23.3 %collective-permute-done.20 = f32[1,512,128]{2,1,0:T(8,128)} collective-permute-done((f32[1,512,128]{2,1,0:T(8,128)S(1)}, f32[1,512,128]{2,1,0:T(8,128)}, u32[]{:S(2)}, u32[]{:S(2)}) %collective-permute-start.20) | collective-permute-done | bytes 262176 | tf_op jit(solution)/shard_map/ppermute | solution.py:254
  119.3 1.3 convolution_select_fusion.refs_0_
  120.9 1.6 %collective-permute-start.23 = (f32[512,128]{1,0:T(8,128)S(1)}, f32[512,128]{1,0:T(8,128)S(1)}, u32[]{:S(2)}, u32[]{:S(2)}) collective-permute-start(f32[512,128]{1,0:T(8,128)S(1)} %convolution_select_fusion.refs_0_), channel_id=1, source_target_pairs={{0,3},{1,0},{2,1},{3,2},{4,7},{5,4},{6,5},{7,6},{8,11},{9,8},{10,9... | collective-permute-start | bytes 786440 | tf_op jit(solution)/shard_map/ppermute | solution.py:73
  122.5 6.1 %collective-permute-done.21.refs_1_ = f32[512,128]{1,0:T(8,128)S(1)} collective-permute-done((f32[512,128]{1,0:T(8,128)S(1)}, f32[512,128]{1,0:T(8,128)S(1)}, u32[]{:S(2)}, u32[]{:S(2)}) %collective-permute-start.21) | collective-permute-done | bytes 262176 | tf_op jit(solution)/shard_map/ppermute | solution.py:73
  128.6 1.4 collective-permute-done.22.refs_2_
  130.0 2.5 %collective-permute-done.23.refs_3_ = f32[512,128]{1,0:T(8,128)S(1)} collective-permute-done((f32[512,128]{1,0:T(8,128)S(1)}, f32[512,128]{1,0:T(8,128)S(1)}, u32[]{:S(2)}, u32[]{:S(2)}) %collective-permute-start.23) | collective-permute-done | bytes 262176 | tf_op jit(solution)/shard_map/ppermute | solution.py:73
  132.5 0.7 copy-done.7
  133.2 3.5 %shard_map.105 = (bf16[512,128]{1,0:T(8,128)(2,1)}, bf16[512,128]{1,0:T(8,128)(2,1)}, bf16[512,128]{1,0:T(8,128)(2,1)}, bf16[512,128]{1,0:T(8,128)(2,1)}, f32[4,64,128]{2,1,0:T(8,128)}) custom-call(s32[4]{0:T(128)} %bitcast.128, s32[4]{0:T(128)} %get-tuple-element.14.dests_ref, s32[4]{0:T(128)} %copy-done.11, s32[1]{0:T(128)} %bitcast.4.start_ref, ...), custom_call_target="tpu_custom_call" | custom-call | tf_op jit(solution)/shard_map/pallas_call | solution.py:127
  136.7 1.9 %collective-permute-start.24 = (bf16[512,128]{1,0:T(8,128)(2,1)}, bf16[512,128]{1,0:T(8,128)(2,1)S(1)}, u32[]{:S(2)}, u32[]{:S(2)}) collective-permute-start(bf16[512,128]{1,0:T(8,128)(2,1)} %get-tuple-element.10), channel_id=1, source_target_pairs={{0,3},{1,0},{2,1},{3,2},{4,7},{5,4},{6,5},{7,6},{8,11},{9,8},{10,9... | collective-permute-start | bytes 393224 | tf_op jit(solution)/shard_map/ppermute | solution.py:73
  138.6 2.7 %collective-permute-start.25 = (bf16[512,128]{1,0:T(8,128)(2,1)}, bf16[512,128]{1,0:T(8,128)(2,1)S(1)}, u32[]{:S(2)}, u32[]{:S(2)}) collective-permute-start(bf16[512,128]{1,0:T(8,128)(2,1)} %get-tuple-element.11), channel_id=1, source_target_pairs={{0,2},{1,3},{2,0},{3,1},{4,6},{5,7},{6,4},{7,5},{8,10},{9,11},{10,... | collective-permute-start | bytes 393224 | tf_op jit(solution)/shard_map/ppermute | solution.py:73
  141.3 0.8 collective-permute-done.24.refs_1_
  142.1 6.1 %collective-permute-done.25.refs_2_ = bf16[512,128]{1,0:T(8,128)(2,1)S(1)} collective-permute-done((bf16[512,128]{1,0:T(8,128)(2,1)}, bf16[512,128]{1,0:T(8,128)(2,1)S(1)}, u32[]{:S(2)}, u32[]{:S(2)}) %collective-permute-start.25) | collective-permute-done | bytes 131104 | tf_op jit(solution)/shard_map/ppermute | solution.py:73
  148.2 0.6 copy-done.9
  148.9 2.3 %shard_map.106 = f32[1,512,128]{2,1,0:T(8,128)} custom-call(bf16[512,128]{1,0:T(8,128)(2,1)} %copy-done.2, bf16[1,512,512]{2,1,0:T(8,128)(2,1)} %inv_ref.1, bf16[512,128]{1,0:T(8,128)(2,1)} %get-tuple-element.9.refs_0_, bf16[512,128]{1,0:T(8,128)(2,1)} %copy-done.8, bf16[512,128]{1,0:T(8,128)(2,1)} %copy-done.9, bf16[512,128]{1,0:T(8,128)(2,1)} %copy-done.10), custom_call_target="tpu_custom_call" | custom-call | tf_op jit(solution)/shard_map/pallas_call | solution.py:150
  (58 shorter events, 1.9 us)
Async XLA Ops:
  0.6 8.0 %copy-start = (bf16[6,64,512]{2,1,0:T(8,128)(2,1)S(1)}, bf16[6,64,512]{2,1,0:T(8,128)(2,1)}, u32[]{:S(2)}) copy-start(bf16[6,64,512]{2,1,0:T(8,128)(2,1)} %param.16) | copy-start | bytes 1179652
  2.1 14.0 %copy-start.2 = (bf16[512,128]{1,0:T(8,128)(2,1)}, bf16[512,128]{1,0:T(8,128)(2,1)S(1)}, u32[]{:S(2)}) copy-start(bf16[512,128]{1,0:T(8,128)(2,1)S(1)} %convolution_convert_fusion.4.forward_ref) | copy-start | bytes 393220
  2.1 7.8 %collective-permute-start.9 = (bf16[512,128]{1,0:T(8,128)(2,1)S(1)}, bf16[512,128]{1,0:T(8,128)(2,1)S(1)}, u32[]{:S(2)}, u32[]{:S(2)}) collective-permute-start(bf16[512,128]{1,0:T(8,128)(2,1)S(1)} %convolution_convert_fusion.4.forward_ref), channel_id=1, source_target_pairs={{0,3},{1,0},{2,1},{3,2},{4,7},{5,4},{6,5},{7,6},{8,11},{9,8},{10,9... | collective-permute-start | bytes 393224 | tf_op jit(solution)/shard_map/ppermute | solution.py:73
  4.6 7.5 %collective-permute-start.8 = (bf16[512,128]{1,0:T(8,128)(2,1)S(1)}, bf16[512,128]{1,0:T(8,128)(2,1)S(1)}, u32[]{:S(2)}, u32[]{:S(2)}) collective-permute-start(bf16[512,128]{1,0:T(8,128)(2,1)S(1)} %convolution_convert_fusion.4.forward_ref), channel_id=1, source_target_pairs={{0,2},{1,3},{2,0},{3,1},{4,6},{5,7},{6,4},{7,5},{8,10},{9,11},{10,... | collective-permute-start | bytes 393224 | tf_op jit(solution)/shard_map/ppermute | solution.py:73
  5.2 6.9 %collective-permute-start.7 = (bf16[512,128]{1,0:T(8,128)(2,1)S(1)}, bf16[512,128]{1,0:T(8,128)(2,1)S(1)}, u32[]{:S(2)}, u32[]{:S(2)}) collective-permute-start(bf16[512,128]{1,0:T(8,128)(2,1)S(1)} %convolution_convert_fusion.4.forward_ref), channel_id=1, source_target_pairs={{0,1},{1,2},{2,3},{3,0},{4,5},{5,6},{6,7},{7,4},{8,9},{9,10},{10,1... | collective-permute-start | bytes 393224 | tf_op jit(solution)/shard_map/ppermute | solution.py:73
  5.4 10.7 %copy-start.11 = (s32[4]{0:T(128)}, s32[4]{0:T(128)S(1)}, u32[]{:S(2)}) copy-start(s32[4]{0:T(128)S(1)} %and_select_fusion.table_ref) | copy-start | bytes 52
  16.0 5.3 %copy-start.1 = (bf16[4,512,128]{2,1,0:T(8,128)(2,1)S(1)}, bf16[4,512,128]{2,1,0:T(8,128)(2,1)}, u32[]{:S(2)}) copy-start(bf16[4,512,128]{2,1,0:T(8,128)(2,1)} %shard_map.104) | copy-start | bytes 1572868
  17.8 3.5 %collective-permute-start.10 = (bf16[2,512,128]{2,1,0:T(8,128)(2,1)}, bf16[2,512,128]{2,1,0:T(8,128)(2,1)}, u32[]{:S(2)}, u32[]{:S(2)}) collective-permute-start(bf16[2,512,128]{2,1,0:T(8,128)(2,1)} %dynamic-slice_bitcast_fusion), channel_id=1, source_target_pairs={{0,1},{1,0},{2,3},{3,2},{4,5},{5,4},{6,7},{7,6},{8,9},{9,8},{10,11... | collective-permute-start | bytes 786440 | tf_op jit(solution)/shard_map/ppermute | solution.py:77
  19.7 12.2 %collective-permute-start = (bf16[4,64,512]{2,1,0:T(8,128)(2,1)}, bf16[4,64,512]{2,1,0:T(8,128)(2,1)S(1)}, u32[]{:S(2)}, u32[]{:S(2)}) collective-permute-start(bf16[4,64,512]{2,1,0:T(8,128)(2,1)} %get-tuple-element.16), channel_id=1, source_target_pairs={{0,4},{4,8},{8,12},{12,16},{16,20},{20,24},{24,28},{28,0},{1,5},{5... | collective-permute-start | bytes 786440 | tf_op jit(solution)/shard_map/ppermute | solution.py:73
  23.0 9.8 %collective-permute-start.11 = (bf16[1,512,128]{2,1,0:T(8,128)(2,1)}, bf16[1,512,128]{2,1,0:T(8,128)(2,1)}, u32[]{:S(2)}, u32[]{:S(2)}) collective-permute-start(bf16[1,512,128]{2,1,0:T(8,128)(2,1)} %constant_dynamic-slice_fusion), channel_id=1, source_target_pairs={{0,2},{1,3},{2,0},{3,1},{4,6},{5,7},{6,4},{7,5},{8,10},{9,11},{10,... | collective-permute-start | bytes 393224 | tf_op jit(solution)/shard_map/ppermute | solution.py:77
  25.1 11.5 %collective-permute-start.1 = (bf16[4,64,512]{2,1,0:T(8,128)(2,1)}, bf16[4,64,512]{2,1,0:T(8,128)(2,1)}, u32[]{:S(2)}, u32[]{:S(2)}) collective-permute-start(bf16[4,64,512]{2,1,0:T(8,128)(2,1)} %get-tuple-element.16), channel_id=1, source_target_pairs={{0,8},{4,12},{8,16},{12,20},{16,24},{20,28},{24,0},{28,4},{1,9},{5... | collective-permute-start | bytes 786440 | tf_op jit(solution)/shard_map/ppermute | solution.py:73
  26.7 27.5 %collective-permute-start.2 = (bf16[4,64,512]{2,1,0:T(8,128)(2,1)}, bf16[4,64,512]{2,1,0:T(8,128)(2,1)S(1)}, u32[]{:S(2)}, u32[]{:S(2)}) collective-permute-start(bf16[4,64,512]{2,1,0:T(8,128)(2,1)} %get-tuple-element.16), channel_id=1, source_target_pairs={{0,12},{4,16},{8,20},{12,24},{16,28},{20,0},{24,4},{28,8},{1,13},{... | collective-permute-start | bytes 786440 | tf_op jit(solution)/shard_map/ppermute | solution.py:73
  28.6 40.1 %collective-permute-start.3 = (bf16[4,64,512]{2,1,0:T(8,128)(2,1)}, bf16[4,64,512]{2,1,0:T(8,128)(2,1)S(1)}, u32[]{:S(2)}, u32[]{:S(2)}) collective-permute-start(bf16[4,64,512]{2,1,0:T(8,128)(2,1)} %get-tuple-element.16), channel_id=1, source_target_pairs={{0,16},{4,20},{8,24},{12,28},{16,0},{20,4},{24,8},{28,12},{1,17},{... | collective-permute-start | bytes 786440 | tf_op jit(solution)/shard_map/ppermute | solution.py:73
  31.8 36.9 %collective-permute-start.4 = (bf16[4,64,512]{2,1,0:T(8,128)(2,1)}, bf16[4,64,512]{2,1,0:T(8,128)(2,1)S(1)}, u32[]{:S(2)}, u32[]{:S(2)}) collective-permute-start(bf16[4,64,512]{2,1,0:T(8,128)(2,1)} %get-tuple-element.16), channel_id=1, source_target_pairs={{0,20},{4,24},{8,28},{12,0},{16,4},{20,8},{24,12},{28,16},{1,21},{... | collective-permute-start | bytes 786440 | tf_op jit(solution)/shard_map/ppermute | solution.py:73
  32.9 44.1 %collective-permute-start.5 = (bf16[4,64,512]{2,1,0:T(8,128)(2,1)}, bf16[4,64,512]{2,1,0:T(8,128)(2,1)S(1)}, u32[]{:S(2)}, u32[]{:S(2)}) collective-permute-start(bf16[4,64,512]{2,1,0:T(8,128)(2,1)} %get-tuple-element.16), channel_id=1, source_target_pairs={{0,24},{4,28},{8,0},{12,4},{16,8},{20,12},{24,16},{28,20},{1,25},{... | collective-permute-start | bytes 786440 | tf_op jit(solution)/shard_map/ppermute | solution.py:73
  36.6 17.6 %collective-permute-start.12 = (bf16[512,128]{1,0:T(8,128)(2,1)S(1)}, bf16[512,128]{1,0:T(8,128)(2,1)S(1)}, u32[]{:S(2)}, u32[]{:S(2)}) collective-permute-start(bf16[512,128]{1,0:T(8,128)(2,1)S(1)} %fusion.16), channel_id=1, source_target_pairs={{0,4},{4,0},{8,12},{12,8},{16,20},{20,16},{24,28},{28,24},{1,5},{5... | collective-permute-start | bytes 393224 | tf_op jit(solution)/shard_map/ppermute | solution.py:77
  54.2 22.8 %collective-permute-start.6 = (bf16[4,64,512]{2,1,0:T(8,128)(2,1)}, bf16[4,64,512]{2,1,0:T(8,128)(2,1)S(1)}, u32[]{:S(2)}, u32[]{:S(2)}) collective-permute-start(bf16[4,64,512]{2,1,0:T(8,128)(2,1)} %get-tuple-element.16), channel_id=1, source_target_pairs={{0,28},{4,0},{8,4},{12,8},{16,12},{20,16},{24,20},{28,24},{1,29},{... | collective-permute-start | bytes 786440 | tf_op jit(solution)/shard_map/ppermute | solution.py:73
  54.3 17.4 %collective-permute-start.13 = (bf16[512,128]{1,0:T(8,128)(2,1)S(1)}, bf16[512,128]{1,0:T(8,128)(2,1)S(1)}, u32[]{:S(2)}, u32[]{:S(2)}) collective-permute-start(bf16[512,128]{1,0:T(8,128)(2,1)S(1)} %add_convert_fusion.2), channel_id=1, source_target_pairs={{0,8},{4,12},{8,0},{12,4},{16,24},{20,28},{24,16},{28,20},{1,9},{5... | collective-permute-start | bytes 393224 | tf_op jit(solution)/shard_map/ppermute | solution.py:77
  71.7 11.8 %collective-permute-start.14 = (bf16[512,128]{1,0:T(8,128)(2,1)S(1)}, bf16[512,128]{1,0:T(8,128)(2,1)S(1)}, u32[]{:S(2)}, u32[]{:S(2)}) collective-permute-start(bf16[512,128]{1,0:T(8,128)(2,1)S(1)} %add_convert_fusion.1), channel_id=1, source_target_pairs={{0,16},{4,20},{8,24},{12,28},{16,0},{20,4},{24,8},{28,12},{1,17},{... | collective-permute-start | bytes 393224 | tf_op jit(solution)/shard_map/ppermute | solution.py:77
  83.8 4.6 %copy-start.4 = (bf16[512,128]{1,0:T(8,128)(2,1)}, bf16[512,128]{1,0:T(8,128)(2,1)S(1)}, u32[]{:S(2)}) copy-start(bf16[512,128]{1,0:T(8,128)(2,1)S(1)} %convolution_convert_fusion.3) | copy-start | bytes 393220
  84.4 3.2 %collective-permute-start.15 = (f32[3,512,128]{2,1,0:T(8,128)S(1)}, f32[3,512,128]{2,1,0:T(8,128)S(1)}, u32[]{:S(2)}, u32[]{:S(2)}) collective-permute-start(f32[3,512,128]{2,1,0:T(8,128)S(1)} %fusion.35), channel_id=1, source_target_pairs={{0,1},{4,5},{8,9},{12,13},{16,17},{20,21},{24,25},{28,29}} | collective-permute-start | bytes 2359304 | tf_op jit(solution)/shard_map/ppermute | solution.py:241
  88.4 0.7 collective-permute-start.16
  89.7 0.7 collective-permute-start.17
  91.8 0.7 collective-permute-start.18
  93.3 0.7 collective-permute-start.19
  94.7 24.6 %collective-permute-start.20 = (f32[1,512,128]{2,1,0:T(8,128)S(1)}, f32[1,512,128]{2,1,0:T(8,128)}, u32[]{:S(2)}, u32[]{:S(2)}) collective-permute-start(f32[1,512,128]{2,1,0:T(8,128)S(1)} %slice_add_fusion.2), channel_id=1, source_target_pairs={{1,0},{5,4},{9,8},{13,12},{17,16},{21,20},{25,24},{29,28}} | collective-permute-start | bytes 786440 | tf_op jit(solution)/shard_map/ppermute | solution.py:254
  120.7 11.8 %copy-start.3 = (f32[512,128]{1,0:T(8,128)}, f32[512,128]{1,0:T(8,128)S(1)}, u32[]{:S(2)}) copy-start(f32[512,128]{1,0:T(8,128)S(1)} %convolution_select_fusion.refs_0_) | copy-start | bytes 786436
  120.7 7.9 %collective-permute-start.21 = (f32[512,128]{1,0:T(8,128)S(1)}, f32[512,128]{1,0:T(8,128)S(1)}, u32[]{:S(2)}, u32[]{:S(2)}) collective-permute-start(f32[512,128]{1,0:T(8,128)S(1)} %convolution_select_fusion.refs_0_), channel_id=1, source_target_pairs={{0,1},{1,2},{2,3},{3,0},{4,5},{5,6},{6,7},{7,4},{8,9},{9,10},{10,1... | collective-permute-start | bytes 786440 | tf_op jit(solution)/shard_map/ppermute | solution.py:73
  120.9 9.2 %collective-permute-start.22 = (f32[512,128]{1,0:T(8,128)S(1)}, f32[512,128]{1,0:T(8,128)S(1)}, u32[]{:S(2)}, u32[]{:S(2)}) collective-permute-start(f32[512,128]{1,0:T(8,128)S(1)} %convolution_select_fusion.refs_0_), channel_id=1, source_target_pairs={{0,2},{1,3},{2,0},{3,1},{4,6},{5,7},{6,4},{7,5},{8,10},{9,11},{10,... | collective-permute-start | bytes 786440 | tf_op jit(solution)/shard_map/ppermute | solution.py:73
  120.9 11.6 %collective-permute-start.23 = (f32[512,128]{1,0:T(8,128)S(1)}, f32[512,128]{1,0:T(8,128)S(1)}, u32[]{:S(2)}, u32[]{:S(2)}) collective-permute-start(f32[512,128]{1,0:T(8,128)S(1)} %convolution_select_fusion.refs_0_), channel_id=1, source_target_pairs={{0,3},{1,0},{2,1},{3,2},{4,7},{5,4},{6,5},{7,6},{8,11},{9,8},{10,9... | collective-permute-start | bytes 786440 | tf_op jit(solution)/shard_map/ppermute | solution.py:73
  128.6 3.9 %copy-start.5 = (f32[512,128]{1,0:T(8,128)}, f32[512,128]{1,0:T(8,128)S(1)}, u32[]{:S(2)}) copy-start(f32[512,128]{1,0:T(8,128)S(1)} %collective-permute-done.21.refs_1_) | copy-start | bytes 786436
  130.0 2.5 %copy-start.6 = (f32[512,128]{1,0:T(8,128)}, f32[512,128]{1,0:T(8,128)S(1)}, u32[]{:S(2)}) copy-start(f32[512,128]{1,0:T(8,128)S(1)} %collective-permute-done.22.refs_2_) | copy-start | bytes 786436
  132.5 0.7 copy-start.7
  136.7 5.4 %collective-permute-start.24 = (bf16[512,128]{1,0:T(8,128)(2,1)}, bf16[512,128]{1,0:T(8,128)(2,1)S(1)}, u32[]{:S(2)}, u32[]{:S(2)}) collective-permute-start(bf16[512,128]{1,0:T(8,128)(2,1)} %get-tuple-element.10), channel_id=1, source_target_pairs={{0,3},{1,0},{2,1},{3,2},{4,7},{5,4},{6,5},{7,6},{8,11},{9,8},{10,9... | collective-permute-start | bytes 393224 | tf_op jit(solution)/shard_map/ppermute | solution.py:73
  138.6 9.6 %collective-permute-start.25 = (bf16[512,128]{1,0:T(8,128)(2,1)}, bf16[512,128]{1,0:T(8,128)(2,1)S(1)}, u32[]{:S(2)}, u32[]{:S(2)}) collective-permute-start(bf16[512,128]{1,0:T(8,128)(2,1)} %get-tuple-element.11), channel_id=1, source_target_pairs={{0,2},{1,3},{2,0},{3,1},{4,6},{5,7},{6,4},{7,5},{8,10},{9,11},{10,... | collective-permute-start | bytes 393224 | tf_op jit(solution)/shard_map/ppermute | solution.py:73
  141.3 6.9 %collective-permute-start.26 = (bf16[512,128]{1,0:T(8,128)(2,1)}, bf16[512,128]{1,0:T(8,128)(2,1)S(1)}, u32[]{:S(2)}, u32[]{:S(2)}) collective-permute-start(bf16[512,128]{1,0:T(8,128)(2,1)} %get-tuple-element.12), channel_id=1, source_target_pairs={{0,1},{1,2},{2,3},{3,0},{4,5},{5,6},{6,7},{7,4},{8,9},{9,10},{10,1... | collective-permute-start | bytes 393224 | tf_op jit(solution)/shard_map/ppermute | solution.py:73
  142.1 6.1 %copy-start.8 = (bf16[512,128]{1,0:T(8,128)(2,1)}, bf16[512,128]{1,0:T(8,128)(2,1)S(1)}, u32[]{:S(2)}) copy-start(bf16[512,128]{1,0:T(8,128)(2,1)S(1)} %collective-permute-done.24.refs_1_) | copy-start | bytes 393220
  148.1 0.6 copy-start.9
  148.2 0.7 copy-start.10

commit v12 on v10

--- a/solution.py
+++ b/solution.py
@@ -153,6 +153,88 @@
         in_specs=[VMEM] * (2 + len(terms)),
         out_specs=VMEM,
     )(forward, inv, *terms)
+
+
+def upper_kernel(levels, peers, rows_ref, dests_ref, table_ref, start_ref, tiles_ref, *refs):
+    x_refs = refs[:peers]
+    acc_ref = refs[peers]
+    slices_ref = refs[peers + 1]
+    share = slices_ref.shape[1]
+    start = pl.multiple_of(start_ref[0], 8)
+    for t in range(1, levels):
+        for p in range(peers):
+
+            @pl.when(table_ref[t] == p)
+            def _():
+                slices_ref[t] = x_refs[p][pl.ds(start, share), :]
+
+    acc_ref[...] = jnp.zeros_like(acc_ref)
+    for s in range(tiles_ref.shape[0]):
+        level = rows_ref[s]
+        piece = table_ref[jnp.maximum(level, 0)]
+        for p in range(peers):
+
+            @pl.when((level >= 1) & (piece == p))
+            def _():
+                prod = lax.dot_general(
+                    tiles_ref[s],
+                    x_refs[p][...].astype(jnp.bfloat16),
+                    (((0,), (0,)), ((), ())),
+                    preferred_element_type=jnp.float32,
+                )
+                acc_ref[dests_ref[s]] += prod
+
+
+def upper_terms(slot_rows, dests, table, start, tiles, pieces, levels, share):
+    peers = len(pieces)
+    shape = pieces[0].shape
+    outs = [
+        jax.ShapeDtypeStruct((peers,) + shape, jnp.float32),
+        jax.ShapeDtypeStruct((levels, share, shape[1]), jnp.float32),
+    ]
+    return pl.pallas_call(
+        functools.partial(upper_kernel, levels, peers),
+        out_shape=outs,
+        in_specs=[SMEM] * 4 + [VMEM] * (1 + peers),
+        out_specs=[VMEM, VMEM],
+    )(slot_rows, dests, table, start, tiles, *pieces)
+
+
+def first_kernel(peers, rows_ref, dests_ref, start_ref, tiles_ref, x_ref, upper_ref, rows_in_ref, *refs):
+    term_refs = refs[:peers]
+    slices_ref = refs[peers]
+    acc_ref = refs[peers + 1]
+    share = slices_ref.shape[1]
+    start = pl.multiple_of(start_ref[0], 8)
+    slices_ref[...] = rows_in_ref[...]
+    slices_ref[0] = x_ref[pl.ds(start, share), :]
+    acc_ref[...] = upper_ref[...]
+    first = x_ref[...].astype(jnp.bfloat16)
+    for s in range(tiles_ref.shape[0]):
+
+        @pl.when(rows_ref[s] == 0)
+        def _():
+            prod = lax.dot_general(
+                tiles_ref[s], first, (((0,), (0,)), ((), ())), preferred_element_type=jnp.float32
+            )
+            acc_ref[dests_ref[s]] += prod
+
+    for p in range(peers):
+        term_refs[p][...] = acc_ref[p].astype(jnp.bfloat16)
+
+
+def first_terms(slot_rows, dests, start, tiles, first, upper, upper_rows):
+    peers = upper.shape[0]
+    outs = [jax.ShapeDtypeStruct(first.shape, jnp.bfloat16) for _ in range(peers)]
+    outs.append(jax.ShapeDtypeStruct(upper_rows.shape, jnp.float32))
+    result = pl.pallas_call(
+        functools.partial(first_kernel, peers),
+        out_shape=outs,
+        in_specs=[SMEM] * 3 + [VMEM] * 4,
+        out_specs=[VMEM] * (peers + 1),
+        scratch_shapes=[pltpu.VMEM(upper.shape, jnp.float32)],
+    )(slot_rows, dests, start, tiles, first, upper, upper_rows)
+    return result[:peers], result[peers]
 
 
 def pair_index(t, u):
@@ -245,6 +327,9 @@
             )
             pushed = later if level == 0 else pushed[1:] + later
     own_solution = None
+    table = ((me - jnp.arange(levels)) % peers).astype(jnp.int32)
+    dests = ((me - slot_cols) % peers).astype(jnp.int32)
+    start = (position * share)[None].astype(jnp.int32)
     for level in reversed(range(levels)):
         update = top_forward[level].astype(jnp.float32)
         if level < levels - 1:
@@ -259,11 +344,11 @@
                 "uab,ac->ubc", mats[1 : level + 1], solved.astype(jnp.bfloat16), preferred_element_type=jnp.float32
             )
             pushed = earlier if level == levels - 1 else pushed[:level] + earlier
-    pieces = [own_solution] + [shifted(own_solution, "col", peers, s) for s in range(1, peers)]
-    table = ((me - jnp.arange(levels)) % peers).astype(jnp.int32)
-    dests = ((me - slot_cols) % peers).astype(jnp.int32)
-    start = (position * share)[None].astype(jnp.int32)
-    terms, top_rows = tail_terms(slot_rows, dests, table, start, own_tiles, pieces, levels, share)
+        if level == 1:
+            pieces = [own_solution] + [shifted(own_solution, "col", peers, s) for s in range(1, peers)]
+            upper, upper_rows = upper_terms(slot_rows, dests, table, start, own_tiles, pieces, levels, share)
+    first = broadcast_from(solved, 0, me, "col", peers)
+    terms, top_rows = first_terms(slot_rows, dests, start, own_tiles, first, upper, upper_rows)
     returned = [terms[0]] + [shifted(terms[s], "col", peers, peers - s) for s in range(1, peers)]
     low_solution = last_solve(low_forward, low_inv, returned)
     return (low_solution, top_rows)

time: 146 us -> 154 us (1.055)
  starting transfers between devices: 22.8 us -> 54.5 us
  waiting for transfers between devices: 79.3 us -> 49.1 us
  Pallas kernels: 8.63 us -> 11.9 us
  matrix products: 10.4 us -> 13.1 us
    ppermute x3, waiting for transfers between devices: 23.3 us -> 0.01 us  [local(): pushed = lax.ppermute(pushed, 'col', [(level + 1, level)])]
    ppermute x9, starting transfers between devices: 9.26 us -> 31.6 us  [shifted(): return lax.ppermute(x, axis, [(i, (i + shift) % size) for i in range(size)])]
    ppermute x9, waiting for transfers between devices: 21.7 us -> 13 us  [shifted(): return lax.ppermute(x, axis, [(i, (i + shift) % size) for i in range(size)])]
    ppermute x0 -> x3, starting transfers between devices: none -> 7.92 us  [broadcast_from(): part = lax.ppermute(x, axis, [(owner, (owner + s) % size)])]
    pallas_call x1 -> x2, Pallas kernels: 3.31 us -> 6.57 us  [the longest x1 3.67 us: upper_terms(): pl.pallas_call(functools.partial(upper_kernel, levels, peers), out_shape=...]
    ppermute x0 -> x3, waiting for transfers between devices: none -> 1.94 us  [broadcast_from(): part = lax.ppermute(x, axis, [(owner, (owner + s) % size)])]
    dot_general x3, matrix products: 1.43 us -> 3.29 us  [local(): jnp.einsum('uab,ac->ubc', mats[1:level + 1], solved.astype(jnp.bfloat16),...]
  transfers between devices with their start and end apart: 21 -> 24, of which waited for: 15 -> 13; matrix products, arithmetic and copies ran while one was open for 4% -> 4% of each run, Pallas kernels for 2% -> 4%
where the time goes in v12:
time: 154 us
  starting transfers between devices  54.5 us (35%)
  waiting for transfers between devices  49.1 us (32%)
  between operations  14.4 us (9%)
  matrix products  13.1 us (9%)
  Pallas kernels  11.9 us (8%)
  other arithmetic  6.93 us (4%)
  local copies, waits for them, and re-layouts  3.8 us (2%)
    ppermute x9, starting transfers between devices, shifted(): return lax.ppermute(x, axis, [(i, (i + shift) % size) for i in range(size)])  31.6 us
    ppermute x5, waiting for transfers between devices, swapped(): return lax.ppermute(x, axis, [(i, i ^ bit) for i in range(size)])  31.5 us
    ppermute x9, waiting for transfers between devices, shifted(): return lax.ppermute(x, axis, [(i, (i + shift) % size) for i in range(size)])  13 us
    ppermute x3, starting transfers between devices, broadcast_from(): part = lax.ppermute(x, axis, [(owner, (owner + s) % size)])  7.92 us
    ppermute x5, starting transfers between devices, swapped(): return lax.ppermute(x, axis, [(i, i ^ bit) for i in range(size)])  7.6 us
    ppermute x3, starting transfers between devices, local(): pushed = lax.ppermute(pushed, 'col', [(level - 1, level)])  3.89 us
    pallas_call x1, Pallas kernels, upper_terms(): pl.pallas_call(functools.partial(upper_kernel, levels, peers), out_shape=...  3.67 us
    dot_general x4, matrix products, local(): lax.dot_general(inv, update.astype(jnp.bfloat16), (((0,), (0,)), ((), ())...  3.64 us
  transfers between devices with their start and end apart: 24, of which 13 were waited for; matrix products, arithmetic and copies ran while one was open for 4% of the time, Pallas kernels for 4%

profile of v12, /device:TPU:0, one launch (start us, length us, event | category | flops | bytes accessed | tf_op | source)
XLA Modules:
  0.0 153.7 jit_solution(12977281241323870980)
XLA Ops:
  7.2 0.7 fusion.47
  8.0 0.7 compare_and_fusion
  8.7 0.9 constant_dynamic-slice_fusion.2
  9.5 0.6 gather_fusion
  10.2 0.7 pad_maximum_fusion.1
  11.0 1.4 convolution_convert_fusion.4.forward_ref
  12.3 2.5 %collective-permute-start.2 = (bf16[512,128]{1,0:T(8,128)(2,1)S(1)}, bf16[512,128]{1,0:T(8,128)(2,1)S(1)}, u32[]{:S(2)}, u32[]{:S(2)}) collective-permute-start(bf16[512,128]{1,0:T(8,128)(2,1)S(1)} %convolution_convert_fusion.4.forward_ref), channel_id=1, source_target_pairs={{0,3},{1,0},{2,1},{3,2},{4,7},{5,4},{6,5},{7,6},{8,11},{9,8},{10,9... | collective-permute-start | bytes 393224 | tf_op jit(solution)/shard_map/ppermute | solution.py:73
  14.8 0.6 collective-permute-start.1
  15.6 0.5 and_select_fusion.1
  16.1 0.7 iota_reduce_fusion
  16.8 0.7 pad_add_fusion.fold_ref
  17.5 1.1 collective-permute-done.2
  18.6 3.8 %collective-permute-done.1 = bf16[512,128]{1,0:T(8,128)(2,1)S(1)} collective-permute-done((bf16[512,128]{1,0:T(8,128)(2,1)S(1)}, bf16[512,128]{1,0:T(8,128)(2,1)S(1)}, u32[]{:S(2)}, u32[]{:S(2)}) %collective-permute-start.1) | collective-permute-done | bytes 131104 | tf_op jit(solution)/shard_map/ppermute | solution.py:73
  22.4 0.9 pad_maximum_fusion.panels_ref
  23.2 3.0 %shard_map.104 = bf16[4,512,128]{2,1,0:T(8,128)(2,1)} custom-call(s32[4]{0:T(128)} %bitcast.133, s32[4]{0:T(128)} %get-tuple-element.10.picks_ref, s32[2]{0:T(128)} %pad_add_fusion.fold_ref, bf16[4,512,512]{2,1,0:T(8,128)(2,1)} %bitcast.124, bf16[4,512,128]{2,1,0:T(8,128)(2,1)} %pad_maximum_fusion.panels_ref, bf16[4,64,128]{2,1,0:T(8,128)(2,1)} %rhs_ref.1), custom_call_target="tpu_custom_call" | custom-call | tf_op jit(solution)/shard_map/pallas_call | solution.py:37
  26.3 1.0 dynamic-slice_bitcast_fusion
  27.4 1.5 collective-permute-done.3
  28.8 1.0 fusion.1
  29.9 1.7 %collective-permute-start.4 = (bf16[1,512,128]{2,1,0:T(8,128)(2,1)S(1)}, bf16[1,512,128]{2,1,0:T(8,128)(2,1)S(1)}, u32[]{:S(2)}, u32[]{:S(2)}) collective-permute-start(bf16[1,512,128]{2,1,0:T(8,128)(2,1)S(1)} %constant_dynamic-slice_fusion), channel_id=1, source_target_pairs={{0,2},{1,3},{2,0},{3,1},{4,6},{5,7},{6,4},{7,5},{8,10},{9,11},{10,... | collective-permute-start | bytes 393224 | tf_op jit(solution)/shard_map/ppermute | solution.py:77
  31.6 3.9 %collective-permute-done.4 = bf16[1,512,128]{2,1,0:T(8,128)(2,1)S(1)} collective-permute-done((bf16[1,512,128]{2,1,0:T(8,128)(2,1)S(1)}, bf16[1,512,128]{2,1,0:T(8,128)(2,1)S(1)}, u32[]{:S(2)}, u32[]{:S(2)}) %collective-permute-start.4) | collective-permute-done | bytes 131104 | tf_op jit(solution)/shard_map/ppermute | solution.py:77
  35.5 1.7 %collective-permute-start.5 = (bf16[512,128]{1,0:T(8,128)(2,1)S(1)}, bf16[512,128]{1,0:T(8,128)(2,1)S(1)}, u32[]{:S(2)}, u32[]{:S(2)}) collective-permute-start(bf16[512,128]{1,0:T(8,128)(2,1)S(1)} %fusion.17), channel_id=1, source_target_pairs={{0,4},{4,0},{8,12},{12,8},{16,20},{20,16},{24,28},{28,24},{1,5},{5... | collective-permute-start | bytes 393224 | tf_op jit(solution)/shard_map/ppermute | solution.py:77
  37.3 3.3 %collective-permute-done.5 = bf16[512,128]{1,0:T(8,128)(2,1)S(1)} collective-permute-done((bf16[512,128]{1,0:T(8,128)(2,1)S(1)}, bf16[512,128]{1,0:T(8,128)(2,1)S(1)}, u32[]{:S(2)}, u32[]{:S(2)}) %collective-permute-start.5) | collective-permute-done | bytes 131104 | tf_op jit(solution)/shard_map/ppermute | solution.py:77
  40.6 1.8 %collective-permute-start.6 = (bf16[512,128]{1,0:T(8,128)(2,1)S(1)}, bf16[512,128]{1,0:T(8,128)(2,1)S(1)}, u32[]{:S(2)}, u32[]{:S(2)}) collective-permute-start(bf16[512,128]{1,0:T(8,128)(2,1)S(1)} %add_convert_fusion.2), channel_id=1, source_target_pairs={{0,8},{4,12},{8,0},{12,4},{16,24},{20,28},{24,16},{28,20},{1,9},{5... | collective-permute-start | bytes 393224 | tf_op jit(solution)/shard_map/ppermute | solution.py:77
  42.4 9.5 %collective-permute-done.6 = bf16[512,128]{1,0:T(8,128)(2,1)S(1)} collective-permute-done((bf16[512,128]{1,0:T(8,128)(2,1)S(1)}, bf16[512,128]{1,0:T(8,128)(2,1)S(1)}, u32[]{:S(2)}, u32[]{:S(2)}) %collective-permute-start.6) | collective-permute-done | bytes 131104 | tf_op jit(solution)/shard_map/ppermute | solution.py:77
  51.9 2.3 %collective-permute-start.7 = (bf16[512,128]{1,0:T(8,128)(2,1)S(1)}, bf16[512,128]{1,0:T(8,128)(2,1)S(1)}, u32[]{:S(2)}, u32[]{:S(2)}) collective-permute-start(bf16[512,128]{1,0:T(8,128)(2,1)S(1)} %add_convert_fusion.1), channel_id=1, source_target_pairs={{0,16},{4,20},{8,24},{12,28},{16,0},{20,4},{24,8},{28,12},{1,17},{... | collective-permute-start | bytes 393224 | tf_op jit(solution)/shard_map/ppermute | solution.py:77
  54.2 13.3 %collective-permute-done.7 = bf16[512,128]{1,0:T(8,128)(2,1)S(1)} collective-permute-done((bf16[512,128]{1,0:T(8,128)(2,1)S(1)}, bf16[512,128]{1,0:T(8,128)(2,1)S(1)}, u32[]{:S(2)}, u32[]{:S(2)}) %collective-permute-start.7) | collective-permute-done | bytes 131104 | tf_op jit(solution)/shard_map/ppermute | solution.py:77
  67.6 0.8 all-gather.2.cloned.1.call-done
  68.4 1.5 convolution_convert_fusion.3
  69.9 2.0 %fusion.36 = f32[3,512,128]{2,1,0:T(8,128)S(1)} fusion(bf16[4,512,512]{2,1,0:T(8,128)(2,1)} %all-gather.2.cloned.1.call-done, bf16[512,128]{1,0:T(8,128)(2,1)S(1)} %convolution_convert_fusion.3), kind=kOutput, calls=%fused_computation.57 | convolution fusion | flops 201326592 | bytes 3014656 | tf_op jit(solution)/shard_map/kab,bc->kac/dot_general | solution.py:325
  71.8 1.8 %collective-permute-start.8 = (f32[3,512,128]{2,1,0:T(8,128)S(1)}, f32[3,512,128]{2,1,0:T(8,128)S(1)}, u32[]{:S(2)}, u32[]{:S(2)}) collective-permute-start(f32[3,512,128]{2,1,0:T(8,128)S(1)} %fusion.36), channel_id=1, source_target_pairs={{0,1},{4,5},{8,9},{12,13},{16,17},{20,21},{24,25},{28,29}} | collective-permute-start | bytes 2359304 | tf_op jit(solution)/shard_map/ppermute | solution.py:320
  73.7 1.8 %collective-permute-done.8 = f32[3,512,128]{2,1,0:T(8,128)S(1)} collective-permute-done((f32[3,512,128]{2,1,0:T(8,128)S(1)}, f32[3,512,128]{2,1,0:T(8,128)S(1)}, u32[]{:S(2)}, u32[]{:S(2)}) %collective-permute-start.8) | collective-permute-done | bytes 786464 | tf_op jit(solution)/shard_map/ppermute | solution.py:320
  75.5 0.3 convolution_convert_fusion.2
  75.8 0.4 slice_add_fusion.1
  76.3 0.7 collective-permute-start.9
  77.0 0.3 convolution_convert_fusion.1
  77.3 0.3 slice_add_fusion.3
  77.6 1.4 collective-permute-start.10
  79.0 1.7 %fusion = f32[512,128]{1,0:T(8,128)S(1)} fusion(bf16[4,512,512]{2,1,0:T(8,128)(2,1)S(1)} %copy-done.1, f32[1,512,128]{2,1,0:T(8,128)} %collective-permute-done.10, bf16[512,128]{1,0:T(8,128)(2,1)S(1)} %add_convert_fusion), kind=kOutput, calls=%fused_computation.8 | convolution fusion | flops 134545408 | bytes 1703936 | tf_op jit(solution)/shard_map/dot_general | solution.py:338
  80.7 0.6 fusion.30
  81.3 0.7 collective-permute-start.11
  82.0 0.3 fusion.15
  82.4 1.3 slice_add_fusion
  83.6 1.5 collective-permute-start.12
  85.1 1.3 select_select_fusion
  86.4 1.4 slice_add_fusion.2
  87.8 1.3 collective-permute-start.13
  89.1 24.1 %collective-permute-start.17 = (f32[512,128]{1,0:T(8,128)S(1)}, f32[512,128]{1,0:T(8,128)S(1)}, u32[]{:S(2)}, u32[]{:S(2)}) collective-permute-start(f32[512,128]{1,0:T(8,128)S(1)} %get-tuple-element.20.refs_0_), channel_id=1, source_target_pairs={{0,1},{1,2},{2,3},{3,0},{4,5},{5,6},{6,7},{7,4},{8,9},{9,10},{10,1... | collective-permute-start | bytes 786440 | tf_op jit(solution)/shard_map/ppermute | solution.py:73
  113.3 1.4 collective-permute-start.19
  114.7 0.3 fusion.16
  115.0 2.6 %collective-permute-start.16 = (f32[512,128]{1,0:T(8,128)S(1)}, f32[512,128]{1,0:T(8,128)S(1)}, u32[]{:S(2)}, u32[]{:S(2)}) collective-permute-start(f32[512,128]{1,0:T(8,128)S(1)} %fusion.16), channel_id=1, source_target_pairs={{0,3},{4,7},{8,11},{12,15},{16,19},{20,23},{24,27},{28,31}} | collective-permute-start | bytes 786440 | tf_op jit(solution)/shard_map/ppermute | solution.py:83
  117.7 1.3 collective-permute-start.14
  119.0 0.7 copy-done.4
  119.7 4.0 %collective-permute-start.15 = (f32[512,128]{1,0:T(8,128)S(1)}, f32[512,128]{1,0:T(8,128)S(1)}, u32[]{:S(2)}, u32[]{:S(2)}) collective-permute-start(f32[512,128]{1,0:T(8,128)S(1)} %fusion.16), channel_id=1, source_target_pairs={{0,2},{4,6},{8,10},{12,14},{16,18},{20,22},{24,26},{28,30}} | collective-permute-start | bytes 786440 | tf_op jit(solution)/shard_map/ppermute | solution.py:83
  123.7 1.2 collective-permute-done.19.refs_3_
  124.9 3.7 %shard_map.105 = (f32[4,512,128]{2,1,0:T(8,128)}, f32[4,64,128]{2,1,0:T(8,128)}) custom-call(s32[4]{0:T(128)} %bitcast.134, s32[4]{0:T(128)} %get-tuple-element.18.dests_ref, s32[4]{0:T(128)} %copy-done.8, s32[1]{0:T(128)} %bitcast.4.start_ref, bf16[4,512,512]{2,1,0:T(8,128)(2,1)} %bitcast.125, f32[512,128]{1,0:T(8,128)} %copy-done.3, f32[512,128]{1,0:T(8,128)} %copy-done.4, ...), custom_call_target="tpu_custom_call" | custom-call | tf_op jit(solution)/shard_map/pallas_call | solution.py:195
  128.6 1.9 %collective-permute-done.15 = f32[512,128]{1,0:T(8,128)S(1)} collective-permute-done((f32[512,128]{1,0:T(8,128)S(1)}, f32[512,128]{1,0:T(8,128)S(1)}, u32[]{:S(2)}, u32[]{:S(2)}) %collective-permute-start.15) | collective-permute-done | bytes 262176 | tf_op jit(solution)/shard_map/ppermute | solution.py:83
  130.5 0.8 add_select_fusion.x_ref
  131.3 2.9 %shard_map.106 = (bf16[512,128]{1,0:T(8,128)(2,1)}, bf16[512,128]{1,0:T(8,128)(2,1)}, bf16[512,128]{1,0:T(8,128)(2,1)}, bf16[512,128]{1,0:T(8,128)(2,1)}, f32[4,64,128]{2,1,0:T(8,128)}) custom-call(s32[4]{0:T(128)} %bitcast.135, s32[4]{0:T(128)} %get-tuple-element.18.dests_ref, s32[1]{0:T(128)} %bitcast.4.start_ref, bf16[4,512,512]{2,1,0:T(8,128)(2,1)} %bitcast.126, ...), custom_call_target="tpu_custom_call" | custom-call | tf_op jit(solution)/shard_map/pallas_call | solution.py:230
  134.3 2.5 %collective-permute-start.21 = (bf16[512,128]{1,0:T(8,128)(2,1)}, bf16[512,128]{1,0:T(8,128)(2,1)S(1)}, u32[]{:S(2)}, u32[]{:S(2)}) collective-permute-start(bf16[512,128]{1,0:T(8,128)(2,1)} %get-tuple-element.15), channel_id=1, source_target_pairs={{0,2},{1,3},{2,0},{3,1},{4,6},{5,7},{6,4},{7,5},{8,10},{9,11},{10,... | collective-permute-start | bytes 393224 | tf_op jit(solution)/shard_map/ppermute | solution.py:73
  136.7 0.2 collective-permute-start.22
  136.9 0.2 collective-permute-done.20.refs_1_
  137.1 6.7 %collective-permute-done.21.refs_2_ = bf16[512,128]{1,0:T(8,128)(2,1)S(1)} collective-permute-done((bf16[512,128]{1,0:T(8,128)(2,1)}, bf16[512,128]{1,0:T(8,128)(2,1)S(1)}, u32[]{:S(2)}, u32[]{:S(2)}) %collective-permute-start.21) | collective-permute-done | bytes 131104 | tf_op jit(solution)/shard_map/ppermute | solution.py:73
  143.8 0.6 copy-done.6
  144.5 2.3 %shard_map.107 = f32[1,512,128]{2,1,0:T(8,128)} custom-call(bf16[512,128]{1,0:T(8,128)(2,1)} %copy-done.2, bf16[1,512,512]{2,1,0:T(8,128)(2,1)} %inv_ref.1, bf16[512,128]{1,0:T(8,128)(2,1)} %get-tuple-element.13.refs_0_, bf16[512,128]{1,0:T(8,128)(2,1)} %copy-done.5, bf16[512,128]{1,0:T(8,128)(2,1)} %copy-done.6, bf16[512,128]{1,0:T(8,128)(2,1)} %copy-done.7), custom_call_target="tpu_custom_call" | custom-call | tf_op jit(solution)/shard_map/pallas_call | solution.py:150
  (42 shorter events, 0.7 us)
Async XLA Ops:
  7.2 2.4 %copy-start = (bf16[6,64,512]{2,1,0:T(8,128)(2,1)S(1)}, bf16[6,64,512]{2,1,0:T(8,128)(2,1)}, u32[]{:S(2)}) copy-start(bf16[6,64,512]{2,1,0:T(8,128)(2,1)} %param.16) | copy-start | bytes 1179652
  7.2 8.4 %copy-start.9 = (s32[1,4]{1,0:T(1,128)S(1)}, s32[1,4]{1,0:T(1,128)}, u32[]{:S(2)}) copy-start(s32[1,4]{1,0:T(1,128)} %param.13) | copy-start | bytes 52
  7.2 61.2 %all-gather.2.cloned.1.call-start = ((), (), s32[]{:S(2)}) async-start(), calls=%async_computation | async-start | bytes 2359296 | tf_op jit(solution)/shard_map/all_gather | solution.py:293
  12.3 14.0 %copy-start.2 = (bf16[512,128]{1,0:T(8,128)(2,1)}, bf16[512,128]{1,0:T(8,128)(2,1)S(1)}, u32[]{:S(2)}) copy-start(bf16[512,128]{1,0:T(8,128)(2,1)S(1)} %convolution_convert_fusion.4.forward_ref) | copy-start | bytes 393220
  12.3 6.3 %collective-permute-start.2 = (bf16[512,128]{1,0:T(8,128)(2,1)S(1)}, bf16[512,128]{1,0:T(8,128)(2,1)S(1)}, u32[]{:S(2)}, u32[]{:S(2)}) collective-permute-start(bf16[512,128]{1,0:T(8,128)(2,1)S(1)} %convolution_convert_fusion.4.forward_ref), channel_id=1, source_target_pairs={{0,3},{1,0},{2,1},{3,2},{4,7},{5,4},{6,5},{7,6},{8,11},{9,8},{10,9... | collective-permute-start | bytes 393224 | tf_op jit(solution)/shard_map/ppermute | solution.py:73
  14.8 7.5 %collective-permute-start.1 = (bf16[512,128]{1,0:T(8,128)(2,1)S(1)}, bf16[512,128]{1,0:T(8,128)(2,1)S(1)}, u32[]{:S(2)}, u32[]{:S(2)}) collective-permute-start(bf16[512,128]{1,0:T(8,128)(2,1)S(1)} %convolution_convert_fusion.4.forward_ref), channel_id=1, source_target_pairs={{0,2},{1,3},{2,0},{3,1},{4,6},{5,7},{6,4},{7,5},{8,10},{9,11},{10,... | collective-permute-start | bytes 393224 | tf_op jit(solution)/shard_map/ppermute | solution.py:73
  15.5 6.9 %collective-permute-start = (bf16[512,128]{1,0:T(8,128)(2,1)S(1)}, bf16[512,128]{1,0:T(8,128)(2,1)S(1)}, u32[]{:S(2)}, u32[]{:S(2)}) collective-permute-start(bf16[512,128]{1,0:T(8,128)(2,1)S(1)} %convolution_convert_fusion.4.forward_ref), channel_id=1, source_target_pairs={{0,1},{1,2},{2,3},{3,0},{4,5},{5,6},{6,7},{7,4},{8,9},{9,10},{10,1... | collective-permute-start | bytes 393224 | tf_op jit(solution)/shard_map/ppermute | solution.py:73
  16.1 10.2 %copy-start.8 = (s32[4]{0:T(128)}, s32[4]{0:T(128)S(1)}, u32[]{:S(2)}) copy-start(s32[4]{0:T(128)S(1)} %get-tuple-element.22.table_ref) | copy-start | bytes 52
  27.2 1.6 %collective-permute-start.3 = (bf16[2,512,128]{2,1,0:T(8,128)(2,1)S(1)}, bf16[2,512,128]{2,1,0:T(8,128)(2,1)S(1)}, u32[]{:S(2)}, u32[]{:S(2)}) collective-permute-start(bf16[2,512,128]{2,1,0:T(8,128)(2,1)S(1)} %dynamic-slice_bitcast_fusion), channel_id=1, source_target_pairs={{0,1},{1,0},{2,3},{3,2},{4,5},{5,4},{6,7},{7,6},{8,9},{9,8},{10,11... | collective-permute-start | bytes 786440 | tf_op jit(solution)/shard_map/ppermute | solution.py:77
  29.9 5.6 %collective-permute-start.4 = (bf16[1,512,128]{2,1,0:T(8,128)(2,1)S(1)}, bf16[1,512,128]{2,1,0:T(8,128)(2,1)S(1)}, u32[]{:S(2)}, u32[]{:S(2)}) collective-permute-start(bf16[1,512,128]{2,1,0:T(8,128)(2,1)S(1)} %constant_dynamic-slice_fusion), channel_id=1, source_target_pairs={{0,2},{1,3},{2,0},{3,1},{4,6},{5,7},{6,4},{7,5},{8,10},{9,11},{10,... | collective-permute-start | bytes 393224 | tf_op jit(solution)/shard_map/ppermute | solution.py:77
  35.5 5.0 %collective-permute-start.5 = (bf16[512,128]{1,0:T(8,128)(2,1)S(1)}, bf16[512,128]{1,0:T(8,128)(2,1)S(1)}, u32[]{:S(2)}, u32[]{:S(2)}) collective-permute-start(bf16[512,128]{1,0:T(8,128)(2,1)S(1)} %fusion.17), channel_id=1, source_target_pairs={{0,4},{4,0},{8,12},{12,8},{16,20},{20,16},{24,28},{28,24},{1,5},{5... | collective-permute-start | bytes 393224 | tf_op jit(solution)/shard_map/ppermute | solution.py:77
  40.6 11.3 %collective-permute-start.6 = (bf16[512,128]{1,0:T(8,128)(2,1)S(1)}, bf16[512,128]{1,0:T(8,128)(2,1)S(1)}, u32[]{:S(2)}, u32[]{:S(2)}) collective-permute-start(bf16[512,128]{1,0:T(8,128)(2,1)S(1)} %add_convert_fusion.2), channel_id=1, source_target_pairs={{0,8},{4,12},{8,0},{12,4},{16,24},{20,28},{24,16},{28,20},{1,9},{5... | collective-permute-start | bytes 393224 | tf_op jit(solution)/shard_map/ppermute | solution.py:77
  51.9 15.6 %collective-permute-start.7 = (bf16[512,128]{1,0:T(8,128)(2,1)S(1)}, bf16[512,128]{1,0:T(8,128)(2,1)S(1)}, u32[]{:S(2)}, u32[]{:S(2)}) collective-permute-start(bf16[512,128]{1,0:T(8,128)(2,1)S(1)} %add_convert_fusion.1), channel_id=1, source_target_pairs={{0,16},{4,20},{8,24},{12,28},{16,0},{20,4},{24,8},{28,12},{1,17},{... | collective-permute-start | bytes 393224 | tf_op jit(solution)/shard_map/ppermute | solution.py:77
  68.4 7.1 %copy-start.1 = (bf16[4,512,512]{2,1,0:T(8,128)(2,1)S(1)}, bf16[4,512,512]{2,1,0:T(8,128)(2,1)}, u32[]{:S(2)}) copy-start(bf16[4,512,512]{2,1,0:T(8,128)(2,1)} %all-gather.2.cloned.1.call-done) | copy-start | bytes 6291460
  71.8 3.7 %collective-permute-start.8 = (f32[3,512,128]{2,1,0:T(8,128)S(1)}, f32[3,512,128]{2,1,0:T(8,128)S(1)}, u32[]{:S(2)}, u32[]{:S(2)}) collective-permute-start(f32[3,512,128]{2,1,0:T(8,128)S(1)} %fusion.36), channel_id=1, source_target_pairs={{0,1},{4,5},{8,9},{12,13},{16,17},{20,21},{24,25},{28,29}} | collective-permute-start | bytes 2359304 | tf_op jit(solution)/shard_map/ppermute | solution.py:320
  76.3 0.7 collective-permute-start.9
  77.6 1.4 collective-permute-start.10
  81.3 0.7 collective-permute-start.11
  83.6 1.5 collective-permute-start.12
  86.4 38.5 %copy-start.3 = (f32[512,128]{1,0:T(8,128)}, f32[512,128]{1,0:T(8,128)S(1)}, u32[]{:S(2)}) copy-start(f32[512,128]{1,0:T(8,128)S(1)} %get-tuple-element.20.refs_0_) | copy-start | bytes 786436
  87.8 26.9 %collective-permute-start.13 = (f32[1,512,128]{2,1,0:T(8,128)S(1)}, f32[1,512,128]{2,1,0:T(8,128)S(1)}, u32[]{:S(2)}, u32[]{:S(2)}) collective-permute-start(f32[1,512,128]{2,1,0:T(8,128)S(1)} %slice_add_fusion.2), channel_id=1, source_target_pairs={{1,0},{5,4},{9,8},{13,12},{17,16},{21,20},{25,24},{29,28}} | collective-permute-start | bytes 786440 | tf_op jit(solution)/shard_map/ppermute | solution.py:336
  89.1 29.9 %collective-permute-start.17 = (f32[512,128]{1,0:T(8,128)S(1)}, f32[512,128]{1,0:T(8,128)S(1)}, u32[]{:S(2)}, u32[]{:S(2)}) collective-permute-start(f32[512,128]{1,0:T(8,128)S(1)} %get-tuple-element.20.refs_0_), channel_id=1, source_target_pairs={{0,1},{1,2},{2,3},{3,0},{4,5},{5,6},{6,7},{7,4},{8,9},{9,10},{10,1... | collective-permute-start | bytes 786440 | tf_op jit(solution)/shard_map/ppermute | solution.py:73
  113.3 10.4 %collective-permute-start.18 = (f32[512,128]{1,0:T(8,128)S(1)}, f32[512,128]{1,0:T(8,128)}, u32[]{:S(2)}, u32[]{:S(2)}) collective-permute-start(f32[512,128]{1,0:T(8,128)S(1)} %get-tuple-element.20.refs_0_), channel_id=1, source_target_pairs={{0,2},{1,3},{2,0},{3,1},{4,6},{5,7},{6,4},{7,5},{8,10},{9,11},{10,... | collective-permute-start | bytes 786440 | tf_op jit(solution)/shard_map/ppermute | solution.py:73
  113.3 11.6 %collective-permute-start.19 = (f32[512,128]{1,0:T(8,128)S(1)}, f32[512,128]{1,0:T(8,128)}, u32[]{:S(2)}, u32[]{:S(2)}) collective-permute-start(f32[512,128]{1,0:T(8,128)S(1)} %get-tuple-element.20.refs_0_), channel_id=1, source_target_pairs={{0,3},{1,0},{2,1},{3,2},{4,7},{5,4},{6,5},{7,6},{8,11},{9,8},{10,9... | collective-permute-start | bytes 786440 | tf_op jit(solution)/shard_map/ppermute | solution.py:73
  115.0 13.5 %collective-permute-start.16 = (f32[512,128]{1,0:T(8,128)S(1)}, f32[512,128]{1,0:T(8,128)S(1)}, u32[]{:S(2)}, u32[]{:S(2)}) collective-permute-start(f32[512,128]{1,0:T(8,128)S(1)} %fusion.16), channel_id=1, source_target_pairs={{0,3},{4,7},{8,11},{12,15},{16,19},{20,23},{24,27},{28,31}} | collective-permute-start | bytes 786440 | tf_op jit(solution)/shard_map/ppermute | solution.py:83
  117.7 10.9 %collective-permute-start.14 = (f32[512,128]{1,0:T(8,128)S(1)}, f32[512,128]{1,0:T(8,128)S(1)}, u32[]{:S(2)}, u32[]{:S(2)}) collective-permute-start(f32[512,128]{1,0:T(8,128)S(1)} %fusion.16), channel_id=1, source_target_pairs={{0,1},{4,5},{8,9},{12,13},{16,17},{20,21},{24,25},{28,29}} | collective-permute-start | bytes 786440 | tf_op jit(solution)/shard_map/ppermute | solution.py:83
  119.0 0.7 copy-start.4
  119.7 10.8 %collective-permute-start.15 = (f32[512,128]{1,0:T(8,128)S(1)}, f32[512,128]{1,0:T(8,128)S(1)}, u32[]{:S(2)}, u32[]{:S(2)}) collective-permute-start(f32[512,128]{1,0:T(8,128)S(1)} %fusion.16), channel_id=1, source_target_pairs={{0,2},{4,6},{8,10},{12,14},{16,18},{20,22},{24,26},{28,30}} | collective-permute-start | bytes 786440 | tf_op jit(solution)/shard_map/ppermute | solution.py:83
  134.2 2.9 %collective-permute-start.20 = (bf16[512,128]{1,0:T(8,128)(2,1)}, bf16[512,128]{1,0:T(8,128)(2,1)S(1)}, u32[]{:S(2)}, u32[]{:S(2)}) collective-permute-start(bf16[512,128]{1,0:T(8,128)(2,1)} %get-tuple-element.14), channel_id=1, source_target_pairs={{0,3},{1,0},{2,1},{3,2},{4,7},{5,4},{6,5},{7,6},{8,11},{9,8},{10,9... | collective-permute-start | bytes 393224 | tf_op jit(solution)/shard_map/ppermute | solution.py:73
  134.3 9.6 %collective-permute-start.21 = (bf16[512,128]{1,0:T(8,128)(2,1)}, bf16[512,128]{1,0:T(8,128)(2,1)S(1)}, u32[]{:S(2)}, u32[]{:S(2)}) collective-permute-start(bf16[512,128]{1,0:T(8,128)(2,1)} %get-tuple-element.15), channel_id=1, source_target_pairs={{0,2},{1,3},{2,0},{3,1},{4,6},{5,7},{6,4},{7,5},{8,10},{9,11},{10,... | collective-permute-start | bytes 393224 | tf_op jit(solution)/shard_map/ppermute | solution.py:73
  136.7 7.1 %collective-permute-start.22 = (bf16[512,128]{1,0:T(8,128)(2,1)}, bf16[512,128]{1,0:T(8,128)(2,1)S(1)}, u32[]{:S(2)}, u32[]{:S(2)}) collective-permute-start(bf16[512,128]{1,0:T(8,128)(2,1)} %get-tuple-element.16), channel_id=1, source_target_pairs={{0,1},{1,2},{2,3},{3,0},{4,5},{5,6},{6,7},{7,4},{8,9},{9,10},{10,1... | collective-permute-start | bytes 393224 | tf_op jit(solution)/shard_map/ppermute | solution.py:73
  137.1 6.7 %copy-start.5 = (bf16[512,128]{1,0:T(8,128)(2,1)}, bf16[512,128]{1,0:T(8,128)(2,1)S(1)}, u32[]{:S(2)}) copy-start(bf16[512,128]{1,0:T(8,128)(2,1)S(1)} %collective-permute-done.20.refs_1_) | copy-start | bytes 393220
  143.8 0.6 copy-start.6
  143.8 0.7 copy-start.7
Sparse Core Ops, SparseCore 0:
  11.1 57.2 all-gather.1

commit v13 on v10

--- a/solution.py
+++ b/solution.py
@@ -204,10 +204,11 @@
     me = lax.axis_index("col")
     owned = jnp.minimum(me, levels - 1)
 
-    picks = jnp.asarray(tile_table(levels))[owned]
-    mine = jnp.concatenate(
-        [lax.dynamic_index_in_dim(top_inv, owned, 0), jnp.take(top_tiles, picks, axis=0)], axis=0
-    )
+    pieces = [lax.dynamic_slice_in_dim(top_inv, owned, 1, 0)]
+    for j in range(levels - 1):
+        index = jnp.where(j < owned, owned * (owned - 1) // 2 + j, (j + 1) * j // 2 + owned)
+        pieces.append(lax.dynamic_slice_in_dim(top_tiles, index, 1, 0))
+    mine = jnp.concatenate(pieces, axis=0)
     mats = lax.all_gather(mine, "row", axis=1, tiled=True)
     inv = mats[0]
 

time: 146 us -> 146 us (level)
  other arithmetic: 6.23 us -> 4.72 us
  waiting for transfers between devices: 79.3 us -> 80.8 us
    ppermute x5, starting transfers between devices: 7.56 us -> 5.69 us  [swapped(): return lax.ppermute(x, axis, [(i, i ^ bit) for i in range(size)])]
where the time goes in v13:
time: 146 us; the launch traced here: 145 us
  waiting for transfers between devices  80.8 us (55%)
  starting transfers between devices  21.6 us (15%)
  between operations  14.4 us (10%)
  matrix products  11.2 us (8%)
  Pallas kernels  8.72 us (6%)
  other arithmetic  4.72 us (3%)
  local copies, waits for them, and re-layouts  3.36 us (2%)
    ppermute x5, waiting for transfers between devices, swapped(): return lax.ppermute(x, axis, [(i, i ^ bit) for i in range(size)])  33.4 us
    ppermute x3, waiting for transfers between devices, local(): pushed = lax.ppermute(pushed, 'col', [(level + 1, level)])  22.8 us
    ppermute x9, waiting for transfers between devices, shifted(): return lax.ppermute(x, axis, [(i, (i + shift) % size) for i in range(size)])  21.7 us
    ppermute x9, starting transfers between devices, shifted(): return lax.ppermute(x, axis, [(i, (i + shift) % size) for i in range(size)])  9.31 us
    ppermute x5, starting transfers between devices, swapped(): return lax.ppermute(x, axis, [(i, i ^ bit) for i in range(size)])  5.69 us
    ppermute x3, starting transfers between devices, local(): pushed = lax.ppermute(pushed, 'col', [(level - 1, level)])  3.84 us
    dot_general x4, matrix products, local(): lax.dot_general(inv, update.astype(jnp.bfloat16), (((0,), (0,)), ((), ())...  3.66 us
    pallas_call x1, Pallas kernels, tail_terms(): pl.pallas_call(functools.partial(tail_kernel, levels, peers), out_shape=o...  3.31 us
  transfers between devices with their start and end apart: 21, of which 15 were waited for; matrix products, arithmetic and copies ran while one was open for 4% of the time, Pallas kernels for 2%

profile of v13, /device:TPU:0, one launch (start us, length us, event | category | flops | bytes accessed | tf_op | source)
XLA Modules:
  0.0 144.8 jit_solution(3832427658039170578)
XLA Ops:
  7.2 0.0 copy-start
  7.2 0.0 all-gather.2.cloned.1.call-start
  7.3 1.0 constant_dynamic-slice_fusion.3
  8.3 0.7 pad_maximum_fusion.1
  9.0 0.0 all-gather.2.cloned.1.call-update
  9.0 1.3 convolution_convert_fusion.4.forward_ref
  10.4 2.5 %collective-permute-start.2 = (bf16[512,128]{1,0:T(8,128)(2,1)S(1)}, bf16[512,128]{1,0:T(8,128)(2,1)S(1)}, u32[]{:S(2)}, u32[]{:S(2)}) collective-permute-start(bf16[512,128]{1,0:T(8,128)(2,1)S(1)} %convolution_convert_fusion.4.forward_ref), channel_id=1, source_target_pairs={{0,3},{1,0},{2,1},{3,2},{4,7},{5,4},{6,5},{7,6},{8,11},{9,8},{10,9... | collective-permute-start | bytes 393224 | tf_op jit(solution)/shard_map/ppermute | solution.py:73
  12.9 0.6 collective-permute-start.1
  13.5 0.2 collective-permute-start
  13.7 0.6 and_select_fusion.1
  14.3 0.7 iota_reduce_fusion
  15.0 0.6 pad_add_fusion.fold_ref
  15.6 1.1 collective-permute-done.2
  16.7 3.8 %collective-permute-done.1 = bf16[512,128]{1,0:T(8,128)(2,1)S(1)} collective-permute-done((bf16[512,128]{1,0:T(8,128)(2,1)S(1)}, bf16[512,128]{1,0:T(8,128)(2,1)S(1)}, u32[]{:S(2)}, u32[]{:S(2)}) %collective-permute-start.1) | collective-permute-done | bytes 131104 | tf_op jit(solution)/shard_map/ppermute | solution.py:73
  20.4 0.9 pad_maximum_fusion.panels_ref
  21.3 3.1 %shard_map.95 = bf16[4,512,128]{2,1,0:T(8,128)(2,1)} custom-call(s32[4]{0:T(128)} %bitcast.121, s32[4]{0:T(128)} %get-tuple-element.8.picks_ref, s32[2]{0:T(128)} %pad_add_fusion.fold_ref, bf16[4,512,512]{2,1,0:T(8,128)(2,1)} %bitcast.113, bf16[4,512,128]{2,1,0:T(8,128)(2,1)} %pad_maximum_fusion.panels_ref, bf16[4,64,128]{2,1,0:T(8,128)(2,1)} %rhs_ref.1), custom_call_target="tpu_custom_call" | custom-call | tf_op jit(solution)/shard_map/pallas_call | solution.py:37
  24.4 1.0 dynamic-slice_bitcast_fusion
  25.4 0.1 collective-permute-start.3
  25.5 1.5 %collective-permute-done.3 = bf16[2,512,128]{2,1,0:T(8,128)(2,1)S(1)} collective-permute-done((bf16[2,512,128]{2,1,0:T(8,128)(2,1)S(1)}, bf16[2,512,128]{2,1,0:T(8,128)(2,1)S(1)}, u32[]{:S(2)}, u32[]{:S(2)}) %collective-permute-start.3) | collective-permute-done | bytes 262176 | tf_op jit(solution)/shard_map/ppermute | solution.py:77
  27.0 1.0 fusion.1
  28.0 1.7 %collective-permute-start.4 = (bf16[1,512,128]{2,1,0:T(8,128)(2,1)S(1)}, bf16[1,512,128]{2,1,0:T(8,128)(2,1)S(1)}, u32[]{:S(2)}, u32[]{:S(2)}) collective-permute-start(bf16[1,512,128]{2,1,0:T(8,128)(2,1)S(1)} %constant_dynamic-slice_fusion), channel_id=1, source_target_pairs={{0,2},{1,3},{2,0},{3,1},{4,6},{5,7},{6,4},{7,5},{8,10},{9,11},{10,... | collective-permute-start | bytes 393224 | tf_op jit(solution)/shard_map/ppermute | solution.py:77
  29.7 3.9 %collective-permute-done.4 = bf16[1,512,128]{2,1,0:T(8,128)(2,1)S(1)} collective-permute-done((bf16[1,512,128]{2,1,0:T(8,128)(2,1)S(1)}, bf16[1,512,128]{2,1,0:T(8,128)(2,1)S(1)}, u32[]{:S(2)}, u32[]{:S(2)}) %collective-permute-start.4) | collective-permute-done | bytes 131104 | tf_op jit(solution)/shard_map/ppermute | solution.py:77
  33.7 2.3 %collective-permute-start.5 = (bf16[512,128]{1,0:T(8,128)(2,1)S(1)}, bf16[512,128]{1,0:T(8,128)(2,1)S(1)}, u32[]{:S(2)}, u32[]{:S(2)}) collective-permute-start(bf16[512,128]{1,0:T(8,128)(2,1)S(1)} %fusion.16), channel_id=1, source_target_pairs={{0,4},{4,0},{8,12},{12,8},{16,20},{20,16},{24,28},{28,24},{1,5},{5... | collective-permute-start | bytes 393224 | tf_op jit(solution)/shard_map/ppermute | solution.py:77
  36.0 3.3 %collective-permute-done.5 = bf16[512,128]{1,0:T(8,128)(2,1)S(1)} collective-permute-done((bf16[512,128]{1,0:T(8,128)(2,1)S(1)}, bf16[512,128]{1,0:T(8,128)(2,1)S(1)}, u32[]{:S(2)}, u32[]{:S(2)}) %collective-permute-start.5) | collective-permute-done | bytes 131104 | tf_op jit(solution)/shard_map/ppermute | solution.py:77
  39.4 1.4 collective-permute-start.6
  40.7 10.9 %collective-permute-done.6 = bf16[512,128]{1,0:T(8,128)(2,1)S(1)} collective-permute-done((bf16[512,128]{1,0:T(8,128)(2,1)S(1)}, bf16[512,128]{1,0:T(8,128)(2,1)S(1)}, u32[]{:S(2)}, u32[]{:S(2)}) %collective-permute-start.6) | collective-permute-done | bytes 131104 | tf_op jit(solution)/shard_map/ppermute | solution.py:77
  51.7 0.2 collective-permute-start.7
  51.9 13.7 %collective-permute-done.7 = bf16[512,128]{1,0:T(8,128)(2,1)S(1)} collective-permute-done((bf16[512,128]{1,0:T(8,128)(2,1)S(1)}, bf16[512,128]{1,0:T(8,128)(2,1)S(1)}, u32[]{:S(2)}, u32[]{:S(2)}) %collective-permute-start.7) | collective-permute-done | bytes 131104 | tf_op jit(solution)/shard_map/ppermute | solution.py:77
  65.7 1.1 all-gather.2.cloned.1.call-done
  66.8 1.5 %convolution_convert_fusion.3 = bf16[512,128]{1,0:T(8,128)(2,1)S(1)} fusion(bf16[4,512,512]{2,1,0:T(8,128)(2,1)} %all-gather.2.cloned.1.call-done, bf16[512,128]{1,0:T(8,128)(2,1)S(1)} %add_convert_fusion), kind=kOutput, calls=%fused_computation.6 | convolution fusion | flops 67371008 | bytes 786432 | tf_op jit(solution)/shard_map/dot_general | solution.py:241
  68.3 2.0 %fusion.35 = f32[3,512,128]{2,1,0:T(8,128)S(1)} fusion(bf16[4,512,512]{2,1,0:T(8,128)(2,1)} %all-gather.2.cloned.1.call-done, bf16[512,128]{1,0:T(8,128)(2,1)S(1)} %convolution_convert_fusion.3), kind=kOutput, calls=%fused_computation.53 | convolution fusion | flops 201326592 | bytes 3014656 | tf_op jit(solution)/shard_map/kab,bc->kac/dot_general | solution.py:244
  70.3 1.8 %collective-permute-start.8 = (f32[3,512,128]{2,1,0:T(8,128)S(1)}, f32[3,512,128]{2,1,0:T(8,128)S(1)}, u32[]{:S(2)}, u32[]{:S(2)}) collective-permute-start(f32[3,512,128]{2,1,0:T(8,128)S(1)} %fusion.35), channel_id=1, source_target_pairs={{0,1},{4,5},{8,9},{12,13},{16,17},{20,21},{24,25},{28,29}} | collective-permute-start | bytes 2359304 | tf_op jit(solution)/shard_map/ppermute | solution.py:239
  72.1 1.8 %collective-permute-done.8 = f32[3,512,128]{2,1,0:T(8,128)S(1)} collective-permute-done((f32[3,512,128]{2,1,0:T(8,128)S(1)}, f32[3,512,128]{2,1,0:T(8,128)S(1)}, u32[]{:S(2)}, u32[]{:S(2)}) %collective-permute-start.8) | collective-permute-done | bytes 786464 | tf_op jit(solution)/shard_map/ppermute | solution.py:239
  73.9 0.3 convolution_convert_fusion.2
  74.2 0.4 slice_add_fusion.1
  74.7 0.7 collective-permute-start.9
  75.4 0.3 convolution_convert_fusion.1
  75.7 0.3 slice_add_fusion.3
  76.0 1.4 collective-permute-start.10
  77.4 1.7 %fusion = f32[512,128]{1,0:T(8,128)S(1)} fusion(bf16[4,512,512]{2,1,0:T(8,128)(2,1)S(1)} %copy-done.1, f32[1,512,128]{2,1,0:T(8,128)} %collective-permute-done.10, bf16[512,128]{1,0:T(8,128)(2,1)S(1)} %add_convert_fusion), kind=kOutput, calls=%fused_computation.8 | convolution fusion | flops 134545408 | bytes 1703936 | tf_op jit(solution)/shard_map/dot_general | solution.py:254
  79.0 0.6 fusion.29
  79.7 0.7 collective-permute-start.11
  80.4 0.3 fusion.15
  80.7 0.5 slice_add_fusion
  81.2 0.7 collective-permute-start.12
  81.9 0.3 fusion.14
  82.3 0.3 slice_add_fusion.2
  82.6 1.3 collective-permute-start.13
  84.0 22.8 %collective-permute-done.13 = f32[1,512,128]{2,1,0:T(8,128)} collective-permute-done((f32[1,512,128]{2,1,0:T(8,128)S(1)}, f32[1,512,128]{2,1,0:T(8,128)}, u32[]{:S(2)}, u32[]{:S(2)}) %collective-permute-start.13) | collective-permute-done | bytes 262176 | tf_op jit(solution)/shard_map/ppermute | solution.py:252
  106.7 1.3 convolution_select_fusion.refs_0_
  108.0 0.2 collective-permute-start.14
  108.2 1.6 %collective-permute-start.16 = (f32[512,128]{1,0:T(8,128)S(1)}, f32[512,128]{1,0:T(8,128)S(1)}, u32[]{:S(2)}, u32[]{:S(2)}) collective-permute-start(f32[512,128]{1,0:T(8,128)S(1)} %convolution_select_fusion.refs_0_), channel_id=1, source_target_pairs={{0,3},{1,0},{2,1},{3,2},{4,7},{5,4},{6,5},{7,6},{8,11},{9,8},{10,9... | collective-permute-start | bytes 786440 | tf_op jit(solution)/shard_map/ppermute | solution.py:73
  109.8 6.1 %collective-permute-done.14.refs_1_ = f32[512,128]{1,0:T(8,128)S(1)} collective-permute-done((f32[512,128]{1,0:T(8,128)S(1)}, f32[512,128]{1,0:T(8,128)S(1)}, u32[]{:S(2)}, u32[]{:S(2)}) %collective-permute-start.14) | collective-permute-done | bytes 262176 | tf_op jit(solution)/shard_map/ppermute | solution.py:73
  116.0 1.4 collective-permute-done.15.refs_2_
  117.4 2.5 %collective-permute-done.16.refs_3_ = f32[512,128]{1,0:T(8,128)S(1)} collective-permute-done((f32[512,128]{1,0:T(8,128)S(1)}, f32[512,128]{1,0:T(8,128)S(1)}, u32[]{:S(2)}, u32[]{:S(2)}) %collective-permute-start.16) | collective-permute-done | bytes 262176 | tf_op jit(solution)/shard_map/ppermute | solution.py:73
  119.9 0.7 copy-done.6
  120.5 3.3 %shard_map.96 = (bf16[512,128]{1,0:T(8,128)(2,1)}, bf16[512,128]{1,0:T(8,128)(2,1)}, bf16[512,128]{1,0:T(8,128)(2,1)}, bf16[512,128]{1,0:T(8,128)(2,1)}, f32[4,64,128]{2,1,0:T(8,128)}) custom-call(s32[4]{0:T(128)} %bitcast.122, s32[4]{0:T(128)} %get-tuple-element.14.dests_ref, s32[4]{0:T(128)} %copy-done.10, s32[1]{0:T(128)} %bitcast.4.start_ref, ...), custom_call_target="tpu_custom_call" | custom-call | tf_op jit(solution)/shard_map/pallas_call | solution.py:127
  123.9 1.9 %collective-permute-start.17 = (bf16[512,128]{1,0:T(8,128)(2,1)}, bf16[512,128]{1,0:T(8,128)(2,1)S(1)}, u32[]{:S(2)}, u32[]{:S(2)}) collective-permute-start(bf16[512,128]{1,0:T(8,128)(2,1)} %get-tuple-element.10), channel_id=1, source_target_pairs={{0,3},{1,0},{2,1},{3,2},{4,7},{5,4},{6,5},{7,6},{8,11},{9,8},{10,9... | collective-permute-start | bytes 393224 | tf_op jit(solution)/shard_map/ppermute | solution.py:73
  125.8 2.3 %collective-permute-start.18 = (bf16[512,128]{1,0:T(8,128)(2,1)}, bf16[512,128]{1,0:T(8,128)(2,1)S(1)}, u32[]{:S(2)}, u32[]{:S(2)}) collective-permute-start(bf16[512,128]{1,0:T(8,128)(2,1)} %get-tuple-element.11), channel_id=1, source_target_pairs={{0,2},{1,3},{2,0},{3,1},{4,6},{5,7},{6,4},{7,5},{8,10},{9,11},{10,... | collective-permute-start | bytes 393224 | tf_op jit(solution)/shard_map/ppermute | solution.py:73
  128.1 1.8 %collective-permute-done.17.refs_1_ = bf16[512,128]{1,0:T(8,128)(2,1)S(1)} collective-permute-done((bf16[512,128]{1,0:T(8,128)(2,1)}, bf16[512,128]{1,0:T(8,128)(2,1)S(1)}, u32[]{:S(2)}, u32[]{:S(2)}) %collective-permute-start.17) | collective-permute-done | bytes 131104 | tf_op jit(solution)/shard_map/ppermute | solution.py:73
  129.9 5.1 %collective-permute-done.18.refs_2_ = bf16[512,128]{1,0:T(8,128)(2,1)S(1)} collective-permute-done((bf16[512,128]{1,0:T(8,128)(2,1)}, bf16[512,128]{1,0:T(8,128)(2,1)S(1)}, u32[]{:S(2)}, u32[]{:S(2)}) %collective-permute-start.18) | collective-permute-done | bytes 131104 | tf_op jit(solution)/shard_map/ppermute | solution.py:73
  135.0 0.6 copy-done.8
  135.6 0.1 copy-done.9
  135.6 2.3 %shard_map.97 = f32[1,512,128]{2,1,0:T(8,128)} custom-call(bf16[512,128]{1,0:T(8,128)(2,1)} %copy-done.2, bf16[1,512,512]{2,1,0:T(8,128)(2,1)} %inv_ref.1, bf16[512,128]{1,0:T(8,128)(2,1)} %get-tuple-element.9.refs_0_, bf16[512,128]{1,0:T(8,128)(2,1)} %copy-done.7, bf16[512,128]{1,0:T(8,128)(2,1)} %copy-done.8, bf16[512,128]{1,0:T(8,128)(2,1)} %copy-done.9), custom_call_target="tpu_custom_call" | custom-call | tf_op jit(solution)/shard_map/pallas_call | solution.py:150
  (33 shorter events, 0.2 us)
Async XLA Ops:
  7.2 1.9 %copy-start = (bf16[1,512,128]{2,1,0:T(8,128)(2,1)S(1)}, bf16[1,512,128]{2,1,0:T(8,128)(2,1)}, u32[]{:S(2)}) copy-start(bf16[1,512,128]{2,1,0:T(8,128)(2,1)} %param.8) | copy-start | bytes 393220
  7.2 6.5 %copy-start.11 = (s32[1,4]{1,0:T(1,128)S(1)}, s32[1,4]{1,0:T(1,128)}, u32[]{:S(2)}) copy-start(s32[1,4]{1,0:T(1,128)} %param.12) | copy-start | bytes 52
  7.2 59.6 %all-gather.2.cloned.1.call-start = ((), (), s32[]{:S(2)}) async-start(), calls=%async_computation | async-start | bytes 2359296 | tf_op jit(solution)/shard_map/all_gather | solution.py:212
  10.4 14.0 %copy-start.2 = (bf16[512,128]{1,0:T(8,128)(2,1)}, bf16[512,128]{1,0:T(8,128)(2,1)S(1)}, u32[]{:S(2)}) copy-start(bf16[512,128]{1,0:T(8,128)(2,1)S(1)} %convolution_convert_fusion.4.forward_ref) | copy-start | bytes 393220
  10.4 6.3 %collective-permute-start.2 = (bf16[512,128]{1,0:T(8,128)(2,1)S(1)}, bf16[512,128]{1,0:T(8,128)(2,1)S(1)}, u32[]{:S(2)}, u32[]{:S(2)}) collective-permute-start(bf16[512,128]{1,0:T(8,128)(2,1)S(1)} %convolution_convert_fusion.4.forward_ref), channel_id=1, source_target_pairs={{0,3},{1,0},{2,1},{3,2},{4,7},{5,4},{6,5},{7,6},{8,11},{9,8},{10,9... | collective-permute-start | bytes 393224 | tf_op jit(solution)/shard_map/ppermute | solution.py:73
  12.9 7.5 %collective-permute-start.1 = (bf16[512,128]{1,0:T(8,128)(2,1)S(1)}, bf16[512,128]{1,0:T(8,128)(2,1)S(1)}, u32[]{:S(2)}, u32[]{:S(2)}) collective-permute-start(bf16[512,128]{1,0:T(8,128)(2,1)S(1)} %convolution_convert_fusion.4.forward_ref), channel_id=1, source_target_pairs={{0,2},{1,3},{2,0},{3,1},{4,6},{5,7},{6,4},{7,5},{8,10},{9,11},{10,... | collective-permute-start | bytes 393224 | tf_op jit(solution)/shard_map/ppermute | solution.py:73
  13.5 6.9 %collective-permute-start = (bf16[512,128]{1,0:T(8,128)(2,1)S(1)}, bf16[512,128]{1,0:T(8,128)(2,1)S(1)}, u32[]{:S(2)}, u32[]{:S(2)}) collective-permute-start(bf16[512,128]{1,0:T(8,128)(2,1)S(1)} %convolution_convert_fusion.4.forward_ref), channel_id=1, source_target_pairs={{0,1},{1,2},{2,3},{3,0},{4,5},{5,6},{6,7},{7,4},{8,9},{9,10},{10,1... | collective-permute-start | bytes 393224 | tf_op jit(solution)/shard_map/ppermute | solution.py:73
  14.2 10.1 %copy-start.10 = (s32[4]{0:T(128)}, s32[4]{0:T(128)S(1)}, u32[]{:S(2)}) copy-start(s32[4]{0:T(128)S(1)} %get-tuple-element.19.table_ref) | copy-start | bytes 52
  25.4 1.6 %collective-permute-start.3 = (bf16[2,512,128]{2,1,0:T(8,128)(2,1)S(1)}, bf16[2,512,128]{2,1,0:T(8,128)(2,1)S(1)}, u32[]{:S(2)}, u32[]{:S(2)}) collective-permute-start(bf16[2,512,128]{2,1,0:T(8,128)(2,1)S(1)} %dynamic-slice_bitcast_fusion), channel_id=1, source_target_pairs={{0,1},{1,0},{2,3},{3,2},{4,5},{5,4},{6,7},{7,6},{8,9},{9,8},{10,11... | collective-permute-start | bytes 786440 | tf_op jit(solution)/shard_map/ppermute | solution.py:77
  28.0 5.6 %collective-permute-start.4 = (bf16[1,512,128]{2,1,0:T(8,128)(2,1)S(1)}, bf16[1,512,128]{2,1,0:T(8,128)(2,1)S(1)}, u32[]{:S(2)}, u32[]{:S(2)}) collective-permute-start(bf16[1,512,128]{2,1,0:T(8,128)(2,1)S(1)} %constant_dynamic-slice_fusion), channel_id=1, source_target_pairs={{0,2},{1,3},{2,0},{3,1},{4,6},{5,7},{6,4},{7,5},{8,10},{9,11},{10,... | collective-permute-start | bytes 393224 | tf_op jit(solution)/shard_map/ppermute | solution.py:77
  33.7 5.7 %collective-permute-start.5 = (bf16[512,128]{1,0:T(8,128)(2,1)S(1)}, bf16[512,128]{1,0:T(8,128)(2,1)S(1)}, u32[]{:S(2)}, u32[]{:S(2)}) collective-permute-start(bf16[512,128]{1,0:T(8,128)(2,1)S(1)} %fusion.16), channel_id=1, source_target_pairs={{0,4},{4,0},{8,12},{12,8},{16,20},{20,16},{24,28},{28,24},{1,5},{5... | collective-permute-start | bytes 393224 | tf_op jit(solution)/shard_map/ppermute | solution.py:77
  39.4 12.3 %collective-permute-start.6 = (bf16[512,128]{1,0:T(8,128)(2,1)S(1)}, bf16[512,128]{1,0:T(8,128)(2,1)S(1)}, u32[]{:S(2)}, u32[]{:S(2)}) collective-permute-start(bf16[512,128]{1,0:T(8,128)(2,1)S(1)} %add_convert_fusion.2), channel_id=1, source_target_pairs={{0,8},{4,12},{8,0},{12,4},{16,24},{20,28},{24,16},{28,20},{1,9},{5... | collective-permute-start | bytes 393224 | tf_op jit(solution)/shard_map/ppermute | solution.py:77
  51.7 14.0 %collective-permute-start.7 = (bf16[512,128]{1,0:T(8,128)(2,1)S(1)}, bf16[512,128]{1,0:T(8,128)(2,1)S(1)}, u32[]{:S(2)}, u32[]{:S(2)}) collective-permute-start(bf16[512,128]{1,0:T(8,128)(2,1)S(1)} %add_convert_fusion.1), channel_id=1, source_target_pairs={{0,16},{4,20},{8,24},{12,28},{16,0},{20,4},{24,8},{28,12},{1,17},{... | collective-permute-start | bytes 393224 | tf_op jit(solution)/shard_map/ppermute | solution.py:77
  66.8 7.1 %copy-start.1 = (bf16[4,512,512]{2,1,0:T(8,128)(2,1)S(1)}, bf16[4,512,512]{2,1,0:T(8,128)(2,1)}, u32[]{:S(2)}) copy-start(bf16[4,512,512]{2,1,0:T(8,128)(2,1)} %all-gather.2.cloned.1.call-done) | copy-start | bytes 6291460
  70.3 3.6 %collective-permute-start.8 = (f32[3,512,128]{2,1,0:T(8,128)S(1)}, f32[3,512,128]{2,1,0:T(8,128)S(1)}, u32[]{:S(2)}, u32[]{:S(2)}) collective-permute-start(f32[3,512,128]{2,1,0:T(8,128)S(1)} %fusion.35), channel_id=1, source_target_pairs={{0,1},{4,5},{8,9},{12,13},{16,17},{20,21},{24,25},{28,29}} | collective-permute-start | bytes 2359304 | tf_op jit(solution)/shard_map/ppermute | solution.py:239
  74.7 0.7 collective-permute-start.9
  76.0 1.4 collective-permute-start.10
  79.7 0.7 collective-permute-start.11
  81.2 0.7 collective-permute-start.12
  82.6 24.1 %collective-permute-start.13 = (f32[1,512,128]{2,1,0:T(8,128)S(1)}, f32[1,512,128]{2,1,0:T(8,128)}, u32[]{:S(2)}, u32[]{:S(2)}) collective-permute-start(f32[1,512,128]{2,1,0:T(8,128)S(1)} %slice_add_fusion.2), channel_id=1, source_target_pairs={{1,0},{5,4},{9,8},{13,12},{17,16},{21,20},{25,24},{29,28}} | collective-permute-start | bytes 786440 | tf_op jit(solution)/shard_map/ppermute | solution.py:252
  108.0 11.8 %copy-start.3 = (f32[512,128]{1,0:T(8,128)}, f32[512,128]{1,0:T(8,128)S(1)}, u32[]{:S(2)}) copy-start(f32[512,128]{1,0:T(8,128)S(1)} %convolution_select_fusion.refs_0_) | copy-start | bytes 786436
  108.0 7.9 %collective-permute-start.14 = (f32[512,128]{1,0:T(8,128)S(1)}, f32[512,128]{1,0:T(8,128)S(1)}, u32[]{:S(2)}, u32[]{:S(2)}) collective-permute-start(f32[512,128]{1,0:T(8,128)S(1)} %convolution_select_fusion.refs_0_), channel_id=1, source_target_pairs={{0,1},{1,2},{2,3},{3,0},{4,5},{5,6},{6,7},{7,4},{8,9},{9,10},{10,1... | collective-permute-start | bytes 786440 | tf_op jit(solution)/shard_map/ppermute | solution.py:73
  108.2 9.2 %collective-permute-start.15 = (f32[512,128]{1,0:T(8,128)S(1)}, f32[512,128]{1,0:T(8,128)S(1)}, u32[]{:S(2)}, u32[]{:S(2)}) collective-permute-start(f32[512,128]{1,0:T(8,128)S(1)} %convolution_select_fusion.refs_0_), channel_id=1, source_target_pairs={{0,2},{1,3},{2,0},{3,1},{4,6},{5,7},{6,4},{7,5},{8,10},{9,11},{10,... | collective-permute-start | bytes 786440 | tf_op jit(solution)/shard_map/ppermute | solution.py:73
  108.2 11.6 %collective-permute-start.16 = (f32[512,128]{1,0:T(8,128)S(1)}, f32[512,128]{1,0:T(8,128)S(1)}, u32[]{:S(2)}, u32[]{:S(2)}) collective-permute-start(f32[512,128]{1,0:T(8,128)S(1)} %convolution_select_fusion.refs_0_), channel_id=1, source_target_pairs={{0,3},{1,0},{2,1},{3,2},{4,7},{5,4},{6,5},{7,6},{8,11},{9,8},{10,9... | collective-permute-start | bytes 786440 | tf_op jit(solution)/shard_map/ppermute | solution.py:73
  116.0 3.9 %copy-start.4 = (f32[512,128]{1,0:T(8,128)}, f32[512,128]{1,0:T(8,128)S(1)}, u32[]{:S(2)}) copy-start(f32[512,128]{1,0:T(8,128)S(1)} %collective-permute-done.14.refs_1_) | copy-start | bytes 786436
  117.4 2.5 %copy-start.5 = (f32[512,128]{1,0:T(8,128)}, f32[512,128]{1,0:T(8,128)S(1)}, u32[]{:S(2)}) copy-start(f32[512,128]{1,0:T(8,128)S(1)} %collective-permute-done.15.refs_2_) | copy-start | bytes 786436
  119.8 0.7 copy-start.6
  123.9 6.0 %collective-permute-start.17 = (bf16[512,128]{1,0:T(8,128)(2,1)}, bf16[512,128]{1,0:T(8,128)(2,1)S(1)}, u32[]{:S(2)}, u32[]{:S(2)}) collective-permute-start(bf16[512,128]{1,0:T(8,128)(2,1)} %get-tuple-element.10), channel_id=1, source_target_pairs={{0,3},{1,0},{2,1},{3,2},{4,7},{5,4},{6,5},{7,6},{8,11},{9,8},{10,9... | collective-permute-start | bytes 393224 | tf_op jit(solution)/shard_map/ppermute | solution.py:73
  125.8 9.2 %collective-permute-start.18 = (bf16[512,128]{1,0:T(8,128)(2,1)}, bf16[512,128]{1,0:T(8,128)(2,1)S(1)}, u32[]{:S(2)}, u32[]{:S(2)}) collective-permute-start(bf16[512,128]{1,0:T(8,128)(2,1)} %get-tuple-element.11), channel_id=1, source_target_pairs={{0,2},{1,3},{2,0},{3,1},{4,6},{5,7},{6,4},{7,5},{8,10},{9,11},{10,... | collective-permute-start | bytes 393224 | tf_op jit(solution)/shard_map/ppermute | solution.py:73
  128.1 6.9 %collective-permute-start.19 = (bf16[512,128]{1,0:T(8,128)(2,1)}, bf16[512,128]{1,0:T(8,128)(2,1)S(1)}, u32[]{:S(2)}, u32[]{:S(2)}) collective-permute-start(bf16[512,128]{1,0:T(8,128)(2,1)} %get-tuple-element.12), channel_id=1, source_target_pairs={{0,1},{1,2},{2,3},{3,0},{4,5},{5,6},{6,7},{7,4},{8,9},{9,10},{10,1... | collective-permute-start | bytes 393224 | tf_op jit(solution)/shard_map/ppermute | solution.py:73
  129.9 5.1 %copy-start.7 = (bf16[512,128]{1,0:T(8,128)(2,1)}, bf16[512,128]{1,0:T(8,128)(2,1)S(1)}, u32[]{:S(2)}) copy-start(bf16[512,128]{1,0:T(8,128)(2,1)S(1)} %collective-permute-done.17.refs_1_) | copy-start | bytes 393220
  135.0 0.6 copy-start.8
  135.0 0.7 copy-start.9
Sparse Core Ops, SparseCore 0:
  10.8 56.0 all-gather.1

commit v14 on v13

--- a/solution.py
+++ b/solution.py
@@ -153,6 +153,13 @@
         in_specs=[VMEM] * (2 + len(terms)),
         out_specs=VMEM,
     )(forward, inv, *terms)
+
+
+def hop(x, source, target):
+    if source // 2 == target // 2:
+        return lax.ppermute(x, "col", [(source, target)])
+    sent = lax.ppermute(x.astype(jnp.bfloat16), "col", [(source, target)])
+    return sent.astype(jnp.float32)
 
 
 def pair_index(t, u):
@@ -236,7 +243,7 @@
     for level in range(levels):
         residue = rhs_level
         if level > 0:
-            pushed = lax.ppermute(pushed, "col", [(level - 1, level)])
+            pushed = hop(pushed, level - 1, level)
             residue = residue - pushed[0]
         solved = jnp.dot(inv, residue.astype(jnp.bfloat16), preferred_element_type=jnp.float32)
         top_forward[level] = solved.astype(jnp.bfloat16)
@@ -249,7 +256,7 @@
     for level in reversed(range(levels)):
         update = top_forward[level].astype(jnp.float32)
         if level < levels - 1:
-            pushed = lax.ppermute(pushed, "col", [(level + 1, level)])
+            pushed = hop(pushed, level + 1, level)
             update = update - pushed[level]
         solved = lax.dot_general(
             inv, update.astype(jnp.bfloat16), (((0,), (0,)), ((), ())), preferred_element_type=jnp.float32

time: 146 us -> 138 us (0.945)
  waiting for transfers between devices: 80.8 us -> 74.6 us
    ppermute x6, waiting for transfers between devices: 24.6 us -> 19.6 us  [the longest x4 19.6 us: hop(): return lax.ppermute(x, 'col', [(source, target)])]
  transfers between devices with their start and end apart: 21 -> 21, of which waited for: 15 -> 15; matrix products, arithmetic and copies ran while one was open for 4% -> 5% of each run, Pallas kernels for 2% -> 2%
where the time goes in v14:
time: 138 us
  waiting for transfers between devices  74.6 us (54%)
  starting transfers between devices  21.7 us (16%)
  between operations  14.4 us (10%)
  matrix products  10.3 us (7%)
  Pallas kernels  8.72 us (6%)
  other arithmetic  4.79 us (3%)
  local copies, waits for them, and re-layouts  3.36 us (2%)
    ppermute x5, waiting for transfers between devices, swapped(): return lax.ppermute(x, axis, [(i, i ^ bit) for i in range(size)])  32.6 us
    ppermute x9, waiting for transfers between devices, shifted(): return lax.ppermute(x, axis, [(i, (i + shift) % size) for i in range(size)])  21.7 us
    ppermute x4, waiting for transfers between devices, hop(): return lax.ppermute(x, 'col', [(source, target)])  19.6 us
    ppermute x9, starting transfers between devices, shifted(): return lax.ppermute(x, axis, [(i, (i + shift) % size) for i in range(size)])  9.65 us
    ppermute x5, starting transfers between devices, swapped(): return lax.ppermute(x, axis, [(i, i ^ bit) for i in range(size)])  6.23 us
    ppermute x4, starting transfers between devices, hop(): return lax.ppermute(x, 'col', [(source, target)])  4.4 us
    pallas_call x1, Pallas kernels, tail_terms(): pl.pallas_call(functools.partial(tail_kernel, levels, peers), out_shape=o...  3.31 us
    pallas_call x1, Pallas kernels, coupling_terms(): pl.pallas_call(coupling_kernel, out_shape=jax.ShapeDtypeStruct(shape, jnp...  3.11 us
  transfers between devices with their start and end apart: 21, of which 15 were waited for; matrix products, arithmetic and copies ran while one was open for 5% of the time, Pallas kernels for 2%

profile of v14, /device:TPU:0, one launch (start us, length us, event | category | flops | bytes accessed | tf_op | source)
XLA Modules:
  0.0 137.8 jit_solution(6569929687600269060)
XLA Ops:
  7.2 0.0 copy-start
  7.2 0.0 all-gather.2.cloned.1.call-start
  7.3 1.0 constant_dynamic-slice_fusion.3
  8.3 0.7 pad_maximum_fusion.1
  9.0 0.0 all-gather.2.cloned.1.call-update
  9.0 1.3 convolution_convert_fusion.4.forward_ref
  10.4 2.5 %collective-permute-start.2 = (bf16[512,128]{1,0:T(8,128)(2,1)S(1)}, bf16[512,128]{1,0:T(8,128)(2,1)S(1)}, u32[]{:S(2)}, u32[]{:S(2)}) collective-permute-start(bf16[512,128]{1,0:T(8,128)(2,1)S(1)} %convolution_convert_fusion.4.forward_ref), channel_id=1, source_target_pairs={{0,3},{1,0},{2,1},{3,2},{4,7},{5,4},{6,5},{7,6},{8,11},{9,8},{10,9... | collective-permute-start | bytes 393224 | tf_op jit(solution)/shard_map/ppermute | solution.py:73
  12.9 0.6 collective-permute-start.1
  13.5 0.2 collective-permute-start
  13.7 0.6 and_select_fusion.1
  14.3 0.7 iota_reduce_fusion
  15.0 0.6 pad_add_fusion.fold_ref
  15.6 1.1 collective-permute-done.2
  16.7 3.8 %collective-permute-done.1 = bf16[512,128]{1,0:T(8,128)(2,1)S(1)} collective-permute-done((bf16[512,128]{1,0:T(8,128)(2,1)S(1)}, bf16[512,128]{1,0:T(8,128)(2,1)S(1)}, u32[]{:S(2)}, u32[]{:S(2)}) %collective-permute-start.1) | collective-permute-done | bytes 131104 | tf_op jit(solution)/shard_map/ppermute | solution.py:73
  20.4 0.9 pad_maximum_fusion.panels_ref
  21.3 3.1 %shard_map.95 = bf16[4,512,128]{2,1,0:T(8,128)(2,1)} custom-call(s32[4]{0:T(128)} %bitcast.121, s32[4]{0:T(128)} %get-tuple-element.8.picks_ref, s32[2]{0:T(128)} %pad_add_fusion.fold_ref, bf16[4,512,512]{2,1,0:T(8,128)(2,1)} %bitcast.113, bf16[4,512,128]{2,1,0:T(8,128)(2,1)} %pad_maximum_fusion.panels_ref, bf16[4,64,128]{2,1,0:T(8,128)(2,1)} %rhs_ref.1), custom_call_target="tpu_custom_call" | custom-call | tf_op jit(solution)/shard_map/pallas_call | solution.py:37
  24.4 1.0 dynamic-slice_bitcast_fusion
  25.4 0.1 collective-permute-start.3
  25.5 1.5 %collective-permute-done.3 = bf16[2,512,128]{2,1,0:T(8,128)(2,1)S(1)} collective-permute-done((bf16[2,512,128]{2,1,0:T(8,128)(2,1)S(1)}, bf16[2,512,128]{2,1,0:T(8,128)(2,1)S(1)}, u32[]{:S(2)}, u32[]{:S(2)}) %collective-permute-start.3) | collective-permute-done | bytes 262176 | tf_op jit(solution)/shard_map/ppermute | solution.py:77
  27.0 1.0 fusion.3
  28.0 1.7 %collective-permute-start.4 = (bf16[1,512,128]{2,1,0:T(8,128)(2,1)S(1)}, bf16[1,512,128]{2,1,0:T(8,128)(2,1)S(1)}, u32[]{:S(2)}, u32[]{:S(2)}) collective-permute-start(bf16[1,512,128]{2,1,0:T(8,128)(2,1)S(1)} %constant_dynamic-slice_fusion), channel_id=1, source_target_pairs={{0,2},{1,3},{2,0},{3,1},{4,6},{5,7},{6,4},{7,5},{8,10},{9,11},{10,... | collective-permute-start | bytes 393224 | tf_op jit(solution)/shard_map/ppermute | solution.py:77
  29.7 3.9 %collective-permute-done.4 = bf16[1,512,128]{2,1,0:T(8,128)(2,1)S(1)} collective-permute-done((bf16[1,512,128]{2,1,0:T(8,128)(2,1)S(1)}, bf16[1,512,128]{2,1,0:T(8,128)(2,1)S(1)}, u32[]{:S(2)}, u32[]{:S(2)}) %collective-permute-start.4) | collective-permute-done | bytes 131104 | tf_op jit(solution)/shard_map/ppermute | solution.py:77
  33.7 2.6 %collective-permute-start.5 = (bf16[512,128]{1,0:T(8,128)(2,1)S(1)}, bf16[512,128]{1,0:T(8,128)(2,1)S(1)}, u32[]{:S(2)}, u32[]{:S(2)}) collective-permute-start(bf16[512,128]{1,0:T(8,128)(2,1)S(1)} %fusion.18), channel_id=1, source_target_pairs={{0,4},{4,0},{8,12},{12,8},{16,20},{20,16},{24,28},{28,24},{1,5},{5... | collective-permute-start | bytes 393224 | tf_op jit(solution)/shard_map/ppermute | solution.py:77
  36.3 3.0 %collective-permute-done.5 = bf16[512,128]{1,0:T(8,128)(2,1)S(1)} collective-permute-done((bf16[512,128]{1,0:T(8,128)(2,1)S(1)}, bf16[512,128]{1,0:T(8,128)(2,1)S(1)}, u32[]{:S(2)}, u32[]{:S(2)}) %collective-permute-start.5) | collective-permute-done | bytes 131104 | tf_op jit(solution)/shard_map/ppermute | solution.py:77
  39.4 1.8 %collective-permute-start.6 = (bf16[512,128]{1,0:T(8,128)(2,1)S(1)}, bf16[512,128]{1,0:T(8,128)(2,1)S(1)}, u32[]{:S(2)}, u32[]{:S(2)}) collective-permute-start(bf16[512,128]{1,0:T(8,128)(2,1)S(1)} %add_convert_fusion.2), channel_id=1, source_target_pairs={{0,8},{4,12},{8,0},{12,4},{16,24},{20,28},{24,16},{28,20},{1,9},{5... | collective-permute-start | bytes 393224 | tf_op jit(solution)/shard_map/ppermute | solution.py:77
  41.2 11.4 %collective-permute-done.6 = bf16[512,128]{1,0:T(8,128)(2,1)S(1)} collective-permute-done((bf16[512,128]{1,0:T(8,128)(2,1)S(1)}, bf16[512,128]{1,0:T(8,128)(2,1)S(1)}, u32[]{:S(2)}, u32[]{:S(2)}) %collective-permute-start.6) | collective-permute-done | bytes 131104 | tf_op jit(solution)/shard_map/ppermute | solution.py:77
  52.6 0.1 collective-permute-start.7
  52.7 12.8 %collective-permute-done.7 = bf16[512,128]{1,0:T(8,128)(2,1)S(1)} collective-permute-done((bf16[512,128]{1,0:T(8,128)(2,1)S(1)}, bf16[512,128]{1,0:T(8,128)(2,1)S(1)}, u32[]{:S(2)}, u32[]{:S(2)}) %collective-permute-start.7) | collective-permute-done | bytes 131104 | tf_op jit(solution)/shard_map/ppermute | solution.py:77
  65.5 0.7 all-gather.2.cloned.1.call-done
  66.2 1.5 %convolution_convert_fusion.3 = bf16[512,128]{1,0:T(8,128)(2,1)S(1)} fusion(bf16[4,512,512]{2,1,0:T(8,128)(2,1)} %all-gather.2.cloned.1.call-done, bf16[512,128]{1,0:T(8,128)(2,1)S(1)} %add_convert_fusion), kind=kOutput, calls=%fused_computation.6 | convolution fusion | flops 67371008 | bytes 786432 | tf_op jit(solution)/shard_map/dot_general | solution.py:248
  67.7 2.0 %fusion.37 = f32[3,512,128]{2,1,0:T(8,128)S(1)} fusion(bf16[4,512,512]{2,1,0:T(8,128)(2,1)} %all-gather.2.cloned.1.call-done, bf16[512,128]{1,0:T(8,128)(2,1)S(1)} %convolution_convert_fusion.3), kind=kOutput, calls=%fused_computation.55 | convolution fusion | flops 201326592 | bytes 3014656 | tf_op jit(solution)/shard_map/kab,bc->kac/dot_general | solution.py:251
  69.7 1.7 %collective-permute-start.8 = (f32[3,512,128]{2,1,0:T(8,128)S(1)}, f32[3,512,128]{2,1,0:T(8,128)S(1)}, u32[]{:S(2)}, u32[]{:S(2)}) collective-permute-start(f32[3,512,128]{2,1,0:T(8,128)S(1)} %fusion.37), channel_id=1, source_target_pairs={{0,1},{4,5},{8,9},{12,13},{16,17},{20,21},{24,25},{28,29}} | collective-permute-start | bytes 2359304 | tf_op jit(solution)/shard_map/ppermute | solution.py:160
  71.4 1.8 %collective-permute-done.8 = f32[3,512,128]{2,1,0:T(8,128)S(1)} collective-permute-done((f32[3,512,128]{2,1,0:T(8,128)S(1)}, f32[3,512,128]{2,1,0:T(8,128)S(1)}, u32[]{:S(2)}, u32[]{:S(2)}) %collective-permute-start.8) | collective-permute-done | bytes 786464 | tf_op jit(solution)/shard_map/ppermute | solution.py:160
  73.2 0.3 convolution_convert_fusion.2
  73.5 0.4 fusion.2
  74.0 0.7 collective-permute-start.9
  74.7 0.3 convolution_convert_fusion.1
  75.0 0.3 slice_add_fusion.3
  75.3 0.7 collective-permute-start.10
  76.0 0.7 fusion
  76.8 0.6 fusion.31
  77.4 0.7 collective-permute-start.11
  78.1 0.3 fusion.17
  78.5 0.5 fusion.1
  79.0 0.7 collective-permute-start.12
  79.7 0.3 fusion.16
  80.0 0.3 slice_add_fusion.2
  80.4 1.3 collective-permute-start.13
  81.7 17.7 %collective-permute-done.13 = f32[1,512,128]{2,1,0:T(8,128)} collective-permute-done((f32[1,512,128]{2,1,0:T(8,128)S(1)}, f32[1,512,128]{2,1,0:T(8,128)}, u32[]{:S(2)}, u32[]{:S(2)}) %collective-permute-start.13) | collective-permute-done | bytes 262176 | tf_op jit(solution)/shard_map/ppermute | solution.py:160
  99.4 1.3 convolution_select_fusion.refs_0_
  100.7 0.2 collective-permute-start.14
  100.9 1.6 %collective-permute-start.16 = (f32[512,128]{1,0:T(8,128)S(1)}, f32[512,128]{1,0:T(8,128)S(1)}, u32[]{:S(2)}, u32[]{:S(2)}) collective-permute-start(f32[512,128]{1,0:T(8,128)S(1)} %convolution_select_fusion.refs_0_), channel_id=1, source_target_pairs={{0,3},{1,0},{2,1},{3,2},{4,7},{5,4},{6,5},{7,6},{8,11},{9,8},{10,9... | collective-permute-start | bytes 786440 | tf_op jit(solution)/shard_map/ppermute | solution.py:73
  102.5 6.1 %collective-permute-done.14.refs_1_ = f32[512,128]{1,0:T(8,128)S(1)} collective-permute-done((f32[512,128]{1,0:T(8,128)S(1)}, f32[512,128]{1,0:T(8,128)S(1)}, u32[]{:S(2)}, u32[]{:S(2)}) %collective-permute-start.14) | collective-permute-done | bytes 262176 | tf_op jit(solution)/shard_map/ppermute | solution.py:73
  108.7 1.4 %collective-permute-done.15.refs_2_ = f32[512,128]{1,0:T(8,128)S(1)} collective-permute-done((f32[512,128]{1,0:T(8,128)S(1)}, f32[512,128]{1,0:T(8,128)S(1)}, u32[]{:S(2)}, u32[]{:S(2)}) %collective-permute-start.15) | collective-permute-done | bytes 262176 | tf_op jit(solution)/shard_map/ppermute | solution.py:73
  110.1 2.5 %collective-permute-done.16.refs_3_ = f32[512,128]{1,0:T(8,128)S(1)} collective-permute-done((f32[512,128]{1,0:T(8,128)S(1)}, f32[512,128]{1,0:T(8,128)S(1)}, u32[]{:S(2)}, u32[]{:S(2)}) %collective-permute-start.16) | collective-permute-done | bytes 262176 | tf_op jit(solution)/shard_map/ppermute | solution.py:73
  112.5 0.7 copy-done.6
  113.2 3.3 %shard_map.96 = (bf16[512,128]{1,0:T(8,128)(2,1)}, bf16[512,128]{1,0:T(8,128)(2,1)}, bf16[512,128]{1,0:T(8,128)(2,1)}, bf16[512,128]{1,0:T(8,128)(2,1)}, f32[4,64,128]{2,1,0:T(8,128)}) custom-call(s32[4]{0:T(128)} %bitcast.122, s32[4]{0:T(128)} %get-tuple-element.14.dests_ref, s32[4]{0:T(128)} %copy-done.10, s32[1]{0:T(128)} %bitcast.4.start_ref, ...), custom_call_target="tpu_custom_call" | custom-call | tf_op jit(solution)/shard_map/pallas_call | solution.py:127
  116.5 2.2 %collective-permute-start.17 = (bf16[512,128]{1,0:T(8,128)(2,1)}, bf16[512,128]{1,0:T(8,128)(2,1)S(1)}, u32[]{:S(2)}, u32[]{:S(2)}) collective-permute-start(bf16[512,128]{1,0:T(8,128)(2,1)} %get-tuple-element.10), channel_id=1, source_target_pairs={{0,3},{1,0},{2,1},{3,2},{4,7},{5,4},{6,5},{7,6},{8,11},{9,8},{10,9... | collective-permute-start | bytes 393224 | tf_op jit(solution)/shard_map/ppermute | solution.py:73
  118.8 2.3 %collective-permute-start.18 = (bf16[512,128]{1,0:T(8,128)(2,1)}, bf16[512,128]{1,0:T(8,128)(2,1)S(1)}, u32[]{:S(2)}, u32[]{:S(2)}) collective-permute-start(bf16[512,128]{1,0:T(8,128)(2,1)} %get-tuple-element.11), channel_id=1, source_target_pairs={{0,2},{1,3},{2,0},{3,1},{4,6},{5,7},{6,4},{7,5},{8,10},{9,11},{10,... | collective-permute-start | bytes 393224 | tf_op jit(solution)/shard_map/ppermute | solution.py:73
  121.1 1.8 %collective-permute-done.17.refs_1_ = bf16[512,128]{1,0:T(8,128)(2,1)S(1)} collective-permute-done((bf16[512,128]{1,0:T(8,128)(2,1)}, bf16[512,128]{1,0:T(8,128)(2,1)S(1)}, u32[]{:S(2)}, u32[]{:S(2)}) %collective-permute-start.17) | collective-permute-done | bytes 131104 | tf_op jit(solution)/shard_map/ppermute | solution.py:73
  122.9 5.1 %collective-permute-done.18.refs_2_ = bf16[512,128]{1,0:T(8,128)(2,1)S(1)} collective-permute-done((bf16[512,128]{1,0:T(8,128)(2,1)}, bf16[512,128]{1,0:T(8,128)(2,1)S(1)}, u32[]{:S(2)}, u32[]{:S(2)}) %collective-permute-start.18) | collective-permute-done | bytes 131104 | tf_op jit(solution)/shard_map/ppermute | solution.py:73
  128.0 0.6 copy-done.8
  128.6 0.1 copy-done.9
  128.7 2.3 %shard_map.97 = f32[1,512,128]{2,1,0:T(8,128)} custom-call(bf16[512,128]{1,0:T(8,128)(2,1)} %copy-done.2, bf16[1,512,512]{2,1,0:T(8,128)(2,1)} %inv_ref.1, bf16[512,128]{1,0:T(8,128)(2,1)} %get-tuple-element.9.refs_0_, bf16[512,128]{1,0:T(8,128)(2,1)} %copy-done.7, bf16[512,128]{1,0:T(8,128)(2,1)} %copy-done.8, bf16[512,128]{1,0:T(8,128)(2,1)} %copy-done.9), custom_call_target="tpu_custom_call" | custom-call | tf_op jit(solution)/shard_map/pallas_call | solution.py:150
  (35 shorter events, 0.3 us)
Async XLA Ops:
  7.2 1.9 %copy-start = (bf16[1,512,128]{2,1,0:T(8,128)(2,1)S(1)}, bf16[1,512,128]{2,1,0:T(8,128)(2,1)}, u32[]{:S(2)}) copy-start(bf16[1,512,128]{2,1,0:T(8,128)(2,1)} %param.8) | copy-start | bytes 393220
  7.2 6.5 %copy-start.11 = (s32[1,4]{1,0:T(1,128)S(1)}, s32[1,4]{1,0:T(1,128)}, u32[]{:S(2)}) copy-start(s32[1,4]{1,0:T(1,128)} %param.12) | copy-start | bytes 52
  7.2 59.0 %all-gather.2.cloned.1.call-start = ((), (), s32[]{:S(2)}) async-start(), calls=%async_computation | async-start | bytes 2359296 | tf_op jit(solution)/shard_map/all_gather | solution.py:219
  10.4 14.0 %copy-start.2 = (bf16[512,128]{1,0:T(8,128)(2,1)}, bf16[512,128]{1,0:T(8,128)(2,1)S(1)}, u32[]{:S(2)}) copy-start(bf16[512,128]{1,0:T(8,128)(2,1)S(1)} %convolution_convert_fusion.4.forward_ref) | copy-start | bytes 393220
  10.4 6.3 %collective-permute-start.2 = (bf16[512,128]{1,0:T(8,128)(2,1)S(1)}, bf16[512,128]{1,0:T(8,128)(2,1)S(1)}, u32[]{:S(2)}, u32[]{:S(2)}) collective-permute-start(bf16[512,128]{1,0:T(8,128)(2,1)S(1)} %convolution_convert_fusion.4.forward_ref), channel_id=1, source_target_pairs={{0,3},{1,0},{2,1},{3,2},{4,7},{5,4},{6,5},{7,6},{8,11},{9,8},{10,9... | collective-permute-start | bytes 393224 | tf_op jit(solution)/shard_map/ppermute | solution.py:73
  12.9 7.5 %collective-permute-start.1 = (bf16[512,128]{1,0:T(8,128)(2,1)S(1)}, bf16[512,128]{1,0:T(8,128)(2,1)S(1)}, u32[]{:S(2)}, u32[]{:S(2)}) collective-permute-start(bf16[512,128]{1,0:T(8,128)(2,1)S(1)} %convolution_convert_fusion.4.forward_ref), channel_id=1, source_target_pairs={{0,2},{1,3},{2,0},{3,1},{4,6},{5,7},{6,4},{7,5},{8,10},{9,11},{10,... | collective-permute-start | bytes 393224 | tf_op jit(solution)/shard_map/ppermute | solution.py:73
  13.5 6.9 %collective-permute-start = (bf16[512,128]{1,0:T(8,128)(2,1)S(1)}, bf16[512,128]{1,0:T(8,128)(2,1)S(1)}, u32[]{:S(2)}, u32[]{:S(2)}) collective-permute-start(bf16[512,128]{1,0:T(8,128)(2,1)S(1)} %convolution_convert_fusion.4.forward_ref), channel_id=1, source_target_pairs={{0,1},{1,2},{2,3},{3,0},{4,5},{5,6},{6,7},{7,4},{8,9},{9,10},{10,1... | collective-permute-start | bytes 393224 | tf_op jit(solution)/shard_map/ppermute | solution.py:73
  14.2 10.1 %copy-start.10 = (s32[4]{0:T(128)}, s32[4]{0:T(128)S(1)}, u32[]{:S(2)}) copy-start(s32[4]{0:T(128)S(1)} %get-tuple-element.19.table_ref) | copy-start | bytes 52
  25.4 1.6 %collective-permute-start.3 = (bf16[2,512,128]{2,1,0:T(8,128)(2,1)S(1)}, bf16[2,512,128]{2,1,0:T(8,128)(2,1)S(1)}, u32[]{:S(2)}, u32[]{:S(2)}) collective-permute-start(bf16[2,512,128]{2,1,0:T(8,128)(2,1)S(1)} %dynamic-slice_bitcast_fusion), channel_id=1, source_target_pairs={{0,1},{1,0},{2,3},{3,2},{4,5},{5,4},{6,7},{7,6},{8,9},{9,8},{10,11... | collective-permute-start | bytes 786440 | tf_op jit(solution)/shard_map/ppermute | solution.py:77
  28.0 5.6 %collective-permute-start.4 = (bf16[1,512,128]{2,1,0:T(8,128)(2,1)S(1)}, bf16[1,512,128]{2,1,0:T(8,128)(2,1)S(1)}, u32[]{:S(2)}, u32[]{:S(2)}) collective-permute-start(bf16[1,512,128]{2,1,0:T(8,128)(2,1)S(1)} %constant_dynamic-slice_fusion), channel_id=1, source_target_pairs={{0,2},{1,3},{2,0},{3,1},{4,6},{5,7},{6,4},{7,5},{8,10},{9,11},{10,... | collective-permute-start | bytes 393224 | tf_op jit(solution)/shard_map/ppermute | solution.py:77
  33.7 5.7 %collective-permute-start.5 = (bf16[512,128]{1,0:T(8,128)(2,1)S(1)}, bf16[512,128]{1,0:T(8,128)(2,1)S(1)}, u32[]{:S(2)}, u32[]{:S(2)}) collective-permute-start(bf16[512,128]{1,0:T(8,128)(2,1)S(1)} %fusion.18), channel_id=1, source_target_pairs={{0,4},{4,0},{8,12},{12,8},{16,20},{20,16},{24,28},{28,24},{1,5},{5... | collective-permute-start | bytes 393224 | tf_op jit(solution)/shard_map/ppermute | solution.py:77
  39.4 13.1 %collective-permute-start.6 = (bf16[512,128]{1,0:T(8,128)(2,1)S(1)}, bf16[512,128]{1,0:T(8,128)(2,1)S(1)}, u32[]{:S(2)}, u32[]{:S(2)}) collective-permute-start(bf16[512,128]{1,0:T(8,128)(2,1)S(1)} %add_convert_fusion.2), channel_id=1, source_target_pairs={{0,8},{4,12},{8,0},{12,4},{16,24},{20,28},{24,16},{28,20},{1,9},{5... | collective-permute-start | bytes 393224 | tf_op jit(solution)/shard_map/ppermute | solution.py:77
  52.6 12.9 %collective-permute-start.7 = (bf16[512,128]{1,0:T(8,128)(2,1)S(1)}, bf16[512,128]{1,0:T(8,128)(2,1)S(1)}, u32[]{:S(2)}, u32[]{:S(2)}) collective-permute-start(bf16[512,128]{1,0:T(8,128)(2,1)S(1)} %add_convert_fusion.1), channel_id=1, source_target_pairs={{0,16},{4,20},{8,24},{12,28},{16,0},{20,4},{24,8},{28,12},{1,17},{... | collective-permute-start | bytes 393224 | tf_op jit(solution)/shard_map/ppermute | solution.py:77
  66.2 7.0 %copy-start.1 = (bf16[4,512,512]{2,1,0:T(8,128)(2,1)S(1)}, bf16[4,512,512]{2,1,0:T(8,128)(2,1)}, u32[]{:S(2)}) copy-start(bf16[4,512,512]{2,1,0:T(8,128)(2,1)} %all-gather.2.cloned.1.call-done) | copy-start | bytes 6291460
  69.7 3.6 %collective-permute-start.8 = (f32[3,512,128]{2,1,0:T(8,128)S(1)}, f32[3,512,128]{2,1,0:T(8,128)S(1)}, u32[]{:S(2)}, u32[]{:S(2)}) collective-permute-start(f32[3,512,128]{2,1,0:T(8,128)S(1)} %fusion.37), channel_id=1, source_target_pairs={{0,1},{4,5},{8,9},{12,13},{16,17},{20,21},{24,25},{28,29}} | collective-permute-start | bytes 2359304 | tf_op jit(solution)/shard_map/ppermute | solution.py:160
  74.0 0.7 collective-permute-start.9
  75.3 0.7 collective-permute-start.10
  77.4 0.7 collective-permute-start.11
  79.0 0.7 collective-permute-start.12
  80.4 19.0 %collective-permute-start.13 = (f32[1,512,128]{2,1,0:T(8,128)S(1)}, f32[1,512,128]{2,1,0:T(8,128)}, u32[]{:S(2)}, u32[]{:S(2)}) collective-permute-start(f32[1,512,128]{2,1,0:T(8,128)S(1)} %slice_add_fusion.2), channel_id=1, source_target_pairs={{1,0},{5,4},{9,8},{13,12},{17,16},{21,20},{25,24},{29,28}} | collective-permute-start | bytes 786440 | tf_op jit(solution)/shard_map/ppermute | solution.py:160
  100.7 11.8 %copy-start.3 = (f32[512,128]{1,0:T(8,128)}, f32[512,128]{1,0:T(8,128)S(1)}, u32[]{:S(2)}) copy-start(f32[512,128]{1,0:T(8,128)S(1)} %convolution_select_fusion.refs_0_) | copy-start | bytes 786436
  100.7 7.9 %collective-permute-start.14 = (f32[512,128]{1,0:T(8,128)S(1)}, f32[512,128]{1,0:T(8,128)S(1)}, u32[]{:S(2)}, u32[]{:S(2)}) collective-permute-start(f32[512,128]{1,0:T(8,128)S(1)} %convolution_select_fusion.refs_0_), channel_id=1, source_target_pairs={{0,1},{1,2},{2,3},{3,0},{4,5},{5,6},{6,7},{7,4},{8,9},{9,10},{10,1... | collective-permute-start | bytes 786440 | tf_op jit(solution)/shard_map/ppermute | solution.py:73
  100.9 9.2 %collective-permute-start.15 = (f32[512,128]{1,0:T(8,128)S(1)}, f32[512,128]{1,0:T(8,128)S(1)}, u32[]{:S(2)}, u32[]{:S(2)}) collective-permute-start(f32[512,128]{1,0:T(8,128)S(1)} %convolution_select_fusion.refs_0_), channel_id=1, source_target_pairs={{0,2},{1,3},{2,0},{3,1},{4,6},{5,7},{6,4},{7,5},{8,10},{9,11},{10,... | collective-permute-start | bytes 786440 | tf_op jit(solution)/shard_map/ppermute | solution.py:73
  100.9 11.6 %collective-permute-start.16 = (f32[512,128]{1,0:T(8,128)S(1)}, f32[512,128]{1,0:T(8,128)S(1)}, u32[]{:S(2)}, u32[]{:S(2)}) collective-permute-start(f32[512,128]{1,0:T(8,128)S(1)} %convolution_select_fusion.refs_0_), channel_id=1, source_target_pairs={{0,3},{1,0},{2,1},{3,2},{4,7},{5,4},{6,5},{7,6},{8,11},{9,8},{10,9... | collective-permute-start | bytes 786440 | tf_op jit(solution)/shard_map/ppermute | solution.py:73
  108.7 3.9 %copy-start.4 = (f32[512,128]{1,0:T(8,128)}, f32[512,128]{1,0:T(8,128)S(1)}, u32[]{:S(2)}) copy-start(f32[512,128]{1,0:T(8,128)S(1)} %collective-permute-done.14.refs_1_) | copy-start | bytes 786436
  110.1 2.5 %copy-start.5 = (f32[512,128]{1,0:T(8,128)}, f32[512,128]{1,0:T(8,128)S(1)}, u32[]{:S(2)}) copy-start(f32[512,128]{1,0:T(8,128)S(1)} %collective-permute-done.15.refs_2_) | copy-start | bytes 786436
  112.5 0.7 copy-start.6
  116.5 6.4 %collective-permute-start.17 = (bf16[512,128]{1,0:T(8,128)(2,1)}, bf16[512,128]{1,0:T(8,128)(2,1)S(1)}, u32[]{:S(2)}, u32[]{:S(2)}) collective-permute-start(bf16[512,128]{1,0:T(8,128)(2,1)} %get-tuple-element.10), channel_id=1, source_target_pairs={{0,3},{1,0},{2,1},{3,2},{4,7},{5,4},{6,5},{7,6},{8,11},{9,8},{10,9... | collective-permute-start | bytes 393224 | tf_op jit(solution)/shard_map/ppermute | solution.py:73
  118.8 9.2 %collective-permute-start.18 = (bf16[512,128]{1,0:T(8,128)(2,1)}, bf16[512,128]{1,0:T(8,128)(2,1)S(1)}, u32[]{:S(2)}, u32[]{:S(2)}) collective-permute-start(bf16[512,128]{1,0:T(8,128)(2,1)} %get-tuple-element.11), channel_id=1, source_target_pairs={{0,2},{1,3},{2,0},{3,1},{4,6},{5,7},{6,4},{7,5},{8,10},{9,11},{10,... | collective-permute-start | bytes 393224 | tf_op jit(solution)/shard_map/ppermute | solution.py:73
  121.1 6.9 %collective-permute-start.19 = (bf16[512,128]{1,0:T(8,128)(2,1)}, bf16[512,128]{1,0:T(8,128)(2,1)S(1)}, u32[]{:S(2)}, u32[]{:S(2)}) collective-permute-start(bf16[512,128]{1,0:T(8,128)(2,1)} %get-tuple-element.12), channel_id=1, source_target_pairs={{0,1},{1,2},{2,3},{3,0},{4,5},{5,6},{6,7},{7,4},{8,9},{9,10},{10,1... | collective-permute-start | bytes 393224 | tf_op jit(solution)/shard_map/ppermute | solution.py:73
  122.9 5.1 %copy-start.7 = (bf16[512,128]{1,0:T(8,128)(2,1)}, bf16[512,128]{1,0:T(8,128)(2,1)S(1)}, u32[]{:S(2)}) copy-start(bf16[512,128]{1,0:T(8,128)(2,1)S(1)} %collective-permute-done.17.refs_1_) | copy-start | bytes 393220
  128.0 0.6 copy-start.8
  128.0 0.7 copy-start.9
Sparse Core Ops, SparseCore 0:
  10.8 55.3 all-gather.1

commit v15 on v14

--- a/solution.py
+++ b/solution.py
@@ -97,7 +97,9 @@
 
             @pl.when(table_ref[t] == p)
             def _():
-                slices_ref[t] = x_refs[p][pl.ds(start, share), :]
+                bulk = x_refs[p].shape[0] - share
+                high = x_refs[p][pl.ds(start, share), :].astype(jnp.float32)
+                slices_ref[t] = high + x_refs[p][pl.ds(bulk, share), :].astype(jnp.float32)
 
     acc_ref[...] = jnp.zeros_like(acc_ref)
     for s in range(tiles_ref.shape[0]):
@@ -109,7 +111,7 @@
             def _():
                 prod = lax.dot_general(
                     tiles_ref[s],
-                    x_refs[p][...].astype(jnp.bfloat16),
+                    x_refs[p][pl.ds(0, tiles_ref.shape[2]), :],
                     (((0,), (0,)), ((), ())),
                     preferred_element_type=jnp.float32,
                 )
@@ -121,7 +123,7 @@
 
 def tail_terms(slot_rows, dests, table, start, tiles, pieces, levels, share):
     peers = len(pieces)
-    shape = pieces[0].shape
+    shape = (tiles.shape[2], pieces[0].shape[1])
     outs = [jax.ShapeDtypeStruct(shape, jnp.bfloat16) for _ in range(peers)]
     outs.append(jax.ShapeDtypeStruct((levels, share, shape[1]), jnp.float32))
     result = pl.pallas_call(
@@ -267,7 +269,10 @@
                 "uab,ac->ubc", mats[1 : level + 1], solved.astype(jnp.bfloat16), preferred_element_type=jnp.float32
             )
             pushed = earlier if level == levels - 1 else pushed[:level] + earlier
-    pieces = [own_solution] + [shifted(own_solution, "col", peers, s) for s in range(1, peers)]
+    high = own_solution.astype(jnp.bfloat16)
+    rows_here = lax.dynamic_slice_in_dim(own_solution - high.astype(jnp.float32), position * share, share, 0)
+    packed = jnp.concatenate([high, rows_here.astype(jnp.bfloat16)], axis=0)
+    pieces = [packed] + [shifted(packed, "col", peers, s) for s in range(1, peers)]
     table = ((me - jnp.arange(levels)) % peers).astype(jnp.int32)
     dests = ((me - slot_cols) % peers).astype(jnp.int32)
     start = (position * share)[None].astype(jnp.int32)

time: 138 us -> 134 us (0.971)
  waiting for transfers between devices: 74.6 us -> 68.1 us
  starting transfers between devices: 21.7 us -> 23.7 us
    ppermute x9, waiting for transfers between devices: 21.7 us -> 16.7 us  [shifted(): return lax.ppermute(x, axis, [(i, (i + shift) % size) for i in range(size)])]
    ppermute x5, starting transfers between devices: 6.23 us -> 8.2 us  [swapped(): return lax.ppermute(x, axis, [(i, i ^ bit) for i in range(size)])]
    ppermute x5, waiting for transfers between devices: 32.6 us -> 31.2 us  [swapped(): return lax.ppermute(x, axis, [(i, i ^ bit) for i in range(size)])]
  transfers between devices with their start and end apart: 21 -> 21, of which waited for: 15 -> 14; matrix products, arithmetic and copies ran while one was open for 5% -> 5% of each run, Pallas kernels for 2% -> 2%
where the time goes in v15:
time: 134 us
  waiting for transfers between devices  68.1 us (51%)
  starting transfers between devices  23.7 us (18%)
  between operations  14.4 us (11%)
  matrix products  11 us (8%)
  Pallas kernels  8.7 us (6%)
  other arithmetic  4.85 us (4%)
  local copies, waits for them, and re-layouts  3.36 us (3%)
    ppermute x5, waiting for transfers between devices, swapped(): return lax.ppermute(x, axis, [(i, i ^ bit) for i in range(size)])  31.2 us
    ppermute x4, waiting for transfers between devices, hop(): return lax.ppermute(x, 'col', [(source, target)])  19.1 us
    ppermute x9, waiting for transfers between devices, shifted(): return lax.ppermute(x, axis, [(i, (i + shift) % size) for i in range(size)])  16.7 us
    ppermute x9, starting transfers between devices, shifted(): return lax.ppermute(x, axis, [(i, (i + shift) % size) for i in range(size)])  8.88 us
    ppermute x5, starting transfers between devices, swapped(): return lax.ppermute(x, axis, [(i, i ^ bit) for i in range(size)])  8.2 us
    ppermute x4, starting transfers between devices, hop(): return lax.ppermute(x, 'col', [(source, target)])  5.25 us
    pallas_call x1, Pallas kernels, tail_terms(): pl.pallas_call(functools.partial(tail_kernel, levels, peers), out_shape=o...  3.28 us
    pallas_call x1, Pallas kernels, coupling_terms(): pl.pallas_call(coupling_kernel, out_shape=jax.ShapeDtypeStruct(shape, jnp...  3.13 us
  transfers between devices with their start and end apart: 21, of which 14 were waited for; matrix products, arithmetic and copies ran while one was open for 5% of the time, Pallas kernels for 2%

profile of v15, /device:TPU:0, one launch (start us, length us, event | category | flops | bytes accessed | tf_op | source)
XLA Modules:
  0.0 134.1 jit_solution(10816871312512271945)
XLA Ops:
  7.2 0.0 copy-start
  7.2 0.0 all-gather.2.cloned.1.call-start
  7.3 1.0 constant_dynamic-slice_fusion.3
  8.3 0.7 pad_maximum_fusion.1
  9.0 0.0 all-gather.2.cloned.1.call-update
  9.0 1.3 convolution_convert_fusion.4.forward_ref
  10.4 2.5 %collective-permute-start.2 = (bf16[512,128]{1,0:T(8,128)(2,1)S(1)}, bf16[512,128]{1,0:T(8,128)(2,1)S(1)}, u32[]{:S(2)}, u32[]{:S(2)}) collective-permute-start(bf16[512,128]{1,0:T(8,128)(2,1)S(1)} %convolution_convert_fusion.4.forward_ref), channel_id=1, source_target_pairs={{0,3},{1,0},{2,1},{3,2},{4,7},{5,4},{6,5},{7,6},{8,11},{9,8},{10,9... | collective-permute-start | bytes 393224 | tf_op jit(solution)/shard_map/ppermute | solution.py:73
  12.9 0.6 collective-permute-start.1
  13.5 0.2 collective-permute-start
  13.7 0.6 and_select_fusion.1
  14.3 0.8 iota_reduce_fusion
  15.0 0.6 pad_add_fusion.fold_ref
  15.6 1.0 collective-permute-done.2
  16.7 3.8 %collective-permute-done.1 = bf16[512,128]{1,0:T(8,128)(2,1)S(1)} collective-permute-done((bf16[512,128]{1,0:T(8,128)(2,1)S(1)}, bf16[512,128]{1,0:T(8,128)(2,1)S(1)}, u32[]{:S(2)}, u32[]{:S(2)}) %collective-permute-start.1) | collective-permute-done | bytes 131104 | tf_op jit(solution)/shard_map/ppermute | solution.py:73
  20.4 0.9 pad_maximum_fusion.panels_ref
  21.3 3.1 %shard_map.95 = bf16[4,512,128]{2,1,0:T(8,128)(2,1)} custom-call(s32[4]{0:T(128)} %bitcast.125, s32[4]{0:T(128)} %get-tuple-element.8.picks_ref, s32[2]{0:T(128)} %pad_add_fusion.fold_ref, bf16[4,512,512]{2,1,0:T(8,128)(2,1)} %bitcast.117, bf16[4,512,128]{2,1,0:T(8,128)(2,1)} %pad_maximum_fusion.panels_ref, bf16[4,64,128]{2,1,0:T(8,128)(2,1)} %rhs_ref.1), custom_call_target="tpu_custom_call" | custom-call | tf_op jit(solution)/shard_map/pallas_call | solution.py:37
  24.4 1.0 dynamic-slice_bitcast_fusion
  25.4 0.1 collective-permute-start.3
  25.5 1.5 %collective-permute-done.3 = bf16[2,512,128]{2,1,0:T(8,128)(2,1)S(1)} collective-permute-done((bf16[2,512,128]{2,1,0:T(8,128)(2,1)S(1)}, bf16[2,512,128]{2,1,0:T(8,128)(2,1)S(1)}, u32[]{:S(2)}, u32[]{:S(2)}) %collective-permute-start.3) | collective-permute-done | bytes 262176 | tf_op jit(solution)/shard_map/ppermute | solution.py:77
  27.0 1.0 fusion.3
  28.0 1.7 %collective-permute-start.4 = (bf16[1,512,128]{2,1,0:T(8,128)(2,1)S(1)}, bf16[1,512,128]{2,1,0:T(8,128)(2,1)S(1)}, u32[]{:S(2)}, u32[]{:S(2)}) collective-permute-start(bf16[1,512,128]{2,1,0:T(8,128)(2,1)S(1)} %constant_dynamic-slice_fusion), channel_id=1, source_target_pairs={{0,2},{1,3},{2,0},{3,1},{4,6},{5,7},{6,4},{7,5},{8,10},{9,11},{10,... | collective-permute-start | bytes 393224 | tf_op jit(solution)/shard_map/ppermute | solution.py:77
  29.7 3.9 %collective-permute-done.4 = bf16[1,512,128]{2,1,0:T(8,128)(2,1)S(1)} collective-permute-done((bf16[1,512,128]{2,1,0:T(8,128)(2,1)S(1)}, bf16[1,512,128]{2,1,0:T(8,128)(2,1)S(1)}, u32[]{:S(2)}, u32[]{:S(2)}) %collective-permute-start.4) | collective-permute-done | bytes 131104 | tf_op jit(solution)/shard_map/ppermute | solution.py:77
  33.7 2.3 %collective-permute-start.5 = (bf16[512,128]{1,0:T(8,128)(2,1)S(1)}, bf16[512,128]{1,0:T(8,128)(2,1)S(1)}, u32[]{:S(2)}, u32[]{:S(2)}) collective-permute-start(bf16[512,128]{1,0:T(8,128)(2,1)S(1)} %fusion.18), channel_id=1, source_target_pairs={{0,4},{4,0},{8,12},{12,8},{16,20},{20,16},{24,28},{28,24},{1,5},{5... | collective-permute-start | bytes 393224 | tf_op jit(solution)/shard_map/ppermute | solution.py:77
  36.0 3.0 %collective-permute-done.5 = bf16[512,128]{1,0:T(8,128)(2,1)S(1)} collective-permute-done((bf16[512,128]{1,0:T(8,128)(2,1)S(1)}, bf16[512,128]{1,0:T(8,128)(2,1)S(1)}, u32[]{:S(2)}, u32[]{:S(2)}) %collective-permute-start.5) | collective-permute-done | bytes 131104 | tf_op jit(solution)/shard_map/ppermute | solution.py:77
  39.1 1.9 %collective-permute-start.6 = (bf16[512,128]{1,0:T(8,128)(2,1)S(1)}, bf16[512,128]{1,0:T(8,128)(2,1)S(1)}, u32[]{:S(2)}, u32[]{:S(2)}) collective-permute-start(bf16[512,128]{1,0:T(8,128)(2,1)S(1)} %add_convert_fusion.2), channel_id=1, source_target_pairs={{0,8},{4,12},{8,0},{12,4},{16,24},{20,28},{24,16},{28,20},{1,9},{5... | collective-permute-start | bytes 393224 | tf_op jit(solution)/shard_map/ppermute | solution.py:77
  41.0 9.7 %collective-permute-done.6 = bf16[512,128]{1,0:T(8,128)(2,1)S(1)} collective-permute-done((bf16[512,128]{1,0:T(8,128)(2,1)S(1)}, bf16[512,128]{1,0:T(8,128)(2,1)S(1)}, u32[]{:S(2)}, u32[]{:S(2)}) %collective-permute-start.6) | collective-permute-done | bytes 131104 | tf_op jit(solution)/shard_map/ppermute | solution.py:77
  50.8 2.2 %collective-permute-start.7 = (bf16[512,128]{1,0:T(8,128)(2,1)S(1)}, bf16[512,128]{1,0:T(8,128)(2,1)S(1)}, u32[]{:S(2)}, u32[]{:S(2)}) collective-permute-start(bf16[512,128]{1,0:T(8,128)(2,1)S(1)} %add_convert_fusion.1), channel_id=1, source_target_pairs={{0,16},{4,20},{8,24},{12,28},{16,0},{20,4},{24,8},{28,12},{1,17},{... | collective-permute-start | bytes 393224 | tf_op jit(solution)/shard_map/ppermute | solution.py:77
  52.9 13.1 %collective-permute-done.7 = bf16[512,128]{1,0:T(8,128)(2,1)S(1)} collective-permute-done((bf16[512,128]{1,0:T(8,128)(2,1)S(1)}, bf16[512,128]{1,0:T(8,128)(2,1)S(1)}, u32[]{:S(2)}, u32[]{:S(2)}) %collective-permute-start.7) | collective-permute-done | bytes 131104 | tf_op jit(solution)/shard_map/ppermute | solution.py:77
  66.1 1.0 all-gather.2.cloned.1.call-done
  67.1 1.5 %convolution_convert_fusion.3 = bf16[512,128]{1,0:T(8,128)(2,1)S(1)} fusion(bf16[4,512,512]{2,1,0:T(8,128)(2,1)} %all-gather.2.cloned.1.call-done, bf16[512,128]{1,0:T(8,128)(2,1)S(1)} %add_convert_fusion), kind=kOutput, calls=%fused_computation.6 | convolution fusion | flops 67371008 | bytes 786432 | tf_op jit(solution)/shard_map/dot_general | solution.py:250
  68.6 2.0 %fusion.37 = f32[3,512,128]{2,1,0:T(8,128)S(1)} fusion(bf16[4,512,512]{2,1,0:T(8,128)(2,1)} %all-gather.2.cloned.1.call-done, bf16[512,128]{1,0:T(8,128)(2,1)S(1)} %convolution_convert_fusion.3), kind=kOutput, calls=%fused_computation.56 | convolution fusion | flops 201326592 | bytes 3014656 | tf_op jit(solution)/shard_map/kab,bc->kac/dot_general | solution.py:253
  70.6 1.9 %collective-permute-start.8 = (f32[3,512,128]{2,1,0:T(8,128)S(1)}, f32[3,512,128]{2,1,0:T(8,128)S(1)}, u32[]{:S(2)}, u32[]{:S(2)}) collective-permute-start(f32[3,512,128]{2,1,0:T(8,128)S(1)} %fusion.37), channel_id=1, source_target_pairs={{0,1},{4,5},{8,9},{12,13},{16,17},{20,21},{24,25},{28,29}} | collective-permute-start | bytes 2359304 | tf_op jit(solution)/shard_map/ppermute | solution.py:162
  72.5 1.8 %collective-permute-done.8 = f32[3,512,128]{2,1,0:T(8,128)S(1)} collective-permute-done((f32[3,512,128]{2,1,0:T(8,128)S(1)}, f32[3,512,128]{2,1,0:T(8,128)S(1)}, u32[]{:S(2)}, u32[]{:S(2)}) %collective-permute-start.8) | collective-permute-done | bytes 786464 | tf_op jit(solution)/shard_map/ppermute | solution.py:162
  74.3 0.3 convolution_convert_fusion.2
  74.6 0.4 fusion.2
  75.0 0.7 collective-permute-start.9
  75.8 0.3 convolution_convert_fusion.1
  76.1 0.3 slice_add_fusion.3
  76.4 1.4 %collective-permute-start.10 = (f32[1,512,128]{2,1,0:T(8,128)S(1)}, f32[1,512,128]{2,1,0:T(8,128)}, u32[]{:S(2)}, u32[]{:S(2)}) collective-permute-start(f32[1,512,128]{2,1,0:T(8,128)S(1)} %slice_add_fusion.3), channel_id=1, source_target_pairs={{2,3},{6,7},{10,11},{14,15},{18,19},{22,23},{26,27},{30,31}} | collective-permute-start | bytes 786440 | tf_op jit(solution)/shard_map/ppermute | solution.py:162
  77.8 1.7 %fusion = f32[512,128]{1,0:T(8,128)S(1)} fusion(bf16[4,512,512]{2,1,0:T(8,128)(2,1)S(1)} %copy-done.1, f32[1,512,128]{2,1,0:T(8,128)} %collective-permute-done.10, bf16[512,128]{1,0:T(8,128)(2,1)S(1)} %add_convert_fusion), kind=kOutput, calls=%fused_computation.8 | convolution fusion | flops 134545408 | bytes 1703936 | tf_op jit(solution)/shard_map/dot_general | solution.py:263
  79.5 0.6 fusion.31
  80.1 0.7 collective-permute-start.11
  80.8 0.3 fusion.17
  81.2 0.5 fusion.1
  81.7 0.7 collective-permute-start.12
  82.4 0.3 fusion.16
  82.8 1.0 slice_add_fusion.2
  83.8 1.3 collective-permute-start.13
  85.1 17.2 %collective-permute-done.13 = f32[1,512,128]{2,1,0:T(8,128)S(1)} collective-permute-done((f32[1,512,128]{2,1,0:T(8,128)}, f32[1,512,128]{2,1,0:T(8,128)S(1)}, u32[]{:S(2)}, u32[]{:S(2)}) %collective-permute-start.13) | collective-permute-done | bytes 262176 | tf_op jit(solution)/shard_map/ppermute | solution.py:162
  102.3 0.3 fusion.49
  102.7 0.2 collective-permute-start.14
  102.9 1.6 %collective-permute-start.16 = (bf16[576,128]{1,0:T(8,128)(2,1)S(1)}, bf16[576,128]{1,0:T(8,128)(2,1)S(1)}, u32[]{:S(2)}, u32[]{:S(2)}) collective-permute-start(bf16[576,128]{1,0:T(8,128)(2,1)S(1)} %pad_maximum_fusion.2.refs_0_), channel_id=1, source_target_pairs={{0,3},{1,0},{2,1},{3,2},{4,7},{5,4},{6,5},{7,6},{8,11},{9,8},{10,9... | collective-permute-start | bytes 442376 | tf_op jit(solution)/shard_map/ppermute | solution.py:73
  104.5 3.7 %collective-permute-done.14.refs_1_ = bf16[576,128]{1,0:T(8,128)(2,1)S(1)} collective-permute-done((bf16[576,128]{1,0:T(8,128)(2,1)S(1)}, bf16[576,128]{1,0:T(8,128)(2,1)S(1)}, u32[]{:S(2)}, u32[]{:S(2)}) %collective-permute-start.14) | collective-permute-done | bytes 147488 | tf_op jit(solution)/shard_map/ppermute | solution.py:73
  108.2 1.4 %collective-permute-done.15.refs_2_ = bf16[576,128]{1,0:T(8,128)(2,1)S(1)} collective-permute-done((bf16[576,128]{1,0:T(8,128)(2,1)S(1)}, bf16[576,128]{1,0:T(8,128)(2,1)S(1)}, u32[]{:S(2)}, u32[]{:S(2)}) %collective-permute-start.15) | collective-permute-done | bytes 147488 | tf_op jit(solution)/shard_map/ppermute | solution.py:73
  109.7 0.6 copy-done.5
  110.3 0.1 copy-done.6
  110.3 3.3 %shard_map.96 = (bf16[512,128]{1,0:T(8,128)(2,1)}, bf16[512,128]{1,0:T(8,128)(2,1)}, bf16[512,128]{1,0:T(8,128)(2,1)}, bf16[512,128]{1,0:T(8,128)(2,1)}, f32[4,64,128]{2,1,0:T(8,128)}) custom-call(s32[4]{0:T(128)} %bitcast.126, s32[4]{0:T(128)} %get-tuple-element.14.dests_ref, s32[4]{0:T(128)} %copy-done.10, s32[1]{0:T(128)} %bitcast.4.start_ref, ...), custom_call_target="tpu_custom_call" | custom-call | tf_op jit(solution)/shard_map/pallas_call | solution.py:129
  113.6 1.9 %collective-permute-start.17 = (bf16[512,128]{1,0:T(8,128)(2,1)}, bf16[512,128]{1,0:T(8,128)(2,1)S(1)}, u32[]{:S(2)}, u32[]{:S(2)}) collective-permute-start(bf16[512,128]{1,0:T(8,128)(2,1)} %get-tuple-element.10), channel_id=1, source_target_pairs={{0,3},{1,0},{2,1},{3,2},{4,7},{5,4},{6,5},{7,6},{8,11},{9,8},{10,9... | collective-permute-start | bytes 393224 | tf_op jit(solution)/shard_map/ppermute | solution.py:73
  115.5 2.0 %collective-permute-start.18 = (bf16[512,128]{1,0:T(8,128)(2,1)}, bf16[512,128]{1,0:T(8,128)(2,1)S(1)}, u32[]{:S(2)}, u32[]{:S(2)}) collective-permute-start(bf16[512,128]{1,0:T(8,128)(2,1)} %get-tuple-element.11), channel_id=1, source_target_pairs={{0,2},{1,3},{2,0},{3,1},{4,6},{5,7},{6,4},{7,5},{8,10},{9,11},{10,... | collective-permute-start | bytes 393224 | tf_op jit(solution)/shard_map/ppermute | solution.py:73
  117.4 2.2 %collective-permute-done.17.refs_1_ = bf16[512,128]{1,0:T(8,128)(2,1)S(1)} collective-permute-done((bf16[512,128]{1,0:T(8,128)(2,1)}, bf16[512,128]{1,0:T(8,128)(2,1)S(1)}, u32[]{:S(2)}, u32[]{:S(2)}) %collective-permute-start.17) | collective-permute-done | bytes 131104 | tf_op jit(solution)/shard_map/ppermute | solution.py:73
  119.7 4.6 %collective-permute-done.18.refs_2_ = bf16[512,128]{1,0:T(8,128)(2,1)S(1)} collective-permute-done((bf16[512,128]{1,0:T(8,128)(2,1)}, bf16[512,128]{1,0:T(8,128)(2,1)S(1)}, u32[]{:S(2)}, u32[]{:S(2)}) %collective-permute-start.18) | collective-permute-done | bytes 131104 | tf_op jit(solution)/shard_map/ppermute | solution.py:73
  124.3 0.6 copy-done.8
  124.9 0.0 copy-done.9
  125.0 2.3 %shard_map.97 = f32[1,512,128]{2,1,0:T(8,128)} custom-call(bf16[512,128]{1,0:T(8,128)(2,1)} %copy-done.2, bf16[1,512,512]{2,1,0:T(8,128)(2,1)} %inv_ref.1, bf16[512,128]{1,0:T(8,128)(2,1)} %get-tuple-element.9.refs_0_, bf16[512,128]{1,0:T(8,128)(2,1)} %copy-done.7, bf16[512,128]{1,0:T(8,128)(2,1)} %copy-done.8, bf16[512,128]{1,0:T(8,128)(2,1)} %copy-done.9), custom_call_target="tpu_custom_call" | custom-call | tf_op jit(solution)/shard_map/pallas_call | solution.py:152
  (38 shorter events, 0.3 us)
Async XLA Ops:
  7.2 1.9 %copy-start = (bf16[1,512,128]{2,1,0:T(8,128)(2,1)S(1)}, bf16[1,512,128]{2,1,0:T(8,128)(2,1)}, u32[]{:S(2)}) copy-start(bf16[1,512,128]{2,1,0:T(8,128)(2,1)} %param.8) | copy-start | bytes 393220
  7.2 6.5 %copy-start.11 = (s32[1,4]{1,0:T(1,128)S(1)}, s32[1,4]{1,0:T(1,128)}, u32[]{:S(2)}) copy-start(s32[1,4]{1,0:T(1,128)} %param.12) | copy-start | bytes 52
  7.2 59.9 %all-gather.2.cloned.1.call-start = ((), (), s32[]{:S(2)}) async-start(), calls=%async_computation | async-start | bytes 2359296 | tf_op jit(solution)/shard_map/all_gather | solution.py:221
  10.4 14.0 %copy-start.2 = (bf16[512,128]{1,0:T(8,128)(2,1)}, bf16[512,128]{1,0:T(8,128)(2,1)S(1)}, u32[]{:S(2)}) copy-start(bf16[512,128]{1,0:T(8,128)(2,1)S(1)} %convolution_convert_fusion.4.forward_ref) | copy-start | bytes 393220
  10.4 6.3 %collective-permute-start.2 = (bf16[512,128]{1,0:T(8,128)(2,1)S(1)}, bf16[512,128]{1,0:T(8,128)(2,1)S(1)}, u32[]{:S(2)}, u32[]{:S(2)}) collective-permute-start(bf16[512,128]{1,0:T(8,128)(2,1)S(1)} %convolution_convert_fusion.4.forward_ref), channel_id=1, source_target_pairs={{0,3},{1,0},{2,1},{3,2},{4,7},{5,4},{6,5},{7,6},{8,11},{9,8},{10,9... | collective-permute-start | bytes 393224 | tf_op jit(solution)/shard_map/ppermute | solution.py:73
  12.9 7.5 %collective-permute-start.1 = (bf16[512,128]{1,0:T(8,128)(2,1)S(1)}, bf16[512,128]{1,0:T(8,128)(2,1)S(1)}, u32[]{:S(2)}, u32[]{:S(2)}) collective-permute-start(bf16[512,128]{1,0:T(8,128)(2,1)S(1)} %convolution_convert_fusion.4.forward_ref), channel_id=1, source_target_pairs={{0,2},{1,3},{2,0},{3,1},{4,6},{5,7},{6,4},{7,5},{8,10},{9,11},{10,... | collective-permute-start | bytes 393224 | tf_op jit(solution)/shard_map/ppermute | solution.py:73
  13.5 6.9 %collective-permute-start = (bf16[512,128]{1,0:T(8,128)(2,1)S(1)}, bf16[512,128]{1,0:T(8,128)(2,1)S(1)}, u32[]{:S(2)}, u32[]{:S(2)}) collective-permute-start(bf16[512,128]{1,0:T(8,128)(2,1)S(1)} %convolution_convert_fusion.4.forward_ref), channel_id=1, source_target_pairs={{0,1},{1,2},{2,3},{3,0},{4,5},{5,6},{6,7},{7,4},{8,9},{9,10},{10,1... | collective-permute-start | bytes 393224 | tf_op jit(solution)/shard_map/ppermute | solution.py:73
  13.7 10.7 %copy-start.10 = (s32[4]{0:T(128)}, s32[4]{0:T(128)S(1)}, u32[]{:S(2)}) copy-start(s32[4]{0:T(128)S(1)} %and_select_fusion.table_ref) | copy-start | bytes 52
  25.4 1.6 %collective-permute-start.3 = (bf16[2,512,128]{2,1,0:T(8,128)(2,1)S(1)}, bf16[2,512,128]{2,1,0:T(8,128)(2,1)S(1)}, u32[]{:S(2)}, u32[]{:S(2)}) collective-permute-start(bf16[2,512,128]{2,1,0:T(8,128)(2,1)S(1)} %dynamic-slice_bitcast_fusion), channel_id=1, source_target_pairs={{0,1},{1,0},{2,3},{3,2},{4,5},{5,4},{6,7},{7,6},{8,9},{9,8},{10,11... | collective-permute-start | bytes 786440 | tf_op jit(solution)/shard_map/ppermute | solution.py:77
  28.0 5.6 %collective-permute-start.4 = (bf16[1,512,128]{2,1,0:T(8,128)(2,1)S(1)}, bf16[1,512,128]{2,1,0:T(8,128)(2,1)S(1)}, u32[]{:S(2)}, u32[]{:S(2)}) collective-permute-start(bf16[1,512,128]{2,1,0:T(8,128)(2,1)S(1)} %constant_dynamic-slice_fusion), channel_id=1, source_target_pairs={{0,2},{1,3},{2,0},{3,1},{4,6},{5,7},{6,4},{7,5},{8,10},{9,11},{10,... | collective-permute-start | bytes 393224 | tf_op jit(solution)/shard_map/ppermute | solution.py:77
  33.7 5.4 %collective-permute-start.5 = (bf16[512,128]{1,0:T(8,128)(2,1)S(1)}, bf16[512,128]{1,0:T(8,128)(2,1)S(1)}, u32[]{:S(2)}, u32[]{:S(2)}) collective-permute-start(bf16[512,128]{1,0:T(8,128)(2,1)S(1)} %fusion.18), channel_id=1, source_target_pairs={{0,4},{4,0},{8,12},{12,8},{16,20},{20,16},{24,28},{28,24},{1,5},{5... | collective-permute-start | bytes 393224 | tf_op jit(solution)/shard_map/ppermute | solution.py:77
  39.1 11.6 %collective-permute-start.6 = (bf16[512,128]{1,0:T(8,128)(2,1)S(1)}, bf16[512,128]{1,0:T(8,128)(2,1)S(1)}, u32[]{:S(2)}, u32[]{:S(2)}) collective-permute-start(bf16[512,128]{1,0:T(8,128)(2,1)S(1)} %add_convert_fusion.2), channel_id=1, source_target_pairs={{0,8},{4,12},{8,0},{12,4},{16,24},{20,28},{24,16},{28,20},{1,9},{5... | collective-permute-start | bytes 393224 | tf_op jit(solution)/shard_map/ppermute | solution.py:77
  50.8 15.3 %collective-permute-start.7 = (bf16[512,128]{1,0:T(8,128)(2,1)S(1)}, bf16[512,128]{1,0:T(8,128)(2,1)S(1)}, u32[]{:S(2)}, u32[]{:S(2)}) collective-permute-start(bf16[512,128]{1,0:T(8,128)(2,1)S(1)} %add_convert_fusion.1), channel_id=1, source_target_pairs={{0,16},{4,20},{8,24},{12,28},{16,0},{20,4},{24,8},{28,12},{1,17},{... | collective-permute-start | bytes 393224 | tf_op jit(solution)/shard_map/ppermute | solution.py:77
  67.1 7.2 %copy-start.1 = (bf16[4,512,512]{2,1,0:T(8,128)(2,1)S(1)}, bf16[4,512,512]{2,1,0:T(8,128)(2,1)}, u32[]{:S(2)}) copy-start(bf16[4,512,512]{2,1,0:T(8,128)(2,1)} %all-gather.2.cloned.1.call-done) | copy-start | bytes 6291460
  70.6 3.7 %collective-permute-start.8 = (f32[3,512,128]{2,1,0:T(8,128)S(1)}, f32[3,512,128]{2,1,0:T(8,128)S(1)}, u32[]{:S(2)}, u32[]{:S(2)}) collective-permute-start(f32[3,512,128]{2,1,0:T(8,128)S(1)} %fusion.37), channel_id=1, source_target_pairs={{0,1},{4,5},{8,9},{12,13},{16,17},{20,21},{24,25},{28,29}} | collective-permute-start | bytes 2359304 | tf_op jit(solution)/shard_map/ppermute | solution.py:162
  75.0 0.7 collective-permute-start.9
  76.4 1.4 %collective-permute-start.10 = (f32[1,512,128]{2,1,0:T(8,128)S(1)}, f32[1,512,128]{2,1,0:T(8,128)}, u32[]{:S(2)}, u32[]{:S(2)}) collective-permute-start(f32[1,512,128]{2,1,0:T(8,128)S(1)} %slice_add_fusion.3), channel_id=1, source_target_pairs={{2,3},{6,7},{10,11},{14,15},{18,19},{22,23},{26,27},{30,31}} | collective-permute-start | bytes 786440 | tf_op jit(solution)/shard_map/ppermute | solution.py:162
  80.1 0.7 collective-permute-start.11
  81.7 0.7 collective-permute-start.12
  83.8 18.5 %collective-permute-start.13 = (f32[1,512,128]{2,1,0:T(8,128)}, f32[1,512,128]{2,1,0:T(8,128)S(1)}, u32[]{:S(2)}, u32[]{:S(2)}) collective-permute-start(f32[1,512,128]{2,1,0:T(8,128)} %slice_add_fusion.2), channel_id=1, source_target_pairs={{1,0},{5,4},{9,8},{13,12},{17,16},{21,20},{25,24},{29,28}} | collective-permute-start | bytes 786440 | tf_op jit(solution)/shard_map/ppermute | solution.py:162
  102.7 6.9 %copy-start.3 = (bf16[576,128]{1,0:T(8,128)(2,1)}, bf16[576,128]{1,0:T(8,128)(2,1)S(1)}, u32[]{:S(2)}) copy-start(bf16[576,128]{1,0:T(8,128)(2,1)S(1)} %pad_maximum_fusion.2.refs_0_) | copy-start | bytes 442372
  102.7 5.5 %collective-permute-start.14 = (bf16[576,128]{1,0:T(8,128)(2,1)S(1)}, bf16[576,128]{1,0:T(8,128)(2,1)S(1)}, u32[]{:S(2)}, u32[]{:S(2)}) collective-permute-start(bf16[576,128]{1,0:T(8,128)(2,1)S(1)} %pad_maximum_fusion.2.refs_0_), channel_id=1, source_target_pairs={{0,1},{1,2},{2,3},{3,0},{4,5},{5,6},{6,7},{7,4},{8,9},{9,10},{10,1... | collective-permute-start | bytes 442376 | tf_op jit(solution)/shard_map/ppermute | solution.py:73
  102.9 6.7 %collective-permute-start.15 = (bf16[576,128]{1,0:T(8,128)(2,1)S(1)}, bf16[576,128]{1,0:T(8,128)(2,1)S(1)}, u32[]{:S(2)}, u32[]{:S(2)}) collective-permute-start(bf16[576,128]{1,0:T(8,128)(2,1)S(1)} %pad_maximum_fusion.2.refs_0_), channel_id=1, source_target_pairs={{0,2},{1,3},{2,0},{3,1},{4,6},{5,7},{6,4},{7,5},{8,10},{9,11},{10,... | collective-permute-start | bytes 442376 | tf_op jit(solution)/shard_map/ppermute | solution.py:73
  102.9 6.7 %collective-permute-start.16 = (bf16[576,128]{1,0:T(8,128)(2,1)S(1)}, bf16[576,128]{1,0:T(8,128)(2,1)S(1)}, u32[]{:S(2)}, u32[]{:S(2)}) collective-permute-start(bf16[576,128]{1,0:T(8,128)(2,1)S(1)} %pad_maximum_fusion.2.refs_0_), channel_id=1, source_target_pairs={{0,3},{1,0},{2,1},{3,2},{4,7},{5,4},{6,5},{7,6},{8,11},{9,8},{10,9... | collective-permute-start | bytes 442376 | tf_op jit(solution)/shard_map/ppermute | solution.py:73
  108.2 1.4 %copy-start.4 = (bf16[576,128]{1,0:T(8,128)(2,1)}, bf16[576,128]{1,0:T(8,128)(2,1)S(1)}, u32[]{:S(2)}) copy-start(bf16[576,128]{1,0:T(8,128)(2,1)S(1)} %collective-permute-done.14.refs_1_) | copy-start | bytes 442372
  109.6 0.7 copy-start.5
  109.6 0.7 copy-start.6
  113.6 6.1 %collective-permute-start.17 = (bf16[512,128]{1,0:T(8,128)(2,1)}, bf16[512,128]{1,0:T(8,128)(2,1)S(1)}, u32[]{:S(2)}, u32[]{:S(2)}) collective-permute-start(bf16[512,128]{1,0:T(8,128)(2,1)} %get-tuple-element.10), channel_id=1, source_target_pairs={{0,3},{1,0},{2,1},{3,2},{4,7},{5,4},{6,5},{7,6},{8,11},{9,8},{10,9... | collective-permute-start | bytes 393224 | tf_op jit(solution)/shard_map/ppermute | solution.py:73
  115.5 8.8 %collective-permute-start.18 = (bf16[512,128]{1,0:T(8,128)(2,1)}, bf16[512,128]{1,0:T(8,128)(2,1)S(1)}, u32[]{:S(2)}, u32[]{:S(2)}) collective-permute-start(bf16[512,128]{1,0:T(8,128)(2,1)} %get-tuple-element.11), channel_id=1, source_target_pairs={{0,2},{1,3},{2,0},{3,1},{4,6},{5,7},{6,4},{7,5},{8,10},{9,11},{10,... | collective-permute-start | bytes 393224 | tf_op jit(solution)/shard_map/ppermute | solution.py:73
  117.4 6.9 %collective-permute-start.19 = (bf16[512,128]{1,0:T(8,128)(2,1)}, bf16[512,128]{1,0:T(8,128)(2,1)S(1)}, u32[]{:S(2)}, u32[]{:S(2)}) collective-permute-start(bf16[512,128]{1,0:T(8,128)(2,1)} %get-tuple-element.12), channel_id=1, source_target_pairs={{0,1},{1,2},{2,3},{3,0},{4,5},{5,6},{6,7},{7,4},{8,9},{9,10},{10,1... | collective-permute-start | bytes 393224 | tf_op jit(solution)/shard_map/ppermute | solution.py:73
  119.7 4.6 %copy-start.7 = (bf16[512,128]{1,0:T(8,128)(2,1)}, bf16[512,128]{1,0:T(8,128)(2,1)S(1)}, u32[]{:S(2)}) copy-start(bf16[512,128]{1,0:T(8,128)(2,1)S(1)} %collective-permute-done.17.refs_1_) | copy-start | bytes 393220
  124.3 0.6 copy-start.8
  124.3 0.7 copy-start.9
Sparse Core Ops, SparseCore 0:
  10.8 56.3 all-gather.1

commit v16 on v15

--- a/solution.py
+++ b/solution.py
@@ -158,8 +158,6 @@
 
 
 def hop(x, source, target):
-    if source // 2 == target // 2:
-        return lax.ppermute(x, "col", [(source, target)])
     sent = lax.ppermute(x.astype(jnp.bfloat16), "col", [(source, target)])
     return sent.astype(jnp.float32)
 

time: 134 us -> 130 us (0.970)
  starting transfers between devices: 23.7 us -> 21.4 us
  matrix products: 11 us -> 9.38 us
    ppermute x4 -> x0, waiting for transfers between devices: 19.1 us -> none  [hop(): return lax.ppermute(x, 'col', [(source, target)])]
    ppermute x2 -> x6, waiting for transfers between devices: 0.01 us -> 18 us  [hop(): sent = lax.ppermute(x.astype(jnp.bfloat16), 'col', [(source, target)])]
    ppermute x4 -> x0, starting transfers between devices: 5.25 us -> none  [hop(): return lax.ppermute(x, 'col', [(source, target)])]
    ppermute x2 -> x6, starting transfers between devices: 1.35 us -> 5.71 us  [hop(): sent = lax.ppermute(x.astype(jnp.bfloat16), 'col', [(source, target)])]
    ppermute x5, starting transfers between devices: 8.2 us -> 6.46 us  [swapped(): return lax.ppermute(x, axis, [(i, i ^ bit) for i in range(size)])]
where the time goes in v16:
time: 130 us
  waiting for transfers between devices  67.8 us (52%)
  starting transfers between devices  21.4 us (16%)
  between operations  14.5 us (11%)
  matrix products  9.38 us (7%)
  Pallas kernels  8.69 us (7%)
  other arithmetic  4.96 us (4%)
  local copies, waits for them, and re-layouts  3.36 us (3%)
    ppermute x5, waiting for transfers between devices, swapped(): return lax.ppermute(x, axis, [(i, i ^ bit) for i in range(size)])  32.1 us
    ppermute x6, waiting for transfers between devices, hop(): sent = lax.ppermute(x.astype(jnp.bfloat16), 'col', [(source, target)])  18 us
    ppermute x9, waiting for transfers between devices, shifted(): return lax.ppermute(x, axis, [(i, (i + shift) % size) for i in range(size)])  16.7 us
    ppermute x9, starting transfers between devices, shifted(): return lax.ppermute(x, axis, [(i, (i + shift) % size) for i in range(size)])  9.25 us
    ppermute x5, starting transfers between devices, swapped(): return lax.ppermute(x, axis, [(i, i ^ bit) for i in range(size)])  6.46 us
    ppermute x6, starting transfers between devices, hop(): sent = lax.ppermute(x.astype(jnp.bfloat16), 'col', [(source, target)])  5.71 us
    pallas_call x1, Pallas kernels, tail_terms(): pl.pallas_call(functools.partial(tail_kernel, levels, peers), out_shape=o...  3.28 us
    pallas_call x1, Pallas kernels, coupling_terms(): pl.pallas_call(coupling_kernel, out_shape=jax.ShapeDtypeStruct(shape, jnp...  3.13 us
  transfers between devices with their start and end apart: 21, of which 14 were waited for; matrix products, arithmetic and copies ran while one was open for 5% of the time, Pallas kernels for 2%

profile of v16, /device:TPU:0, one launch (start us, length us, event | category | flops | bytes accessed | tf_op | source)
XLA Modules:
  0.0 130.1 jit_solution(10920947830363627275)
XLA Ops:
  7.2 0.0 all-gather.2.cloned.1.call-start
  7.3 1.0 constant_dynamic-slice_fusion.3
  8.3 0.7 pad_maximum_fusion.1
  9.0 1.3 %convolution_convert_fusion.6.forward_ref = bf16[512,128]{1,0:T(8,128)(2,1)S(1)} fusion(bf16[1,512,512]{2,1,0:T(8,128)(2,1)} %inv_ref.1, bf16[1,512,128]{2,1,0:T(8,128)(2,1)S(1)} %copy-done), kind=kOutput, calls=%fused_computation.9 | convolution fusion | flops 67174400 | bytes 786432 | tf_op jit(solution)/shard_map/dot_general | solution.py:225
  10.4 2.5 %collective-permute-start.2 = (bf16[512,128]{1,0:T(8,128)(2,1)S(1)}, bf16[512,128]{1,0:T(8,128)(2,1)S(1)}, u32[]{:S(2)}, u32[]{:S(2)}) collective-permute-start(bf16[512,128]{1,0:T(8,128)(2,1)S(1)} %convolution_convert_fusion.6.forward_ref), channel_id=1, source_target_pairs={{0,3},{1,0},{2,1},{3,2},{4,7},{5,4},{6,5},{7,6},{8,11},{9,8},{10,9... | collective-permute-start | bytes 393224 | tf_op jit(solution)/shard_map/ppermute | solution.py:73
  12.9 0.6 collective-permute-start.1
  13.5 0.2 collective-permute-start
  13.7 0.6 and_select_fusion.1
  14.3 0.8 iota_reduce_fusion
  15.0 0.6 pad_add_fusion.fold_ref
  15.6 1.0 collective-permute-done.2
  16.7 3.8 %collective-permute-done.1 = bf16[512,128]{1,0:T(8,128)(2,1)S(1)} collective-permute-done((bf16[512,128]{1,0:T(8,128)(2,1)S(1)}, bf16[512,128]{1,0:T(8,128)(2,1)S(1)}, u32[]{:S(2)}, u32[]{:S(2)}) %collective-permute-start.1) | collective-permute-done | bytes 131104 | tf_op jit(solution)/shard_map/ppermute | solution.py:73
  20.4 0.9 pad_maximum_fusion.panels_ref
  21.3 3.1 %shard_map.95 = bf16[4,512,128]{2,1,0:T(8,128)(2,1)} custom-call(s32[4]{0:T(128)} %bitcast.127, s32[4]{0:T(128)} %get-tuple-element.8.picks_ref, s32[2]{0:T(128)} %pad_add_fusion.fold_ref, bf16[4,512,512]{2,1,0:T(8,128)(2,1)} %bitcast.119, bf16[4,512,128]{2,1,0:T(8,128)(2,1)} %pad_maximum_fusion.panels_ref, bf16[4,64,128]{2,1,0:T(8,128)(2,1)} %rhs_ref.1), custom_call_target="tpu_custom_call" | custom-call | tf_op jit(solution)/shard_map/pallas_call | solution.py:37
  24.4 1.0 dynamic-slice_bitcast_fusion
  25.4 0.1 collective-permute-start.3
  25.5 1.5 %collective-permute-done.3 = bf16[2,512,128]{2,1,0:T(8,128)(2,1)S(1)} collective-permute-done((bf16[2,512,128]{2,1,0:T(8,128)(2,1)S(1)}, bf16[2,512,128]{2,1,0:T(8,128)(2,1)S(1)}, u32[]{:S(2)}, u32[]{:S(2)}) %collective-permute-start.3) | collective-permute-done | bytes 262176 | tf_op jit(solution)/shard_map/ppermute | solution.py:77
  27.0 1.0 fusion.3
  28.0 2.0 %collective-permute-start.4 = (bf16[1,512,128]{2,1,0:T(8,128)(2,1)S(1)}, bf16[1,512,128]{2,1,0:T(8,128)(2,1)S(1)}, u32[]{:S(2)}, u32[]{:S(2)}) collective-permute-start(bf16[1,512,128]{2,1,0:T(8,128)(2,1)S(1)} %constant_dynamic-slice_fusion), channel_id=1, source_target_pairs={{0,2},{1,3},{2,0},{3,1},{4,6},{5,7},{6,4},{7,5},{8,10},{9,11},{10,... | collective-permute-start | bytes 393224 | tf_op jit(solution)/shard_map/ppermute | solution.py:77
  30.0 3.8 %collective-permute-done.4 = bf16[1,512,128]{2,1,0:T(8,128)(2,1)S(1)} collective-permute-done((bf16[1,512,128]{2,1,0:T(8,128)(2,1)S(1)}, bf16[1,512,128]{2,1,0:T(8,128)(2,1)S(1)}, u32[]{:S(2)}, u32[]{:S(2)}) %collective-permute-start.4) | collective-permute-done | bytes 131104 | tf_op jit(solution)/shard_map/ppermute | solution.py:77
  33.9 1.9 %collective-permute-start.5 = (bf16[512,128]{1,0:T(8,128)(2,1)S(1)}, bf16[512,128]{1,0:T(8,128)(2,1)S(1)}, u32[]{:S(2)}, u32[]{:S(2)}) collective-permute-start(bf16[512,128]{1,0:T(8,128)(2,1)S(1)} %fusion.20), channel_id=1, source_target_pairs={{0,4},{4,0},{8,12},{12,8},{16,20},{20,16},{24,28},{28,24},{1,5},{5... | collective-permute-start | bytes 393224 | tf_op jit(solution)/shard_map/ppermute | solution.py:77
  35.7 3.2 %collective-permute-done.5 = bf16[512,128]{1,0:T(8,128)(2,1)S(1)} collective-permute-done((bf16[512,128]{1,0:T(8,128)(2,1)S(1)}, bf16[512,128]{1,0:T(8,128)(2,1)S(1)}, u32[]{:S(2)}, u32[]{:S(2)}) %collective-permute-start.5) | collective-permute-done | bytes 131104 | tf_op jit(solution)/shard_map/ppermute | solution.py:77
  39.0 1.9 %collective-permute-start.6 = (bf16[512,128]{1,0:T(8,128)(2,1)S(1)}, bf16[512,128]{1,0:T(8,128)(2,1)S(1)}, u32[]{:S(2)}, u32[]{:S(2)}) collective-permute-start(bf16[512,128]{1,0:T(8,128)(2,1)S(1)} %add_convert_fusion.2), channel_id=1, source_target_pairs={{0,8},{4,12},{8,0},{12,4},{16,24},{20,28},{24,16},{28,20},{1,9},{5... | collective-permute-start | bytes 393224 | tf_op jit(solution)/shard_map/ppermute | solution.py:77
  40.9 10.2 %collective-permute-done.6 = bf16[512,128]{1,0:T(8,128)(2,1)S(1)} collective-permute-done((bf16[512,128]{1,0:T(8,128)(2,1)S(1)}, bf16[512,128]{1,0:T(8,128)(2,1)S(1)}, u32[]{:S(2)}, u32[]{:S(2)}) %collective-permute-start.6) | collective-permute-done | bytes 131104 | tf_op jit(solution)/shard_map/ppermute | solution.py:77
  51.1 0.6 collective-permute-start.7
  51.7 13.5 %collective-permute-done.7 = bf16[512,128]{1,0:T(8,128)(2,1)S(1)} collective-permute-done((bf16[512,128]{1,0:T(8,128)(2,1)S(1)}, bf16[512,128]{1,0:T(8,128)(2,1)S(1)}, u32[]{:S(2)}, u32[]{:S(2)}) %collective-permute-start.7) | collective-permute-done | bytes 131104 | tf_op jit(solution)/shard_map/ppermute | solution.py:77
  65.3 0.9 all-gather.2.cloned.1.call-done
  66.2 1.3 %convolution_convert_fusion.5 = bf16[512,128]{1,0:T(8,128)(2,1)S(1)} fusion(bf16[4,512,512]{2,1,0:T(8,128)(2,1)} %all-gather.2.cloned.1.call-done, bf16[512,128]{1,0:T(8,128)(2,1)S(1)} %add_convert_fusion), kind=kOutput, calls=%fused_computation.8 | convolution fusion | flops 67371008 | bytes 786432 | tf_op jit(solution)/shard_map/dot_general | solution.py:248
  67.5 2.1 %convolution_convert_fusion.1 = bf16[3,512,128]{2,1,0:T(8,128)(2,1)S(1)} fusion(bf16[4,512,512]{2,1,0:T(8,128)(2,1)} %all-gather.2.cloned.1.call-done, bf16[512,128]{1,0:T(8,128)(2,1)S(1)} %convolution_convert_fusion.5), kind=kOutput, calls=%fused_computation.1 | convolution fusion | flops 201523200 | bytes 2621440 | tf_op jit(solution)/shard_map/kab,bc->kac/dot_general | solution.py:251
  69.6 1.7 %collective-permute-start.8 = (bf16[3,512,128]{2,1,0:T(8,128)(2,1)S(1)}, bf16[3,512,128]{2,1,0:T(8,128)(2,1)S(1)}, u32[]{:S(2)}, u32[]{:S(2)}) collective-permute-start(bf16[3,512,128]{2,1,0:T(8,128)(2,1)S(1)} %convolution_convert_fusion.1), channel_id=1, source_target_pairs={{0,1},{4,5},{8,9},{12,13},{16,17},{20,21},{24,25},{28,29}} | collective-permute-start | bytes 1179656 | tf_op jit(solution)/shard_map/ppermute | solution.py:161
  71.4 1.3 %collective-permute-done.8 = bf16[3,512,128]{2,1,0:T(8,128)(2,1)S(1)} collective-permute-done((bf16[3,512,128]{2,1,0:T(8,128)(2,1)S(1)}, bf16[3,512,128]{2,1,0:T(8,128)(2,1)S(1)}, u32[]{:S(2)}, u32[]{:S(2)}) %collective-permute-start.8) | collective-permute-done | bytes 393248 | tf_op jit(solution)/shard_map/ppermute | solution.py:161
  72.7 0.1 convert_element_type.172
  72.7 0.3 convolution_convert_fusion.4
  73.0 0.4 fusion.2
  73.5 0.7 collective-permute-start.9
  74.2 0.3 convolution_convert_fusion.3
  74.6 0.3 fusion.12
  74.9 0.7 collective-permute-start.10
  75.5 0.7 fusion
  76.3 0.6 convolution_convert_fusion
  76.9 0.7 collective-permute-start.11
  77.6 0.1 convert_element_type.184
  77.7 0.3 fusion.19
  78.0 0.5 fusion.1
  78.5 0.7 collective-permute-start.12
  79.3 0.3 fusion.18
  79.6 0.3 fusion.7
  80.0 1.3 collective-permute-start.13
  81.3 16.7 %collective-permute-done.13 = bf16[1,512,128]{2,1,0:T(8,128)(2,1)S(1)} collective-permute-done((bf16[1,512,128]{2,1,0:T(8,128)(2,1)S(1)}, bf16[1,512,128]{2,1,0:T(8,128)(2,1)S(1)}, u32[]{:S(2)}, u32[]{:S(2)}) %collective-permute-start.13) | collective-permute-done | bytes 131104 | tf_op jit(solution)/shard_map/ppermute | solution.py:161
  98.0 0.3 fusion.52
  98.4 0.2 collective-permute-start.14
  98.6 1.6 %collective-permute-start.16 = (bf16[576,128]{1,0:T(8,128)(2,1)S(1)}, bf16[576,128]{1,0:T(8,128)(2,1)S(1)}, u32[]{:S(2)}, u32[]{:S(2)}) collective-permute-start(bf16[576,128]{1,0:T(8,128)(2,1)S(1)} %pad_maximum_fusion.2.refs_0_), channel_id=1, source_target_pairs={{0,3},{1,0},{2,1},{3,2},{4,7},{5,4},{6,5},{7,6},{8,11},{9,8},{10,9... | collective-permute-start | bytes 442376 | tf_op jit(solution)/shard_map/ppermute | solution.py:73
  100.2 3.7 %collective-permute-done.14.refs_1_ = bf16[576,128]{1,0:T(8,128)(2,1)S(1)} collective-permute-done((bf16[576,128]{1,0:T(8,128)(2,1)S(1)}, bf16[576,128]{1,0:T(8,128)(2,1)S(1)}, u32[]{:S(2)}, u32[]{:S(2)}) %collective-permute-start.14) | collective-permute-done | bytes 147488 | tf_op jit(solution)/shard_map/ppermute | solution.py:73
  103.8 1.4 %collective-permute-done.15.refs_2_ = bf16[576,128]{1,0:T(8,128)(2,1)S(1)} collective-permute-done((bf16[576,128]{1,0:T(8,128)(2,1)S(1)}, bf16[576,128]{1,0:T(8,128)(2,1)S(1)}, u32[]{:S(2)}, u32[]{:S(2)}) %collective-permute-start.15) | collective-permute-done | bytes 147488 | tf_op jit(solution)/shard_map/ppermute | solution.py:73
  105.3 0.6 copy-done.5
  105.9 0.1 copy-done.6
  106.0 3.3 %shard_map.96 = (bf16[512,128]{1,0:T(8,128)(2,1)}, bf16[512,128]{1,0:T(8,128)(2,1)}, bf16[512,128]{1,0:T(8,128)(2,1)}, bf16[512,128]{1,0:T(8,128)(2,1)}, f32[4,64,128]{2,1,0:T(8,128)}) custom-call(s32[4]{0:T(128)} %bitcast.128, s32[4]{0:T(128)} %get-tuple-element.14.dests_ref, s32[4]{0:T(128)} %copy-done.10, s32[1]{0:T(128)} %bitcast.4.start_ref, ...), custom_call_target="tpu_custom_call" | custom-call | tf_op jit(solution)/shard_map/pallas_call | solution.py:129
  109.3 2.1 %collective-permute-start.17 = (bf16[512,128]{1,0:T(8,128)(2,1)}, bf16[512,128]{1,0:T(8,128)(2,1)S(1)}, u32[]{:S(2)}, u32[]{:S(2)}) collective-permute-start(bf16[512,128]{1,0:T(8,128)(2,1)} %get-tuple-element.10), channel_id=1, source_target_pairs={{0,3},{1,0},{2,1},{3,2},{4,7},{5,4},{6,5},{7,6},{8,11},{9,8},{10,9... | collective-permute-start | bytes 393224 | tf_op jit(solution)/shard_map/ppermute | solution.py:73
  111.4 2.0 %collective-permute-start.18 = (bf16[512,128]{1,0:T(8,128)(2,1)}, bf16[512,128]{1,0:T(8,128)(2,1)S(1)}, u32[]{:S(2)}, u32[]{:S(2)}) collective-permute-start(bf16[512,128]{1,0:T(8,128)(2,1)} %get-tuple-element.11), channel_id=1, source_target_pairs={{0,2},{1,3},{2,0},{3,1},{4,6},{5,7},{6,4},{7,5},{8,10},{9,11},{10,... | collective-permute-start | bytes 393224 | tf_op jit(solution)/shard_map/ppermute | solution.py:73
  113.4 2.2 %collective-permute-done.17.refs_1_ = bf16[512,128]{1,0:T(8,128)(2,1)S(1)} collective-permute-done((bf16[512,128]{1,0:T(8,128)(2,1)}, bf16[512,128]{1,0:T(8,128)(2,1)S(1)}, u32[]{:S(2)}, u32[]{:S(2)}) %collective-permute-start.17) | collective-permute-done | bytes 131104 | tf_op jit(solution)/shard_map/ppermute | solution.py:73
  115.6 4.7 %collective-permute-done.18.refs_2_ = bf16[512,128]{1,0:T(8,128)(2,1)S(1)} collective-permute-done((bf16[512,128]{1,0:T(8,128)(2,1)}, bf16[512,128]{1,0:T(8,128)(2,1)S(1)}, u32[]{:S(2)}, u32[]{:S(2)}) %collective-permute-start.18) | collective-permute-done | bytes 131104 | tf_op jit(solution)/shard_map/ppermute | solution.py:73
  120.3 0.6 copy-done.8
  120.9 0.0 copy-done.9
  121.0 2.3 %shard_map.97 = f32[1,512,128]{2,1,0:T(8,128)} custom-call(bf16[512,128]{1,0:T(8,128)(2,1)} %copy-done.2, bf16[1,512,512]{2,1,0:T(8,128)(2,1)} %inv_ref.1, bf16[512,128]{1,0:T(8,128)(2,1)} %get-tuple-element.9.refs_0_, bf16[512,128]{1,0:T(8,128)(2,1)} %copy-done.7, bf16[512,128]{1,0:T(8,128)(2,1)} %copy-done.8, bf16[512,128]{1,0:T(8,128)(2,1)} %copy-done.9), custom_call_target="tpu_custom_call" | custom-call | tf_op jit(solution)/shard_map/pallas_call | solution.py:152
  (40 shorter events, 0.4 us)
Async XLA Ops:
  7.2 1.9 %copy-start = (bf16[1,512,128]{2,1,0:T(8,128)(2,1)S(1)}, bf16[1,512,128]{2,1,0:T(8,128)(2,1)}, u32[]{:S(2)}) copy-start(bf16[1,512,128]{2,1,0:T(8,128)(2,1)} %param.8) | copy-start | bytes 393220
  7.2 6.5 %copy-start.11 = (s32[1,4]{1,0:T(1,128)S(1)}, s32[1,4]{1,0:T(1,128)}, u32[]{:S(2)}) copy-start(s32[1,4]{1,0:T(1,128)} %param.12) | copy-start | bytes 52
  7.2 59.0 %all-gather.2.cloned.1.call-start = ((), (), s32[]{:S(2)}) async-start(), calls=%async_computation | async-start | bytes 2359296 | tf_op jit(solution)/shard_map/all_gather | solution.py:219
  10.4 14.0 %copy-start.2 = (bf16[512,128]{1,0:T(8,128)(2,1)}, bf16[512,128]{1,0:T(8,128)(2,1)S(1)}, u32[]{:S(2)}) copy-start(bf16[512,128]{1,0:T(8,128)(2,1)S(1)} %convolution_convert_fusion.6.forward_ref) | copy-start | bytes 393220
  10.4 6.3 %collective-permute-start.2 = (bf16[512,128]{1,0:T(8,128)(2,1)S(1)}, bf16[512,128]{1,0:T(8,128)(2,1)S(1)}, u32[]{:S(2)}, u32[]{:S(2)}) collective-permute-start(bf16[512,128]{1,0:T(8,128)(2,1)S(1)} %convolution_convert_fusion.6.forward_ref), channel_id=1, source_target_pairs={{0,3},{1,0},{2,1},{3,2},{4,7},{5,4},{6,5},{7,6},{8,11},{9,8},{10,9... | collective-permute-start | bytes 393224 | tf_op jit(solution)/shard_map/ppermute | solution.py:73
  12.9 7.5 %collective-permute-start.1 = (bf16[512,128]{1,0:T(8,128)(2,1)S(1)}, bf16[512,128]{1,0:T(8,128)(2,1)S(1)}, u32[]{:S(2)}, u32[]{:S(2)}) collective-permute-start(bf16[512,128]{1,0:T(8,128)(2,1)S(1)} %convolution_convert_fusion.6.forward_ref), channel_id=1, source_target_pairs={{0,2},{1,3},{2,0},{3,1},{4,6},{5,7},{6,4},{7,5},{8,10},{9,11},{10,... | collective-permute-start | bytes 393224 | tf_op jit(solution)/shard_map/ppermute | solution.py:73
  13.5 6.9 %collective-permute-start = (bf16[512,128]{1,0:T(8,128)(2,1)S(1)}, bf16[512,128]{1,0:T(8,128)(2,1)S(1)}, u32[]{:S(2)}, u32[]{:S(2)}) collective-permute-start(bf16[512,128]{1,0:T(8,128)(2,1)S(1)} %convolution_convert_fusion.6.forward_ref), channel_id=1, source_target_pairs={{0,1},{1,2},{2,3},{3,0},{4,5},{5,6},{6,7},{7,4},{8,9},{9,10},{10,1... | collective-permute-start | bytes 393224 | tf_op jit(solution)/shard_map/ppermute | solution.py:73
  13.7 10.7 %copy-start.10 = (s32[4]{0:T(128)}, s32[4]{0:T(128)S(1)}, u32[]{:S(2)}) copy-start(s32[4]{0:T(128)S(1)} %and_select_fusion.table_ref) | copy-start | bytes 52
  25.4 1.6 %collective-permute-start.3 = (bf16[2,512,128]{2,1,0:T(8,128)(2,1)S(1)}, bf16[2,512,128]{2,1,0:T(8,128)(2,1)S(1)}, u32[]{:S(2)}, u32[]{:S(2)}) collective-permute-start(bf16[2,512,128]{2,1,0:T(8,128)(2,1)S(1)} %dynamic-slice_bitcast_fusion), channel_id=1, source_target_pairs={{0,1},{1,0},{2,3},{3,2},{4,5},{5,4},{6,7},{7,6},{8,9},{9,8},{10,11... | collective-permute-start | bytes 786440 | tf_op jit(solution)/shard_map/ppermute | solution.py:77
  28.0 5.8 %collective-permute-start.4 = (bf16[1,512,128]{2,1,0:T(8,128)(2,1)S(1)}, bf16[1,512,128]{2,1,0:T(8,128)(2,1)S(1)}, u32[]{:S(2)}, u32[]{:S(2)}) collective-permute-start(bf16[1,512,128]{2,1,0:T(8,128)(2,1)S(1)} %constant_dynamic-slice_fusion), channel_id=1, source_target_pairs={{0,2},{1,3},{2,0},{3,1},{4,6},{5,7},{6,4},{7,5},{8,10},{9,11},{10,... | collective-permute-start | bytes 393224 | tf_op jit(solution)/shard_map/ppermute | solution.py:77
  33.9 5.0 %collective-permute-start.5 = (bf16[512,128]{1,0:T(8,128)(2,1)S(1)}, bf16[512,128]{1,0:T(8,128)(2,1)S(1)}, u32[]{:S(2)}, u32[]{:S(2)}) collective-permute-start(bf16[512,128]{1,0:T(8,128)(2,1)S(1)} %fusion.20), channel_id=1, source_target_pairs={{0,4},{4,0},{8,12},{12,8},{16,20},{20,16},{24,28},{28,24},{1,5},{5... | collective-permute-start | bytes 393224 | tf_op jit(solution)/shard_map/ppermute | solution.py:77
  39.0 12.1 %collective-permute-start.6 = (bf16[512,128]{1,0:T(8,128)(2,1)S(1)}, bf16[512,128]{1,0:T(8,128)(2,1)S(1)}, u32[]{:S(2)}, u32[]{:S(2)}) collective-permute-start(bf16[512,128]{1,0:T(8,128)(2,1)S(1)} %add_convert_fusion.2), channel_id=1, source_target_pairs={{0,8},{4,12},{8,0},{12,4},{16,24},{20,28},{24,16},{28,20},{1,9},{5... | collective-permute-start | bytes 393224 | tf_op jit(solution)/shard_map/ppermute | solution.py:77
  51.1 14.1 %collective-permute-start.7 = (bf16[512,128]{1,0:T(8,128)(2,1)S(1)}, bf16[512,128]{1,0:T(8,128)(2,1)S(1)}, u32[]{:S(2)}, u32[]{:S(2)}) collective-permute-start(bf16[512,128]{1,0:T(8,128)(2,1)S(1)} %add_convert_fusion.1), channel_id=1, source_target_pairs={{0,16},{4,20},{8,24},{12,28},{16,0},{20,4},{24,8},{28,12},{1,17},{... | collective-permute-start | bytes 393224 | tf_op jit(solution)/shard_map/ppermute | solution.py:77
  67.5 5.2 %copy-start.1 = (bf16[4,512,512]{2,1,0:T(8,128)(2,1)S(1)}, bf16[4,512,512]{2,1,0:T(8,128)(2,1)}, u32[]{:S(2)}) copy-start(bf16[4,512,512]{2,1,0:T(8,128)(2,1)} %all-gather.2.cloned.1.call-done) | copy-start | bytes 6291460
  69.6 3.0 %collective-permute-start.8 = (bf16[3,512,128]{2,1,0:T(8,128)(2,1)S(1)}, bf16[3,512,128]{2,1,0:T(8,128)(2,1)S(1)}, u32[]{:S(2)}, u32[]{:S(2)}) collective-permute-start(bf16[3,512,128]{2,1,0:T(8,128)(2,1)S(1)} %convolution_convert_fusion.1), channel_id=1, source_target_pairs={{0,1},{4,5},{8,9},{12,13},{16,17},{20,21},{24,25},{28,29}} | collective-permute-start | bytes 1179656 | tf_op jit(solution)/shard_map/ppermute | solution.py:161
  73.5 0.7 collective-permute-start.9
  74.9 0.7 collective-permute-start.10
  76.9 0.7 collective-permute-start.11
  78.5 0.7 collective-permute-start.12
  80.0 18.0 %collective-permute-start.13 = (bf16[1,512,128]{2,1,0:T(8,128)(2,1)S(1)}, bf16[1,512,128]{2,1,0:T(8,128)(2,1)S(1)}, u32[]{:S(2)}, u32[]{:S(2)}) collective-permute-start(bf16[1,512,128]{2,1,0:T(8,128)(2,1)S(1)} %fusion.7), channel_id=1, source_target_pairs={{1,0},{5,4},{9,8},{13,12},{17,16},{21,20},{25,24},{29,28}} | collective-permute-start | bytes 393224 | tf_op jit(solution)/shard_map/ppermute | solution.py:161
  98.4 6.9 %copy-start.3 = (bf16[576,128]{1,0:T(8,128)(2,1)}, bf16[576,128]{1,0:T(8,128)(2,1)S(1)}, u32[]{:S(2)}) copy-start(bf16[576,128]{1,0:T(8,128)(2,1)S(1)} %pad_maximum_fusion.2.refs_0_) | copy-start | bytes 442372
  98.4 5.5 %collective-permute-start.14 = (bf16[576,128]{1,0:T(8,128)(2,1)S(1)}, bf16[576,128]{1,0:T(8,128)(2,1)S(1)}, u32[]{:S(2)}, u32[]{:S(2)}) collective-permute-start(bf16[576,128]{1,0:T(8,128)(2,1)S(1)} %pad_maximum_fusion.2.refs_0_), channel_id=1, source_target_pairs={{0,1},{1,2},{2,3},{3,0},{4,5},{5,6},{6,7},{7,4},{8,9},{9,10},{10,1... | collective-permute-start | bytes 442376 | tf_op jit(solution)/shard_map/ppermute | solution.py:73
  98.6 6.7 %collective-permute-start.15 = (bf16[576,128]{1,0:T(8,128)(2,1)S(1)}, bf16[576,128]{1,0:T(8,128)(2,1)S(1)}, u32[]{:S(2)}, u32[]{:S(2)}) collective-permute-start(bf16[576,128]{1,0:T(8,128)(2,1)S(1)} %pad_maximum_fusion.2.refs_0_), channel_id=1, source_target_pairs={{0,2},{1,3},{2,0},{3,1},{4,6},{5,7},{6,4},{7,5},{8,10},{9,11},{10,... | collective-permute-start | bytes 442376 | tf_op jit(solution)/shard_map/ppermute | solution.py:73
  98.6 6.7 %collective-permute-start.16 = (bf16[576,128]{1,0:T(8,128)(2,1)S(1)}, bf16[576,128]{1,0:T(8,128)(2,1)S(1)}, u32[]{:S(2)}, u32[]{:S(2)}) collective-permute-start(bf16[576,128]{1,0:T(8,128)(2,1)S(1)} %pad_maximum_fusion.2.refs_0_), channel_id=1, source_target_pairs={{0,3},{1,0},{2,1},{3,2},{4,7},{5,4},{6,5},{7,6},{8,11},{9,8},{10,9... | collective-permute-start | bytes 442376 | tf_op jit(solution)/shard_map/ppermute | solution.py:73
  103.8 1.5 %copy-start.4 = (bf16[576,128]{1,0:T(8,128)(2,1)}, bf16[576,128]{1,0:T(8,128)(2,1)S(1)}, u32[]{:S(2)}) copy-start(bf16[576,128]{1,0:T(8,128)(2,1)S(1)} %collective-permute-done.14.refs_1_) | copy-start | bytes 442372
  105.3 0.7 copy-start.5
  105.3 0.7 copy-start.6
  109.3 6.3 %collective-permute-start.17 = (bf16[512,128]{1,0:T(8,128)(2,1)}, bf16[512,128]{1,0:T(8,128)(2,1)S(1)}, u32[]{:S(2)}, u32[]{:S(2)}) collective-permute-start(bf16[512,128]{1,0:T(8,128)(2,1)} %get-tuple-element.10), channel_id=1, source_target_pairs={{0,3},{1,0},{2,1},{3,2},{4,7},{5,4},{6,5},{7,6},{8,11},{9,8},{10,9... | collective-permute-start | bytes 393224 | tf_op jit(solution)/shard_map/ppermute | solution.py:73
  111.4 8.9 %collective-permute-start.18 = (bf16[512,128]{1,0:T(8,128)(2,1)}, bf16[512,128]{1,0:T(8,128)(2,1)S(1)}, u32[]{:S(2)}, u32[]{:S(2)}) collective-permute-start(bf16[512,128]{1,0:T(8,128)(2,1)} %get-tuple-element.11), channel_id=1, source_target_pairs={{0,2},{1,3},{2,0},{3,1},{4,6},{5,7},{6,4},{7,5},{8,10},{9,11},{10,... | collective-permute-start | bytes 393224 | tf_op jit(solution)/shard_map/ppermute | solution.py:73
  113.4 6.9 %collective-permute-start.19 = (bf16[512,128]{1,0:T(8,128)(2,1)}, bf16[512,128]{1,0:T(8,128)(2,1)S(1)}, u32[]{:S(2)}, u32[]{:S(2)}) collective-permute-start(bf16[512,128]{1,0:T(8,128)(2,1)} %get-tuple-element.12), channel_id=1, source_target_pairs={{0,1},{1,2},{2,3},{3,0},{4,5},{5,6},{6,7},{7,4},{8,9},{9,10},{10,1... | collective-permute-start | bytes 393224 | tf_op jit(solution)/shard_map/ppermute | solution.py:73
  115.6 4.7 %copy-start.7 = (bf16[512,128]{1,0:T(8,128)(2,1)}, bf16[512,128]{1,0:T(8,128)(2,1)S(1)}, u32[]{:S(2)}) copy-start(bf16[512,128]{1,0:T(8,128)(2,1)S(1)} %collective-permute-done.17.refs_1_) | copy-start | bytes 393220
  120.3 0.6 copy-start.8
  120.3 0.7 copy-start.9
Sparse Core Ops, SparseCore 0:
  10.8 55.3 all-gather.1

commit v17 on v16

--- a/solution.py
+++ b/solution.py
@@ -187,10 +187,17 @@
         bit *= 2
     part = chunks[0]
     bit = 1
-    while bit < rows_n:
+    last = rows_n // 2 if rows_n == 8 else rows_n
+    while bit < last:
         got = swapped(part, "row", rows_n, bit)
         part = (part.astype(jnp.float32) + got.astype(jnp.float32)).astype(jnp.bfloat16)
         bit *= 2
+    if rows_n == 8:
+        row = lax.axis_index("row")
+        got = lax.ppermute(part, "row", [(2, 4), (4, 2), (3, 5), (5, 3)])
+        part = (part.astype(jnp.float32) + got.astype(jnp.float32)).astype(jnp.bfloat16)
+        handed = lax.ppermute(part, "row", [(2, 0), (3, 1), (4, 6), (5, 7)])
+        part = jnp.where((row >= 2) & (row <= 5), part, handed)
     return part
 
 

time: 130 us -> 131 us (level)
    ppermute x0 -> x2, waiting for transfers between devices: none -> 14.7 us  [the longest x1 14.7 us: summed_chunks(): handed = lax.ppermute(part, 'row', [(2, 0), (3, 1), (4, 6), (5, 7)])]
    ppermute x5 -> x4, waiting for transfers between devices: 32.1 us -> 17.8 us  [swapped(): return lax.ppermute(x, axis, [(i, i ^ bit) for i in range(size)])]
    ppermute x0 -> x2, starting transfers between devices: none -> 1.96 us  [the longest x1 1.29 us: summed_chunks(): handed = lax.ppermute(part, 'row', [(2, 0), (3, 1), (4, 6), (5, 7)])]
    ppermute x5 -> x4, starting transfers between devices: 6.46 us -> 5.88 us  [swapped(): return lax.ppermute(x, axis, [(i, i ^ bit) for i in range(size)])]
  transfers between devices with their start and end apart: 21 -> 22, of which waited for: 14 -> 13; matrix products, arithmetic and copies ran while one was open for 5% -> 5% of each run, Pallas kernels for 2% -> 2%
where the time goes in v17:
time: 131 us
  waiting for transfers between devices  67.3 us (51%)
  starting transfers between devices  22.4 us (17%)
  between operations  14.5 us (11%)
  matrix products  9.38 us (7%)
  Pallas kernels  8.69 us (7%)
  other arithmetic  4.94 us (4%)
  local copies, waits for them, and re-layouts  3.37 us (3%)
    ppermute x6, waiting for transfers between devices, hop(): sent = lax.ppermute(x.astype(jnp.bfloat16), 'col', [(source, target)])  18 us
    ppermute x4, waiting for transfers between devices, swapped(): return lax.ppermute(x, axis, [(i, i ^ bit) for i in range(size)])  17.8 us
    ppermute x9, waiting for transfers between devices, shifted(): return lax.ppermute(x, axis, [(i, (i + shift) % size) for i in range(size)])  16.8 us
    ppermute x1, waiting for transfers between devices, summed_chunks(): handed = lax.ppermute(part, 'row', [(2, 0), (3, 1), (4, 6), (5, 7)])  14.7 us
    ppermute x9, starting transfers between devices, shifted(): return lax.ppermute(x, axis, [(i, (i + shift) % size) for i in range(size)])  9.25 us
    ppermute x4, starting transfers between devices, swapped(): return lax.ppermute(x, axis, [(i, i ^ bit) for i in range(size)])  5.88 us
    ppermute x6, starting transfers between devices, hop(): sent = lax.ppermute(x.astype(jnp.bfloat16), 'col', [(source, target)])  5.32 us
    pallas_call x1, Pallas kernels, tail_terms(): pl.pallas_call(functools.partial(tail_kernel, levels, peers), out_shape=o...  3.28 us
  transfers between devices with their start and end apart: 22, of which 13 were waited for; matrix products, arithmetic and copies ran while one was open for 5% of the time, Pallas kernels for 2%

profile of v17, /device:TPU:0, one launch (start us, length us, event | category | flops | bytes accessed | tf_op | source)
XLA Modules:
  0.0 130.7 jit_solution(11410194114937150798)
XLA Ops:
  7.2 0.0 all-gather.2.cloned.1.call-start
  7.3 1.0 constant_dynamic-slice_fusion.3
  8.3 0.7 pad_maximum_fusion.1
  9.0 1.3 %convolution_convert_fusion.6.forward_ref = bf16[512,128]{1,0:T(8,128)(2,1)S(1)} fusion(bf16[1,512,512]{2,1,0:T(8,128)(2,1)} %inv_ref.1, bf16[1,512,128]{2,1,0:T(8,128)(2,1)S(1)} %copy-done), kind=kOutput, calls=%fused_computation.9 | convolution fusion | flops 67174400 | bytes 786432 | tf_op jit(solution)/shard_map/dot_general | solution.py:232
  10.4 2.5 %collective-permute-start.2 = (bf16[512,128]{1,0:T(8,128)(2,1)S(1)}, bf16[512,128]{1,0:T(8,128)(2,1)S(1)}, u32[]{:S(2)}, u32[]{:S(2)}) collective-permute-start(bf16[512,128]{1,0:T(8,128)(2,1)S(1)} %convolution_convert_fusion.6.forward_ref), channel_id=1, source_target_pairs={{0,3},{1,0},{2,1},{3,2},{4,7},{5,4},{6,5},{7,6},{8,11},{9,8},{10,9... | collective-permute-start | bytes 393224 | tf_op jit(solution)/shard_map/ppermute | solution.py:73
  12.9 0.6 collective-permute-start.1
  13.5 0.2 collective-permute-start
  13.7 0.5 and_select_fusion.1
  14.2 0.8 iota_reduce_fusion
  14.9 0.7 pad_add_fusion.fold_ref
  15.6 1.1 collective-permute-done.2
  16.7 3.8 %collective-permute-done.1 = bf16[512,128]{1,0:T(8,128)(2,1)S(1)} collective-permute-done((bf16[512,128]{1,0:T(8,128)(2,1)S(1)}, bf16[512,128]{1,0:T(8,128)(2,1)S(1)}, u32[]{:S(2)}, u32[]{:S(2)}) %collective-permute-start.1) | collective-permute-done | bytes 131104 | tf_op jit(solution)/shard_map/ppermute | solution.py:73
  20.4 0.9 pad_maximum_fusion.panels_ref
  21.3 3.1 %shard_map.95 = bf16[4,512,128]{2,1,0:T(8,128)(2,1)} custom-call(s32[4]{0:T(128)} %bitcast.127, s32[4]{0:T(128)} %get-tuple-element.8.picks_ref, s32[2]{0:T(128)} %pad_add_fusion.fold_ref, bf16[4,512,512]{2,1,0:T(8,128)(2,1)} %bitcast.119, bf16[4,512,128]{2,1,0:T(8,128)(2,1)} %pad_maximum_fusion.panels_ref, bf16[4,64,128]{2,1,0:T(8,128)(2,1)} %rhs_ref.1), custom_call_target="tpu_custom_call" | custom-call | tf_op jit(solution)/shard_map/pallas_call | solution.py:37
  24.4 1.0 dynamic-slice_bitcast_fusion
  25.4 0.1 collective-permute-start.3
  25.5 1.5 %collective-permute-done.3 = bf16[2,512,128]{2,1,0:T(8,128)(2,1)S(1)} collective-permute-done((bf16[2,512,128]{2,1,0:T(8,128)(2,1)S(1)}, bf16[2,512,128]{2,1,0:T(8,128)(2,1)S(1)}, u32[]{:S(2)}, u32[]{:S(2)}) %collective-permute-start.3) | collective-permute-done | bytes 262176 | tf_op jit(solution)/shard_map/ppermute | solution.py:77
  27.0 1.0 fusion.3
  28.0 1.7 %collective-permute-start.4 = (bf16[1,512,128]{2,1,0:T(8,128)(2,1)S(1)}, bf16[1,512,128]{2,1,0:T(8,128)(2,1)S(1)}, u32[]{:S(2)}, u32[]{:S(2)}) collective-permute-start(bf16[1,512,128]{2,1,0:T(8,128)(2,1)S(1)} %constant_dynamic-slice_fusion), channel_id=1, source_target_pairs={{0,2},{1,3},{2,0},{3,1},{4,6},{5,7},{6,4},{7,5},{8,10},{9,11},{10,... | collective-permute-start | bytes 393224 | tf_op jit(solution)/shard_map/ppermute | solution.py:77
  29.7 3.9 %collective-permute-done.4 = bf16[1,512,128]{2,1,0:T(8,128)(2,1)S(1)} collective-permute-done((bf16[1,512,128]{2,1,0:T(8,128)(2,1)S(1)}, bf16[1,512,128]{2,1,0:T(8,128)(2,1)S(1)}, u32[]{:S(2)}, u32[]{:S(2)}) %collective-permute-start.4) | collective-permute-done | bytes 131104 | tf_op jit(solution)/shard_map/ppermute | solution.py:77
  33.7 2.0 %collective-permute-start.5 = (bf16[512,128]{1,0:T(8,128)(2,1)S(1)}, bf16[512,128]{1,0:T(8,128)(2,1)S(1)}, u32[]{:S(2)}, u32[]{:S(2)}) collective-permute-start(bf16[512,128]{1,0:T(8,128)(2,1)S(1)} %fusion.20), channel_id=1, source_target_pairs={{0,4},{4,0},{8,12},{12,8},{16,20},{20,16},{24,28},{28,24},{1,5},{5... | collective-permute-start | bytes 393224 | tf_op jit(solution)/shard_map/ppermute | solution.py:77
  35.7 3.0 %collective-permute-done.5 = bf16[512,128]{1,0:T(8,128)(2,1)S(1)} collective-permute-done((bf16[512,128]{1,0:T(8,128)(2,1)S(1)}, bf16[512,128]{1,0:T(8,128)(2,1)S(1)}, u32[]{:S(2)}, u32[]{:S(2)}) %collective-permute-start.5) | collective-permute-done | bytes 131104 | tf_op jit(solution)/shard_map/ppermute | solution.py:77
  38.8 2.1 %collective-permute-start.6 = (bf16[512,128]{1,0:T(8,128)(2,1)S(1)}, bf16[512,128]{1,0:T(8,128)(2,1)S(1)}, u32[]{:S(2)}, u32[]{:S(2)}) collective-permute-start(bf16[512,128]{1,0:T(8,128)(2,1)S(1)} %add_convert_fusion.2), channel_id=1, source_target_pairs={{0,8},{4,12},{8,0},{12,4},{16,24},{20,28},{24,16},{28,20},{1,9},{5... | collective-permute-start | bytes 393224 | tf_op jit(solution)/shard_map/ppermute | solution.py:77
  40.9 9.4 %collective-permute-done.6 = bf16[512,128]{1,0:T(8,128)(2,1)S(1)} collective-permute-done((bf16[512,128]{1,0:T(8,128)(2,1)S(1)}, bf16[512,128]{1,0:T(8,128)(2,1)S(1)}, u32[]{:S(2)}, u32[]{:S(2)}) %collective-permute-start.6) | collective-permute-done | bytes 131104 | tf_op jit(solution)/shard_map/ppermute | solution.py:77
  50.3 0.7 collective-permute-start.7
  51.0 1.3 collective-permute-start.8
  52.3 14.7 %collective-permute-done.8 = bf16[512,128]{1,0:T(8,128)(2,1)S(1)} collective-permute-done((bf16[512,128]{1,0:T(8,128)(2,1)S(1)}, bf16[512,128]{1,0:T(8,128)(2,1)S(1)}, u32[]{:S(2)}, u32[]{:S(2)}) %collective-permute-start.8) | collective-permute-done | bytes 131104 | tf_op jit(solution)/shard_map/ppermute | solution.py:199
  67.1 1.3 %convolution_convert_fusion.5 = bf16[512,128]{1,0:T(8,128)(2,1)S(1)} fusion(bf16[4,512,512]{2,1,0:T(8,128)(2,1)} %all-gather.2.cloned.1.call-done, bf16[512,128]{1,0:T(8,128)(2,1)S(1)} %broadcast_select_fusion), kind=kOutput, calls=%fused_computation.8 | convolution fusion | flops 67371008 | bytes 786432 | tf_op jit(solution)/shard_map/dot_general | solution.py:255
  68.4 2.1 %convolution_convert_fusion.1 = bf16[3,512,128]{2,1,0:T(8,128)(2,1)S(1)} fusion(bf16[4,512,512]{2,1,0:T(8,128)(2,1)} %all-gather.2.cloned.1.call-done, bf16[512,128]{1,0:T(8,128)(2,1)S(1)} %convolution_convert_fusion.5), kind=kOutput, calls=%fused_computation.1 | convolution fusion | flops 201523200 | bytes 2621440 | tf_op jit(solution)/shard_map/kab,bc->kac/dot_general | solution.py:258
  70.6 1.3 %collective-permute-start.9 = (bf16[3,512,128]{2,1,0:T(8,128)(2,1)S(1)}, bf16[3,512,128]{2,1,0:T(8,128)(2,1)S(1)}, u32[]{:S(2)}, u32[]{:S(2)}) collective-permute-start(bf16[3,512,128]{2,1,0:T(8,128)(2,1)S(1)} %convolution_convert_fusion.1), channel_id=1, source_target_pairs={{0,1},{4,5},{8,9},{12,13},{16,17},{20,21},{24,25},{28,29}} | collective-permute-start | bytes 1179656 | tf_op jit(solution)/shard_map/ppermute | solution.py:161
  71.9 1.3 %collective-permute-done.9 = bf16[3,512,128]{2,1,0:T(8,128)(2,1)S(1)} collective-permute-done((bf16[3,512,128]{2,1,0:T(8,128)(2,1)S(1)}, bf16[3,512,128]{2,1,0:T(8,128)(2,1)S(1)}, u32[]{:S(2)}, u32[]{:S(2)}) %collective-permute-start.9) | collective-permute-done | bytes 393248 | tf_op jit(solution)/shard_map/ppermute | solution.py:161
  73.2 0.1 convert_element_type.172
  73.3 0.3 convolution_convert_fusion.4
  73.6 0.4 fusion.2
  74.0 0.7 collective-permute-start.10
  74.8 0.3 convolution_convert_fusion.3
  75.1 0.3 fusion.12
  75.4 0.7 collective-permute-start.11
  76.1 0.7 fusion
  76.8 0.6 convolution_convert_fusion
  77.4 0.7 collective-permute-start.12
  78.1 0.1 convert_element_type.184
  78.2 0.3 fusion.19
  78.5 0.5 fusion.1
  79.0 0.7 collective-permute-start.13
  79.8 0.3 fusion.18
  80.1 0.3 fusion.7
  80.5 1.3 collective-permute-start.14
  81.8 16.7 %collective-permute-done.14 = bf16[1,512,128]{2,1,0:T(8,128)(2,1)S(1)} collective-permute-done((bf16[1,512,128]{2,1,0:T(8,128)(2,1)S(1)}, bf16[1,512,128]{2,1,0:T(8,128)(2,1)S(1)}, u32[]{:S(2)}, u32[]{:S(2)}) %collective-permute-start.14) | collective-permute-done | bytes 131104 | tf_op jit(solution)/shard_map/ppermute | solution.py:161
  98.5 0.3 fusion.52
  98.9 0.2 collective-permute-start.15
  99.1 1.6 %collective-permute-start.17 = (bf16[576,128]{1,0:T(8,128)(2,1)S(1)}, bf16[576,128]{1,0:T(8,128)(2,1)S(1)}, u32[]{:S(2)}, u32[]{:S(2)}) collective-permute-start(bf16[576,128]{1,0:T(8,128)(2,1)S(1)} %pad_maximum_fusion.2.refs_0_), channel_id=1, source_target_pairs={{0,3},{1,0},{2,1},{3,2},{4,7},{5,4},{6,5},{7,6},{8,11},{9,8},{10,9... | collective-permute-start | bytes 442376 | tf_op jit(solution)/shard_map/ppermute | solution.py:73
  100.7 3.7 %collective-permute-done.15.refs_1_ = bf16[576,128]{1,0:T(8,128)(2,1)S(1)} collective-permute-done((bf16[576,128]{1,0:T(8,128)(2,1)S(1)}, bf16[576,128]{1,0:T(8,128)(2,1)S(1)}, u32[]{:S(2)}, u32[]{:S(2)}) %collective-permute-start.15) | collective-permute-done | bytes 147488 | tf_op jit(solution)/shard_map/ppermute | solution.py:73
  104.3 1.4 %collective-permute-done.16.refs_2_ = bf16[576,128]{1,0:T(8,128)(2,1)S(1)} collective-permute-done((bf16[576,128]{1,0:T(8,128)(2,1)S(1)}, bf16[576,128]{1,0:T(8,128)(2,1)S(1)}, u32[]{:S(2)}, u32[]{:S(2)}) %collective-permute-start.16) | collective-permute-done | bytes 147488 | tf_op jit(solution)/shard_map/ppermute | solution.py:73
  105.8 0.6 copy-done.5
  106.4 0.1 copy-done.6
  106.5 3.3 %shard_map.96 = (bf16[512,128]{1,0:T(8,128)(2,1)}, bf16[512,128]{1,0:T(8,128)(2,1)}, bf16[512,128]{1,0:T(8,128)(2,1)}, bf16[512,128]{1,0:T(8,128)(2,1)}, f32[4,64,128]{2,1,0:T(8,128)}) custom-call(s32[4]{0:T(128)} %bitcast.128, s32[4]{0:T(128)} %get-tuple-element.14.dests_ref, s32[4]{0:T(128)} %copy-done.10, s32[1]{0:T(128)} %bitcast.4.start_ref, ...), custom_call_target="tpu_custom_call" | custom-call | tf_op jit(solution)/shard_map/pallas_call | solution.py:129
  109.8 1.8 %collective-permute-start.18 = (bf16[512,128]{1,0:T(8,128)(2,1)}, bf16[512,128]{1,0:T(8,128)(2,1)S(1)}, u32[]{:S(2)}, u32[]{:S(2)}) collective-permute-start(bf16[512,128]{1,0:T(8,128)(2,1)} %get-tuple-element.10), channel_id=1, source_target_pairs={{0,3},{1,0},{2,1},{3,2},{4,7},{5,4},{6,5},{7,6},{8,11},{9,8},{10,9... | collective-permute-start | bytes 393224 | tf_op jit(solution)/shard_map/ppermute | solution.py:73
  111.6 2.4 %collective-permute-start.19 = (bf16[512,128]{1,0:T(8,128)(2,1)}, bf16[512,128]{1,0:T(8,128)(2,1)S(1)}, u32[]{:S(2)}, u32[]{:S(2)}) collective-permute-start(bf16[512,128]{1,0:T(8,128)(2,1)} %get-tuple-element.11), channel_id=1, source_target_pairs={{0,2},{1,3},{2,0},{3,1},{4,6},{5,7},{6,4},{7,5},{8,10},{9,11},{10,... | collective-permute-start | bytes 393224 | tf_op jit(solution)/shard_map/ppermute | solution.py:73
  114.0 1.7 %collective-permute-done.18.refs_1_ = bf16[512,128]{1,0:T(8,128)(2,1)S(1)} collective-permute-done((bf16[512,128]{1,0:T(8,128)(2,1)}, bf16[512,128]{1,0:T(8,128)(2,1)S(1)}, u32[]{:S(2)}, u32[]{:S(2)}) %collective-permute-start.18) | collective-permute-done | bytes 131104 | tf_op jit(solution)/shard_map/ppermute | solution.py:73
  115.7 5.1 %collective-permute-done.19.refs_2_ = bf16[512,128]{1,0:T(8,128)(2,1)S(1)} collective-permute-done((bf16[512,128]{1,0:T(8,128)(2,1)}, bf16[512,128]{1,0:T(8,128)(2,1)S(1)}, u32[]{:S(2)}, u32[]{:S(2)}) %collective-permute-start.19) | collective-permute-done | bytes 131104 | tf_op jit(solution)/shard_map/ppermute | solution.py:73
  120.8 0.6 copy-done.8
  121.5 0.0 copy-done.9
  121.5 2.3 %shard_map.97 = f32[1,512,128]{2,1,0:T(8,128)} custom-call(bf16[512,128]{1,0:T(8,128)(2,1)} %copy-done.2, bf16[1,512,512]{2,1,0:T(8,128)(2,1)} %inv_ref.1, bf16[512,128]{1,0:T(8,128)(2,1)} %get-tuple-element.9.refs_0_, bf16[512,128]{1,0:T(8,128)(2,1)} %copy-done.7, bf16[512,128]{1,0:T(8,128)(2,1)} %copy-done.8, bf16[512,128]{1,0:T(8,128)(2,1)} %copy-done.9), custom_call_target="tpu_custom_call" | custom-call | tf_op jit(solution)/shard_map/pallas_call | solution.py:152
  (43 shorter events, 0.4 us)
Async XLA Ops:
  7.2 1.9 %copy-start = (bf16[1,512,128]{2,1,0:T(8,128)(2,1)S(1)}, bf16[1,512,128]{2,1,0:T(8,128)(2,1)}, u32[]{:S(2)}) copy-start(bf16[1,512,128]{2,1,0:T(8,128)(2,1)} %param.8) | copy-start | bytes 393220
  7.2 6.5 %copy-start.11 = (s32[1,4]{1,0:T(1,128)S(1)}, s32[1,4]{1,0:T(1,128)}, u32[]{:S(2)}) copy-start(s32[1,4]{1,0:T(1,128)} %param.12) | copy-start | bytes 52
  7.2 59.9 %all-gather.2.cloned.1.call-start = ((), (), s32[]{:S(2)}) async-start(), calls=%async_computation | async-start | bytes 2359296 | tf_op jit(solution)/shard_map/all_gather | solution.py:226
  10.4 14.0 %copy-start.2 = (bf16[512,128]{1,0:T(8,128)(2,1)}, bf16[512,128]{1,0:T(8,128)(2,1)S(1)}, u32[]{:S(2)}) copy-start(bf16[512,128]{1,0:T(8,128)(2,1)S(1)} %convolution_convert_fusion.6.forward_ref) | copy-start | bytes 393220
  10.4 6.3 %collective-permute-start.2 = (bf16[512,128]{1,0:T(8,128)(2,1)S(1)}, bf16[512,128]{1,0:T(8,128)(2,1)S(1)}, u32[]{:S(2)}, u32[]{:S(2)}) collective-permute-start(bf16[512,128]{1,0:T(8,128)(2,1)S(1)} %convolution_convert_fusion.6.forward_ref), channel_id=1, source_target_pairs={{0,3},{1,0},{2,1},{3,2},{4,7},{5,4},{6,5},{7,6},{8,11},{9,8},{10,9... | collective-permute-start | bytes 393224 | tf_op jit(solution)/shard_map/ppermute | solution.py:73
  12.9 7.5 %collective-permute-start.1 = (bf16[512,128]{1,0:T(8,128)(2,1)S(1)}, bf16[512,128]{1,0:T(8,128)(2,1)S(1)}, u32[]{:S(2)}, u32[]{:S(2)}) collective-permute-start(bf16[512,128]{1,0:T(8,128)(2,1)S(1)} %convolution_convert_fusion.6.forward_ref), channel_id=1, source_target_pairs={{0,2},{1,3},{2,0},{3,1},{4,6},{5,7},{6,4},{7,5},{8,10},{9,11},{10,... | collective-permute-start | bytes 393224 | tf_op jit(solution)/shard_map/ppermute | solution.py:73
  13.5 6.9 %collective-permute-start = (bf16[512,128]{1,0:T(8,128)(2,1)S(1)}, bf16[512,128]{1,0:T(8,128)(2,1)S(1)}, u32[]{:S(2)}, u32[]{:S(2)}) collective-permute-start(bf16[512,128]{1,0:T(8,128)(2,1)S(1)} %convolution_convert_fusion.6.forward_ref), channel_id=1, source_target_pairs={{0,1},{1,2},{2,3},{3,0},{4,5},{5,6},{6,7},{7,4},{8,9},{9,10},{10,1... | collective-permute-start | bytes 393224 | tf_op jit(solution)/shard_map/ppermute | solution.py:73
  13.7 10.7 %copy-start.10 = (s32[4]{0:T(128)}, s32[4]{0:T(128)S(1)}, u32[]{:S(2)}) copy-start(s32[4]{0:T(128)S(1)} %and_select_fusion.table_ref) | copy-start | bytes 52
  25.4 1.6 %collective-permute-start.3 = (bf16[2,512,128]{2,1,0:T(8,128)(2,1)S(1)}, bf16[2,512,128]{2,1,0:T(8,128)(2,1)S(1)}, u32[]{:S(2)}, u32[]{:S(2)}) collective-permute-start(bf16[2,512,128]{2,1,0:T(8,128)(2,1)S(1)} %dynamic-slice_bitcast_fusion), channel_id=1, source_target_pairs={{0,1},{1,0},{2,3},{3,2},{4,5},{5,4},{6,7},{7,6},{8,9},{9,8},{10,11... | collective-permute-start | bytes 786440 | tf_op jit(solution)/shard_map/ppermute | solution.py:77
  28.0 5.6 %collective-permute-start.4 = (bf16[1,512,128]{2,1,0:T(8,128)(2,1)S(1)}, bf16[1,512,128]{2,1,0:T(8,128)(2,1)S(1)}, u32[]{:S(2)}, u32[]{:S(2)}) collective-permute-start(bf16[1,512,128]{2,1,0:T(8,128)(2,1)S(1)} %constant_dynamic-slice_fusion), channel_id=1, source_target_pairs={{0,2},{1,3},{2,0},{3,1},{4,6},{5,7},{6,4},{7,5},{8,10},{9,11},{10,... | collective-permute-start | bytes 393224 | tf_op jit(solution)/shard_map/ppermute | solution.py:77
  33.7 5.1 %collective-permute-start.5 = (bf16[512,128]{1,0:T(8,128)(2,1)S(1)}, bf16[512,128]{1,0:T(8,128)(2,1)S(1)}, u32[]{:S(2)}, u32[]{:S(2)}) collective-permute-start(bf16[512,128]{1,0:T(8,128)(2,1)S(1)} %fusion.20), channel_id=1, source_target_pairs={{0,4},{4,0},{8,12},{12,8},{16,20},{20,16},{24,28},{28,24},{1,5},{5... | collective-permute-start | bytes 393224 | tf_op jit(solution)/shard_map/ppermute | solution.py:77
  38.8 11.5 %collective-permute-start.6 = (bf16[512,128]{1,0:T(8,128)(2,1)S(1)}, bf16[512,128]{1,0:T(8,128)(2,1)S(1)}, u32[]{:S(2)}, u32[]{:S(2)}) collective-permute-start(bf16[512,128]{1,0:T(8,128)(2,1)S(1)} %add_convert_fusion.2), channel_id=1, source_target_pairs={{0,8},{4,12},{8,0},{12,4},{16,24},{20,28},{24,16},{28,20},{1,9},{5... | collective-permute-start | bytes 393224 | tf_op jit(solution)/shard_map/ppermute | solution.py:77
  50.3 0.7 collective-permute-start.7
  51.0 16.0 %collective-permute-start.8 = (bf16[512,128]{1,0:T(8,128)(2,1)S(1)}, bf16[512,128]{1,0:T(8,128)(2,1)S(1)}, u32[]{:S(2)}, u32[]{:S(2)}) collective-permute-start(bf16[512,128]{1,0:T(8,128)(2,1)S(1)} %add_convert_fusion), channel_id=1, source_target_pairs={{8,0},{12,4},{16,24},{20,28},{9,1},{13,5},{17,25},{21,29},{10,2},{... | collective-permute-start | bytes 393224 | tf_op jit(solution)/shard_map/ppermute | solution.py:199
  68.4 4.8 %copy-start.1 = (bf16[4,512,512]{2,1,0:T(8,128)(2,1)S(1)}, bf16[4,512,512]{2,1,0:T(8,128)(2,1)}, u32[]{:S(2)}) copy-start(bf16[4,512,512]{2,1,0:T(8,128)(2,1)} %all-gather.2.cloned.1.call-done) | copy-start | bytes 6291460
  70.6 2.6 %collective-permute-start.9 = (bf16[3,512,128]{2,1,0:T(8,128)(2,1)S(1)}, bf16[3,512,128]{2,1,0:T(8,128)(2,1)S(1)}, u32[]{:S(2)}, u32[]{:S(2)}) collective-permute-start(bf16[3,512,128]{2,1,0:T(8,128)(2,1)S(1)} %convolution_convert_fusion.1), channel_id=1, source_target_pairs={{0,1},{4,5},{8,9},{12,13},{16,17},{20,21},{24,25},{28,29}} | collective-permute-start | bytes 1179656 | tf_op jit(solution)/shard_map/ppermute | solution.py:161
  74.0 0.7 collective-permute-start.10
  75.4 0.7 collective-permute-start.11
  77.4 0.7 collective-permute-start.12
  79.0 0.7 collective-permute-start.13
  80.5 18.0 %collective-permute-start.14 = (bf16[1,512,128]{2,1,0:T(8,128)(2,1)S(1)}, bf16[1,512,128]{2,1,0:T(8,128)(2,1)S(1)}, u32[]{:S(2)}, u32[]{:S(2)}) collective-permute-start(bf16[1,512,128]{2,1,0:T(8,128)(2,1)S(1)} %fusion.7), channel_id=1, source_target_pairs={{1,0},{5,4},{9,8},{13,12},{17,16},{21,20},{25,24},{29,28}} | collective-permute-start | bytes 393224 | tf_op jit(solution)/shard_map/ppermute | solution.py:161
  98.9 6.9 %copy-start.3 = (bf16[576,128]{1,0:T(8,128)(2,1)}, bf16[576,128]{1,0:T(8,128)(2,1)S(1)}, u32[]{:S(2)}) copy-start(bf16[576,128]{1,0:T(8,128)(2,1)S(1)} %pad_maximum_fusion.2.refs_0_) | copy-start | bytes 442372
  98.9 5.5 %collective-permute-start.15 = (bf16[576,128]{1,0:T(8,128)(2,1)S(1)}, bf16[576,128]{1,0:T(8,128)(2,1)S(1)}, u32[]{:S(2)}, u32[]{:S(2)}) collective-permute-start(bf16[576,128]{1,0:T(8,128)(2,1)S(1)} %pad_maximum_fusion.2.refs_0_), channel_id=1, source_target_pairs={{0,1},{1,2},{2,3},{3,0},{4,5},{5,6},{6,7},{7,4},{8,9},{9,10},{10,1... | collective-permute-start | bytes 442376 | tf_op jit(solution)/shard_map/ppermute | solution.py:73
  99.1 6.7 %collective-permute-start.16 = (bf16[576,128]{1,0:T(8,128)(2,1)S(1)}, bf16[576,128]{1,0:T(8,128)(2,1)S(1)}, u32[]{:S(2)}, u32[]{:S(2)}) collective-permute-start(bf16[576,128]{1,0:T(8,128)(2,1)S(1)} %pad_maximum_fusion.2.refs_0_), channel_id=1, source_target_pairs={{0,2},{1,3},{2,0},{3,1},{4,6},{5,7},{6,4},{7,5},{8,10},{9,11},{10,... | collective-permute-start | bytes 442376 | tf_op jit(solution)/shard_map/ppermute | solution.py:73
  99.1 6.7 %collective-permute-start.17 = (bf16[576,128]{1,0:T(8,128)(2,1)S(1)}, bf16[576,128]{1,0:T(8,128)(2,1)S(1)}, u32[]{:S(2)}, u32[]{:S(2)}) collective-permute-start(bf16[576,128]{1,0:T(8,128)(2,1)S(1)} %pad_maximum_fusion.2.refs_0_), channel_id=1, source_target_pairs={{0,3},{1,0},{2,1},{3,2},{4,7},{5,4},{6,5},{7,6},{8,11},{9,8},{10,9... | collective-permute-start | bytes 442376 | tf_op jit(solution)/shard_map/ppermute | solution.py:73
  104.3 1.5 %copy-start.4 = (bf16[576,128]{1,0:T(8,128)(2,1)}, bf16[576,128]{1,0:T(8,128)(2,1)S(1)}, u32[]{:S(2)}) copy-start(bf16[576,128]{1,0:T(8,128)(2,1)S(1)} %collective-permute-done.15.refs_1_) | copy-start | bytes 442372
  105.8 0.6 copy-start.5
  105.8 0.7 copy-start.6
  109.8 5.9 %collective-permute-start.18 = (bf16[512,128]{1,0:T(8,128)(2,1)}, bf16[512,128]{1,0:T(8,128)(2,1)S(1)}, u32[]{:S(2)}, u32[]{:S(2)}) collective-permute-start(bf16[512,128]{1,0:T(8,128)(2,1)} %get-tuple-element.10), channel_id=1, source_target_pairs={{0,3},{1,0},{2,1},{3,2},{4,7},{5,4},{6,5},{7,6},{8,11},{9,8},{10,9... | collective-permute-start | bytes 393224 | tf_op jit(solution)/shard_map/ppermute | solution.py:73
  111.6 9.2 %collective-permute-start.19 = (bf16[512,128]{1,0:T(8,128)(2,1)}, bf16[512,128]{1,0:T(8,128)(2,1)S(1)}, u32[]{:S(2)}, u32[]{:S(2)}) collective-permute-start(bf16[512,128]{1,0:T(8,128)(2,1)} %get-tuple-element.11), channel_id=1, source_target_pairs={{0,2},{1,3},{2,0},{3,1},{4,6},{5,7},{6,4},{7,5},{8,10},{9,11},{10,... | collective-permute-start | bytes 393224 | tf_op jit(solution)/shard_map/ppermute | solution.py:73
  114.0 6.9 %collective-permute-start.20 = (bf16[512,128]{1,0:T(8,128)(2,1)}, bf16[512,128]{1,0:T(8,128)(2,1)S(1)}, u32[]{:S(2)}, u32[]{:S(2)}) collective-permute-start(bf16[512,128]{1,0:T(8,128)(2,1)} %get-tuple-element.12), channel_id=1, source_target_pairs={{0,1},{1,2},{2,3},{3,0},{4,5},{5,6},{6,7},{7,4},{8,9},{9,10},{10,1... | collective-permute-start | bytes 393224 | tf_op jit(solution)/shard_map/ppermute | solution.py:73
  115.7 5.1 %copy-start.7 = (bf16[512,128]{1,0:T(8,128)(2,1)}, bf16[512,128]{1,0:T(8,128)(2,1)S(1)}, u32[]{:S(2)}) copy-start(bf16[512,128]{1,0:T(8,128)(2,1)S(1)} %collective-permute-done.18.refs_1_) | copy-start | bytes 393220
  120.8 0.6 copy-start.8
  120.8 0.7 copy-start.9
Sparse Core Ops, SparseCore 0:
  10.8 53.2 all-gather.1

commit v18 on v16

--- a/solution.py
+++ b/solution.py
@@ -215,9 +215,8 @@
     for j in range(levels - 1):
         index = jnp.where(j < owned, owned * (owned - 1) // 2 + j, (j + 1) * j // 2 + owned)
         pieces.append(lax.dynamic_slice_in_dim(top_tiles, index, 1, 0))
-    mine = jnp.concatenate(pieces, axis=0)
-    mats = lax.all_gather(mine, "row", axis=1, tiled=True)
-    inv = mats[0]
+    inv = lax.all_gather(pieces[0], "row", axis=1, tiled=True)[0]
+    tiles_held = lax.all_gather(jnp.concatenate(pieces[1:], axis=0), "row", axis=1, tiled=True)
 
     slot_rows = tile_rows[0]
     slot_cols = tile_cols[0] % peers
@@ -249,7 +248,7 @@
         top_forward[level] = solved.astype(jnp.bfloat16)
         if level < levels - 1:
             later = jnp.einsum(
-                "kab,bc->kac", mats[level + 1 : levels], top_forward[level], preferred_element_type=jnp.float32
+                "kab,bc->kac", tiles_held[level : levels - 1], top_forward[level], preferred_element_type=jnp.float32
             )
             pushed = later if level == 0 else pushed[1:] + later
     own_solution = None
@@ -264,7 +263,7 @@
         own_solution = solved if own_solution is None else jnp.where(me == level, solved, own_solution)
         if level > 0:
             earlier = jnp.einsum(
-                "uab,ac->ubc", mats[1 : level + 1], solved.astype(jnp.bfloat16), preferred_element_type=jnp.float32
+                "uab,ac->ubc", tiles_held[0:level], solved.astype(jnp.bfloat16), preferred_element_type=jnp.float32
             )
             pushed = earlier if level == levels - 1 else pushed[:level] + earlier
     high = own_solution.astype(jnp.bfloat16)

time: 130 us -> 147 us (1.13)
  blocking collectives: 0 us -> 36.2 us
  waiting for transfers between devices: 67.8 us -> 45.3 us
  starting transfers between devices: 21.4 us -> 25.5 us
    all_gather x0 -> x1, blocking collectives: none -> 36.2 us  [local(): inv = lax.all_gather(pieces[0], 'row', axis=1, tiled=True)[0]]
    ppermute x5, waiting for transfers between devices: 32.1 us -> 12.1 us  [swapped(): return lax.ppermute(x, axis, [(i, i ^ bit) for i in range(size)])]
    ppermute x5, starting transfers between devices: 6.46 us -> 10.7 us  [swapped(): return lax.ppermute(x, axis, [(i, i ^ bit) for i in range(size)])]
    ppermute x9, waiting for transfers between devices: 16.7 us -> 15.1 us  [shifted(): return lax.ppermute(x, axis, [(i, (i + shift) % size) for i in range(size)])]
  transfers between devices with their start and end apart: 21 -> 21, of which waited for: 14 -> 11; matrix products, arithmetic and copies ran while one was open for 5% -> 5% of each run, Pallas kernels for 2% -> 2%
where the time goes in v18:
time: 147 us; the launch traced here: 146 us
  waiting for transfers between devices  45.3 us (31%)
  blocking collectives  36.2 us (25%)
  starting transfers between devices  25.5 us (17%)
  between operations  14.4 us (10%)
  Pallas kernels  8.6 us (6%)
  matrix products  8.25 us (6%)
  other arithmetic  4.85 us (3%)
  local copies, waits for them, and re-layouts  3.32 us (2%)
    all_gather x1, blocking collectives, local(): inv = lax.all_gather(pieces[0], 'row', axis=1, tiled=True)[0]  36.2 us
    ppermute x6, waiting for transfers between devices, hop(): sent = lax.ppermute(x.astype(jnp.bfloat16), 'col', [(source, target)])  18 us
    ppermute x9, waiting for transfers between devices, shifted(): return lax.ppermute(x, axis, [(i, (i + shift) % size) for i in range(size)])  15.1 us
    ppermute x5, waiting for transfers between devices, swapped(): return lax.ppermute(x, axis, [(i, i ^ bit) for i in range(size)])  12.1 us
    ppermute x5, starting transfers between devices, swapped(): return lax.ppermute(x, axis, [(i, i ^ bit) for i in range(size)])  10.7 us
    ppermute x9, starting transfers between devices, shifted(): return lax.ppermute(x, axis, [(i, (i + shift) % size) for i in range(size)])  9.25 us
    ppermute x6, starting transfers between devices, hop(): sent = lax.ppermute(x.astype(jnp.bfloat16), 'col', [(source, target)])  5.45 us
    pallas_call x1, Pallas kernels, tail_terms(): pl.pallas_call(functools.partial(tail_kernel, levels, peers), out_shape=o...  3.28 us
  transfers between devices with their start and end apart: 21, of which 11 were waited for; matrix products, arithmetic and copies ran while one was open for 5% of the time, Pallas kernels for 2%

profile of v18, /device:TPU:0, one launch (start us, length us, event | category | flops | bytes accessed | tf_op | source)
XLA Modules:
  0.0 146.4 jit_solution(12128374016175730254)
XLA Ops:
  7.2 0.0 all-gather.2.cloned.1.call-start
  7.2 1.4 convolution_convert_fusion.6.forward_ref
  8.6 2.5 %collective-permute-start.2 = (bf16[512,128]{1,0:T(8,128)(2,1)S(1)}, bf16[512,128]{1,0:T(8,128)(2,1)S(1)}, u32[]{:S(2)}, u32[]{:S(2)}) collective-permute-start(bf16[512,128]{1,0:T(8,128)(2,1)S(1)} %convolution_convert_fusion.6.forward_ref), channel_id=1, source_target_pairs={{0,3},{1,0},{2,1},{3,2},{4,7},{5,4},{6,5},{7,6},{8,11},{9,8},{10,9... | collective-permute-start | bytes 393224 | tf_op jit(solution)/shard_map/ppermute | solution.py:73
  11.1 0.6 collective-permute-start.1
  11.8 0.2 collective-permute-start
  11.9 0.9 constant_dynamic-slice_fusion.2
  12.8 0.7 pad_maximum_fusion.1
  13.5 0.0 all-gather.2.cloned.1.call-update
  13.6 0.6 and_select_fusion.1
  14.2 0.7 iota_reduce_fusion
  14.9 0.6 pad_add_fusion.fold_ref
  15.5 3.2 %collective-permute-done.1 = bf16[512,128]{1,0:T(8,128)(2,1)S(1)} collective-permute-done((bf16[512,128]{1,0:T(8,128)(2,1)S(1)}, bf16[512,128]{1,0:T(8,128)(2,1)S(1)}, u32[]{:S(2)}, u32[]{:S(2)}) %collective-permute-start.1) | collective-permute-done | bytes 131104 | tf_op jit(solution)/shard_map/ppermute | solution.py:73
  18.7 0.9 pad_maximum_fusion.panels_ref
  19.5 3.0 %shard_map.95 = bf16[4,512,128]{2,1,0:T(8,128)(2,1)} custom-call(s32[4]{0:T(128)} %bitcast.133, s32[4]{0:T(128)} %get-tuple-element.8.picks_ref, s32[2]{0:T(128)} %pad_add_fusion.fold_ref, bf16[4,512,512]{2,1,0:T(8,128)(2,1)} %bitcast.125, bf16[4,512,128]{2,1,0:T(8,128)(2,1)} %pad_maximum_fusion.panels_ref, bf16[4,64,128]{2,1,0:T(8,128)(2,1)} %rhs_ref.1), custom_call_target="tpu_custom_call" | custom-call | tf_op jit(solution)/shard_map/pallas_call | solution.py:37
  22.6 1.0 dynamic-slice_bitcast_fusion
  23.5 0.1 collective-permute-start.3
  23.7 1.5 %collective-permute-done.3 = bf16[2,512,128]{2,1,0:T(8,128)(2,1)S(1)} collective-permute-done((bf16[2,512,128]{2,1,0:T(8,128)(2,1)S(1)}, bf16[2,512,128]{2,1,0:T(8,128)(2,1)S(1)}, u32[]{:S(2)}, u32[]{:S(2)}) %collective-permute-start.3) | collective-permute-done | bytes 262176 | tf_op jit(solution)/shard_map/ppermute | solution.py:77
  25.1 1.0 fusion.3
  26.2 2.0 %collective-permute-start.4 = (bf16[1,512,128]{2,1,0:T(8,128)(2,1)S(1)}, bf16[1,512,128]{2,1,0:T(8,128)(2,1)S(1)}, u32[]{:S(2)}, u32[]{:S(2)}) collective-permute-start(bf16[1,512,128]{2,1,0:T(8,128)(2,1)S(1)} %constant_dynamic-slice_fusion.3), channel_id=1, source_target_pairs={{0,2},{1,3},{2,0},{3,1},{4,6},{5,7},{6,4},{7,5},{8,10},{9,11},{10,... | collective-permute-start | bytes 393224 | tf_op jit(solution)/shard_map/ppermute | solution.py:77
  28.2 3.8 %collective-permute-done.4 = bf16[1,512,128]{2,1,0:T(8,128)(2,1)S(1)} collective-permute-done((bf16[1,512,128]{2,1,0:T(8,128)(2,1)S(1)}, bf16[1,512,128]{2,1,0:T(8,128)(2,1)S(1)}, u32[]{:S(2)}, u32[]{:S(2)}) %collective-permute-start.4) | collective-permute-done | bytes 131104 | tf_op jit(solution)/shard_map/ppermute | solution.py:77
  32.0 1.6 %collective-permute-start.5 = (bf16[512,128]{1,0:T(8,128)(2,1)S(1)}, bf16[512,128]{1,0:T(8,128)(2,1)S(1)}, u32[]{:S(2)}, u32[]{:S(2)}) collective-permute-start(bf16[512,128]{1,0:T(8,128)(2,1)S(1)} %fusion.28), channel_id=1, source_target_pairs={{0,4},{4,0},{8,12},{12,8},{16,20},{20,16},{24,28},{28,24},{1,5},{5... | collective-permute-start | bytes 393224 | tf_op jit(solution)/shard_map/ppermute | solution.py:77
  33.6 3.5 %collective-permute-done.5 = bf16[512,128]{1,0:T(8,128)(2,1)S(1)} collective-permute-done((bf16[512,128]{1,0:T(8,128)(2,1)S(1)}, bf16[512,128]{1,0:T(8,128)(2,1)S(1)}, u32[]{:S(2)}, u32[]{:S(2)}) %collective-permute-start.5) | collective-permute-done | bytes 131104 | tf_op jit(solution)/shard_map/ppermute | solution.py:77
  37.1 1.6 %collective-permute-start.6 = (bf16[512,128]{1,0:T(8,128)(2,1)S(1)}, bf16[512,128]{1,0:T(8,128)(2,1)S(1)}, u32[]{:S(2)}, u32[]{:S(2)}) collective-permute-start(bf16[512,128]{1,0:T(8,128)(2,1)S(1)} %add_convert_fusion.2), channel_id=1, source_target_pairs={{0,8},{4,12},{8,0},{12,4},{16,24},{20,28},{24,16},{28,20},{1,9},{5... | collective-permute-start | bytes 393224 | tf_op jit(solution)/shard_map/ppermute | solution.py:77
  38.8 3.4 %collective-permute-done.6 = bf16[512,128]{1,0:T(8,128)(2,1)S(1)} collective-permute-done((bf16[512,128]{1,0:T(8,128)(2,1)S(1)}, bf16[512,128]{1,0:T(8,128)(2,1)S(1)}, u32[]{:S(2)}, u32[]{:S(2)}) %collective-permute-start.6) | collective-permute-done | bytes 131104 | tf_op jit(solution)/shard_map/ppermute | solution.py:77
  42.2 5.5 %collective-permute-start.7 = (bf16[512,128]{1,0:T(8,128)(2,1)S(1)}, bf16[512,128]{1,0:T(8,128)(2,1)S(1)}, u32[]{:S(2)}, u32[]{:S(2)}) collective-permute-start(bf16[512,128]{1,0:T(8,128)(2,1)S(1)} %add_convert_fusion.1), channel_id=1, source_target_pairs={{0,16},{4,20},{8,24},{12,28},{16,0},{20,4},{24,8},{28,12},{1,17},{... | collective-permute-start | bytes 393224 | tf_op jit(solution)/shard_map/ppermute | solution.py:77
  47.7 36.2 %all_gather.6 = bf16[1,512,512]{2,1,0:T(8,128)(2,1)S(1)} all-gather(bf16[1,64,512]{2,1,0:T(8,128)(2,1)S(1)} %constant_dynamic-slice_fusion.4), channel_id=1, replica_groups=mesh['row'=8,'col'=4] {'row'}, dimensions={1}, use_global_device_ids=true | all-gather | bytes 589824 | tf_op jit(solution)/shard_map/all_gather | solution.py:218
  83.9 0.3 convolution_convert_fusion.5
  84.2 0.0 all-gather.2.cloned.1.call-done
  84.2 2.0 %convolution_convert_fusion.1 = bf16[3,512,128]{2,1,0:T(8,128)(2,1)S(1)} fusion(bf16[3,512,512]{2,1,0:T(8,128)(2,1)} %all-gather.2.cloned.1.call-done, bf16[512,128]{1,0:T(8,128)(2,1)S(1)} %convolution_convert_fusion.5), kind=kOutput, calls=%fused_computation.1 | convolution fusion | flops 201523200 | bytes 2097152 | tf_op jit(solution)/shard_map/kab,bc->kac/dot_general | solution.py:250
  86.2 1.4 collective-permute-start.8
  87.6 1.3 collective-permute-done.8
  89.0 0.1 convert_element_type.172
  89.0 0.3 convolution_convert_fusion.4
  89.3 0.5 fusion.2
  89.8 0.7 collective-permute-start.9
  90.5 0.3 convolution_convert_fusion.3
  90.8 0.3 fusion.22
  91.1 0.7 collective-permute-start.10
  91.8 0.7 fusion
  92.6 0.6 convolution_convert_fusion
  93.2 0.7 collective-permute-start.11
  93.9 0.1 convert_element_type.184
  94.0 0.3 fusion.6
  94.3 0.5 fusion.1
  94.8 0.7 collective-permute-start.12
  95.6 0.3 fusion.4
  95.9 0.3 fusion.17
  96.3 1.3 collective-permute-start.13
  97.6 16.7 %collective-permute-done.13 = bf16[1,512,128]{2,1,0:T(8,128)(2,1)S(1)} collective-permute-done((bf16[1,512,128]{2,1,0:T(8,128)(2,1)S(1)}, bf16[1,512,128]{2,1,0:T(8,128)(2,1)S(1)}, u32[]{:S(2)}, u32[]{:S(2)}) %collective-permute-start.13) | collective-permute-done | bytes 131104 | tf_op jit(solution)/shard_map/ppermute | solution.py:161
  114.2 0.3 fusion.60
  114.7 0.2 collective-permute-start.14
  114.9 1.6 %collective-permute-start.16 = (bf16[576,128]{1,0:T(8,128)(2,1)S(1)}, bf16[576,128]{1,0:T(8,128)(2,1)S(1)}, u32[]{:S(2)}, u32[]{:S(2)}) collective-permute-start(bf16[576,128]{1,0:T(8,128)(2,1)S(1)} %pad_maximum_fusion.2.refs_0_), channel_id=1, source_target_pairs={{0,3},{1,0},{2,1},{3,2},{4,7},{5,4},{6,5},{7,6},{8,11},{9,8},{10,9... | collective-permute-start | bytes 442376 | tf_op jit(solution)/shard_map/ppermute | solution.py:73
  116.5 3.7 %collective-permute-done.14.refs_1_ = bf16[576,128]{1,0:T(8,128)(2,1)S(1)} collective-permute-done((bf16[576,128]{1,0:T(8,128)(2,1)S(1)}, bf16[576,128]{1,0:T(8,128)(2,1)S(1)}, u32[]{:S(2)}, u32[]{:S(2)}) %collective-permute-start.14) | collective-permute-done | bytes 147488 | tf_op jit(solution)/shard_map/ppermute | solution.py:73
  120.1 1.4 collective-permute-done.15.refs_2_
  121.6 0.6 copy-done.5
  122.2 0.1 copy-done.6
  122.3 3.3 %shard_map.96 = (bf16[512,128]{1,0:T(8,128)(2,1)}, bf16[512,128]{1,0:T(8,128)(2,1)}, bf16[512,128]{1,0:T(8,128)(2,1)}, bf16[512,128]{1,0:T(8,128)(2,1)}, f32[4,64,128]{2,1,0:T(8,128)}) custom-call(s32[4]{0:T(128)} %bitcast.134, s32[4]{0:T(128)} %get-tuple-element.14.dests_ref, s32[4]{0:T(128)} %copy-done.10, s32[1]{0:T(128)} %bitcast.4.start_ref, ...), custom_call_target="tpu_custom_call" | custom-call | tf_op jit(solution)/shard_map/pallas_call | solution.py:129
  125.6 1.9 %collective-permute-start.17 = (bf16[512,128]{1,0:T(8,128)(2,1)}, bf16[512,128]{1,0:T(8,128)(2,1)S(1)}, u32[]{:S(2)}, u32[]{:S(2)}) collective-permute-start(bf16[512,128]{1,0:T(8,128)(2,1)} %get-tuple-element.10), channel_id=1, source_target_pairs={{0,3},{1,0},{2,1},{3,2},{4,7},{5,4},{6,5},{7,6},{8,11},{9,8},{10,9... | collective-permute-start | bytes 393224 | tf_op jit(solution)/shard_map/ppermute | solution.py:73
  127.4 2.3 %collective-permute-start.18 = (bf16[512,128]{1,0:T(8,128)(2,1)}, bf16[512,128]{1,0:T(8,128)(2,1)S(1)}, u32[]{:S(2)}, u32[]{:S(2)}) collective-permute-start(bf16[512,128]{1,0:T(8,128)(2,1)} %get-tuple-element.11), channel_id=1, source_target_pairs={{0,2},{1,3},{2,0},{3,1},{4,6},{5,7},{6,4},{7,5},{8,10},{9,11},{10,... | collective-permute-start | bytes 393224 | tf_op jit(solution)/shard_map/ppermute | solution.py:73
  129.7 1.8 %collective-permute-done.17.refs_1_ = bf16[512,128]{1,0:T(8,128)(2,1)S(1)} collective-permute-done((bf16[512,128]{1,0:T(8,128)(2,1)}, bf16[512,128]{1,0:T(8,128)(2,1)S(1)}, u32[]{:S(2)}, u32[]{:S(2)}) %collective-permute-start.17) | collective-permute-done | bytes 131104 | tf_op jit(solution)/shard_map/ppermute | solution.py:73
  131.5 5.0 %collective-permute-done.18.refs_2_ = bf16[512,128]{1,0:T(8,128)(2,1)S(1)} collective-permute-done((bf16[512,128]{1,0:T(8,128)(2,1)}, bf16[512,128]{1,0:T(8,128)(2,1)S(1)}, u32[]{:S(2)}, u32[]{:S(2)}) %collective-permute-start.18) | collective-permute-done | bytes 131104 | tf_op jit(solution)/shard_map/ppermute | solution.py:73
  136.6 0.6 copy-done.8
  137.2 0.0 copy-done.9
  137.3 2.3 %shard_map.97 = f32[1,512,128]{2,1,0:T(8,128)} custom-call(bf16[512,128]{1,0:T(8,128)(2,1)} %copy-done.2, bf16[1,512,512]{2,1,0:T(8,128)(2,1)} %inv_ref.1, bf16[512,128]{1,0:T(8,128)(2,1)} %get-tuple-element.9.refs_0_, bf16[512,128]{1,0:T(8,128)(2,1)} %copy-done.7, bf16[512,128]{1,0:T(8,128)(2,1)} %copy-done.8, bf16[512,128]{1,0:T(8,128)(2,1)} %copy-done.9), custom_call_target="tpu_custom_call" | custom-call | tf_op jit(solution)/shard_map/pallas_call | solution.py:152
  (42 shorter events, 0.4 us)
Async XLA Ops:
  7.2 31.6 %copy-start = (bf16[4,64,512]{2,1,0:T(8,128)(2,1)S(1)}, bf16[4,64,512]{2,1,0:T(8,128)(2,1)}, u32[]{:S(2)}) copy-start(bf16[4,64,512]{2,1,0:T(8,128)(2,1)} %param.14) | copy-start | bytes 786436
  7.2 6.4 %copy-start.11 = (s32[1,4]{1,0:T(1,128)S(1)}, s32[1,4]{1,0:T(1,128)}, u32[]{:S(2)}) copy-start(s32[1,4]{1,0:T(1,128)} %param.12) | copy-start | bytes 52
  7.2 77.0 %all-gather.2.cloned.1.call-start = ((), (), s32[]{:S(2)}) async-start(), calls=%async_computation | async-start | bytes 1769472 | tf_op jit(solution)/shard_map/all_gather | solution.py:219
  8.6 13.9 %copy-start.2 = (bf16[512,128]{1,0:T(8,128)(2,1)}, bf16[512,128]{1,0:T(8,128)(2,1)S(1)}, u32[]{:S(2)}) copy-start(bf16[512,128]{1,0:T(8,128)(2,1)S(1)} %convolution_convert_fusion.6.forward_ref) | copy-start | bytes 393220
  8.6 6.9 %collective-permute-start.2 = (bf16[512,128]{1,0:T(8,128)(2,1)S(1)}, bf16[512,128]{1,0:T(8,128)(2,1)S(1)}, u32[]{:S(2)}, u32[]{:S(2)}) collective-permute-start(bf16[512,128]{1,0:T(8,128)(2,1)S(1)} %convolution_convert_fusion.6.forward_ref), channel_id=1, source_target_pairs={{0,3},{1,0},{2,1},{3,2},{4,7},{5,4},{6,5},{7,6},{8,11},{9,8},{10,9... | collective-permute-start | bytes 393224 | tf_op jit(solution)/shard_map/ppermute | solution.py:73
  11.1 7.5 %collective-permute-start.1 = (bf16[512,128]{1,0:T(8,128)(2,1)S(1)}, bf16[512,128]{1,0:T(8,128)(2,1)S(1)}, u32[]{:S(2)}, u32[]{:S(2)}) collective-permute-start(bf16[512,128]{1,0:T(8,128)(2,1)S(1)} %convolution_convert_fusion.6.forward_ref), channel_id=1, source_target_pairs={{0,2},{1,3},{2,0},{3,1},{4,6},{5,7},{6,4},{7,5},{8,10},{9,11},{10,... | collective-permute-start | bytes 393224 | tf_op jit(solution)/shard_map/ppermute | solution.py:73
  11.8 6.9 %collective-permute-start = (bf16[512,128]{1,0:T(8,128)(2,1)S(1)}, bf16[512,128]{1,0:T(8,128)(2,1)S(1)}, u32[]{:S(2)}, u32[]{:S(2)}) collective-permute-start(bf16[512,128]{1,0:T(8,128)(2,1)S(1)} %convolution_convert_fusion.6.forward_ref), channel_id=1, source_target_pairs={{0,1},{1,2},{2,3},{3,0},{4,5},{5,6},{6,7},{7,4},{8,9},{9,10},{10,1... | collective-permute-start | bytes 393224 | tf_op jit(solution)/shard_map/ppermute | solution.py:73
  13.6 9.0 %copy-start.10 = (s32[4]{0:T(128)}, s32[4]{0:T(128)S(1)}, u32[]{:S(2)}) copy-start(s32[4]{0:T(128)S(1)} %and_select_fusion.table_ref) | copy-start | bytes 52
  23.5 1.6 %collective-permute-start.3 = (bf16[2,512,128]{2,1,0:T(8,128)(2,1)S(1)}, bf16[2,512,128]{2,1,0:T(8,128)(2,1)S(1)}, u32[]{:S(2)}, u32[]{:S(2)}) collective-permute-start(bf16[2,512,128]{2,1,0:T(8,128)(2,1)S(1)} %dynamic-slice_bitcast_fusion), channel_id=1, source_target_pairs={{0,1},{1,0},{2,3},{3,2},{4,5},{5,4},{6,7},{7,6},{8,9},{9,8},{10,11... | collective-permute-start | bytes 786440 | tf_op jit(solution)/shard_map/ppermute | solution.py:77
  26.2 5.8 %collective-permute-start.4 = (bf16[1,512,128]{2,1,0:T(8,128)(2,1)S(1)}, bf16[1,512,128]{2,1,0:T(8,128)(2,1)S(1)}, u32[]{:S(2)}, u32[]{:S(2)}) collective-permute-start(bf16[1,512,128]{2,1,0:T(8,128)(2,1)S(1)} %constant_dynamic-slice_fusion.3), channel_id=1, source_target_pairs={{0,2},{1,3},{2,0},{3,1},{4,6},{5,7},{6,4},{7,5},{8,10},{9,11},{10,... | collective-permute-start | bytes 393224 | tf_op jit(solution)/shard_map/ppermute | solution.py:77
  32.0 5.0 %collective-permute-start.5 = (bf16[512,128]{1,0:T(8,128)(2,1)S(1)}, bf16[512,128]{1,0:T(8,128)(2,1)S(1)}, u32[]{:S(2)}, u32[]{:S(2)}) collective-permute-start(bf16[512,128]{1,0:T(8,128)(2,1)S(1)} %fusion.28), channel_id=1, source_target_pairs={{0,4},{4,0},{8,12},{12,8},{16,20},{20,16},{24,28},{28,24},{1,5},{5... | collective-permute-start | bytes 393224 | tf_op jit(solution)/shard_map/ppermute | solution.py:77
  37.1 5.0 %collective-permute-start.6 = (bf16[512,128]{1,0:T(8,128)(2,1)S(1)}, bf16[512,128]{1,0:T(8,128)(2,1)S(1)}, u32[]{:S(2)}, u32[]{:S(2)}) collective-permute-start(bf16[512,128]{1,0:T(8,128)(2,1)S(1)} %add_convert_fusion.2), channel_id=1, source_target_pairs={{0,8},{4,12},{8,0},{12,4},{16,24},{20,28},{24,16},{28,20},{1,9},{5... | collective-permute-start | bytes 393224 | tf_op jit(solution)/shard_map/ppermute | solution.py:77
  42.2 41.7 %collective-permute-start.7 = (bf16[512,128]{1,0:T(8,128)(2,1)S(1)}, bf16[512,128]{1,0:T(8,128)(2,1)S(1)}, u32[]{:S(2)}, u32[]{:S(2)}) collective-permute-start(bf16[512,128]{1,0:T(8,128)(2,1)S(1)} %add_convert_fusion.1), channel_id=1, source_target_pairs={{0,16},{4,20},{8,24},{12,28},{16,0},{20,4},{24,8},{28,12},{1,17},{... | collective-permute-start | bytes 393224 | tf_op jit(solution)/shard_map/ppermute | solution.py:77
  86.2 3.1 %copy-start.1 = (bf16[3,512,512]{2,1,0:T(8,128)(2,1)S(1)}, bf16[3,512,512]{2,1,0:T(8,128)(2,1)}, u32[]{:S(2)}) copy-start(bf16[3,512,512]{2,1,0:T(8,128)(2,1)} %all-gather.2.cloned.1.call-done) | copy-start | bytes 4718596
  86.2 2.8 %collective-permute-start.8 = (bf16[3,512,128]{2,1,0:T(8,128)(2,1)S(1)}, bf16[3,512,128]{2,1,0:T(8,128)(2,1)S(1)}, u32[]{:S(2)}, u32[]{:S(2)}) collective-permute-start(bf16[3,512,128]{2,1,0:T(8,128)(2,1)S(1)} %convolution_convert_fusion.1), channel_id=1, source_target_pairs={{0,1},{4,5},{8,9},{12,13},{16,17},{20,21},{24,25},{28,29}} | collective-permute-start | bytes 1179656 | tf_op jit(solution)/shard_map/ppermute | solution.py:161
  89.8 0.7 collective-permute-start.9
  91.1 0.7 collective-permute-start.10
  93.2 0.7 collective-permute-start.11
  94.8 0.7 collective-permute-start.12
  96.3 18.0 %collective-permute-start.13 = (bf16[1,512,128]{2,1,0:T(8,128)(2,1)S(1)}, bf16[1,512,128]{2,1,0:T(8,128)(2,1)S(1)}, u32[]{:S(2)}, u32[]{:S(2)}) collective-permute-start(bf16[1,512,128]{2,1,0:T(8,128)(2,1)S(1)} %fusion.17), channel_id=1, source_target_pairs={{1,0},{5,4},{9,8},{13,12},{17,16},{21,20},{25,24},{29,28}} | collective-permute-start | bytes 393224 | tf_op jit(solution)/shard_map/ppermute | solution.py:161
  114.6 6.9 %copy-start.3 = (bf16[576,128]{1,0:T(8,128)(2,1)}, bf16[576,128]{1,0:T(8,128)(2,1)S(1)}, u32[]{:S(2)}) copy-start(bf16[576,128]{1,0:T(8,128)(2,1)S(1)} %pad_maximum_fusion.2.refs_0_) | copy-start | bytes 442372
  114.7 5.5 %collective-permute-start.14 = (bf16[576,128]{1,0:T(8,128)(2,1)S(1)}, bf16[576,128]{1,0:T(8,128)(2,1)S(1)}, u32[]{:S(2)}, u32[]{:S(2)}) collective-permute-start(bf16[576,128]{1,0:T(8,128)(2,1)S(1)} %pad_maximum_fusion.2.refs_0_), channel_id=1, source_target_pairs={{0,1},{1,2},{2,3},{3,0},{4,5},{5,6},{6,7},{7,4},{8,9},{9,10},{10,1... | collective-permute-start | bytes 442376 | tf_op jit(solution)/shard_map/ppermute | solution.py:73
  114.9 6.7 %collective-permute-start.15 = (bf16[576,128]{1,0:T(8,128)(2,1)S(1)}, bf16[576,128]{1,0:T(8,128)(2,1)S(1)}, u32[]{:S(2)}, u32[]{:S(2)}) collective-permute-start(bf16[576,128]{1,0:T(8,128)(2,1)S(1)} %pad_maximum_fusion.2.refs_0_), channel_id=1, source_target_pairs={{0,2},{1,3},{2,0},{3,1},{4,6},{5,7},{6,4},{7,5},{8,10},{9,11},{10,... | collective-permute-start | bytes 442376 | tf_op jit(solution)/shard_map/ppermute | solution.py:73
  114.9 6.7 %collective-permute-start.16 = (bf16[576,128]{1,0:T(8,128)(2,1)S(1)}, bf16[576,128]{1,0:T(8,128)(2,1)S(1)}, u32[]{:S(2)}, u32[]{:S(2)}) collective-permute-start(bf16[576,128]{1,0:T(8,128)(2,1)S(1)} %pad_maximum_fusion.2.refs_0_), channel_id=1, source_target_pairs={{0,3},{1,0},{2,1},{3,2},{4,7},{5,4},{6,5},{7,6},{8,11},{9,8},{10,9... | collective-permute-start | bytes 442376 | tf_op jit(solution)/shard_map/ppermute | solution.py:73
  120.1 1.5 copy-start.4
  121.6 0.7 copy-start.5
  121.6 0.7 copy-start.6
  125.6 6.0 %collective-permute-start.17 = (bf16[512,128]{1,0:T(8,128)(2,1)}, bf16[512,128]{1,0:T(8,128)(2,1)S(1)}, u32[]{:S(2)}, u32[]{:S(2)}) collective-permute-start(bf16[512,128]{1,0:T(8,128)(2,1)} %get-tuple-element.10), channel_id=1, source_target_pairs={{0,3},{1,0},{2,1},{3,2},{4,7},{5,4},{6,5},{7,6},{8,11},{9,8},{10,9... | collective-permute-start | bytes 393224 | tf_op jit(solution)/shard_map/ppermute | solution.py:73
  127.4 9.2 %collective-permute-start.18 = (bf16[512,128]{1,0:T(8,128)(2,1)}, bf16[512,128]{1,0:T(8,128)(2,1)S(1)}, u32[]{:S(2)}, u32[]{:S(2)}) collective-permute-start(bf16[512,128]{1,0:T(8,128)(2,1)} %get-tuple-element.11), channel_id=1, source_target_pairs={{0,2},{1,3},{2,0},{3,1},{4,6},{5,7},{6,4},{7,5},{8,10},{9,11},{10,... | collective-permute-start | bytes 393224 | tf_op jit(solution)/shard_map/ppermute | solution.py:73
  129.7 6.9 %collective-permute-start.19 = (bf16[512,128]{1,0:T(8,128)(2,1)}, bf16[512,128]{1,0:T(8,128)(2,1)S(1)}, u32[]{:S(2)}, u32[]{:S(2)}) collective-permute-start(bf16[512,128]{1,0:T(8,128)(2,1)} %get-tuple-element.12), channel_id=1, source_target_pairs={{0,1},{1,2},{2,3},{3,0},{4,5},{5,6},{6,7},{7,4},{8,9},{9,10},{10,1... | collective-permute-start | bytes 393224 | tf_op jit(solution)/shard_map/ppermute | solution.py:73
  131.5 5.1 %copy-start.7 = (bf16[512,128]{1,0:T(8,128)(2,1)}, bf16[512,128]{1,0:T(8,128)(2,1)S(1)}, u32[]{:S(2)}) copy-start(bf16[512,128]{1,0:T(8,128)(2,1)S(1)} %collective-permute-done.17.refs_1_) | copy-start | bytes 393220
  136.6 0.6 copy-start.8
  136.6 0.7 copy-start.9
Sparse Core Ops, SparseCore 0:
  13.7 49.8 all-gather.1
